TPU v7x, 256 devices: a whole 4x4x8 slice. The times are simulated.
256 devices in a mesh: gx: 8 (over y, core), gy: 16 (over x_lo, z), src: 2 (over x_hi).
Axes of the slice: x: 4 (x_hi: 2, x_lo: 2; x = x_hi * 2 + x_lo), y: 4, z: 8, core: 2. Of those that a mesh axis runs over, the one named last changes fastest.
Arguments:
- conductivity: float32 [16, 128, 128], P('gx', 'gy'), may hold values from 0.3 to 3
- electrodes: int32 [128, 2], replicated, may hold values from 0 to 262143
- pair_order: int32 [128], P('src'), may hold values from 0 to 127, each once
- initial_fields: float32 [128, 16, 128, 128], P('src', 'gx', 'gy'), as said below
- adjoint_fields: float32 [128, 16, 128, 128], P('src', 'gx', 'gy'), may hold values from -6 to 6
Outputs:
- potentials: float32 [128, 16, 128, 128], P('src', 'gx', 'gy')
- gradient: float32 [16, 128, 128], P('gx', 'gy', 'src')
Inputs may be any that keep to these rules, and one draw needn't show every extreme that they name: `electrodes`: flat cell index (x * 128 + y) * 128 + z. `pair_order`: each pair appears once. `initial_fields`: every entry lies within 6 / sqrt(262144) in magnitude.
All inputs are finite; a program needn't handle non-finite values.
Results may differ from a plain program's by a relative error of at most 0.00029.
Values sent between devices are 32-bit elements; how exact they have to be, the bound alone decides.
No kernel may reach another device: no remote copies, remote signals or barrier semaphores. Data moves between devices by JAX's collectives and lax.ppermute only.
A program may use at most 64 MiB of HBM per device.

v0:
```python
import jax
import jax.numpy as jnp
from jax import lax
from jax.sharding import PartitionSpec as P

ITERS = 2


INJECT = 4.0


def padded_2(block, sides, width):
    for axis, dim in sides:
        count = lax.axis_size(axis)
        forward = [(i, i + 1) for i in range(count - 1)]
        backward = [(target, source) for source, target in forward]
        low = lax.ppermute(
            lax.slice_in_dim(block, block.shape[dim] - width, None, axis=dim), axis, forward
        )
        high = lax.ppermute(lax.slice_in_dim(block, 0, width, axis=dim), axis, backward)
        block = jnp.concatenate([low, block, high], axis=dim)
    return block


def conductances(sig_pad):
    full = jnp.pad(sig_pad, ((0, 0), (0, 0), (1, 1)))
    cond_x = 0.5 * (full[1:, 1:-1, 1:-1] + full[:-1, 1:-1, 1:-1])
    cond_y = 0.5 * (full[1:-1, 1:, 1:-1] + full[1:-1, :-1, 1:-1])
    cond_z = 0.5 * (full[1:-1, 1:-1, 1:] + full[1:-1, 1:-1, :-1])
    return (cond_x, cond_y, cond_z)


def operator(padded, conds):
    full = jnp.pad(padded, ((0, 0), (0, 0), (0, 0), (1, 1)))
    flux_x = conds[0] * (full[:, 1:, 1:-1, 1:-1] - full[:, :-1, 1:-1, 1:-1])
    flux_y = conds[1] * (full[:, 1:-1, 1:, 1:-1] - full[:, 1:-1, :-1, 1:-1])
    flux_z = conds[2] * (full[:, 1:-1, 1:-1, 1:] - full[:, 1:-1, 1:-1, :-1])
    return (
        flux_x[:, :-1]
        - flux_x[:, 1:]
        + (flux_y[:, :, :-1] - flux_y[:, :, 1:])
        + (flux_z[..., :-1] - flux_z[..., 1:])
    )


def gram_of(left, right):
    return jnp.einsum("axyz,bxyz->ab", left, right, precision=lax.Precision.HIGHEST)


def combine_cols(field, matrix):
    return jnp.einsum("axyz,ab->bxyz", field, matrix, precision=lax.Precision.HIGHEST)


def posdef_solve(matrix, right):
    lower = jnp.linalg.cholesky(matrix)
    middle = lax.linalg.triangular_solve(lower, right, left_side=True, lower=True)
    return lax.linalg.triangular_solve(lower, middle, left_side=True, lower=True, transpose_a=True)


def one_hot(cells, start, count):
    return (cells[:, None] == start + jnp.arange(count, dtype=jnp.int32)[None, :]).astype(
        jnp.float32
    )


def face_terms(field_pad, adjoint_pad):
    fu = jnp.pad(field_pad, ((0, 0), (0, 0), (0, 0), (1, 1)))
    fl = jnp.pad(adjoint_pad, ((0, 0), (0, 0), (0, 0), (1, 1)))
    term_x = jnp.sum(
        (fu[:, 1:, 1:-1, 1:-1] - fu[:, :-1, 1:-1, 1:-1])
        * (fl[:, 1:, 1:-1, 1:-1] - fl[:, :-1, 1:-1, 1:-1]),
        axis=0,
    )
    term_y = jnp.sum(
        (fu[:, 1:-1, 1:, 1:-1] - fu[:, 1:-1, :-1, 1:-1])
        * (fl[:, 1:-1, 1:, 1:-1] - fl[:, 1:-1, :-1, 1:-1]),
        axis=0,
    )
    term_z = jnp.sum(
        (fu[:, 1:-1, 1:-1, 1:] - fu[:, 1:-1, 1:-1, :-1])
        * (fl[:, 1:-1, 1:-1, 1:] - fl[:, 1:-1, 1:-1, :-1]),
        axis=0,
    )
    return (term_x, term_y, term_z)


def on_device(conductivity, electrodes, pair_order, initial_fields, adjoint_fields):
    cells_x, cells_y, cells_z = conductivity.shape
    columns = initial_fields.shape[0]
    total_y = lax.axis_size("gy") * cells_y
    start_x = lax.axis_index("gx") * cells_x
    start_y = lax.axis_index("gy") * cells_y
    picked = jnp.take(electrodes, pair_order, axis=0)

    def point_source(flat):
        xs = flat // (total_y * cells_z)
        ys = flat // cells_z % total_y
        zs = flat % cells_z
        return jnp.einsum(
            "cx,cy,cz->cxyz",
            one_hot(xs, start_x, cells_x),
            one_hot(ys, start_y, cells_y),
            one_hot(zs, 0, cells_z),
        )

    right = INJECT * (point_source(picked[:, 0]) - point_source(picked[:, 1]))
    stacked = jnp.concatenate([conductivity[None], initial_fields], axis=0)
    padded = padded_2(stacked, (("gx", 1), ("gy", 2)), 1)
    conds = conductances(padded[0])
    iterate = initial_fields
    iter_pad = padded[1:]
    residual = right - operator(iter_pad, conds)
    direction = residual
    res_gram = lax.psum(gram_of(residual, residual), ("gx", "gy"))
    for iteration in range(ITERS):
        dir_pad = padded_2(direction, (("gx", 1), ("gy", 2)), 1)
        image = operator(dir_pad, conds)
        curv_gram = lax.psum(gram_of(direction, image), ("gx", "gy"))
        step_mat = posdef_solve(curv_gram, res_gram)
        iterate = iterate + combine_cols(direction, step_mat)
        residual = residual - combine_cols(image, step_mat)
        if iteration + 1 < ITERS:
            new_gram = lax.psum(gram_of(residual, residual), ("gx", "gy"))
            turn_mat = posdef_solve(res_gram, new_gram)
            direction = residual + combine_cols(direction, turn_mat)
            res_gram = new_gram
    both = jnp.concatenate([iterate, adjoint_fields], axis=0)
    both_pad = padded_2(both, (("gx", 1), ("gy", 2)), 1)
    term_x, term_y, term_z = face_terms(both_pad[:columns], both_pad[columns:])
    local_grad = (
        -0.5
        / columns
        * (
            term_x[:-1]
            + term_x[1:]
            + term_y[:, :-1]
            + term_y[:, 1:]
            + term_z[..., :-1]
            + term_z[..., 1:]
        )
    )
    share = cells_z // lax.axis_size("src")
    summed = lax.psum(local_grad, "src")
    gradient = lax.dynamic_slice_in_dim(summed, lax.axis_index("src") * share, share, 2)
    return (iterate, gradient)


def solution(mesh):
    placed = (
        P("gx", "gy", None),
        P(),
        P("src"),
        P("src", "gx", "gy", None),
        P("src", "gx", "gy", None),
    )
    return jax.shard_map(
        on_device,
        mesh=mesh,
        in_specs=placed,
        out_specs=(P("src", "gx", "gy", None), P("gx", "gy", "src")),
        check_vma=False,
    )
```

profile of v0, /device:TPU:4, one launch (start us, length us, event | category | flops | bytes accessed | tf_op | source)
XLA Modules:
  0.0 1779.5 jit_solution(18146952785579994291)
XLA Ops:
  0.6 1.2 copy.47
  1.9 0.8 fusion.36
  2.6 1.8 collective-permute-start
  4.4 1.3 collective-permute-start.1
  5.7 0.7 compare_select_fusion
  6.3 0.7 compare_and_fusion
  7.0 0.8 copy.37
  9.2 3.8 collective-permute-start.2
  13.1 1.3 collective-permute-start.3
  14.4 1.3 collective-permute-done.2
  15.7 4.4 collective-permute-done.3
  20.3 0.8 select_maximum_fusion.8
  22.2 1.3 collective-permute-start.4
  23.5 6.4 collective-permute-start.5
  31.0 1.3 collective-permute-start.6
  32.3 4.6 collective-permute-start.7
  37.0 0.9 collective-permute-done.6
  37.9 1.5 collective-permute-done.7
  39.4 0.7 select_maximum_fusion.4
  41.4 557.6 %all-reduce.6 = (f32[64,64]{0,1:T(8,128)S(1)}, f32[64,64]{0,1:T(8,128)S(1)}) all-reduce(f32[64,64]{0,1:T(8,128)S(1)} %convolution_bitcast_fusion.5, f32[64,64]{0,1:T(8,128)S(1)} %convolution_bitcast_fusion.6), channel_id=1, replica_groups=mesh['gx'=8,'gy'=16,'src'=2] {'gx','gy'}, use_global_device_ids=true, to_apply=%region_3.5 | all-reduce | flops 8192 | bytes 65536 | tf_op jit(solution)/shard_map/psum | solution.py:114
  599.1 5.8 cholesky.70
  605.6 0.7 fusion.38
  606.3 4.9 custom-call.15
  611.3 5.8 cholesky.59
  617.8 0.7 fusion.37
  618.5 4.9 custom-call.13
  625.0 548.6 %psum.37 = f32[64,64]{1,0:T(8,128)S(1)} all-reduce(f32[64,64]{1,0:T(8,128)S(1)} %convolution_bitcast_fusion.3), channel_id=1, replica_groups=mesh['gx'=8,'gy'=16,'src'=2] {'gx','gy'}, use_global_device_ids=true, to_apply=%region_4.8 | all-reduce | flops 4096 | bytes 32768 | tf_op jit(solution)/shard_map/psum | solution.py:123
  1174.8 1.3 collective-permute-start.8
  1176.1 3.0 collective-permute-start.9
  1179.1 0.7 convolution_add_fusion.2
  1180.3 1.3 collective-permute-start.10
  1181.6 4.6 collective-permute-start.11
  1186.3 1.1 collective-permute-done.10
  1187.3 1.7 collective-permute-done.11
  1189.1 0.7 select_maximum_fusion
  1190.3 0.7 convolution_bitcast_fusion.1
  1191.0 550.9 %psum.38 = f32[64,64]{0,1:T(8,128)S(1)} all-reduce(f32[64,64]{0,1:T(8,128)S(1)} %convolution_bitcast_fusion.1), channel_id=1, replica_groups=mesh['gx'=8,'gy'=16,'src'=2] {'gx','gy'}, use_global_device_ids=true, to_apply=%region_5.9 | all-reduce | flops 4096 | bytes 32768 | tf_op jit(solution)/shard_map/psum | solution.py:118
  1741.9 5.8 cholesky.81
  1749.1 4.9 custom-call.17
  1755.2 1.3 collective-permute-start.12
  1756.5 3.1 collective-permute-start.13
  1759.6 1.1 copy.55
  1761.1 1.3 collective-permute-start.14
  1762.4 4.6 collective-permute-start.15
  1767.7 1.7 collective-permute-done.14
  1769.4 1.5 collective-permute-done.15
  1772.3 6.5 psum.39
  1778.8 0.7 constant_dynamic-slice_fusion
  (84 shorter events, 15.4 us)
Async XLA Ops:
  0.6 8.6 copy-start.2
  2.6 6.5 collective-permute-start
  4.4 4.8 collective-permute-start.1
  9.2 6.5 collective-permute-start.2
  13.1 7.0 collective-permute-start.3
  21.6 8.2 copy-start.1
  22.2 8.4 collective-permute-start.4
  23.5 7.5 collective-permute-start.5
  31.0 6.9 collective-permute-start.6
  32.3 7.1 collective-permute-start.7
  623.9 555.3 %copy-start = (f32[64,2,8,128]{3,2,1,0:T(8,128)S(1)}, f32[64,2,8,128]{3,2,1,0:T(8,128)}, u32[]{:S(2)}) copy-start(f32[64,2,8,128]{3,2,1,0:T(8,128)} %param.13) | copy-start | bytes 1572868
  1174.8 5.1 collective-permute-start.8
  1176.1 4.2 collective-permute-start.9
  1180.3 7.1 collective-permute-start.10
  1181.6 7.5 collective-permute-start.11
  1755.2 5.5 collective-permute-start.12
  1756.5 4.6 collective-permute-start.13
  1761.1 8.3 collective-permute-start.14
  1762.4 8.4 collective-permute-start.15
where the time goes:
time: 1790 us; the launch traced here: 1780 us
  blocking collectives  1660 us (93%)
  other arithmetic  45.7 us (3%)
  starting transfers between devices  42.1 us (2%)
    psum x1, blocking collectives, on_device(): res_gram = lax.psum(gram_of(residual, residual), ('gx', 'gy'))  558 us
    psum x1, blocking collectives, on_device(): curv_gram = lax.psum(gram_of(direction, image), ('gx', 'gy'))  551 us
    psum x1, blocking collectives, on_device(): new_gram = lax.psum(gram_of(residual, residual), ('gx', 'gy'))  549 us
  transfers between devices with their start and end apart: 16, of which 12 were waited for; matrix products, arithmetic and copies ran while one was open for 0% of the time, Pallas kernels for 0%

commit v1 on v0

--- a/solution.py
+++ b/solution.py
@@ -10,6 +10,8 @@
 
 
 def padded_2(block, sides, width):
+    (axis_x, dim_x), (axis_y, dim_y) = sides
+    pieces = {}
     for axis, dim in sides:
         count = lax.axis_size(axis)
         forward = [(i, i + 1) for i in range(count - 1)]
@@ -18,8 +20,29 @@
             lax.slice_in_dim(block, block.shape[dim] - width, None, axis=dim), axis, forward
         )
         high = lax.ppermute(lax.slice_in_dim(block, 0, width, axis=dim), axis, backward)
-        block = jnp.concatenate([low, block, high], axis=dim)
-    return block
+        pieces[axis] = (low, high)
+    low_x, high_x = pieces[axis_x]
+    low_y, high_y = pieces[axis_y]
+    middle = jnp.concatenate([low_x, block, high_x], axis=dim_x)
+    rim = [(0, 0)] * block.ndim
+    rim[dim_x] = (width, width)
+    low_y = jnp.pad(low_y, rim)
+    high_y = jnp.pad(high_y, rim)
+    return jnp.concatenate([low_y, middle, high_y], axis=dim_y)
+
+
+def allsum(value, axes):
+    for axis in axes:
+        count = lax.axis_size(axis)
+        if count & (count - 1):
+            value = lax.psum(value, axis)
+            continue
+        step = 1
+        while step < count:
+            pairs = [(i, i ^ step) for i in range(count)]
+            value = value + lax.ppermute(value, axis, pairs)
+            step *= 2
+    return value
 
 
 def conductances(sig_pad):
@@ -110,17 +133,24 @@
     iterate = initial_fields
     iter_pad = padded[1:]
     residual = right - operator(iter_pad, conds)
+    grid_axes = ("gx", "gy")
     direction = residual
-    res_gram = lax.psum(gram_of(residual, residual), ("gx", "gy"))
+    res_gram = None
     for iteration in range(ITERS):
         dir_pad = padded_2(direction, (("gx", 1), ("gy", 2)), 1)
         image = operator(dir_pad, conds)
-        curv_gram = lax.psum(gram_of(direction, image), ("gx", "gy"))
+        if res_gram is None:
+            grams = allsum(
+                jnp.stack([gram_of(residual, residual), gram_of(direction, image)]), grid_axes
+            )
+            res_gram, curv_gram = grams[0], grams[1]
+        else:
+            curv_gram = allsum(gram_of(direction, image), grid_axes)
         step_mat = posdef_solve(curv_gram, res_gram)
         iterate = iterate + combine_cols(direction, step_mat)
         residual = residual - combine_cols(image, step_mat)
         if iteration + 1 < ITERS:
-            new_gram = lax.psum(gram_of(residual, residual), ("gx", "gy"))
+            new_gram = allsum(gram_of(residual, residual), grid_axes)
             turn_mat = posdef_solve(res_gram, new_gram)
             direction = residual + combine_cols(direction, turn_mat)
             res_gram = new_gram
@@ -139,9 +169,17 @@
             + term_z[..., 1:]
         )
     )
-    share = cells_z // lax.axis_size("src")
-    summed = lax.psum(local_grad, "src")
-    gradient = lax.dynamic_slice_in_dim(summed, lax.axis_index("src") * share, share, 2)
+    groups = lax.axis_size("src")
+    share = cells_z // groups
+    own = lax.axis_index("src")
+    if groups == 2:
+        other = 1 - own
+        sent = lax.dynamic_slice_in_dim(local_grad, other * share, share, 2)
+        got = lax.ppermute(sent, "src", [(0, 1), (1, 0)])
+        gradient = lax.dynamic_slice_in_dim(local_grad, own * share, share, 2) + got
+    else:
+        summed = lax.psum(local_grad, "src")
+        gradient = lax.dynamic_slice_in_dim(summed, own * share, share, 2)
     return (iterate, gradient)
 
 

time: 1790 us -> 219 us (0.12)
  the two profiles are of different devices: /device:TPU:4 before, /device:TPU:14 now
where the time goes in v1:
time: 219 us
  waiting for transfers between devices  96.8 us (44%)
  starting transfers between devices  63.2 us (29%)
  other arithmetic  45.9 us (21%)
  matrix products  6.28 us (3%)
  local copies, waits for them, and re-layouts  4.98 us (2%)
    ppermute x21, waiting for transfers between devices, allsum(): value = value + lax.ppermute(value, axis, pairs)  75.5 us
    ppermute x8, starting transfers between devices, padded_2(): lax.ppermute(lax.slice_in_dim(block, 0, width, axis=dim), axis, backward)  28.2 us
    ppermute x8, starting transfers between devices, padded_2(): lax.ppermute(lax.slice_in_dim(block, block.shape[dim] - width, None, axis...  20.7 us
    another operation x9, other arithmetic, posdef_solve(): lower = jnp.linalg.cholesky(matrix)  19.5 us
    another operation x6, other arithmetic, posdef_solve(): lax.linalg.triangular_solve(lower, middle, left_side=True, lower=True, tr...  16.6 us
    ppermute x8, waiting for transfers between devices, padded_2(): lax.ppermute(lax.slice_in_dim(block, block.shape[dim] - width, None, axis...  15.6 us
    ppermute x21, starting transfers between devices, allsum(): value = value + lax.ppermute(value, axis, pairs)  12.9 us
  transfers between devices with their start and end apart: 38, of which 26 were waited for; matrix products, arithmetic and copies ran while one was open for 8% of the time, Pallas kernels for 0%

profile of v1, /device:TPU:14, one launch (start us, length us, event | category | flops | bytes accessed | tf_op | source)
XLA Modules:
  0.0 218.8 jit_solution(6468195889584808182)
XLA Ops:
  2.7 1.9 collective-permute-start.1
  4.6 3.6 %collective-permute-start.2 = (f32[65,1,8,128]{3,0,2,1:T(8,128)S(1)}, f32[65,1,8,128]{3,0,2,1:T(8,128)S(1)}, u32[]{:S(2)}, u32[]{:S(2)}) collective-permute-start(f32[65,1,8,128]{3,0,2,1:T(8,128)S(1)} %get-tuple-element.29), channel_id=1, source_target_pairs={{32,0},{64,32},{96,64},{128,96},{160,128},{192,160},{224,192},{33,... | collective-permute-start | bytes 798728 | tf_op jit(solution)/shard_map/ppermute | solution.py:22
  8.9 3.8 %collective-permute-start = (f32[65,2,1,128]{3,0,2,1:T(8,128)S(1)}, f32[65,2,1,128]{3,0,2,1:T(8,128)S(1)}, u32[]{:S(2)}, u32[]{:S(2)}) collective-permute-start(f32[65,2,1,128]{3,0,2,1:T(8,128)S(1)} %get-tuple-element.30), channel_id=1, source_target_pairs={{0,2},{2,4},{4,6},{6,8},{8,10},{10,12},{12,14},{14,16},{16,18},{18... | collective-permute-start | bytes 199688 | tf_op jit(solution)/shard_map/ppermute | solution.py:19
  12.8 6.1 %collective-permute-start.3 = (f32[65,2,1,128]{3,0,2,1:T(8,128)S(1)}, f32[65,2,1,128]{3,0,2,1:T(8,128)S(1)}, u32[]{:S(2)}, u32[]{:S(2)}) collective-permute-start(f32[65,2,1,128]{3,0,2,1:T(8,128)S(1)} %get-tuple-element.31), channel_id=1, source_target_pairs={{2,0},{4,2},{6,4},{8,6},{10,8},{12,10},{14,12},{16,14},{18,16},{20... | collective-permute-start | bytes 199688 | tf_op jit(solution)/shard_map/ppermute | solution.py:22
  23.0 1.9 collective-permute-start.4
  24.9 2.4 %collective-permute-start.5 = (f32[64,1,8,128]{3,0,2,1:T(8,128)S(1)}, f32[64,1,8,128]{3,0,2,1:T(8,128)S(1)}, u32[]{:S(2)}, u32[]{:S(2)}) collective-permute-start(f32[64,1,8,128]{3,0,2,1:T(8,128)S(1)} %get-tuple-element.36), channel_id=1, source_target_pairs={{0,32},{32,64},{64,96},{96,128},{128,160},{160,192},{192,224},{1,3... | collective-permute-start | bytes 786440 | tf_op jit(solution)/shard_map/ppermute | solution.py:19
  27.4 6.4 %collective-permute-start.6 = (f32[64,2,1,128]{3,0,2,1:T(8,128)S(1)}, f32[64,2,1,128]{3,0,2,1:T(8,128)S(1)}, u32[]{:S(2)}, u32[]{:S(2)}) collective-permute-start(f32[64,2,1,128]{3,0,2,1:T(8,128)S(1)} %get-tuple-element.39), channel_id=1, source_target_pairs={{2,0},{4,2},{6,4},{8,6},{10,8},{12,10},{14,12},{16,14},{18,16},{20... | collective-permute-start | bytes 196616 | tf_op jit(solution)/shard_map/ppermute | solution.py:22
  33.7 1.9 collective-permute-start.7
  36.3 6.4 %collective-permute-done.7 = f32[64,2,1,128]{3,0,2,1:T(8,128)S(1)} collective-permute-done((f32[64,2,1,128]{3,0,2,1:T(8,128)S(1)}, f32[64,2,1,128]{3,0,2,1:T(8,128)S(1)}, u32[]{:S(2)}, u32[]{:S(2)}) %collective-permute-start.7) | collective-permute-done | bytes 65568 | tf_op jit(solution)/shard_map/ppermute | solution.py:19
  46.3 4.3 %collective-permute-done.9 = f32[2,64,64]{1,2,0:T(8,128)S(1)} collective-permute-done((f32[2,64,64]{1,2,0:T(8,128)S(1)}, f32[2,64,64]{1,2,0:T(8,128)S(1)}, u32[]{:S(2)}, u32[]{:S(2)}) %collective-permute-start.9) | collective-permute-done | bytes 32800 | tf_op jit(solution)/shard_map/ppermute | solution.py:43
  50.6 1.7 collective-permute-start.10
  52.3 4.1 %collective-permute-done.10 = f32[2,64,64]{1,2,0:T(8,128)S(1)} collective-permute-done((f32[2,64,64]{1,2,0:T(8,128)S(1)}, f32[2,64,64]{1,2,0:T(8,128)S(1)}, u32[]{:S(2)}, u32[]{:S(2)}) %collective-permute-start.10) | collective-permute-done | bytes 32800 | tf_op jit(solution)/shard_map/ppermute | solution.py:43
  56.6 4.3 %collective-permute-done.11 = f32[2,64,64]{1,2,0:T(8,128)S(1)} collective-permute-done((f32[2,64,64]{1,2,0:T(8,128)S(1)}, f32[2,64,64]{1,2,0:T(8,128)S(1)}, u32[]{:S(2)}, u32[]{:S(2)}) %collective-permute-start.11) | collective-permute-done | bytes 32800 | tf_op jit(solution)/shard_map/ppermute | solution.py:43
  60.9 6.0 %collective-permute-done.12 = f32[2,64,64]{1,2,0:T(8,128)S(1)} collective-permute-done((f32[2,64,64]{1,2,0:T(8,128)S(1)}, f32[2,64,64]{1,2,0:T(8,128)S(1)}, u32[]{:S(2)}, u32[]{:S(2)}) %collective-permute-start.12) | collective-permute-done | bytes 32800 | tf_op jit(solution)/shard_map/ppermute | solution.py:43
  66.9 3.0 %collective-permute-start.13 = (f32[2,64,64]{1,2,0:T(8,128)S(1)}, f32[2,64,64]{1,2,0:T(8,128)S(1)}, u32[]{:S(2)}, u32[]{:S(2)}) collective-permute-start(f32[2,64,64]{1,2,0:T(8,128)S(1)} %add.245), channel_id=1, source_target_pairs={{0,8},{2,10},{4,12},{6,14},{8,0},{10,2},{12,4},{14,6},{16,24},{18,... | collective-permute-start | bytes 98312 | tf_op jit(solution)/shard_map/ppermute | solution.py:43
  69.9 5.4 %collective-permute-done.13 = f32[2,64,64]{1,2,0:T(8,128)S(1)} collective-permute-done((f32[2,64,64]{1,2,0:T(8,128)S(1)}, f32[2,64,64]{1,2,0:T(8,128)S(1)}, u32[]{:S(2)}, u32[]{:S(2)}) %collective-permute-start.13) | collective-permute-done | bytes 32800 | tf_op jit(solution)/shard_map/ppermute | solution.py:43
  75.6 4.3 %collective-permute-done.14 = f32[2,64,64]{1,2,0:T(8,128)S(1)} collective-permute-done((f32[2,64,64]{1,2,0:T(8,128)S(1)}, f32[2,64,64]{1,2,0:T(8,128)S(1)}, u32[]{:S(2)}, u32[]{:S(2)}) %collective-permute-start.14) | collective-permute-done | bytes 32800 | tf_op jit(solution)/shard_map/ppermute | solution.py:43
  80.1 5.8 %cholesky.59 = f32[64,64]{1,0:T(8,128)S(1)} custom-call(f32[64,64]{1,0:T(8,128)S(1)} %get-tuple-element.41), custom_call_target="Cholesky" | custom-call | tf_op jit(solution)/shard_map/jit(cholesky)/cholesky | solution.py:78
  87.3 4.9 %custom-call.13 = f32[1,64,64]{1,2,0:T(8,128)S(1)} custom-call(f32[1,64,64]{2,1,0:T(8,128)S(1)} %fusion.40), custom_call_target="InvertDiagBlocksLowerTriangular" | custom-call | tf_op jit(solution)/shard_map/triangular_solve/custom-call.2 | solution.py:80
  95.3 3.8 %collective-permute-done.16 = f32[64,64]{1,0:T(8,128)S(1)} collective-permute-done((f32[64,64]{1,0:T(8,128)S(1)}, f32[64,64]{1,0:T(8,128)S(1)}, u32[]{:S(2)}, u32[]{:S(2)}) %collective-permute-start.16) | collective-permute-done | bytes 16416 | tf_op jit(solution)/shard_map/ppermute | solution.py:43
  99.1 1.7 collective-permute-start.17
  100.7 3.8 %collective-permute-done.17 = f32[64,64]{1,0:T(8,128)S(1)} collective-permute-done((f32[64,64]{1,0:T(8,128)S(1)}, f32[64,64]{1,0:T(8,128)S(1)}, u32[]{:S(2)}, u32[]{:S(2)}) %collective-permute-start.17) | collective-permute-done | bytes 16416 | tf_op jit(solution)/shard_map/ppermute | solution.py:43
  104.5 5.8 %cholesky.70 = f32[64,64]{1,0:T(8,128)S(1)} custom-call(f32[64,64]{1,0:T(8,128)S(1)} %get-tuple-element.40), custom_call_target="Cholesky" | custom-call | tf_op jit(solution)/shard_map/jit(cholesky)/cholesky | solution.py:78
  110.5 4.8 %collective-permute-done.19 = f32[64,64]{1,0:T(8,128)S(1)} collective-permute-done((f32[64,64]{1,0:T(8,128)S(1)}, f32[64,64]{1,0:T(8,128)S(1)}, u32[]{:S(2)}, u32[]{:S(2)}) %collective-permute-start.19) | collective-permute-done | bytes 16416 | tf_op jit(solution)/shard_map/ppermute | solution.py:43
  115.3 3.1 %collective-permute-start.20 = (f32[64,64]{1,0:T(8,128)S(1)}, f32[64,64]{1,0:T(8,128)S(1)}, u32[]{:S(2)}, u32[]{:S(2)}) collective-permute-start(f32[64,64]{1,0:T(8,128)S(1)} %add.253), channel_id=1, source_target_pairs={{0,8},{2,10},{4,12},{6,14},{8,0},{10,2},{12,4},{14,6},{16,24},{18,... | collective-permute-start | bytes 49160 | tf_op jit(solution)/shard_map/ppermute | solution.py:43
  119.0 4.4 %collective-permute-done.20 = f32[64,64]{1,0:T(8,128)S(1)} collective-permute-done((f32[64,64]{1,0:T(8,128)S(1)}, f32[64,64]{1,0:T(8,128)S(1)}, u32[]{:S(2)}, u32[]{:S(2)}) %collective-permute-start.20) | collective-permute-done | bytes 16416 | tf_op jit(solution)/shard_map/ppermute | solution.py:43
  124.1 4.9 %custom-call.15 = f32[1,64,64]{1,2,0:T(8,128)S(1)} custom-call(f32[1,64,64]{2,1,0:T(8,128)S(1)} %fusion.41), custom_call_target="InvertDiagBlocksLowerTriangular" | custom-call | tf_op jit(solution)/shard_map/triangular_solve/custom-call.2 | solution.py:80
  130.2 1.9 collective-permute-start.22
  132.1 2.4 %collective-permute-start.23 = (f32[64,1,8,128]{3,0,2,1:T(8,128)S(1)}, f32[64,1,8,128]{3,0,2,1:T(8,128)S(1)}, u32[]{:S(2)}, u32[]{:S(2)}) collective-permute-start(f32[64,1,8,128]{3,0,2,1:T(8,128)S(1)} %get-tuple-element.32), channel_id=1, source_target_pairs={{0,32},{32,64},{64,96},{96,128},{128,160},{160,192},{192,224},{1,3... | collective-permute-start | bytes 786440 | tf_op jit(solution)/shard_map/ppermute | solution.py:19
  134.5 4.3 %collective-permute-start.24 = (f32[64,2,1,128]{3,0,2,1:T(8,128)S(1)}, f32[64,2,1,128]{3,0,2,1:T(8,128)S(1)}, u32[]{:S(2)}, u32[]{:S(2)}) collective-permute-start(f32[64,2,1,128]{3,0,2,1:T(8,128)S(1)} %get-tuple-element.35), channel_id=1, source_target_pairs={{2,0},{4,2},{6,4},{8,6},{10,8},{12,10},{14,12},{16,14},{18,16},{20... | collective-permute-start | bytes 196616 | tf_op jit(solution)/shard_map/ppermute | solution.py:22
  138.9 1.9 collective-permute-start.25
  141.3 6.2 %collective-permute-done.25 = f32[64,2,1,128]{3,0,2,1:T(8,128)S(1)} collective-permute-done((f32[64,2,1,128]{3,0,2,1:T(8,128)S(1)}, f32[64,2,1,128]{3,0,2,1:T(8,128)S(1)}, u32[]{:S(2)}, u32[]{:S(2)}) %collective-permute-start.25) | collective-permute-done | bytes 65568 | tf_op jit(solution)/shard_map/ppermute | solution.py:19
  151.1 3.9 %collective-permute-done.27 = f32[64,64]{0,1:T(8,128)S(1)} collective-permute-done((f32[64,64]{0,1:T(8,128)S(1)}, f32[64,64]{0,1:T(8,128)S(1)}, u32[]{:S(2)}, u32[]{:S(2)}) %collective-permute-start.27) | collective-permute-done | bytes 16416 | tf_op jit(solution)/shard_map/ppermute | solution.py:43
  156.3 4.1 %collective-permute-done.28 = f32[64,64]{0,1:T(8,128)S(1)} collective-permute-done((f32[64,64]{0,1:T(8,128)S(1)}, f32[64,64]{0,1:T(8,128)S(1)}, u32[]{:S(2)}, u32[]{:S(2)}) %collective-permute-start.28) | collective-permute-done | bytes 16416 | tf_op jit(solution)/shard_map/ppermute | solution.py:43
  160.5 3.9 %collective-permute-done.29 = f32[64,64]{0,1:T(8,128)S(1)} collective-permute-done((f32[64,64]{0,1:T(8,128)S(1)}, f32[64,64]{0,1:T(8,128)S(1)}, u32[]{:S(2)}, u32[]{:S(2)}) %collective-permute-start.29) | collective-permute-done | bytes 16416 | tf_op jit(solution)/shard_map/ppermute | solution.py:43
  164.4 4.9 %collective-permute-done.30 = f32[64,64]{0,1:T(8,128)S(1)} collective-permute-done((f32[64,64]{0,1:T(8,128)S(1)}, f32[64,64]{0,1:T(8,128)S(1)}, u32[]{:S(2)}, u32[]{:S(2)}) %collective-permute-start.30) | collective-permute-done | bytes 16416 | tf_op jit(solution)/shard_map/ppermute | solution.py:43
  170.2 6.9 %collective-permute-done.31 = f32[64,64]{0,1:T(8,128)S(1)} collective-permute-done((f32[64,64]{0,1:T(8,128)S(1)}, f32[64,64]{0,1:T(8,128)S(1)}, u32[]{:S(2)}, u32[]{:S(2)}) %collective-permute-start.31) | collective-permute-done | bytes 16416 | tf_op jit(solution)/shard_map/ppermute | solution.py:43
  177.9 3.2 %collective-permute-done.32 = f32[64,64]{0,1:T(8,128)S(1)} collective-permute-done((f32[64,64]{0,1:T(8,128)S(1)}, f32[64,64]{0,1:T(8,128)S(1)}, u32[]{:S(2)}, u32[]{:S(2)}) %collective-permute-start.32) | collective-permute-done | bytes 16416 | tf_op jit(solution)/shard_map/ppermute | solution.py:43
  181.1 5.8 %cholesky.81 = f32[64,64]{1,0:T(8,128)S(1)} custom-call(f32[64,64]{1,0:T(8,128)S(1)} %fusion.58), custom_call_target="Cholesky" | custom-call | tf_op jit(solution)/shard_map/jit(cholesky)/cholesky | solution.py:78
  188.3 4.9 %custom-call.17 = f32[1,64,64]{1,2,0:T(8,128)S(1)} custom-call(f32[1,64,64]{2,1,0:T(8,128)S(1)} %fusion.42), custom_call_target="InvertDiagBlocksLowerTriangular" | custom-call | tf_op jit(solution)/shard_map/triangular_solve/custom-call.2 | solution.py:80
  194.4 1.9 collective-permute-start.33
  196.3 2.4 %collective-permute-start.34 = (f32[128,1,8,128]{3,0,2,1:T(8,128)S(1)}, f32[128,1,8,128]{3,0,2,1:T(8,128)S(1)}, u32[]{:S(2)}, u32[]{:S(2)}) collective-permute-start(f32[128,1,8,128]{3,0,2,1:T(8,128)S(1)} %get-tuple-element.26), channel_id=1, source_target_pairs={{0,32},{32,64},{64,96},{96,128},{128,160},{160,192},{192,224},{1,3... | collective-permute-start | bytes 1572872 | tf_op jit(solution)/shard_map/ppermute | solution.py:19
  198.8 1.9 collective-permute-start.35
  200.7 3.9 %collective-permute-start.36 = (f32[128,2,1,128]{3,0,2,1:T(8,128)S(1)}, f32[128,2,1,128]{3,0,2,1:T(8,128)S(1)}, u32[]{:S(2)}, u32[]{:S(2)}) collective-permute-start(f32[128,2,1,128]{3,0,2,1:T(8,128)S(1)} %get-tuple-element.24), channel_id=1, source_target_pairs={{0,2},{2,4},{4,6},{6,8},{8,10},{10,12},{12,14},{14,16},{16,18},{18... | collective-permute-start | bytes 393224 | tf_op jit(solution)/shard_map/ppermute | solution.py:19
  204.6 2.1 collective-permute-done.35
  207.6 3.0 %collective-permute-done.36 = f32[128,2,1,128]{3,0,2,1:T(8,128)S(1)} collective-permute-done((f32[128,2,1,128]{3,0,2,1:T(8,128)S(1)}, f32[128,2,1,128]{3,0,2,1:T(8,128)S(1)}, u32[]{:S(2)}, u32[]{:S(2)}) %collective-permute-start.36) | collective-permute-done | bytes 131104 | tf_op jit(solution)/shard_map/ppermute | solution.py:19
  213.0 1.4 collective-permute-start.37
  215.5 2.7 %collective-permute-done.37 = f32[2,8,64]{2,1,0:T(8,128)S(1)} collective-permute-done((f32[2,8,64]{2,1,0:T(8,128)S(1)}, f32[2,8,64]{2,1,0:T(8,128)S(1)}, u32[]{:S(2)}, u32[]{:S(2)}) %collective-permute-start.37) | collective-permute-done | bytes 4128 | tf_op jit(solution)/shard_map/ppermute | solution.py:178
  (159 shorter events, 32.9 us)
Async XLA Ops:
  0.6 20.3 %copy-start.2 = (f32[2,8,128]{2,1,0:T(8,128)S(1)}, f32[2,8,128]{2,1,0:T(8,128)}, u32[]{:S(2)}) copy-start(f32[2,8,128]{2,1,0:T(8,128)} %param.10) | copy-start | bytes 24580
  0.6 18.3 %copy-start.4 = (s32[64]{0:T(128)S(1)}, s32[64]{0:T(128)}, u32[]{:S(2)}) copy-start(s32[64]{0:T(128)} %param.12) | copy-start | bytes 772
  0.7 18.3 %copy-start.3 = (s32[128,2]{0,1:T(2,128)S(1)}, s32[128,2]{0,1:T(2,128)}, u32[]{:S(2)}) copy-start(s32[128,2]{0,1:T(2,128)} %param.11) | copy-start | bytes 3076
  2.7 18.2 %collective-permute-start.1 = (f32[65,1,8,128]{3,0,2,1:T(8,128)S(1)}, f32[65,1,8,128]{3,0,2,1:T(8,128)S(1)}, u32[]{:S(2)}, u32[]{:S(2)}) collective-permute-start(f32[65,1,8,128]{3,0,2,1:T(8,128)S(1)} %get-tuple-element.28), channel_id=1, source_target_pairs={{0,32},{32,64},{64,96},{96,128},{128,160},{160,192},{192,224},{1,3... | collective-permute-start | bytes 798728 | tf_op jit(solution)/shard_map/ppermute | solution.py:19
  4.6 16.3 %collective-permute-start.2 = (f32[65,1,8,128]{3,0,2,1:T(8,128)S(1)}, f32[65,1,8,128]{3,0,2,1:T(8,128)S(1)}, u32[]{:S(2)}, u32[]{:S(2)}) collective-permute-start(f32[65,1,8,128]{3,0,2,1:T(8,128)S(1)} %get-tuple-element.29), channel_id=1, source_target_pairs={{32,0},{64,32},{96,64},{128,96},{160,128},{192,160},{224,192},{33,... | collective-permute-start | bytes 798728 | tf_op jit(solution)/shard_map/ppermute | solution.py:22
  8.9 11.4 %collective-permute-start = (f32[65,2,1,128]{3,0,2,1:T(8,128)S(1)}, f32[65,2,1,128]{3,0,2,1:T(8,128)S(1)}, u32[]{:S(2)}, u32[]{:S(2)}) collective-permute-start(f32[65,2,1,128]{3,0,2,1:T(8,128)S(1)} %get-tuple-element.30), channel_id=1, source_target_pairs={{0,2},{2,4},{4,6},{6,8},{8,10},{10,12},{12,14},{14,16},{16,18},{18... | collective-permute-start | bytes 199688 | tf_op jit(solution)/shard_map/ppermute | solution.py:19
  12.8 8.1 %collective-permute-start.3 = (f32[65,2,1,128]{3,0,2,1:T(8,128)S(1)}, f32[65,2,1,128]{3,0,2,1:T(8,128)S(1)}, u32[]{:S(2)}, u32[]{:S(2)}) collective-permute-start(f32[65,2,1,128]{3,0,2,1:T(8,128)S(1)} %get-tuple-element.31), channel_id=1, source_target_pairs={{2,0},{4,2},{6,4},{8,6},{10,8},{12,10},{14,12},{16,14},{18,16},{20... | collective-permute-start | bytes 199688 | tf_op jit(solution)/shard_map/ppermute | solution.py:22
  23.0 19.7 %collective-permute-start.4 = (f32[64,1,8,128]{3,0,2,1:T(8,128)S(1)}, f32[64,1,8,128]{3,0,2,1:T(8,128)S(1)}, u32[]{:S(2)}, u32[]{:S(2)}) collective-permute-start(f32[64,1,8,128]{3,0,2,1:T(8,128)S(1)} %get-tuple-element.37), channel_id=1, source_target_pairs={{32,0},{64,32},{96,64},{128,96},{160,128},{192,160},{224,192},{33,... | collective-permute-start | bytes 786440 | tf_op jit(solution)/shard_map/ppermute | solution.py:22
  24.9 17.8 %collective-permute-start.5 = (f32[64,1,8,128]{3,0,2,1:T(8,128)S(1)}, f32[64,1,8,128]{3,0,2,1:T(8,128)S(1)}, u32[]{:S(2)}, u32[]{:S(2)}) collective-permute-start(f32[64,1,8,128]{3,0,2,1:T(8,128)S(1)} %get-tuple-element.36), channel_id=1, source_target_pairs={{0,32},{32,64},{64,96},{96,128},{128,160},{160,192},{192,224},{1,3... | collective-permute-start | bytes 786440 | tf_op jit(solution)/shard_map/ppermute | solution.py:19
  27.4 8.9 %collective-permute-start.6 = (f32[64,2,1,128]{3,0,2,1:T(8,128)S(1)}, f32[64,2,1,128]{3,0,2,1:T(8,128)S(1)}, u32[]{:S(2)}, u32[]{:S(2)}) collective-permute-start(f32[64,2,1,128]{3,0,2,1:T(8,128)S(1)} %get-tuple-element.39), channel_id=1, source_target_pairs={{2,0},{4,2},{6,4},{8,6},{10,8},{12,10},{14,12},{16,14},{18,16},{20... | collective-permute-start | bytes 196616 | tf_op jit(solution)/shard_map/ppermute | solution.py:22
  33.7 8.9 %collective-permute-start.7 = (f32[64,2,1,128]{3,0,2,1:T(8,128)S(1)}, f32[64,2,1,128]{3,0,2,1:T(8,128)S(1)}, u32[]{:S(2)}, u32[]{:S(2)}) collective-permute-start(f32[64,2,1,128]{3,0,2,1:T(8,128)S(1)} %get-tuple-element.38), channel_id=1, source_target_pairs={{0,2},{2,4},{4,6},{6,8},{8,10},{10,12},{12,14},{14,16},{16,18},{18... | collective-permute-start | bytes 196616 | tf_op jit(solution)/shard_map/ppermute | solution.py:19
  44.9 1.3 collective-permute-start.8
  46.2 4.4 %collective-permute-start.9 = (f32[2,64,64]{1,2,0:T(8,128)S(1)}, f32[2,64,64]{1,2,0:T(8,128)S(1)}, u32[]{:S(2)}, u32[]{:S(2)}) collective-permute-start(f32[2,64,64]{1,2,0:T(8,128)S(1)} %fusion.76), channel_id=1, source_target_pairs={{0,64},{32,96},{64,0},{96,32},{128,192},{160,224},{192,128},{224,1... | collective-permute-start | bytes 98312 | tf_op jit(solution)/shard_map/ppermute | solution.py:43
  50.6 5.9 %collective-permute-start.10 = (f32[2,64,64]{1,2,0:T(8,128)S(1)}, f32[2,64,64]{1,2,0:T(8,128)S(1)}, u32[]{:S(2)}, u32[]{:S(2)}) collective-permute-start(f32[2,64,64]{1,2,0:T(8,128)S(1)} %fusion.102), channel_id=1, source_target_pairs={{0,128},{32,160},{64,192},{96,224},{128,0},{160,32},{192,64},{224,... | collective-permute-start | bytes 98312 | tf_op jit(solution)/shard_map/ppermute | solution.py:43
  56.5 4.4 %collective-permute-start.11 = (f32[2,64,64]{1,2,0:T(8,128)S(1)}, f32[2,64,64]{1,2,0:T(8,128)S(1)}, u32[]{:S(2)}, u32[]{:S(2)}) collective-permute-start(f32[2,64,64]{1,2,0:T(8,128)S(1)} %add.243), channel_id=1, source_target_pairs={{0,2},{2,0},{4,6},{6,4},{8,10},{10,8},{12,14},{14,12},{16,18},{18,... | collective-permute-start | bytes 98312 | tf_op jit(solution)/shard_map/ppermute | solution.py:43
  60.8 6.1 %collective-permute-start.12 = (f32[2,64,64]{1,2,0:T(8,128)S(1)}, f32[2,64,64]{1,2,0:T(8,128)S(1)}, u32[]{:S(2)}, u32[]{:S(2)}) collective-permute-start(f32[2,64,64]{1,2,0:T(8,128)S(1)} %add.244), channel_id=1, source_target_pairs={{0,4},{2,6},{4,0},{6,2},{8,12},{10,14},{12,8},{14,10},{16,20},{18,... | collective-permute-start | bytes 98312 | tf_op jit(solution)/shard_map/ppermute | solution.py:43
  66.9 8.4 %collective-permute-start.13 = (f32[2,64,64]{1,2,0:T(8,128)S(1)}, f32[2,64,64]{1,2,0:T(8,128)S(1)}, u32[]{:S(2)}, u32[]{:S(2)}) collective-permute-start(f32[2,64,64]{1,2,0:T(8,128)S(1)} %add.245), channel_id=1, source_target_pairs={{0,8},{2,10},{4,12},{6,14},{8,0},{10,2},{12,4},{14,6},{16,24},{18,... | collective-permute-start | bytes 98312 | tf_op jit(solution)/shard_map/ppermute | solution.py:43
  75.4 4.5 %collective-permute-start.14 = (f32[2,64,64]{1,2,0:T(8,128)S(1)}, f32[2,64,64]{1,2,0:T(8,128)S(1)}, u32[]{:S(2)}, u32[]{:S(2)}) collective-permute-start(f32[2,64,64]{1,2,0:T(8,128)S(1)} %add.246), channel_id=1, source_target_pairs={{0,16},{2,18},{4,20},{6,22},{8,24},{10,26},{12,28},{14,30},{16,0},... | collective-permute-start | bytes 98312 | tf_op jit(solution)/shard_map/ppermute | solution.py:43
  93.8 1.3 collective-permute-start.15
  95.1 3.9 %collective-permute-start.16 = (f32[64,64]{1,0:T(8,128)S(1)}, f32[64,64]{1,0:T(8,128)S(1)}, u32[]{:S(2)}, u32[]{:S(2)}) collective-permute-start(f32[64,64]{1,0:T(8,128)S(1)} %add.249), channel_id=1, source_target_pairs={{0,64},{32,96},{64,0},{96,32},{128,192},{160,224},{192,128},{224,1... | collective-permute-start | bytes 49160 | tf_op jit(solution)/shard_map/ppermute | solution.py:43
  99.1 5.4 %collective-permute-start.17 = (f32[64,64]{1,0:T(8,128)S(1)}, f32[64,64]{1,0:T(8,128)S(1)}, u32[]{:S(2)}, u32[]{:S(2)}) collective-permute-start(f32[64,64]{1,0:T(8,128)S(1)} %add.250), channel_id=1, source_target_pairs={{0,128},{32,160},{64,192},{96,224},{128,0},{160,32},{192,64},{224,... | collective-permute-start | bytes 49160 | tf_op jit(solution)/shard_map/ppermute | solution.py:43
  104.5 5.9 %collective-permute-start.18 = (f32[64,64]{1,0:T(8,128)S(1)}, f32[64,64]{1,0:T(8,128)S(1)}, u32[]{:S(2)}, u32[]{:S(2)}) collective-permute-start(f32[64,64]{1,0:T(8,128)S(1)} %add.251), channel_id=1, source_target_pairs={{0,2},{2,0},{4,6},{6,4},{8,10},{10,8},{12,14},{14,12},{16,18},{18,... | collective-permute-start | bytes 49160 | tf_op jit(solution)/shard_map/ppermute | solution.py:43
  110.4 4.9 %collective-permute-start.19 = (f32[64,64]{1,0:T(8,128)S(1)}, f32[64,64]{1,0:T(8,128)S(1)}, u32[]{:S(2)}, u32[]{:S(2)}) collective-permute-start(f32[64,64]{1,0:T(8,128)S(1)} %add.252), channel_id=1, source_target_pairs={{0,4},{2,6},{4,0},{6,2},{8,12},{10,14},{12,8},{14,10},{16,20},{18,... | collective-permute-start | bytes 49160 | tf_op jit(solution)/shard_map/ppermute | solution.py:43
  115.3 8.2 %collective-permute-start.20 = (f32[64,64]{1,0:T(8,128)S(1)}, f32[64,64]{1,0:T(8,128)S(1)}, u32[]{:S(2)}, u32[]{:S(2)}) collective-permute-start(f32[64,64]{1,0:T(8,128)S(1)} %add.253), channel_id=1, source_target_pairs={{0,8},{2,10},{4,12},{6,14},{8,0},{10,2},{12,4},{14,6},{16,24},{18,... | collective-permute-start | bytes 49160 | tf_op jit(solution)/shard_map/ppermute | solution.py:43
  123.5 5.6 %collective-permute-start.21 = (f32[64,64]{1,0:T(8,128)S(1)}, f32[64,64]{1,0:T(8,128)S(1)}, u32[]{:S(2)}, u32[]{:S(2)}) collective-permute-start(f32[64,64]{1,0:T(8,128)S(1)} %add.254), channel_id=1, source_target_pairs={{0,16},{2,18},{4,20},{6,22},{8,24},{10,26},{12,28},{14,30},{16,0},... | collective-permute-start | bytes 49160 | tf_op jit(solution)/shard_map/ppermute | solution.py:43
  130.2 17.3 %collective-permute-start.22 = (f32[64,1,8,128]{3,0,2,1:T(8,128)S(1)}, f32[64,1,8,128]{3,0,2,1:T(8,128)S(1)}, u32[]{:S(2)}, u32[]{:S(2)}) collective-permute-start(f32[64,1,8,128]{3,0,2,1:T(8,128)S(1)} %get-tuple-element.33), channel_id=1, source_target_pairs={{32,0},{64,32},{96,64},{128,96},{160,128},{192,160},{224,192},{33,... | collective-permute-start | bytes 786440 | tf_op jit(solution)/shard_map/ppermute | solution.py:22
  132.1 15.4 %collective-permute-start.23 = (f32[64,1,8,128]{3,0,2,1:T(8,128)S(1)}, f32[64,1,8,128]{3,0,2,1:T(8,128)S(1)}, u32[]{:S(2)}, u32[]{:S(2)}) collective-permute-start(f32[64,1,8,128]{3,0,2,1:T(8,128)S(1)} %get-tuple-element.32), channel_id=1, source_target_pairs={{0,32},{32,64},{64,96},{96,128},{128,160},{160,192},{192,224},{1,3... | collective-permute-start | bytes 786440 | tf_op jit(solution)/shard_map/ppermute | solution.py:19
  134.5 6.8 %collective-permute-start.24 = (f32[64,2,1,128]{3,0,2,1:T(8,128)S(1)}, f32[64,2,1,128]{3,0,2,1:T(8,128)S(1)}, u32[]{:S(2)}, u32[]{:S(2)}) collective-permute-start(f32[64,2,1,128]{3,0,2,1:T(8,128)S(1)} %get-tuple-element.35), channel_id=1, source_target_pairs={{2,0},{4,2},{6,4},{8,6},{10,8},{12,10},{14,12},{16,14},{18,16},{20... | collective-permute-start | bytes 196616 | tf_op jit(solution)/shard_map/ppermute | solution.py:22
  138.9 8.6 %collective-permute-start.25 = (f32[64,2,1,128]{3,0,2,1:T(8,128)S(1)}, f32[64,2,1,128]{3,0,2,1:T(8,128)S(1)}, u32[]{:S(2)}, u32[]{:S(2)}) collective-permute-start(f32[64,2,1,128]{3,0,2,1:T(8,128)S(1)} %get-tuple-element.34), channel_id=1, source_target_pairs={{0,2},{2,4},{4,6},{6,8},{8,10},{10,12},{12,14},{14,16},{16,18},{18... | collective-permute-start | bytes 196616 | tf_op jit(solution)/shard_map/ppermute | solution.py:19
  148.8 21.3 %copy-start.1 = (f32[64,2,8,128]{3,2,1,0:T(8,128)S(1)}, f32[64,2,8,128]{3,2,1,0:T(8,128)}, u32[]{:S(2)}) copy-start(f32[64,2,8,128]{3,2,1,0:T(8,128)} %param.14) | copy-start | bytes 1572868
  148.8 28.4 %copy-start = (f32[64,2,8,128]{3,2,1,0:T(8,128)S(1)}, f32[64,2,8,128]{3,2,1,0:T(8,128)}, u32[]{:S(2)}) copy-start(f32[64,2,8,128]{3,2,1,0:T(8,128)} %param.13) | copy-start | bytes 1572868
  149.6 1.5 collective-permute-start.26
  151.1 3.9 %collective-permute-start.27 = (f32[64,64]{0,1:T(8,128)S(1)}, f32[64,64]{0,1:T(8,128)S(1)}, u32[]{:S(2)}, u32[]{:S(2)}) collective-permute-start(f32[64,64]{0,1:T(8,128)S(1)} %add.259), channel_id=1, source_target_pairs={{0,64},{32,96},{64,0},{96,32},{128,192},{160,224},{192,128},{224,1... | collective-permute-start | bytes 49160 | tf_op jit(solution)/shard_map/ppermute | solution.py:43
  155.0 5.4 %collective-permute-start.28 = (f32[64,64]{0,1:T(8,128)S(1)}, f32[64,64]{0,1:T(8,128)S(1)}, u32[]{:S(2)}, u32[]{:S(2)}) collective-permute-start(f32[64,64]{0,1:T(8,128)S(1)} %add.260), channel_id=1, source_target_pairs={{0,128},{32,160},{64,192},{96,224},{128,0},{160,32},{192,64},{224,... | collective-permute-start | bytes 49160 | tf_op jit(solution)/shard_map/ppermute | solution.py:43
  160.5 3.9 %collective-permute-start.29 = (f32[64,64]{0,1:T(8,128)S(1)}, f32[64,64]{0,1:T(8,128)S(1)}, u32[]{:S(2)}, u32[]{:S(2)}) collective-permute-start(f32[64,64]{0,1:T(8,128)S(1)} %add.261), channel_id=1, source_target_pairs={{0,2},{2,0},{4,6},{6,4},{8,10},{10,8},{12,14},{14,12},{16,18},{18,... | collective-permute-start | bytes 49160 | tf_op jit(solution)/shard_map/ppermute | solution.py:43
  164.4 4.9 %collective-permute-start.30 = (f32[64,64]{0,1:T(8,128)S(1)}, f32[64,64]{0,1:T(8,128)S(1)}, u32[]{:S(2)}, u32[]{:S(2)}) collective-permute-start(f32[64,64]{0,1:T(8,128)S(1)} %add.262), channel_id=1, source_target_pairs={{0,4},{2,6},{4,0},{6,2},{8,12},{10,14},{12,8},{14,10},{16,20},{18,... | collective-permute-start | bytes 49160 | tf_op jit(solution)/shard_map/ppermute | solution.py:43
  169.3 7.8 %collective-permute-start.31 = (f32[64,64]{0,1:T(8,128)S(1)}, f32[64,64]{0,1:T(8,128)S(1)}, u32[]{:S(2)}, u32[]{:S(2)}) collective-permute-start(f32[64,64]{0,1:T(8,128)S(1)} %add.263), channel_id=1, source_target_pairs={{0,8},{2,10},{4,12},{6,14},{8,0},{10,2},{12,4},{14,6},{16,24},{18,... | collective-permute-start | bytes 49160 | tf_op jit(solution)/shard_map/ppermute | solution.py:43
  177.1 3.9 %collective-permute-start.32 = (f32[64,64]{0,1:T(8,128)S(1)}, f32[64,64]{0,1:T(8,128)S(1)}, u32[]{:S(2)}, u32[]{:S(2)}) collective-permute-start(f32[64,64]{0,1:T(8,128)S(1)} %add.264), channel_id=1, source_target_pairs={{0,16},{2,18},{4,20},{6,22},{8,24},{10,26},{12,28},{14,30},{16,0},... | collective-permute-start | bytes 49160 | tf_op jit(solution)/shard_map/ppermute | solution.py:43
  194.4 16.3 %collective-permute-start.33 = (f32[128,1,8,128]{3,0,2,1:T(8,128)S(1)}, f32[128,1,8,128]{3,0,2,1:T(8,128)S(1)}, u32[]{:S(2)}, u32[]{:S(2)}) collective-permute-start(f32[128,1,8,128]{3,0,2,1:T(8,128)S(1)} %get-tuple-element.27), channel_id=1, source_target_pairs={{32,0},{64,32},{96,64},{128,96},{160,128},{192,160},{224,192},{33,... | collective-permute-start | bytes 1572872 | tf_op jit(solution)/shard_map/ppermute | solution.py:22
  196.3 14.4 %collective-permute-start.34 = (f32[128,1,8,128]{3,0,2,1:T(8,128)S(1)}, f32[128,1,8,128]{3,0,2,1:T(8,128)S(1)}, u32[]{:S(2)}, u32[]{:S(2)}) collective-permute-start(f32[128,1,8,128]{3,0,2,1:T(8,128)S(1)} %get-tuple-element.26), channel_id=1, source_target_pairs={{0,32},{32,64},{64,96},{96,128},{128,160},{160,192},{192,224},{1,3... | collective-permute-start | bytes 1572872 | tf_op jit(solution)/shard_map/ppermute | solution.py:19
  198.8 8.0 %collective-permute-start.35 = (f32[128,2,1,128]{3,0,2,1:T(8,128)S(1)}, f32[128,2,1,128]{3,0,2,1:T(8,128)}, u32[]{:S(2)}, u32[]{:S(2)}) collective-permute-start(f32[128,2,1,128]{3,0,2,1:T(8,128)S(1)} %get-tuple-element.25), channel_id=1, source_target_pairs={{2,0},{4,2},{6,4},{8,6},{10,8},{12,10},{14,12},{16,14},{18,16},{20... | collective-permute-start | bytes 393224 | tf_op jit(solution)/shard_map/ppermute | solution.py:22
  200.7 10.0 %collective-permute-start.36 = (f32[128,2,1,128]{3,0,2,1:T(8,128)S(1)}, f32[128,2,1,128]{3,0,2,1:T(8,128)S(1)}, u32[]{:S(2)}, u32[]{:S(2)}) collective-permute-start(f32[128,2,1,128]{3,0,2,1:T(8,128)S(1)} %get-tuple-element.24), channel_id=1, source_target_pairs={{0,2},{2,4},{4,6},{6,8},{8,10},{10,12},{12,14},{14,16},{16,18},{18... | collective-permute-start | bytes 393224 | tf_op jit(solution)/shard_map/ppermute | solution.py:19
  213.0 5.2 %collective-permute-start.37 = (f32[2,8,64]{2,1,0:T(8,128)S(1)}, f32[2,8,64]{2,1,0:T(8,128)S(1)}, u32[]{:S(2)}, u32[]{:S(2)}) collective-permute-start(f32[2,8,64]{2,1,0:T(8,128)S(1)} %constant_dynamic-slice_fusion), channel_id=1, source_target_pairs={{0,1},{1,0},{2,3},{3,2},{4,5},{5,4},{6,7},{7,6},{8,9},{9,8},{10,11... | collective-permute-start | bytes 12296 | tf_op jit(solution)/shard_map/ppermute | solution.py:178

commit v2 on v1

--- a/solution.py
+++ b/solution.py
@@ -127,36 +127,53 @@
         )
 
     right = INJECT * (point_source(picked[:, 0]) - point_source(picked[:, 1]))
-    stacked = jnp.concatenate([conductivity[None], initial_fields], axis=0)
-    padded = padded_2(stacked, (("gx", 1), ("gy", 2)), 1)
+    sides = (("gx", 1), ("gy", 2))
+    grid_axes = ("gx", "gy")
+    stacked = jnp.concatenate([conductivity[None], initial_fields, adjoint_fields], axis=0)
+    padded = padded_2(stacked, sides, 1)
     conds = conductances(padded[0])
-    iterate = initial_fields
-    iter_pad = padded[1:]
+    iter_pad = padded[1 : 1 + columns]
+    adjoint_pad = padded[1 + columns :]
     residual = right - operator(iter_pad, conds)
-    grid_axes = ("gx", "gy")
-    direction = residual
-    res_gram = None
-    for iteration in range(ITERS):
-        dir_pad = padded_2(direction, (("gx", 1), ("gy", 2)), 1)
-        image = operator(dir_pad, conds)
-        if res_gram is None:
-            grams = allsum(
-                jnp.stack([gram_of(residual, residual), gram_of(direction, image)]), grid_axes
-            )
-            res_gram, curv_gram = grams[0], grams[1]
-        else:
-            curv_gram = allsum(gram_of(direction, image), grid_axes)
-        step_mat = posdef_solve(curv_gram, res_gram)
-        iterate = iterate + combine_cols(direction, step_mat)
-        residual = residual - combine_cols(image, step_mat)
-        if iteration + 1 < ITERS:
-            new_gram = allsum(gram_of(residual, residual), grid_axes)
-            turn_mat = posdef_solve(res_gram, new_gram)
-            direction = residual + combine_cols(direction, turn_mat)
-            res_gram = new_gram
-    both = jnp.concatenate([iterate, adjoint_fields], axis=0)
-    both_pad = padded_2(both, (("gx", 1), ("gy", 2)), 1)
-    term_x, term_y, term_z = face_terms(both_pad[:columns], both_pad[columns:])
+    res_pad = padded_2(residual, sides, 1)
+    image = operator(res_pad, conds)
+    image_pad = padded_2(image, sides, 1)
+    image2 = operator(image_pad, conds)
+    grams = allsum(
+        jnp.stack(
+            [
+                gram_of(residual, residual),
+                gram_of(residual, image),
+                gram_of(image, image),
+                gram_of(image, image2),
+            ]
+        ),
+        grid_axes,
+    )
+    g_rr, g_rq, g_qq, g_qw = grams[0], grams[1], grams[2], grams[3]
+
+    def mm(left, right):
+        return jnp.matmul(left, right, precision=lax.Precision.HIGHEST)
+
+    step0 = posdef_solve(g_rq, g_rr)
+    cross = mm(g_rq, step0)
+    new_gram = g_rr - cross - cross.T + mm(step0.T, mm(g_qq, step0))
+    turn = posdef_solve(g_rr, new_gram)
+    keep = jnp.eye(columns, dtype=turn.dtype) + turn
+    back = -step0
+    curv = (
+        mm(keep.T, mm(g_rq, keep))
+        + mm(keep.T, mm(g_qq, back))
+        + mm(back.T, mm(g_qq, keep))
+        + mm(back.T, mm(g_qw, back))
+    )
+    step1 = posdef_solve(curv, new_gram)
+    res1_pad = res_pad - combine_cols(image_pad, step0)
+    dir1_pad = res1_pad + combine_cols(res_pad, turn)
+    it1_pad = iter_pad + combine_cols(res_pad, step0)
+    it2_pad = it1_pad + combine_cols(dir1_pad, step1)
+    iterate = it2_pad[:, 1:-1, 1:-1]
+    term_x, term_y, term_z = face_terms(it2_pad, adjoint_pad)
     local_grad = (
         -0.5
         / columns

time: 219 us -> 200 us (0.913)
  the two profiles are of different devices: /device:TPU:14 before, /device:TPU:4 now
where the time goes in v2:
time: 200 us; the launch traced here: 197 us
  starting transfers between devices  63.5 us (32%)
  other arithmetic  62.9 us (31%)
  waiting for transfers between devices  26.8 us (13%)
  matrix products  25.4 us (13%)
  local copies, waits for them, and re-layouts  17 us (8%)
    ppermute x7, starting transfers between devices, allsum(): value = value + lax.ppermute(value, axis, pairs)  30.7 us
    another operation x9, other arithmetic, posdef_solve(): lower = jnp.linalg.cholesky(matrix)  24.5 us
    ppermute x6, starting transfers between devices, padded_2(): lax.ppermute(lax.slice_in_dim(block, block.shape[dim] - width, None, axis...  24.5 us
    another operation x6, other arithmetic, posdef_solve(): lax.linalg.triangular_solve(lower, middle, left_side=True, lower=True, tr...  23.5 us
    ppermute x7, waiting for transfers between devices, allsum(): value = value + lax.ppermute(value, axis, pairs)  19.6 us
    dot_general x11, matrix products, mm(): return jnp.matmul(left, right, precision=lax.Precision.HIGHEST)  9.71 us
    dot_general x4, matrix products, combine_cols(): jnp.einsum('axyz,ab->bxyz', field, matrix, precision=lax.Precision.HIGHEST)  8.27 us
    ppermute x6, starting transfers between devices, padded_2(): lax.ppermute(lax.slice_in_dim(block, 0, width, axis=dim), axis, backward)  7.75 us
  transfers between devices with their start and end apart: 20, of which 11 were waited for; matrix products, arithmetic and copies ran while one was open for 6% of the time, Pallas kernels for 0%

profile of v2, /device:TPU:4, one launch (start us, length us, event | category | flops | bytes accessed | tf_op | source)
XLA Modules:
  0.0 197.3 jit_solution(4066614174016259246)
XLA Ops:
  0.7 1.3 copy.79
  2.2 1.3 collective-permute-start.3
  3.8 1.3 collective-permute-start.2
  6.0 3.9 %collective-permute-start.1 = (f32[129,1,8,128]{3,2,1,0:T(8,128)}, f32[129,1,8,128]{3,2,1,0:T(8,128)}, u32[]{:S(2)}, u32[]{:S(2)}) collective-permute-start(f32[129,1,8,128]{3,2,1,0:T(8,128)} %copy.80), channel_id=1, source_target_pairs={{0,32},{32,64},{64,96},{96,128},{128,160},{160,192},{192,224},{1,3... | collective-permute-start | bytes 1585160 | tf_op jit(solution)/shard_map/ppermute | solution.py:19
  9.8 4.5 %collective-permute-start = (f32[129,2,1,128]{3,0,2,1:T(8,128)S(1)}, f32[129,2,1,128]{3,0,2,1:T(8,128)S(1)}, u32[]{:S(2)}, u32[]{:S(2)}) collective-permute-start(f32[129,2,1,128]{3,0,2,1:T(8,128)S(1)} %get-tuple-element.24), channel_id=1, source_target_pairs={{0,2},{2,4},{4,6},{6,8},{8,10},{10,12},{12,14},{14,16},{16,18},{18... | collective-permute-start | bytes 396296 | tf_op jit(solution)/shard_map/ppermute | solution.py:19
  15.9 1.9 collective-permute-done
  17.9 1.3 copy.83
  19.1 1.1 copy.82
  20.6 1.5 copy-done.1
  23.4 1.3 collective-permute-start.4
  24.7 3.0 %collective-permute-start.5 = (f32[64,1,8,128]{3,0,2,1:T(8,128)S(1)}, f32[64,1,8,128]{3,0,2,1:T(8,128)S(1)}, u32[]{:S(2)}, u32[]{:S(2)}) collective-permute-start(f32[64,1,8,128]{3,0,2,1:T(8,128)S(1)} %get-tuple-element.32), channel_id=1, source_target_pairs={{0,32},{32,64},{64,96},{96,128},{128,160},{160,192},{192,224},{1,3... | collective-permute-start | bytes 786440 | tf_op jit(solution)/shard_map/ppermute | solution.py:19
  27.8 1.3 collective-permute-start.6
  29.1 5.0 %collective-permute-start.7 = (f32[64,2,1,128]{3,0,2,1:T(8,128)S(1)}, f32[64,2,1,128]{3,0,2,1:T(8,128)S(1)}, u32[]{:S(2)}, u32[]{:S(2)}) collective-permute-start(f32[64,2,1,128]{3,0,2,1:T(8,128)S(1)} %get-tuple-element.30), channel_id=1, source_target_pairs={{0,2},{2,4},{4,6},{6,8},{8,10},{10,12},{12,14},{14,16},{16,18},{18... | collective-permute-start | bytes 196616 | tf_op jit(solution)/shard_map/ppermute | solution.py:19
  35.1 1.3 collective-permute-done.7
  37.7 1.3 collective-permute-start.10
  39.0 1.3 collective-permute-start.8
  40.3 3.0 %collective-permute-start.9 = (f32[64,1,8,128]{3,0,2,1:T(8,128)S(1)}, f32[64,1,8,128]{3,0,2,1:T(8,128)S(1)}, u32[]{:S(2)}, u32[]{:S(2)}) collective-permute-start(f32[64,1,8,128]{3,0,2,1:T(8,128)S(1)} %get-tuple-element.28), channel_id=1, source_target_pairs={{0,32},{32,64},{64,96},{96,128},{128,160},{160,192},{192,224},{1,3... | collective-permute-start | bytes 786440 | tf_op jit(solution)/shard_map/ppermute | solution.py:19
  43.3 5.0 %collective-permute-start.11 = (f32[64,2,1,128]{3,0,2,1:T(8,128)S(1)}, f32[64,2,1,128]{3,0,2,1:T(8,128)S(1)}, u32[]{:S(2)}, u32[]{:S(2)}) collective-permute-start(f32[64,2,1,128]{3,0,2,1:T(8,128)S(1)} %get-tuple-element.26), channel_id=1, source_target_pairs={{0,2},{2,4},{4,6},{6,8},{8,10},{10,12},{12,14},{14,16},{16,18},{18... | collective-permute-start | bytes 196616 | tf_op jit(solution)/shard_map/ppermute | solution.py:19
  54.8 4.8 %collective-permute-done.13 = f32[4,64,64]{1,2,0:T(8,128)S(1)} collective-permute-done((f32[4,64,64]{1,2,0:T(8,128)S(1)}, f32[4,64,64]{1,2,0:T(8,128)S(1)}, u32[]{:S(2)}, u32[]{:S(2)}) %collective-permute-start.13) | collective-permute-done | bytes 65568 | tf_op jit(solution)/shard_map/ppermute | solution.py:43
  59.7 2.8 %collective-permute-start.14 = (f32[4,64,64]{1,2,0:T(8,128)S(1)}, f32[4,64,64]{1,2,0:T(8,128)S(1)}, u32[]{:S(2)}, u32[]{:S(2)}) collective-permute-start(f32[4,64,64]{1,2,0:T(8,128)S(1)} %fusion.128), channel_id=1, source_target_pairs={{0,128},{32,160},{64,192},{96,224},{128,0},{160,32},{192,64},{224,... | collective-permute-start | bytes 196616 | tf_op jit(solution)/shard_map/ppermute | solution.py:43
  62.5 3.7 %collective-permute-done.14 = f32[4,64,64]{1,2,0:T(8,128)S(1)} collective-permute-done((f32[4,64,64]{1,2,0:T(8,128)S(1)}, f32[4,64,64]{1,2,0:T(8,128)S(1)}, u32[]{:S(2)}, u32[]{:S(2)}) %collective-permute-start.14) | collective-permute-done | bytes 65568 | tf_op jit(solution)/shard_map/ppermute | solution.py:43
  66.2 2.4 %collective-permute-start.15 = (f32[4,64,64]{1,2,0:T(8,128)S(1)}, f32[4,64,64]{1,2,0:T(8,128)S(1)}, u32[]{:S(2)}, u32[]{:S(2)}) collective-permute-start(f32[4,64,64]{1,2,0:T(8,128)S(1)} %add.214), channel_id=1, source_target_pairs={{0,2},{2,0},{4,6},{6,4},{8,10},{10,8},{12,14},{14,12},{16,18},{18,... | collective-permute-start | bytes 196616 | tf_op jit(solution)/shard_map/ppermute | solution.py:43
  68.7 2.9 %collective-permute-done.15 = f32[4,64,64]{1,2,0:T(8,128)S(1)} collective-permute-done((f32[4,64,64]{1,2,0:T(8,128)S(1)}, f32[4,64,64]{1,2,0:T(8,128)S(1)}, u32[]{:S(2)}, u32[]{:S(2)}) %collective-permute-start.15) | collective-permute-done | bytes 65568 | tf_op jit(solution)/shard_map/ppermute | solution.py:43
  71.6 6.6 %collective-permute-start.16 = (f32[4,64,64]{1,2,0:T(8,128)S(1)}, f32[4,64,64]{1,2,0:T(8,128)S(1)}, u32[]{:S(2)}, u32[]{:S(2)}) collective-permute-start(f32[4,64,64]{1,2,0:T(8,128)S(1)} %add.215), channel_id=1, source_target_pairs={{0,4},{2,6},{4,0},{6,2},{8,12},{10,14},{12,8},{14,10},{16,20},{18,... | collective-permute-start | bytes 196616 | tf_op jit(solution)/shard_map/ppermute | solution.py:43
  78.2 2.9 %collective-permute-done.16 = f32[4,64,64]{1,2,0:T(8,128)S(1)} collective-permute-done((f32[4,64,64]{1,2,0:T(8,128)S(1)}, f32[4,64,64]{1,2,0:T(8,128)S(1)}, u32[]{:S(2)}, u32[]{:S(2)}) %collective-permute-start.16) | collective-permute-done | bytes 65568 | tf_op jit(solution)/shard_map/ppermute | solution.py:43
  81.8 8.9 %collective-permute-start.17 = (f32[4,64,64]{1,2,0:T(8,128)}, f32[4,64,64]{1,2,0:T(8,128)}, u32[]{:S(2)}, u32[]{:S(2)}) collective-permute-start(f32[4,64,64]{1,2,0:T(8,128)} %add.216), channel_id=1, source_target_pairs={{0,8},{2,10},{4,12},{6,14},{8,0},{10,2},{12,4},{14,6},{16,24},{18,... | collective-permute-start | bytes 196616 | tf_op jit(solution)/shard_map/ppermute | solution.py:43
  90.7 4.1 %collective-permute-done.17 = f32[4,64,64]{1,2,0:T(8,128)} collective-permute-done((f32[4,64,64]{1,2,0:T(8,128)}, f32[4,64,64]{1,2,0:T(8,128)}, u32[]{:S(2)}, u32[]{:S(2)}) %collective-permute-start.17) | collective-permute-done | bytes 65568 | tf_op jit(solution)/shard_map/ppermute | solution.py:43
  95.8 8.6 %collective-permute-start.18 = (f32[4,64,64]{1,2,0:T(8,128)S(1)}, f32[4,64,64]{1,2,0:T(8,128)S(1)}, u32[]{:S(2)}, u32[]{:S(2)}) collective-permute-start(f32[4,64,64]{1,2,0:T(8,128)S(1)} %add.217), channel_id=1, source_target_pairs={{0,16},{2,18},{4,20},{6,22},{8,24},{10,26},{12,28},{14,30},{16,0},... | collective-permute-start | bytes 196616 | tf_op jit(solution)/shard_map/ppermute | solution.py:43
  104.4 4.0 %select_maximum_fusion = f32[64,4,10,130]{3,0,2,1:T(8,128)} fusion(f32[129,4,1,128]{3,0,2,1:T(8,128)S(1)} %pad.41, f32[129,4,1,128]{3,0,2,1:T(8,128)} %copy-done.2, f32[129,1,8,128]{3,0,2,1:T(8,128)S(1)} %copy.83, f32[129,1,8,128]{3,0,2,1:T(8,128)S(1)} %copy.82, f32[64,2,8,128]{3,0,2,1:T(8,128)S(1)} %copy.79, f32[64,2,8,128]{3,0,2,1:T(8,128)S(1)} %copy.78, ...), kind=kLoop, calls=%fused_computation.12 | loop fusion | flops 5324800 | bytes 3973120 | tf_op jit(solution)/shard_map/slice | solution.py:136
  110.6 1.4 fusion.52
  112.0 6.6 %cholesky.59 = f32[64,64]{1,0:T(8,128)S(1)} custom-call(f32[64,64]{1,0:T(8,128)} %get-tuple-element.35), custom_call_target="Cholesky" | custom-call | tf_op jit(solution)/shard_map/jit(cholesky)/cholesky | solution.py:78
  119.3 1.3 fusion.38
  120.6 5.7 %custom-call.13 = f32[1,64,64]{1,2,0:T(8,128)S(1)} custom-call(f32[1,64,64]{2,1,0:T(8,128)} %fusion.38), custom_call_target="InvertDiagBlocksLowerTriangular" | custom-call | tf_op jit(solution)/shard_map/triangular_solve/custom-call.2 | solution.py:80
  129.4 1.6 fusion.78
  132.5 7.2 %cholesky.70 = f32[64,64]{1,0:T(8,128)} custom-call(f32[64,64]{1,0:T(8,128)} %get-tuple-element.34), custom_call_target="Cholesky" | custom-call | tf_op jit(solution)/shard_map/jit(cholesky)/cholesky | solution.py:78
  141.2 2.0 %fusion.39 = f32[1,64,64]{2,1,0:T(8,128)} fusion(f32[64,64]{1,0:T(8,128)} %cholesky.70, pred[]{:T(512)} %compare_reduce_fusion.1), kind=kLoop, calls=%fused_computation.142 | loop fusion | flops 16384 | bytes 32769 | tf_op jit(solution)/shard_map/triangular_solve/reshape.10 | solution.py:80
  143.2 6.3 %custom-call.15 = f32[1,64,64]{1,2,0:T(8,128)} custom-call(f32[1,64,64]{2,1,0:T(8,128)} %fusion.39), custom_call_target="InvertDiagBlocksLowerTriangular" | custom-call | tf_op jit(solution)/shard_map/triangular_solve/custom-call.2 | solution.py:80
  158.1 1.4 copy.104
  159.6 1.4 fusion.59
  161.0 7.2 %cholesky.81 = f32[64,64]{1,0:T(8,128)} custom-call(f32[64,64]{1,0:T(8,128)} %fusion.59), custom_call_target="Cholesky" | custom-call | tf_op jit(solution)/shard_map/jit(cholesky)/cholesky | solution.py:78
  169.6 2.0 %fusion.40 = f32[1,64,64]{2,1,0:T(8,128)} fusion(f32[64,64]{1,0:T(8,128)} %cholesky.81, pred[]{:T(512)} %compare_reduce_fusion), kind=kLoop, calls=%fused_computation.143 | loop fusion | flops 16384 | bytes 32769 | tf_op jit(solution)/shard_map/triangular_solve/reshape.10 | solution.py:80
  171.6 6.3 %custom-call.17 = f32[1,64,64]{1,2,0:T(8,128)} custom-call(f32[1,64,64]{2,1,0:T(8,128)} %fusion.40), custom_call_target="InvertDiagBlocksLowerTriangular" | custom-call | tf_op jit(solution)/shard_map/triangular_solve/custom-call.2 | solution.py:80
  180.0 2.5 %fusion.54 = f32[64,4,10,128]{3,0,2,1:T(8,128)S(1)} fusion(f32[64,64]{1,0:T(8,128)S(1)} %fusion.63, f32[64,4,1,128]{3,0,2,1:T(8,128)} %copy-done.9, f32[64,1,8,128]{3,0,2,1:T(8,128)} %copy-done.5, f32[64,2,8,128]{3,0,2,1:T(8,128)S(1)} %fusion.36, f32[64,1,8,128]{3,0,2,1:T(8,128)} %copy-done.7, f32[64,4,1,128]{3,0,2,1:T(8,128)} %copy-done.11), kind=kOutput, calls=%fused_computation.161 | convolution fusion | flops 252968960 | bytes 2637824 | tf_op jit(solution)/shard_map/axyz,ab->bxyz/dot_general | solution.py:74
  182.5 1.4 fusion.1
  183.9 1.3 fusion.105
  185.2 3.2 %fusion.2 = f32[64,4,10,128]{3,0,2,1:T(8,128)S(1)} fusion(f32[64,4,10,128]{3,0,2,1:T(8,128)S(1)} %fusion.105, f32[64,64]{1,0:T(8,128)S(1)} %fusion.69, f32[129,4,10,128]{3,0,2,1:T(8,128)} %copy-done.1, f32[64,4,1,128]{3,0,2,1:T(8,128)S(1)} %copy-done.10, f32[64,1,8,128]{3,0,2,1:T(8,128)S(1)} %copy-done.6, f32[64,2,8,128]{3,0,2,1:T(8,128)S(1)} %fusion.36, ...), kind=kOutput, calls=%fused_computation.22 | convolution fusion | flops 253624320 | bytes 5259264 | tf_op jit(solution)/shard_map/axyz,ab->bxyz/dot_general | solution.py:74
  189.5 1.1 copy-done.4
  194.1 2.5 %collective-permute-done.19 = f32[2,8,64]{2,1,0:T(8,128)S(1)} collective-permute-done((f32[2,8,64]{2,1,0:T(8,128)S(1)}, f32[2,8,64]{2,1,0:T(8,128)S(1)}, u32[]{:S(2)}, u32[]{:S(2)}) %collective-permute-start.19) | collective-permute-done | bytes 4128 | tf_op jit(solution)/shard_map/ppermute | solution.py:195
  (169 shorter events, 40.8 us)
Async XLA Ops:
  0.6 1.3 copy-start.24
  0.6 1.5 copy-start.22
  2.2 13.7 %collective-permute-start.3 = (f32[129,2,1,128]{3,0,2,1:T(8,128)S(1)}, f32[129,2,1,128]{3,0,2,1:T(8,128)S(1)}, u32[]{:S(2)}, u32[]{:S(2)}) collective-permute-start(f32[129,2,1,128]{3,0,2,1:T(8,128)S(1)} %get-tuple-element.25), channel_id=1, source_target_pairs={{2,0},{4,2},{6,4},{8,6},{10,8},{12,10},{14,12},{16,14},{18,16},{20... | collective-permute-start | bytes 396296 | tf_op jit(solution)/shard_map/ppermute | solution.py:22
  3.6 10.7 %copy-start.27 = (s32[64]{0:T(128)S(1)}, s32[64]{0:T(128)}, u32[]{:S(2)}) copy-start(s32[64]{0:T(128)} %param.12) | copy-start | bytes 772
  3.6 10.8 %copy-start.26 = (s32[128,2]{0,1:T(2,128)S(1)}, s32[128,2]{0,1:T(2,128)}, u32[]{:S(2)}) copy-start(s32[128,2]{0,1:T(2,128)} %param.11) | copy-start | bytes 3076
  3.8 14.1 %collective-permute-start.2 = (f32[129,1,8,128]{3,2,1,0:T(8,128)S(1)}, f32[129,1,8,128]{3,2,1,0:T(8,128)}, u32[]{:S(2)}, u32[]{:S(2)}) collective-permute-start(f32[129,1,8,128]{3,2,1,0:T(8,128)S(1)} %copy.81), channel_id=1, source_target_pairs={{32,0},{64,32},{96,64},{128,96},{160,128},{192,160},{224,192},{33,... | collective-permute-start | bytes 1585160 | tf_op jit(solution)/shard_map/ppermute | solution.py:22
  6.0 13.2 %collective-permute-start.1 = (f32[129,1,8,128]{3,2,1,0:T(8,128)}, f32[129,1,8,128]{3,2,1,0:T(8,128)}, u32[]{:S(2)}, u32[]{:S(2)}) collective-permute-start(f32[129,1,8,128]{3,2,1,0:T(8,128)} %copy.80), channel_id=1, source_target_pairs={{0,32},{32,64},{64,96},{96,128},{128,160},{160,192},{192,224},{1,3... | collective-permute-start | bytes 1585160 | tf_op jit(solution)/shard_map/ppermute | solution.py:19
  9.8 8.0 %collective-permute-start = (f32[129,2,1,128]{3,0,2,1:T(8,128)S(1)}, f32[129,2,1,128]{3,0,2,1:T(8,128)S(1)}, u32[]{:S(2)}, u32[]{:S(2)}) collective-permute-start(f32[129,2,1,128]{3,0,2,1:T(8,128)S(1)} %get-tuple-element.24), channel_id=1, source_target_pairs={{0,2},{2,4},{4,6},{6,8},{8,10},{10,12},{12,14},{14,16},{16,18},{18... | collective-permute-start | bytes 396296 | tf_op jit(solution)/shard_map/ppermute | solution.py:19
  17.9 4.5 %copy-start.2 = (f32[129,4,1,128]{3,0,2,1:T(8,128)}, f32[129,4,1,128]{3,0,2,1:T(8,128)S(1)}, u32[]{:S(2)}) copy-start(f32[129,4,1,128]{3,0,2,1:T(8,128)S(1)} %pad.40) | copy-start | bytes 792580
  20.5 1.6 copy-start.1
  23.4 13.0 %collective-permute-start.4 = (f32[64,1,8,128]{3,0,2,1:T(8,128)S(1)}, f32[64,1,8,128]{3,0,2,1:T(8,128)S(1)}, u32[]{:S(2)}, u32[]{:S(2)}) collective-permute-start(f32[64,1,8,128]{3,0,2,1:T(8,128)S(1)} %get-tuple-element.33), channel_id=1, source_target_pairs={{32,0},{64,32},{96,64},{128,96},{160,128},{192,160},{224,192},{33,... | collective-permute-start | bytes 786440 | tf_op jit(solution)/shard_map/ppermute | solution.py:22
  24.7 11.7 %collective-permute-start.5 = (f32[64,1,8,128]{3,0,2,1:T(8,128)S(1)}, f32[64,1,8,128]{3,0,2,1:T(8,128)S(1)}, u32[]{:S(2)}, u32[]{:S(2)}) collective-permute-start(f32[64,1,8,128]{3,0,2,1:T(8,128)S(1)} %get-tuple-element.32), channel_id=1, source_target_pairs={{0,32},{32,64},{64,96},{96,128},{128,160},{160,192},{192,224},{1,3... | collective-permute-start | bytes 786440 | tf_op jit(solution)/shard_map/ppermute | solution.py:19
  27.8 7.3 %collective-permute-start.6 = (f32[64,2,1,128]{3,0,2,1:T(8,128)S(1)}, f32[64,2,1,128]{3,0,2,1:T(8,128)S(1)}, u32[]{:S(2)}, u32[]{:S(2)}) collective-permute-start(f32[64,2,1,128]{3,0,2,1:T(8,128)S(1)} %get-tuple-element.31), channel_id=1, source_target_pairs={{2,0},{4,2},{6,4},{8,6},{10,8},{12,10},{14,12},{16,14},{18,16},{20... | collective-permute-start | bytes 196616 | tf_op jit(solution)/shard_map/ppermute | solution.py:22
  29.1 7.3 %collective-permute-start.7 = (f32[64,2,1,128]{3,0,2,1:T(8,128)S(1)}, f32[64,2,1,128]{3,0,2,1:T(8,128)S(1)}, u32[]{:S(2)}, u32[]{:S(2)}) collective-permute-start(f32[64,2,1,128]{3,0,2,1:T(8,128)S(1)} %get-tuple-element.30), channel_id=1, source_target_pairs={{0,2},{2,4},{4,6},{6,8},{8,10},{10,12},{12,14},{14,16},{16,18},{18... | collective-permute-start | bytes 196616 | tf_op jit(solution)/shard_map/ppermute | solution.py:19
  35.1 1.8 copy-start.9
  36.4 0.7 copy-start.11
  36.4 0.7 copy-start.5
  36.4 0.8 copy-start.7
  37.7 11.8 %collective-permute-start.10 = (f32[64,2,1,128]{3,0,2,1:T(8,128)S(1)}, f32[64,2,1,128]{3,0,2,1:T(8,128)S(1)}, u32[]{:S(2)}, u32[]{:S(2)}) collective-permute-start(f32[64,2,1,128]{3,0,2,1:T(8,128)S(1)} %get-tuple-element.27), channel_id=1, source_target_pairs={{2,0},{4,2},{6,4},{8,6},{10,8},{12,10},{14,12},{16,14},{18,16},{20... | collective-permute-start | bytes 196616 | tf_op jit(solution)/shard_map/ppermute | solution.py:22
  39.0 11.7 %collective-permute-start.8 = (f32[64,1,8,128]{3,0,2,1:T(8,128)S(1)}, f32[64,1,8,128]{3,0,2,1:T(8,128)S(1)}, u32[]{:S(2)}, u32[]{:S(2)}) collective-permute-start(f32[64,1,8,128]{3,0,2,1:T(8,128)S(1)} %get-tuple-element.29), channel_id=1, source_target_pairs={{32,0},{64,32},{96,64},{128,96},{160,128},{192,160},{224,192},{33,... | collective-permute-start | bytes 786440 | tf_op jit(solution)/shard_map/ppermute | solution.py:22
  40.3 10.4 %collective-permute-start.9 = (f32[64,1,8,128]{3,0,2,1:T(8,128)S(1)}, f32[64,1,8,128]{3,0,2,1:T(8,128)S(1)}, u32[]{:S(2)}, u32[]{:S(2)}) collective-permute-start(f32[64,1,8,128]{3,0,2,1:T(8,128)S(1)} %get-tuple-element.28), channel_id=1, source_target_pairs={{0,32},{32,64},{64,96},{96,128},{128,160},{160,192},{192,224},{1,3... | collective-permute-start | bytes 786440 | tf_op jit(solution)/shard_map/ppermute | solution.py:19
  43.3 7.3 %collective-permute-start.11 = (f32[64,2,1,128]{3,0,2,1:T(8,128)S(1)}, f32[64,2,1,128]{3,0,2,1:T(8,128)S(1)}, u32[]{:S(2)}, u32[]{:S(2)}) collective-permute-start(f32[64,2,1,128]{3,0,2,1:T(8,128)S(1)} %get-tuple-element.26), channel_id=1, source_target_pairs={{0,2},{2,4},{4,6},{6,8},{8,10},{10,12},{12,14},{14,16},{16,18},{18... | collective-permute-start | bytes 196616 | tf_op jit(solution)/shard_map/ppermute | solution.py:19
  49.5 1.7 copy-start.18
  50.7 0.6 copy-start.20
  50.7 0.7 copy-start.13
  50.7 0.8 copy-start.15
  52.4 1.4 collective-permute-start.12
  53.8 5.8 %collective-permute-start.13 = (f32[4,64,64]{1,2,0:T(8,128)S(1)}, f32[4,64,64]{1,2,0:T(8,128)S(1)}, u32[]{:S(2)}, u32[]{:S(2)}) collective-permute-start(f32[4,64,64]{1,2,0:T(8,128)S(1)} %fusion.98), channel_id=1, source_target_pairs={{0,64},{32,96},{64,0},{96,32},{128,192},{160,224},{192,128},{224,1... | collective-permute-start | bytes 196616 | tf_op jit(solution)/shard_map/ppermute | solution.py:43
  59.7 6.6 %collective-permute-start.14 = (f32[4,64,64]{1,2,0:T(8,128)S(1)}, f32[4,64,64]{1,2,0:T(8,128)S(1)}, u32[]{:S(2)}, u32[]{:S(2)}) collective-permute-start(f32[4,64,64]{1,2,0:T(8,128)S(1)} %fusion.128), channel_id=1, source_target_pairs={{0,128},{32,160},{64,192},{96,224},{128,0},{160,32},{192,64},{224,... | collective-permute-start | bytes 196616 | tf_op jit(solution)/shard_map/ppermute | solution.py:43
  66.2 5.4 %collective-permute-start.15 = (f32[4,64,64]{1,2,0:T(8,128)S(1)}, f32[4,64,64]{1,2,0:T(8,128)S(1)}, u32[]{:S(2)}, u32[]{:S(2)}) collective-permute-start(f32[4,64,64]{1,2,0:T(8,128)S(1)} %add.214), channel_id=1, source_target_pairs={{0,2},{2,0},{4,6},{6,4},{8,10},{10,8},{12,14},{14,12},{16,18},{18,... | collective-permute-start | bytes 196616 | tf_op jit(solution)/shard_map/ppermute | solution.py:43
  71.6 9.5 %collective-permute-start.16 = (f32[4,64,64]{1,2,0:T(8,128)S(1)}, f32[4,64,64]{1,2,0:T(8,128)S(1)}, u32[]{:S(2)}, u32[]{:S(2)}) collective-permute-start(f32[4,64,64]{1,2,0:T(8,128)S(1)} %add.215), channel_id=1, source_target_pairs={{0,4},{2,6},{4,0},{6,2},{8,12},{10,14},{12,8},{14,10},{16,20},{18,... | collective-permute-start | bytes 196616 | tf_op jit(solution)/shard_map/ppermute | solution.py:43
  81.8 13.0 %collective-permute-start.17 = (f32[4,64,64]{1,2,0:T(8,128)}, f32[4,64,64]{1,2,0:T(8,128)}, u32[]{:S(2)}, u32[]{:S(2)}) collective-permute-start(f32[4,64,64]{1,2,0:T(8,128)} %add.216), channel_id=1, source_target_pairs={{0,8},{2,10},{4,12},{6,14},{8,0},{10,2},{12,4},{14,6},{16,24},{18,... | collective-permute-start | bytes 196616 | tf_op jit(solution)/shard_map/ppermute | solution.py:43
  95.8 12.6 %collective-permute-start.18 = (f32[4,64,64]{1,2,0:T(8,128)S(1)}, f32[4,64,64]{1,2,0:T(8,128)S(1)}, u32[]{:S(2)}, u32[]{:S(2)}) collective-permute-start(f32[4,64,64]{1,2,0:T(8,128)S(1)} %add.217), channel_id=1, source_target_pairs={{0,16},{2,18},{4,20},{6,22},{8,24},{10,26},{12,28},{14,30},{16,0},... | collective-permute-start | bytes 196616 | tf_op jit(solution)/shard_map/ppermute | solution.py:43
  108.5 0.7 copy-start.17
  150.3 0.6 copy-start.25
  179.9 2.6 %copy-start.6 = (f32[64,1,8,128]{3,0,2,1:T(8,128)S(1)}, f32[64,1,8,128]{3,0,2,1:T(8,128)}, u32[]{:S(2)}) copy-start(f32[64,1,8,128]{3,0,2,1:T(8,128)} %copy-done.5) | copy-start | bytes 786436
  179.9 2.6 %copy-start.8 = (f32[64,1,8,128]{3,0,2,1:T(8,128)S(1)}, f32[64,1,8,128]{3,0,2,1:T(8,128)}, u32[]{:S(2)}) copy-start(f32[64,1,8,128]{3,0,2,1:T(8,128)} %copy-done.7) | copy-start | bytes 786436
  179.9 2.6 %copy-start.10 = (f32[64,4,1,128]{3,0,2,1:T(8,128)S(1)}, f32[64,4,1,128]{3,0,2,1:T(8,128)}, u32[]{:S(2)}) copy-start(f32[64,4,1,128]{3,0,2,1:T(8,128)} %copy-done.9) | copy-start | bytes 393220
  179.9 2.6 %copy-start.12 = (f32[64,4,1,128]{3,0,2,1:T(8,128)S(1)}, f32[64,4,1,128]{3,0,2,1:T(8,128)}, u32[]{:S(2)}) copy-start(f32[64,4,1,128]{3,0,2,1:T(8,128)} %copy-done.11) | copy-start | bytes 393220
  179.9 2.6 %copy-start.14 = (f32[64,1,8,128]{3,0,2,1:T(8,128)S(1)}, f32[64,1,8,128]{3,0,2,1:T(8,128)}, u32[]{:S(2)}) copy-start(f32[64,1,8,128]{3,0,2,1:T(8,128)} %copy-done.13) | copy-start | bytes 786436
  180.0 2.6 %copy-start.16 = (f32[64,1,8,128]{3,0,2,1:T(8,128)S(1)}, f32[64,1,8,128]{3,0,2,1:T(8,128)}, u32[]{:S(2)}) copy-start(f32[64,1,8,128]{3,0,2,1:T(8,128)} %copy-done.15) | copy-start | bytes 786436
  180.0 2.6 %copy-start.19 = (f32[64,4,1,128]{3,0,2,1:T(8,128)S(1)}, f32[64,4,1,128]{3,0,2,1:T(8,128)}, u32[]{:S(2)}) copy-start(f32[64,4,1,128]{3,0,2,1:T(8,128)} %copy-done.18) | copy-start | bytes 393220
  180.0 2.6 %copy-start.21 = (f32[64,4,1,128]{3,0,2,1:T(8,128)S(1)}, f32[64,4,1,128]{3,0,2,1:T(8,128)}, u32[]{:S(2)}) copy-start(f32[64,4,1,128]{3,0,2,1:T(8,128)} %copy-done.20) | copy-start | bytes 393220
  185.2 3.2 %copy-start.3 = (f32[129,4,1,128]{3,0,2,1:T(8,128)S(1)}, f32[129,4,1,128]{3,0,2,1:T(8,128)}, u32[]{:S(2)}) copy-start(f32[129,4,1,128]{3,0,2,1:T(8,128)} %copy-done.2) | copy-start | bytes 792580
  185.2 3.2 %copy-start.23 = (f32[2,8,128]{2,1,0:T(8,128)S(1)}, f32[2,8,128]{2,1,0:T(8,128)}, u32[]{:S(2)}) copy-start(f32[2,8,128]{2,1,0:T(8,128)} %param.10) | copy-start | bytes 24580
  188.4 1.1 copy-start
  188.6 2.1 %copy-start.4 = (f32[64,4,10,130]{3,0,2,1:T(8,128)S(1)}, f32[64,4,10,130]{3,0,2,1:T(8,128)}, u32[]{:S(2)}) copy-start(f32[64,4,10,130]{3,0,2,1:T(8,128)} %select_maximum_fusion) | copy-start | bytes 3993604
  191.4 5.2 %collective-permute-start.19 = (f32[2,8,64]{2,1,0:T(8,128)S(1)}, f32[2,8,64]{2,1,0:T(8,128)S(1)}, u32[]{:S(2)}, u32[]{:S(2)}) collective-permute-start(f32[2,8,64]{2,1,0:T(8,128)S(1)} %constant_dynamic-slice_fusion), channel_id=1, source_target_pairs={{0,1},{1,0},{2,3},{3,2},{4,5},{5,4},{6,7},{7,6},{8,9},{9,8},{10,11... | collective-permute-start | bytes 12296 | tf_op jit(solution)/shard_map/ppermute | solution.py:195

commit v3 on v2

--- a/solution.py
+++ b/solution.py
@@ -2,6 +2,7 @@
 import jax.numpy as jnp
 from jax import lax
 from jax.sharding import PartitionSpec as P
+from jax.experimental import pallas as pl
 
 ITERS = 2
 
@@ -105,6 +106,62 @@
         axis=0,
     )
     return (term_x, term_y, term_z)
+
+
+HI = lax.Precision.HIGHEST
+
+def _mm(a, b):
+    return jnp.dot(a, b, precision=HI, preferred_element_type=jnp.float32)
+
+def _tr(a):
+    return jnp.transpose(a)
+
+def _solve(matrix, right):
+    n = matrix.shape[0]
+    rows = lax.broadcasted_iota(jnp.int32, matrix.shape, 0)
+    lanes = lax.broadcasted_iota(jnp.int32, matrix.shape, 1)
+    lane_r = lax.broadcasted_iota(jnp.int32, (1, n), 1)
+
+    def step(j, carry):
+        m, r = carry
+        pick = rows == j
+        row_m = jnp.sum(jnp.where(pick, m, 0.0), axis=0, keepdims=True)
+        row_r = jnp.sum(jnp.where(pick, r, 0.0), axis=0, keepdims=True)
+        pivot = jnp.sum(jnp.where(lane_r == j, row_m, 0.0), axis=1, keepdims=True)
+        col = jnp.sum(jnp.where(lanes == j, m, 0.0), axis=1, keepdims=True)
+        row_m = row_m / pivot
+        row_r = row_r / pivot
+        m = jnp.where(pick, row_m, m - col * row_m)
+        r = jnp.where(pick, row_r, r - col * row_r)
+        return m, r
+
+    _, out = lax.fori_loop(0, n, step, (matrix, right))
+    return out
+
+def steps_kernel(grams_ref, out_ref):
+    g_rr = grams_ref[0]
+    g_rq = grams_ref[1]
+    g_qq = grams_ref[2]
+    g_qw = grams_ref[3]
+    n = g_rr.shape[0]
+    step0 = _solve(g_rq, g_rr)
+    cross = _mm(g_rq, step0)
+    step0_t = _tr(step0)
+    new_gram = g_rr - cross - _tr(cross) + _mm(step0_t, _mm(g_qq, step0))
+    turn = _solve(g_rr, new_gram)
+    eye = (lax.broadcasted_iota(jnp.int32, (n, n), 0) == lax.broadcasted_iota(jnp.int32, (n, n), 1)).astype(jnp.float32)
+    keep = eye + turn
+    keep_t = _tr(keep)
+    curv = (_mm(keep_t, _mm(g_rq, keep)) - _mm(keep_t, _mm(g_qq, step0))
+            - _mm(step0_t, _mm(g_qq, keep)) + _mm(step0_t, _mm(g_qw, step0)))
+    step1 = _solve(curv, new_gram)
+    out_ref[0] = step0
+    out_ref[1] = turn
+    out_ref[2] = step1
+
+def steps(grams):
+    n = grams.shape[1]
+    return pl.pallas_call(steps_kernel, out_shape=jax.ShapeDtypeStruct((3, n, n), jnp.float32))(grams)
 
 
 def on_device(conductivity, electrodes, pair_order, initial_fields, adjoint_fields):
@@ -150,24 +207,9 @@
         ),
         grid_axes,
     )
-    g_rr, g_rq, g_qq, g_qw = grams[0], grams[1], grams[2], grams[3]
-
-    def mm(left, right):
-        return jnp.matmul(left, right, precision=lax.Precision.HIGHEST)
-
-    step0 = posdef_solve(g_rq, g_rr)
-    cross = mm(g_rq, step0)
-    new_gram = g_rr - cross - cross.T + mm(step0.T, mm(g_qq, step0))
-    turn = posdef_solve(g_rr, new_gram)
-    keep = jnp.eye(columns, dtype=turn.dtype) + turn
-    back = -step0
-    curv = (
-        mm(keep.T, mm(g_rq, keep))
-        + mm(keep.T, mm(g_qq, back))
-        + mm(back.T, mm(g_qq, keep))
-        + mm(back.T, mm(g_qw, back))
-    )
-    step1 = posdef_solve(curv, new_gram)
+
+    solved = steps(grams)
+    step0, turn, step1 = solved[0], solved[1], solved[2]
     res1_pad = res_pad - combine_cols(image_pad, step0)
     dir1_pad = res1_pad + combine_cols(res_pad, turn)
     it1_pad = iter_pad + combine_cols(res_pad, step0)

time: 200 us -> 150 us (0.75)
  other arithmetic: 62.9 us -> 12.6 us
  Pallas kernels: 0 us -> 23.2 us
  matrix products: 25.4 us -> 10.5 us
  local copies, waits for them, and re-layouts: 17 us -> 10.9 us
    another operation x18 -> x3, other arithmetic: 48.3 us -> 0.23 us  [the longest x9 24.5 us: posdef_solve(): lower = jnp.linalg.cholesky(matrix)]
    pallas_call x0 -> x1, Pallas kernels: none -> 23.2 us  [steps(): pl.pallas_call(steps_kernel, out_shape=jax.ShapeDtypeStruct((3, n, n), jn...]
    dot_general x11 -> x0, matrix products: 9.71 us -> none  [mm(): return jnp.matmul(left, right, precision=lax.Precision.HIGHEST)]
    another operation x6 -> x0, matrix products: 5.07 us -> none  [the longest x3 3 us: posdef_solve(): lax.linalg.triangular_solve(lower, right, left_side=True, lower=True)]
    div x2 -> x0, other arithmetic: 2.79 us -> none  [posdef_solve(): lower = jnp.linalg.cholesky(matrix)]
    unnamed x60 -> x56, local copies, waits for them, and re-layouts: 7.73 us -> 6.43 us
  transfers between devices with their start and end apart: 20 -> 20, of which waited for: 11 -> 11; matrix products, arithmetic and copies ran while one was open for 6% -> 7% of each run, Pallas kernels for 0% -> 0%
where the time goes in v3:
time: 150 us; the launch traced here: 149 us
  starting transfers between devices  63.3 us (42%)
  waiting for transfers between devices  27.2 us (18%)
  Pallas kernels  23.2 us (15%)
  other arithmetic  12.6 us (8%)
  local copies, waits for them, and re-layouts  10.9 us (7%)
  matrix products  10.5 us (7%)
  between operations  1.52 us (1%)
    ppermute x7, starting transfers between devices, allsum(): value = value + lax.ppermute(value, axis, pairs)  30.5 us
    ppermute x6, starting transfers between devices, padded_2(): lax.ppermute(lax.slice_in_dim(block, block.shape[dim] - width, None, axis...  24.5 us
    pallas_call x1, Pallas kernels, steps(): pl.pallas_call(steps_kernel, out_shape=jax.ShapeDtypeStruct((3, n, n), jn...  23.2 us
    ppermute x7, waiting for transfers between devices, allsum(): value = value + lax.ppermute(value, axis, pairs)  20 us
    dot_general x4, matrix products, combine_cols(): jnp.einsum('axyz,ab->bxyz', field, matrix, precision=lax.Precision.HIGHEST)  8.07 us
    ppermute x6, starting transfers between devices, padded_2(): lax.ppermute(lax.slice_in_dim(block, 0, width, axis=dim), axis, backward)  7.74 us
    unnamed x56, local copies, waits for them, and re-layouts  6.43 us
    ppermute x6, waiting for transfers between devices, padded_2(): lax.ppermute(lax.slice_in_dim(block, block.shape[dim] - width, None, axis...  4.42 us
  transfers between devices with their start and end apart: 20, of which 11 were waited for; matrix products, arithmetic and copies ran while one was open for 7% of the time, Pallas kernels for 0%

profile of v3, /device:TPU:4, one launch (start us, length us, event | category | flops | bytes accessed | tf_op | source)
XLA Modules:
  0.0 149.1 jit_solution(13086038748659419654)
XLA Ops:
  0.6 1.3 copy.42
  2.1 0.7 pad_maximum_fusion.33
  2.8 1.3 collective-permute-start.3
  4.4 1.3 collective-permute-start.2
  5.7 0.9 copy.43
  6.6 3.8 %collective-permute-start.1 = (f32[129,1,8,128]{3,2,1,0:T(8,128)}, f32[129,1,8,128]{3,2,1,0:T(8,128)}, u32[]{:S(2)}, u32[]{:S(2)}) collective-permute-start(f32[129,1,8,128]{3,2,1,0:T(8,128)} %copy.43), channel_id=1, source_target_pairs={{0,32},{32,64},{64,96},{96,128},{128,160},{160,192},{192,224},{1,3... | collective-permute-start | bytes 1585160 | tf_op jit(solution)/shard_map/ppermute | solution.py:20
  10.5 4.5 %collective-permute-start = (f32[129,2,1,128]{3,0,2,1:T(8,128)S(1)}, f32[129,2,1,128]{3,0,2,1:T(8,128)S(1)}, u32[]{:S(2)}, u32[]{:S(2)}) collective-permute-start(f32[129,2,1,128]{3,0,2,1:T(8,128)S(1)} %get-tuple-element.21), channel_id=1, source_target_pairs={{0,2},{2,4},{4,6},{6,8},{8,10},{10,12},{12,14},{14,16},{16,18},{18... | collective-permute-start | bytes 396296 | tf_op jit(solution)/shard_map/ppermute | solution.py:20
  16.5 2.0 %collective-permute-done = f32[129,2,1,128]{3,0,2,1:T(8,128)S(1)} collective-permute-done((f32[129,2,1,128]{3,0,2,1:T(8,128)S(1)}, f32[129,2,1,128]{3,0,2,1:T(8,128)S(1)}, u32[]{:S(2)}, u32[]{:S(2)}) %collective-permute-start) | collective-permute-done | bytes 132128 | tf_op jit(solution)/shard_map/ppermute | solution.py:20
  18.6 1.1 copy.45
  20.1 1.4 copy-done.1
  22.9 1.3 collective-permute-start.4
  24.2 3.0 %collective-permute-start.5 = (f32[64,1,8,128]{3,0,2,1:T(8,128)S(1)}, f32[64,1,8,128]{3,0,2,1:T(8,128)S(1)}, u32[]{:S(2)}, u32[]{:S(2)}) collective-permute-start(f32[64,1,8,128]{3,0,2,1:T(8,128)S(1)} %get-tuple-element.29), channel_id=1, source_target_pairs={{0,32},{32,64},{64,96},{96,128},{128,160},{160,192},{192,224},{1,3... | collective-permute-start | bytes 786440 | tf_op jit(solution)/shard_map/ppermute | solution.py:20
  27.3 1.3 collective-permute-start.6
  28.6 5.0 %collective-permute-start.7 = (f32[64,2,1,128]{3,0,2,1:T(8,128)S(1)}, f32[64,2,1,128]{3,0,2,1:T(8,128)S(1)}, u32[]{:S(2)}, u32[]{:S(2)}) collective-permute-start(f32[64,2,1,128]{3,0,2,1:T(8,128)S(1)} %get-tuple-element.27), channel_id=1, source_target_pairs={{0,2},{2,4},{4,6},{6,8},{8,10},{10,12},{12,14},{14,16},{16,18},{18... | collective-permute-start | bytes 196616 | tf_op jit(solution)/shard_map/ppermute | solution.py:20
  34.6 1.4 collective-permute-done.7
  37.2 1.3 collective-permute-start.10
  38.5 1.3 collective-permute-start.8
  39.8 3.0 %collective-permute-start.9 = (f32[64,1,8,128]{3,0,2,1:T(8,128)S(1)}, f32[64,1,8,128]{3,0,2,1:T(8,128)S(1)}, u32[]{:S(2)}, u32[]{:S(2)}) collective-permute-start(f32[64,1,8,128]{3,0,2,1:T(8,128)S(1)} %get-tuple-element.25), channel_id=1, source_target_pairs={{0,32},{32,64},{64,96},{96,128},{128,160},{160,192},{192,224},{1,3... | collective-permute-start | bytes 786440 | tf_op jit(solution)/shard_map/ppermute | solution.py:20
  42.9 5.0 %collective-permute-start.11 = (f32[64,2,1,128]{3,0,2,1:T(8,128)S(1)}, f32[64,2,1,128]{3,0,2,1:T(8,128)S(1)}, u32[]{:S(2)}, u32[]{:S(2)}) collective-permute-start(f32[64,2,1,128]{3,0,2,1:T(8,128)S(1)} %get-tuple-element.23), channel_id=1, source_target_pairs={{0,2},{2,4},{4,6},{6,8},{8,10},{10,12},{12,14},{14,16},{16,18},{18... | collective-permute-start | bytes 196616 | tf_op jit(solution)/shard_map/ppermute | solution.py:20
  49.1 1.1 collective-permute-done.11
  51.2 0.7 convolution_bitcast_fusion
  52.3 1.0 collective-permute-done.12
  53.4 1.1 collective-permute-start.13
  54.5 4.7 %collective-permute-done.13 = f32[4,64,64]{2,1,0:T(8,128)S(1)} collective-permute-done((f32[4,64,64]{2,1,0:T(8,128)S(1)}, f32[4,64,64]{2,1,0:T(8,128)S(1)}, u32[]{:S(2)}, u32[]{:S(2)}) %collective-permute-start.13) | collective-permute-done | bytes 65568 | tf_op jit(solution)/shard_map/ppermute | solution.py:44
  59.2 2.8 %collective-permute-start.14 = (f32[4,64,64]{2,1,0:T(8,128)S(1)}, f32[4,64,64]{2,1,0:T(8,128)S(1)}, u32[]{:S(2)}, u32[]{:S(2)}) collective-permute-start(f32[4,64,64]{2,1,0:T(8,128)S(1)} %fusion.75), channel_id=1, source_target_pairs={{0,128},{32,160},{64,192},{96,224},{128,0},{160,32},{192,64},{224,... | collective-permute-start | bytes 196616 | tf_op jit(solution)/shard_map/ppermute | solution.py:44
  62.0 3.7 %collective-permute-done.14 = f32[4,64,64]{2,1,0:T(8,128)S(1)} collective-permute-done((f32[4,64,64]{2,1,0:T(8,128)S(1)}, f32[4,64,64]{2,1,0:T(8,128)S(1)}, u32[]{:S(2)}, u32[]{:S(2)}) %collective-permute-start.14) | collective-permute-done | bytes 65568 | tf_op jit(solution)/shard_map/ppermute | solution.py:44
  65.8 2.4 %collective-permute-start.15 = (f32[4,64,64]{2,1,0:T(8,128)S(1)}, f32[4,64,64]{2,1,0:T(8,128)S(1)}, u32[]{:S(2)}, u32[]{:S(2)}) collective-permute-start(f32[4,64,64]{2,1,0:T(8,128)S(1)} %add.190), channel_id=1, source_target_pairs={{0,2},{2,0},{4,6},{6,4},{8,10},{10,8},{12,14},{14,12},{16,18},{18,... | collective-permute-start | bytes 196616 | tf_op jit(solution)/shard_map/ppermute | solution.py:44
  68.2 2.9 %collective-permute-done.15 = f32[4,64,64]{2,1,0:T(8,128)S(1)} collective-permute-done((f32[4,64,64]{2,1,0:T(8,128)S(1)}, f32[4,64,64]{2,1,0:T(8,128)S(1)}, u32[]{:S(2)}, u32[]{:S(2)}) %collective-permute-start.15) | collective-permute-done | bytes 65568 | tf_op jit(solution)/shard_map/ppermute | solution.py:44
  71.2 6.6 %collective-permute-start.16 = (f32[4,64,64]{2,1,0:T(8,128)S(1)}, f32[4,64,64]{2,1,0:T(8,128)S(1)}, u32[]{:S(2)}, u32[]{:S(2)}) collective-permute-start(f32[4,64,64]{2,1,0:T(8,128)S(1)} %add.191), channel_id=1, source_target_pairs={{0,4},{2,6},{4,0},{6,2},{8,12},{10,14},{12,8},{14,10},{16,20},{18,... | collective-permute-start | bytes 196616 | tf_op jit(solution)/shard_map/ppermute | solution.py:44
  77.8 2.9 %collective-permute-done.16 = f32[4,64,64]{2,1,0:T(8,128)S(1)} collective-permute-done((f32[4,64,64]{2,1,0:T(8,128)S(1)}, f32[4,64,64]{2,1,0:T(8,128)S(1)}, u32[]{:S(2)}, u32[]{:S(2)}) %collective-permute-start.16) | collective-permute-done | bytes 65568 | tf_op jit(solution)/shard_map/ppermute | solution.py:44
  80.7 0.7 add.192
  81.4 7.4 %collective-permute-start.17 = (f32[4,64,64]{2,1,0:T(8,128)}, f32[4,64,64]{2,1,0:T(8,128)}, u32[]{:S(2)}, u32[]{:S(2)}) collective-permute-start(f32[4,64,64]{2,1,0:T(8,128)} %add.192), channel_id=1, source_target_pairs={{0,8},{2,10},{4,12},{6,14},{8,0},{10,2},{12,4},{14,6},{16,24},{18,... | collective-permute-start | bytes 196616 | tf_op jit(solution)/shard_map/ppermute | solution.py:44
  88.7 4.6 %collective-permute-done.17 = f32[4,64,64]{2,1,0:T(8,128)} collective-permute-done((f32[4,64,64]{2,1,0:T(8,128)}, f32[4,64,64]{2,1,0:T(8,128)}, u32[]{:S(2)}, u32[]{:S(2)}) %collective-permute-start.17) | collective-permute-done | bytes 65568 | tf_op jit(solution)/shard_map/ppermute | solution.py:44
  93.3 1.0 add.193
  94.3 9.8 %collective-permute-start.18 = (f32[4,64,64]{2,1,0:T(8,128)S(1)}, f32[4,64,64]{2,1,0:T(8,128)S(1)}, u32[]{:S(2)}, u32[]{:S(2)}) collective-permute-start(f32[4,64,64]{2,1,0:T(8,128)S(1)} %add.193), channel_id=1, source_target_pairs={{0,16},{2,18},{4,20},{6,22},{8,24},{10,26},{12,28},{14,30},{16,0},... | collective-permute-start | bytes 196616 | tf_op jit(solution)/shard_map/ppermute | solution.py:44
  104.1 4.0 %select_maximum_fusion = f32[64,4,10,130]{3,0,2,1:T(8,128)} fusion(f32[129,4,1,128]{3,0,2,1:T(8,128)S(1)} %pad.41, f32[129,4,1,128]{3,0,2,1:T(8,128)} %copy-done.2, f32[129,1,8,128]{3,0,2,1:T(8,128)S(1)} %copy.46, f32[129,1,8,128]{3,0,2,1:T(8,128)S(1)} %copy.45, f32[64,2,8,128]{3,0,2,1:T(8,128)S(1)} %copy.42, f32[64,2,8,128]{3,0,2,1:T(8,128)S(1)} %copy.41, ...), kind=kLoop, calls=%fused_computation.12 | loop fusion | flops 5324800 | bytes 3973120 | tf_op jit(solution)/shard_map/slice | solution.py:193
  108.1 0.7 add.194.grams_ref
  108.8 23.2 %shard_map.68 = f32[3,64,64]{2,1,0:T(8,128)} custom-call(f32[4,64,64]{2,1,0:T(8,128)} %add.194.grams_ref), custom_call_target="tpu_custom_call" | custom-call | tf_op jit(solution)/shard_map/pallas_call | solution.py:164
  132.1 2.5 %fusion.48 = f32[64,4,10,128]{3,0,2,1:T(8,128)S(1)} fusion(f32[3,64,64]{2,1,0:T(8,128)} %shard_map.68, f32[64,4,1,128]{3,0,2,1:T(8,128)} %copy-done.9, f32[64,1,8,128]{3,0,2,1:T(8,128)} %copy-done.5, f32[64,2,8,128]{3,0,2,1:T(8,128)S(1)} %fusion.36, f32[64,1,8,128]{3,0,2,1:T(8,128)} %copy-done.7, f32[64,4,1,128]{3,0,2,1:T(8,128)} %copy-done.11), kind=kOutput, calls=%fused_computation.145 | convolution fusion | flops 252968960 | bytes 2654208 | tf_op jit(solution)/shard_map/axyz,ab->bxyz/dot_general | solution.py:75
  134.7 1.4 fusion.1
  136.0 1.3 fusion.49
  137.3 2.9 %fusion.2 = f32[64,4,10,128]{3,0,2,1:T(8,128)S(1)} fusion(f32[64,4,10,128]{3,0,2,1:T(8,128)S(1)} %fusion.49, f32[3,64,64]{2,1,0:T(8,128)S(1)} %copy-done.23, f32[129,4,10,128]{3,0,2,1:T(8,128)} %copy-done.1, f32[64,4,1,128]{3,0,2,1:T(8,128)S(1)} %copy-done.10, f32[64,1,8,128]{3,0,2,1:T(8,128)S(1)} %copy-done.6, f32[64,2,8,128]{3,0,2,1:T(8,128)S(1)} %fusion.36, ...), kind=kOutput, calls=%fused_computation.22 | convolution fusion | flops 253624320 | bytes 5275648 | tf_op jit(solution)/shard_map/axyz,ab->bxyz/dot_general | solution.py:75
  140.7 0.7 copy-done
  141.4 1.1 copy-done.4
  143.8 1.1 slice.408
  144.9 1.1 copy.58
  146.0 2.5 %collective-permute-done.19 = f32[2,8,64]{2,1,0:T(8,128)S(1)} collective-permute-done((f32[2,8,64]{2,1,0:T(8,128)S(1)}, f32[2,8,64]{2,1,0:T(8,128)S(1)}, u32[]{:S(2)}, u32[]{:S(2)}) %collective-permute-start.19) | collective-permute-done | bytes 4128 | tf_op jit(solution)/shard_map/ppermute | solution.py:237
  148.5 0.7 dynamic-slice_add_fusion
  (126 shorter events, 10.0 us)
Async XLA Ops:
  0.6 1.3 copy-start.22
  0.6 1.5 copy-start.21
  2.8 13.7 %collective-permute-start.3 = (f32[129,2,1,128]{3,0,2,1:T(8,128)}, f32[129,2,1,128]{3,0,2,1:T(8,128)S(1)}, u32[]{:S(2)}, u32[]{:S(2)}) collective-permute-start(f32[129,2,1,128]{3,0,2,1:T(8,128)} %get-tuple-element.22), channel_id=1, source_target_pairs={{2,0},{4,2},{6,4},{8,6},{10,8},{12,10},{14,12},{16,14},{18,16},{20... | collective-permute-start | bytes 396296 | tf_op jit(solution)/shard_map/ppermute | solution.py:23
  4.3 10.7 %copy-start.25 = (s32[64]{0:T(128)S(1)}, s32[64]{0:T(128)}, u32[]{:S(2)}) copy-start(s32[64]{0:T(128)} %param.7) | copy-start | bytes 772
  4.3 10.8 %copy-start.24 = (s32[128,2]{0,1:T(2,128)S(1)}, s32[128,2]{0,1:T(2,128)}, u32[]{:S(2)}) copy-start(s32[128,2]{0,1:T(2,128)} %param.6) | copy-start | bytes 3076
  4.4 14.1 %collective-permute-start.2 = (f32[129,1,8,128]{3,2,1,0:T(8,128)S(1)}, f32[129,1,8,128]{3,2,1,0:T(8,128)S(1)}, u32[]{:S(2)}, u32[]{:S(2)}) collective-permute-start(f32[129,1,8,128]{3,2,1,0:T(8,128)S(1)} %copy.44), channel_id=1, source_target_pairs={{32,0},{64,32},{96,64},{128,96},{160,128},{192,160},{224,192},{33,... | collective-permute-start | bytes 1585160 | tf_op jit(solution)/shard_map/ppermute | solution.py:23
  6.6 12.0 %collective-permute-start.1 = (f32[129,1,8,128]{3,2,1,0:T(8,128)}, f32[129,1,8,128]{3,2,1,0:T(8,128)}, u32[]{:S(2)}, u32[]{:S(2)}) collective-permute-start(f32[129,1,8,128]{3,2,1,0:T(8,128)} %copy.43), channel_id=1, source_target_pairs={{0,32},{32,64},{64,96},{96,128},{128,160},{160,192},{192,224},{1,3... | collective-permute-start | bytes 1585160 | tf_op jit(solution)/shard_map/ppermute | solution.py:20
  10.5 8.0 %collective-permute-start = (f32[129,2,1,128]{3,0,2,1:T(8,128)S(1)}, f32[129,2,1,128]{3,0,2,1:T(8,128)S(1)}, u32[]{:S(2)}, u32[]{:S(2)}) collective-permute-start(f32[129,2,1,128]{3,0,2,1:T(8,128)S(1)} %get-tuple-element.21), channel_id=1, source_target_pairs={{0,2},{2,4},{4,6},{6,8},{8,10},{10,12},{12,14},{14,16},{16,18},{18... | collective-permute-start | bytes 396296 | tf_op jit(solution)/shard_map/ppermute | solution.py:20
  18.5 3.3 %copy-start.2 = (f32[129,4,1,128]{3,0,2,1:T(8,128)}, f32[129,4,1,128]{3,0,2,1:T(8,128)S(1)}, u32[]{:S(2)}) copy-start(f32[129,4,1,128]{3,0,2,1:T(8,128)S(1)} %pad.40) | copy-start | bytes 792580
  20.0 1.5 %copy-start.1 = (f32[129,4,10,128]{3,0,2,1:T(8,128)}, f32[129,4,10,128]{3,0,2,1:T(8,128)S(1)}, u32[]{:S(2)}) copy-start(f32[129,4,10,128]{3,0,2,1:T(8,128)S(1)} %pad_maximum_fusion) | copy-start | bytes 7925764
  22.9 13.0 %collective-permute-start.4 = (f32[64,1,8,128]{3,0,2,1:T(8,128)S(1)}, f32[64,1,8,128]{3,0,2,1:T(8,128)S(1)}, u32[]{:S(2)}, u32[]{:S(2)}) collective-permute-start(f32[64,1,8,128]{3,0,2,1:T(8,128)S(1)} %get-tuple-element.30), channel_id=1, source_target_pairs={{32,0},{64,32},{96,64},{128,96},{160,128},{192,160},{224,192},{33,... | collective-permute-start | bytes 786440 | tf_op jit(solution)/shard_map/ppermute | solution.py:23
  24.2 11.7 %collective-permute-start.5 = (f32[64,1,8,128]{3,0,2,1:T(8,128)S(1)}, f32[64,1,8,128]{3,0,2,1:T(8,128)S(1)}, u32[]{:S(2)}, u32[]{:S(2)}) collective-permute-start(f32[64,1,8,128]{3,0,2,1:T(8,128)S(1)} %get-tuple-element.29), channel_id=1, source_target_pairs={{0,32},{32,64},{64,96},{96,128},{128,160},{160,192},{192,224},{1,3... | collective-permute-start | bytes 786440 | tf_op jit(solution)/shard_map/ppermute | solution.py:20
  27.3 7.2 %collective-permute-start.6 = (f32[64,2,1,128]{3,0,2,1:T(8,128)S(1)}, f32[64,2,1,128]{3,0,2,1:T(8,128)S(1)}, u32[]{:S(2)}, u32[]{:S(2)}) collective-permute-start(f32[64,2,1,128]{3,0,2,1:T(8,128)S(1)} %get-tuple-element.28), channel_id=1, source_target_pairs={{2,0},{4,2},{6,4},{8,6},{10,8},{12,10},{14,12},{16,14},{18,16},{20... | collective-permute-start | bytes 196616 | tf_op jit(solution)/shard_map/ppermute | solution.py:23
  28.6 7.3 %collective-permute-start.7 = (f32[64,2,1,128]{3,0,2,1:T(8,128)S(1)}, f32[64,2,1,128]{3,0,2,1:T(8,128)S(1)}, u32[]{:S(2)}, u32[]{:S(2)}) collective-permute-start(f32[64,2,1,128]{3,0,2,1:T(8,128)S(1)} %get-tuple-element.27), channel_id=1, source_target_pairs={{0,2},{2,4},{4,6},{6,8},{8,10},{10,12},{12,14},{14,16},{16,18},{18... | collective-permute-start | bytes 196616 | tf_op jit(solution)/shard_map/ppermute | solution.py:20
  34.5 1.9 %copy-start.9 = (f32[64,4,1,128]{3,0,2,1:T(8,128)}, f32[64,4,1,128]{3,0,2,1:T(8,128)S(1)}, u32[]{:S(2)}) copy-start(f32[64,4,1,128]{3,0,2,1:T(8,128)S(1)} %pad.44) | copy-start | bytes 393220
  35.9 0.7 copy-start.11
  36.0 0.7 copy-start.5
  36.0 0.8 copy-start.7
  37.2 11.8 %collective-permute-start.10 = (f32[64,2,1,128]{3,0,2,1:T(8,128)S(1)}, f32[64,2,1,128]{3,0,2,1:T(8,128)S(1)}, u32[]{:S(2)}, u32[]{:S(2)}) collective-permute-start(f32[64,2,1,128]{3,0,2,1:T(8,128)S(1)} %get-tuple-element.24), channel_id=1, source_target_pairs={{2,0},{4,2},{6,4},{8,6},{10,8},{12,10},{14,12},{16,14},{18,16},{20... | collective-permute-start | bytes 196616 | tf_op jit(solution)/shard_map/ppermute | solution.py:23
  38.5 11.7 %collective-permute-start.8 = (f32[64,1,8,128]{3,0,2,1:T(8,128)S(1)}, f32[64,1,8,128]{3,0,2,1:T(8,128)S(1)}, u32[]{:S(2)}, u32[]{:S(2)}) collective-permute-start(f32[64,1,8,128]{3,0,2,1:T(8,128)S(1)} %get-tuple-element.26), channel_id=1, source_target_pairs={{32,0},{64,32},{96,64},{128,96},{160,128},{192,160},{224,192},{33,... | collective-permute-start | bytes 786440 | tf_op jit(solution)/shard_map/ppermute | solution.py:23
  39.8 10.4 %collective-permute-start.9 = (f32[64,1,8,128]{3,0,2,1:T(8,128)S(1)}, f32[64,1,8,128]{3,0,2,1:T(8,128)S(1)}, u32[]{:S(2)}, u32[]{:S(2)}) collective-permute-start(f32[64,1,8,128]{3,0,2,1:T(8,128)S(1)} %get-tuple-element.25), channel_id=1, source_target_pairs={{0,32},{32,64},{64,96},{96,128},{128,160},{160,192},{192,224},{1,3... | collective-permute-start | bytes 786440 | tf_op jit(solution)/shard_map/ppermute | solution.py:20
  42.9 7.3 %collective-permute-start.11 = (f32[64,2,1,128]{3,0,2,1:T(8,128)S(1)}, f32[64,2,1,128]{3,0,2,1:T(8,128)S(1)}, u32[]{:S(2)}, u32[]{:S(2)}) collective-permute-start(f32[64,2,1,128]{3,0,2,1:T(8,128)S(1)} %get-tuple-element.23), channel_id=1, source_target_pairs={{0,2},{2,4},{4,6},{6,8},{8,10},{10,12},{12,14},{14,16},{16,18},{18... | collective-permute-start | bytes 196616 | tf_op jit(solution)/shard_map/ppermute | solution.py:20
  49.1 1.7 %copy-start.17 = (f32[64,4,1,128]{3,0,2,1:T(8,128)}, f32[64,4,1,128]{3,0,2,1:T(8,128)S(1)}, u32[]{:S(2)}) copy-start(f32[64,4,1,128]{3,0,2,1:T(8,128)S(1)} %pad.47) | copy-start | bytes 393220
  50.2 0.7 copy-start.19
  50.2 0.7 copy-start.13
  50.2 0.8 copy-start.15
  51.9 1.4 collective-permute-start.12
  53.4 5.8 %collective-permute-start.13 = (f32[4,64,64]{2,1,0:T(8,128)S(1)}, f32[4,64,64]{2,1,0:T(8,128)S(1)}, u32[]{:S(2)}, u32[]{:S(2)}) collective-permute-start(f32[4,64,64]{2,1,0:T(8,128)S(1)} %fusion.61), channel_id=1, source_target_pairs={{0,64},{32,96},{64,0},{96,32},{128,192},{160,224},{192,128},{224,1... | collective-permute-start | bytes 196616 | tf_op jit(solution)/shard_map/ppermute | solution.py:44
  59.2 6.6 %collective-permute-start.14 = (f32[4,64,64]{2,1,0:T(8,128)S(1)}, f32[4,64,64]{2,1,0:T(8,128)S(1)}, u32[]{:S(2)}, u32[]{:S(2)}) collective-permute-start(f32[4,64,64]{2,1,0:T(8,128)S(1)} %fusion.75), channel_id=1, source_target_pairs={{0,128},{32,160},{64,192},{96,224},{128,0},{160,32},{192,64},{224,... | collective-permute-start | bytes 196616 | tf_op jit(solution)/shard_map/ppermute | solution.py:44
  65.8 5.4 %collective-permute-start.15 = (f32[4,64,64]{2,1,0:T(8,128)S(1)}, f32[4,64,64]{2,1,0:T(8,128)S(1)}, u32[]{:S(2)}, u32[]{:S(2)}) collective-permute-start(f32[4,64,64]{2,1,0:T(8,128)S(1)} %add.190), channel_id=1, source_target_pairs={{0,2},{2,0},{4,6},{6,4},{8,10},{10,8},{12,14},{14,12},{16,18},{18,... | collective-permute-start | bytes 196616 | tf_op jit(solution)/shard_map/ppermute | solution.py:44
  71.2 9.5 %collective-permute-start.16 = (f32[4,64,64]{2,1,0:T(8,128)S(1)}, f32[4,64,64]{2,1,0:T(8,128)S(1)}, u32[]{:S(2)}, u32[]{:S(2)}) collective-permute-start(f32[4,64,64]{2,1,0:T(8,128)S(1)} %add.191), channel_id=1, source_target_pairs={{0,4},{2,6},{4,0},{6,2},{8,12},{10,14},{12,8},{14,10},{16,20},{18,... | collective-permute-start | bytes 196616 | tf_op jit(solution)/shard_map/ppermute | solution.py:44
  81.4 11.9 %collective-permute-start.17 = (f32[4,64,64]{2,1,0:T(8,128)}, f32[4,64,64]{2,1,0:T(8,128)}, u32[]{:S(2)}, u32[]{:S(2)}) collective-permute-start(f32[4,64,64]{2,1,0:T(8,128)} %add.192), channel_id=1, source_target_pairs={{0,8},{2,10},{4,12},{6,14},{8,0},{10,2},{12,4},{14,6},{16,24},{18,... | collective-permute-start | bytes 196616 | tf_op jit(solution)/shard_map/ppermute | solution.py:44
  94.3 13.8 %collective-permute-start.18 = (f32[4,64,64]{2,1,0:T(8,128)S(1)}, f32[4,64,64]{2,1,0:T(8,128)S(1)}, u32[]{:S(2)}, u32[]{:S(2)}) collective-permute-start(f32[4,64,64]{2,1,0:T(8,128)S(1)} %add.193), channel_id=1, source_target_pairs={{0,16},{2,18},{4,20},{6,22},{8,24},{10,26},{12,28},{14,30},{16,0},... | collective-permute-start | bytes 196616 | tf_op jit(solution)/shard_map/ppermute | solution.py:44
  132.0 2.6 %copy-start.6 = (f32[64,1,8,128]{3,0,2,1:T(8,128)S(1)}, f32[64,1,8,128]{3,0,2,1:T(8,128)}, u32[]{:S(2)}) copy-start(f32[64,1,8,128]{3,0,2,1:T(8,128)} %copy-done.5) | copy-start | bytes 786436
  132.0 2.6 %copy-start.8 = (f32[64,1,8,128]{3,0,2,1:T(8,128)S(1)}, f32[64,1,8,128]{3,0,2,1:T(8,128)}, u32[]{:S(2)}) copy-start(f32[64,1,8,128]{3,0,2,1:T(8,128)} %copy-done.7) | copy-start | bytes 786436
  132.0 2.6 %copy-start.10 = (f32[64,4,1,128]{3,0,2,1:T(8,128)S(1)}, f32[64,4,1,128]{3,0,2,1:T(8,128)}, u32[]{:S(2)}) copy-start(f32[64,4,1,128]{3,0,2,1:T(8,128)} %copy-done.9) | copy-start | bytes 393220
  132.0 2.6 %copy-start.12 = (f32[64,4,1,128]{3,0,2,1:T(8,128)S(1)}, f32[64,4,1,128]{3,0,2,1:T(8,128)}, u32[]{:S(2)}) copy-start(f32[64,4,1,128]{3,0,2,1:T(8,128)} %copy-done.11) | copy-start | bytes 393220
  132.0 2.6 %copy-start.14 = (f32[64,1,8,128]{3,0,2,1:T(8,128)S(1)}, f32[64,1,8,128]{3,0,2,1:T(8,128)}, u32[]{:S(2)}) copy-start(f32[64,1,8,128]{3,0,2,1:T(8,128)} %copy-done.13) | copy-start | bytes 786436
  132.0 2.6 %copy-start.16 = (f32[64,1,8,128]{3,0,2,1:T(8,128)S(1)}, f32[64,1,8,128]{3,0,2,1:T(8,128)}, u32[]{:S(2)}) copy-start(f32[64,1,8,128]{3,0,2,1:T(8,128)} %copy-done.15) | copy-start | bytes 786436
  132.0 2.6 %copy-start.18 = (f32[64,4,1,128]{3,0,2,1:T(8,128)S(1)}, f32[64,4,1,128]{3,0,2,1:T(8,128)}, u32[]{:S(2)}) copy-start(f32[64,4,1,128]{3,0,2,1:T(8,128)} %copy-done.17) | copy-start | bytes 393220
  132.0 2.6 %copy-start.20 = (f32[64,4,1,128]{3,0,2,1:T(8,128)S(1)}, f32[64,4,1,128]{3,0,2,1:T(8,128)}, u32[]{:S(2)}) copy-start(f32[64,4,1,128]{3,0,2,1:T(8,128)} %copy-done.19) | copy-start | bytes 393220
  132.0 2.6 %copy-start.23 = (f32[3,64,64]{2,1,0:T(8,128)S(1)}, f32[3,64,64]{2,1,0:T(8,128)}, u32[]{:S(2)}) copy-start(f32[3,64,64]{2,1,0:T(8,128)} %shard_map.68) | copy-start | bytes 147460
  137.3 3.0 %copy-start.3 = (f32[129,4,1,128]{3,0,2,1:T(8,128)S(1)}, f32[129,4,1,128]{3,0,2,1:T(8,128)}, u32[]{:S(2)}) copy-start(f32[129,4,1,128]{3,0,2,1:T(8,128)} %copy-done.2) | copy-start | bytes 792580
  140.3 1.1 copy-start
  140.4 2.1 %copy-start.4 = (f32[64,4,10,130]{3,0,2,1:T(8,128)S(1)}, f32[64,4,10,130]{3,0,2,1:T(8,128)}, u32[]{:S(2)}) copy-start(f32[64,4,10,130]{3,0,2,1:T(8,128)} %select_maximum_fusion) | copy-start | bytes 3993604
  143.3 5.2 %collective-permute-start.19 = (f32[2,8,64]{2,1,0:T(8,128)S(1)}, f32[2,8,64]{2,1,0:T(8,128)S(1)}, u32[]{:S(2)}, u32[]{:S(2)}) collective-permute-start(f32[2,8,64]{2,1,0:T(8,128)S(1)} %constant_dynamic-slice_fusion), channel_id=1, source_target_pairs={{0,1},{1,0},{2,3},{3,2},{4,5},{5,4},{6,7},{7,6},{8,9},{9,8},{10,11... | collective-permute-start | bytes 12296 | tf_op jit(solution)/shard_map/ppermute | solution.py:237

commit v4 on v3

--- a/solution.py
+++ b/solution.py
@@ -38,11 +38,17 @@
         if count & (count - 1):
             value = lax.psum(value, axis)
             continue
-        step = 1
-        while step < count:
-            pairs = [(i, i ^ step) for i in range(count)]
-            value = value + lax.ppermute(value, axis, pairs)
-            step *= 2
+        shift = 0
+        if (count.bit_length() - 1) % 2:
+            value = value + lax.ppermute(value, axis, [(i, i ^ 1) for i in range(count)])
+            shift = 1
+        while (1 << shift) < count:
+            got = [
+                lax.ppermute(value, axis, [(i, i ^ (d << shift)) for i in range(count)])
+                for d in (1, 2, 3)
+            ]
+            value = (value + got[0]) + (got[1] + got[2])
+            shift += 2
     return value
 
 

time: 150 us -> 150 us (level)
    ppermute x7 -> x10, starting transfers between devices: 30.5 us -> 29.7 us  [the longest x9 29 us: allsum(): lax.ppermute(value, axis, [(i, i ^ d << shift) for i in range(count)])]
    ppermute x7 -> x10, waiting for transfers between devices: 20 us -> 20.7 us  [the longest x9 19.7 us: allsum(): lax.ppermute(value, axis, [(i, i ^ d << shift) for i in range(count)])]
  transfers between devices with their start and end apart: 20 -> 23, of which waited for: 11 -> 11; matrix products, arithmetic and copies ran while one was open for 7% -> 8% of each run, Pallas kernels for 0% -> 0%
where the time goes in v4:
time: 150 us; the launch traced here: 148 us
  starting transfers between devices  62.3 us (42%)
  waiting for transfers between devices  26.6 us (18%)
  Pallas kernels  23.2 us (15%)
  other arithmetic  12.7 us (8%)
  local copies, waits for them, and re-layouts  10.9 us (7%)
  matrix products  10.5 us (7%)
  between operations  1.52 us (1%)
    ppermute x9, starting transfers between devices, allsum(): lax.ppermute(value, axis, [(i, i ^ d << shift) for i in range(count)])  29 us
    ppermute x6, starting transfers between devices, padded_2(): lax.ppermute(lax.slice_in_dim(block, block.shape[dim] - width, None, axis...  24.4 us
    pallas_call x1, Pallas kernels, steps(): pl.pallas_call(steps_kernel, out_shape=jax.ShapeDtypeStruct((3, n, n), jn...  23.2 us
    ppermute x9, waiting for transfers between devices, allsum(): lax.ppermute(value, axis, [(i, i ^ d << shift) for i in range(count)])  19.7 us
    dot_general x4, matrix products, combine_cols(): jnp.einsum('axyz,ab->bxyz', field, matrix, precision=lax.Precision.HIGHEST)  8.07 us
    ppermute x6, starting transfers between devices, padded_2(): lax.ppermute(lax.slice_in_dim(block, 0, width, axis=dim), axis, backward)  7.74 us
    unnamed x56, local copies, waits for them, and re-layouts  6.49 us
    slice x1, other arithmetic, on_device(): adjoint_pad = padded[1 + columns:]  4.07 us
  transfers between devices with their start and end apart: 23, of which 11 were waited for; matrix products, arithmetic and copies ran while one was open for 8% of the time, Pallas kernels for 0%

profile of v4, /device:TPU:4, one launch (start us, length us, event | category | flops | bytes accessed | tf_op | source)
XLA Modules:
  0.0 147.7 jit_solution(13091071647831539278)
XLA Ops:
  0.6 1.3 copy.42
  2.1 0.7 pad_maximum_fusion.33
  2.8 1.3 collective-permute-start.3
  4.4 1.3 collective-permute-start.2
  5.8 3.1 %collective-permute-start.1 = (f32[129,1,8,128]{3,2,1,0:T(8,128)S(1)}, f32[129,1,8,128]{3,2,1,0:T(8,128)S(1)}, u32[]{:S(2)}, u32[]{:S(2)}) collective-permute-start(f32[129,1,8,128]{3,2,1,0:T(8,128)S(1)} %copy.43), channel_id=1, source_target_pairs={{0,32},{32,64},{64,96},{96,128},{128,160},{160,192},{192,224},{1,3... | collective-permute-start | bytes 1585160 | tf_op jit(solution)/shard_map/ppermute | solution.py:20
  8.9 5.2 %collective-permute-start = (f32[129,2,1,128]{3,0,2,1:T(8,128)}, f32[129,2,1,128]{3,0,2,1:T(8,128)}, u32[]{:S(2)}, u32[]{:S(2)}) collective-permute-start(f32[129,2,1,128]{3,0,2,1:T(8,128)} %get-tuple-element.21), channel_id=1, source_target_pairs={{0,2},{2,4},{4,6},{6,8},{8,10},{10,12},{12,14},{14,16},{16,18},{18... | collective-permute-start | bytes 396296 | tf_op jit(solution)/shard_map/ppermute | solution.py:20
  15.6 0.9 pad.41
  16.5 1.1 collective-permute-done
  17.6 0.9 pad.40
  19.1 1.4 copy-done.1
  21.9 1.3 collective-permute-start.4
  23.2 3.0 %collective-permute-start.5 = (f32[64,1,8,128]{3,0,2,1:T(8,128)S(1)}, f32[64,1,8,128]{3,0,2,1:T(8,128)S(1)}, u32[]{:S(2)}, u32[]{:S(2)}) collective-permute-start(f32[64,1,8,128]{3,0,2,1:T(8,128)S(1)} %get-tuple-element.29), channel_id=1, source_target_pairs={{0,32},{32,64},{64,96},{96,128},{128,160},{160,192},{192,224},{1,3... | collective-permute-start | bytes 786440 | tf_op jit(solution)/shard_map/ppermute | solution.py:20
  26.3 1.3 collective-permute-start.6
  27.6 5.0 %collective-permute-start.7 = (f32[64,2,1,128]{3,0,2,1:T(8,128)S(1)}, f32[64,2,1,128]{3,0,2,1:T(8,128)S(1)}, u32[]{:S(2)}, u32[]{:S(2)}) collective-permute-start(f32[64,2,1,128]{3,0,2,1:T(8,128)S(1)} %get-tuple-element.27), channel_id=1, source_target_pairs={{0,2},{2,4},{4,6},{6,8},{8,10},{10,12},{12,14},{14,16},{16,18},{18... | collective-permute-start | bytes 196616 | tf_op jit(solution)/shard_map/ppermute | solution.py:20
  33.2 1.5 %collective-permute-done.7 = f32[64,2,1,128]{3,0,2,1:T(8,128)S(1)} collective-permute-done((f32[64,2,1,128]{3,0,2,1:T(8,128)S(1)}, f32[64,2,1,128]{3,0,2,1:T(8,128)S(1)}, u32[]{:S(2)}, u32[]{:S(2)}) %collective-permute-start.7) | collective-permute-done | bytes 65568 | tf_op jit(solution)/shard_map/ppermute | solution.py:20
  36.0 1.3 collective-permute-start.10
  37.3 1.3 collective-permute-start.8
  38.6 3.0 %collective-permute-start.9 = (f32[64,1,8,128]{3,0,2,1:T(8,128)S(1)}, f32[64,1,8,128]{3,0,2,1:T(8,128)S(1)}, u32[]{:S(2)}, u32[]{:S(2)}) collective-permute-start(f32[64,1,8,128]{3,0,2,1:T(8,128)S(1)} %get-tuple-element.25), channel_id=1, source_target_pairs={{0,32},{32,64},{64,96},{96,128},{128,160},{160,192},{192,224},{1,3... | collective-permute-start | bytes 786440 | tf_op jit(solution)/shard_map/ppermute | solution.py:20
  41.7 5.0 %collective-permute-start.11 = (f32[64,2,1,128]{3,0,2,1:T(8,128)S(1)}, f32[64,2,1,128]{3,0,2,1:T(8,128)S(1)}, u32[]{:S(2)}, u32[]{:S(2)}) collective-permute-start(f32[64,2,1,128]{3,0,2,1:T(8,128)S(1)} %get-tuple-element.23), channel_id=1, source_target_pairs={{0,2},{2,4},{4,6},{6,8},{8,10},{10,12},{12,14},{14,16},{16,18},{18... | collective-permute-start | bytes 196616 | tf_op jit(solution)/shard_map/ppermute | solution.py:20
  47.9 0.8 collective-permute-done.11
  49.7 0.7 convolution_bitcast_fusion
  50.4 0.7 collective-permute-start.12
  51.1 1.0 collective-permute-done.12
  52.1 3.4 %collective-permute-start.14 = (f32[4,64,64]{2,1,0:T(8,128)S(1)}, f32[4,64,64]{2,1,0:T(8,128)S(1)}, u32[]{:S(2)}, u32[]{:S(2)}) collective-permute-start(f32[4,64,64]{2,1,0:T(8,128)S(1)} %fusion.61), channel_id=1, source_target_pairs={{0,128},{32,160},{64,192},{96,224},{128,0},{160,32},{192,64},{224,... | collective-permute-start | bytes 196616 | tf_op jit(solution)/shard_map/ppermute | solution.py:47
  55.5 0.8 collective-permute-start.15
  56.3 3.3 %collective-permute-done.14 = f32[4,64,64]{2,1,0:T(8,128)S(1)} collective-permute-done((f32[4,64,64]{2,1,0:T(8,128)S(1)}, f32[4,64,64]{2,1,0:T(8,128)S(1)}, u32[]{:S(2)}, u32[]{:S(2)}) %collective-permute-start.14) | collective-permute-done | bytes 65568 | tf_op jit(solution)/shard_map/ppermute | solution.py:47
  59.5 2.8 %collective-permute-done.15 = f32[4,64,64]{2,1,0:T(8,128)S(1)} collective-permute-done((f32[4,64,64]{2,1,0:T(8,128)S(1)}, f32[4,64,64]{2,1,0:T(8,128)S(1)}, u32[]{:S(2)}, u32[]{:S(2)}) %collective-permute-start.15) | collective-permute-done | bytes 65568 | tf_op jit(solution)/shard_map/ppermute | solution.py:47
  62.3 0.7 add_add_fusion.2
  63.0 5.3 %collective-permute-start.17 = (f32[4,64,64]{2,1,0:T(8,128)}, f32[4,64,64]{2,1,0:T(8,128)}, u32[]{:S(2)}, u32[]{:S(2)}) collective-permute-start(f32[4,64,64]{2,1,0:T(8,128)} %add_add_fusion.2), channel_id=1, source_target_pairs={{0,4},{2,6},{4,0},{6,2},{8,12},{10,14},{12,8},{14,10},{16,20},{18,... | collective-permute-start | bytes 196616 | tf_op jit(solution)/shard_map/ppermute | solution.py:47
  68.3 2.9 %collective-permute-start.18 = (f32[4,64,64]{2,1,0:T(8,128)}, f32[4,64,64]{2,1,0:T(8,128)}, u32[]{:S(2)}, u32[]{:S(2)}) collective-permute-start(f32[4,64,64]{2,1,0:T(8,128)} %add_add_fusion.2), channel_id=1, source_target_pairs={{0,6},{2,4},{4,2},{6,0},{8,14},{10,12},{12,10},{14,8},{16,22},{18,... | collective-permute-start | bytes 196616 | tf_op jit(solution)/shard_map/ppermute | solution.py:47
  71.9 6.9 %collective-permute-done.18 = f32[4,64,64]{2,1,0:T(8,128)} collective-permute-done((f32[4,64,64]{2,1,0:T(8,128)}, f32[4,64,64]{2,1,0:T(8,128)}, u32[]{:S(2)}, u32[]{:S(2)}) %collective-permute-start.18) | collective-permute-done | bytes 65568 | tf_op jit(solution)/shard_map/ppermute | solution.py:47
  78.9 1.1 add_add_fusion.1
  80.0 10.5 %collective-permute-start.20 = (f32[4,64,64]{2,1,0:T(8,128)S(1)}, f32[4,64,64]{2,1,0:T(8,128)S(1)}, u32[]{:S(2)}, u32[]{:S(2)}) collective-permute-start(f32[4,64,64]{2,1,0:T(8,128)S(1)} %add_add_fusion.1), channel_id=1, source_target_pairs={{0,16},{2,18},{4,20},{6,22},{8,24},{10,26},{12,28},{14,30},{16,0},... | collective-permute-start | bytes 196616 | tf_op jit(solution)/shard_map/ppermute | solution.py:47
  90.6 5.5 %collective-permute-start.19 = (f32[4,64,64]{2,1,0:T(8,128)S(1)}, f32[4,64,64]{2,1,0:T(8,128)S(1)}, u32[]{:S(2)}, u32[]{:S(2)}) collective-permute-start(f32[4,64,64]{2,1,0:T(8,128)S(1)} %add_add_fusion.1), channel_id=1, source_target_pairs={{0,8},{2,10},{4,12},{6,14},{8,0},{10,2},{12,4},{14,6},{16,24},{18,... | collective-permute-start | bytes 196616 | tf_op jit(solution)/shard_map/ppermute | solution.py:47
  96.0 4.1 %select_maximum_fusion = f32[64,4,10,130]{3,0,2,1:T(8,128)} fusion(f32[129,4,1,128]{3,0,2,1:T(8,128)S(1)} %pad.41, f32[129,4,1,128]{3,0,2,1:T(8,128)} %copy-done.2, f32[129,1,8,128]{3,0,2,1:T(8,128)S(1)} %copy.46, f32[129,1,8,128]{3,0,2,1:T(8,128)S(1)} %copy.45, f32[64,2,8,128]{3,0,2,1:T(8,128)S(1)} %copy.42, f32[64,2,8,128]{3,0,2,1:T(8,128)S(1)} %copy.41, ...), kind=kLoop, calls=%fused_computation.12 | loop fusion | flops 5324800 | bytes 3973120 | tf_op jit(solution)/shard_map/slice | solution.py:199
  100.1 6.4 %collective-permute-done.21 = f32[4,64,64]{2,1,0:T(8,128)S(1)} collective-permute-done((f32[4,64,64]{2,1,0:T(8,128)S(1)}, f32[4,64,64]{2,1,0:T(8,128)S(1)}, u32[]{:S(2)}, u32[]{:S(2)}) %collective-permute-start.21) | collective-permute-done | bytes 65568 | tf_op jit(solution)/shard_map/ppermute | solution.py:47
  106.7 0.7 add_add_fusion.grams_ref
  107.3 23.2 %shard_map.68 = f32[3,64,64]{2,1,0:T(8,128)} custom-call(f32[4,64,64]{2,1,0:T(8,128)} %add_add_fusion.grams_ref), custom_call_target="tpu_custom_call" | custom-call | tf_op jit(solution)/shard_map/pallas_call | solution.py:170
  130.6 2.5 %fusion.48 = f32[64,4,10,128]{3,0,2,1:T(8,128)S(1)} fusion(f32[3,64,64]{2,1,0:T(8,128)} %shard_map.68, f32[64,4,1,128]{3,0,2,1:T(8,128)} %copy-done.9, f32[64,1,8,128]{3,0,2,1:T(8,128)} %copy-done.5, f32[64,2,8,128]{3,0,2,1:T(8,128)S(1)} %fusion.36, f32[64,1,8,128]{3,0,2,1:T(8,128)} %copy-done.7, f32[64,4,1,128]{3,0,2,1:T(8,128)} %copy-done.11), kind=kOutput, calls=%fused_computation.148 | convolution fusion | flops 252968960 | bytes 2654208 | tf_op jit(solution)/shard_map/axyz,ab->bxyz/dot_general | solution.py:81
  133.2 1.4 fusion.1
  134.6 1.3 fusion.49
  135.9 2.9 %fusion.2 = f32[64,4,10,128]{3,0,2,1:T(8,128)S(1)} fusion(f32[64,4,10,128]{3,0,2,1:T(8,128)S(1)} %fusion.49, f32[3,64,64]{2,1,0:T(8,128)S(1)} %copy-done.23, f32[129,4,10,128]{3,0,2,1:T(8,128)} %copy-done.1, f32[64,4,1,128]{3,0,2,1:T(8,128)S(1)} %copy-done.10, f32[64,1,8,128]{3,0,2,1:T(8,128)S(1)} %copy-done.6, f32[64,2,8,128]{3,0,2,1:T(8,128)S(1)} %fusion.36, ...), kind=kOutput, calls=%fused_computation.22 | convolution fusion | flops 253624320 | bytes 5275648 | tf_op jit(solution)/shard_map/axyz,ab->bxyz/dot_general | solution.py:81
  139.2 0.7 copy-done
  139.9 1.1 copy-done.4
  142.4 1.1 slice.408
  143.5 1.1 copy.58
  144.6 2.4 %collective-permute-done.22 = f32[2,8,64]{2,1,0:T(8,128)S(1)} collective-permute-done((f32[2,8,64]{2,1,0:T(8,128)S(1)}, f32[2,8,64]{2,1,0:T(8,128)S(1)}, u32[]{:S(2)}, u32[]{:S(2)}) %collective-permute-start.22) | collective-permute-done | bytes 4128 | tf_op jit(solution)/shard_map/ppermute | solution.py:243
  147.0 0.7 dynamic-slice_add_fusion
  (129 shorter events, 10.2 us)
Async XLA Ops:
  0.6 1.3 copy-start.22
  0.6 1.5 copy-start.21
  2.8 12.8 %collective-permute-start.3 = (f32[129,2,1,128]{3,0,2,1:T(8,128)S(1)}, f32[129,2,1,128]{3,0,2,1:T(8,128)}, u32[]{:S(2)}, u32[]{:S(2)}) collective-permute-start(f32[129,2,1,128]{3,0,2,1:T(8,128)S(1)} %get-tuple-element.22), channel_id=1, source_target_pairs={{2,0},{4,2},{6,4},{8,6},{10,8},{12,10},{14,12},{16,14},{18,16},{20... | collective-permute-start | bytes 396296 | tf_op jit(solution)/shard_map/ppermute | solution.py:23
  4.3 9.8 %copy-start.25 = (s32[64]{0:T(128)S(1)}, s32[64]{0:T(128)}, u32[]{:S(2)}) copy-start(s32[64]{0:T(128)} %param.7) | copy-start | bytes 772
  4.3 9.8 %copy-start.24 = (s32[128,2]{0,1:T(2,128)S(1)}, s32[128,2]{0,1:T(2,128)}, u32[]{:S(2)}) copy-start(s32[128,2]{0,1:T(2,128)} %param.6) | copy-start | bytes 3076
  4.4 14.2 %collective-permute-start.2 = (f32[129,1,8,128]{3,2,1,0:T(8,128)S(1)}, f32[129,1,8,128]{3,2,1,0:T(8,128)S(1)}, u32[]{:S(2)}, u32[]{:S(2)}) collective-permute-start(f32[129,1,8,128]{3,2,1,0:T(8,128)S(1)} %copy.44), channel_id=1, source_target_pairs={{32,0},{64,32},{96,64},{128,96},{160,128},{192,160},{224,192},{33,... | collective-permute-start | bytes 1585160 | tf_op jit(solution)/shard_map/ppermute | solution.py:23
  5.8 12.9 %collective-permute-start.1 = (f32[129,1,8,128]{3,2,1,0:T(8,128)S(1)}, f32[129,1,8,128]{3,2,1,0:T(8,128)S(1)}, u32[]{:S(2)}, u32[]{:S(2)}) collective-permute-start(f32[129,1,8,128]{3,2,1,0:T(8,128)S(1)} %copy.43), channel_id=1, source_target_pairs={{0,32},{32,64},{64,96},{96,128},{128,160},{160,192},{192,224},{1,3... | collective-permute-start | bytes 1585160 | tf_op jit(solution)/shard_map/ppermute | solution.py:20
  8.9 8.7 %collective-permute-start = (f32[129,2,1,128]{3,0,2,1:T(8,128)}, f32[129,2,1,128]{3,0,2,1:T(8,128)}, u32[]{:S(2)}, u32[]{:S(2)}) collective-permute-start(f32[129,2,1,128]{3,0,2,1:T(8,128)} %get-tuple-element.21), channel_id=1, source_target_pairs={{0,2},{2,4},{4,6},{6,8},{8,10},{10,12},{12,14},{14,16},{16,18},{18... | collective-permute-start | bytes 396296 | tf_op jit(solution)/shard_map/ppermute | solution.py:20
  18.5 2.2 %copy-start.2 = (f32[129,4,1,128]{3,0,2,1:T(8,128)}, f32[129,4,1,128]{3,0,2,1:T(8,128)S(1)}, u32[]{:S(2)}) copy-start(f32[129,4,1,128]{3,0,2,1:T(8,128)S(1)} %pad.40) | copy-start | bytes 792580
  19.0 1.5 %copy-start.1 = (f32[129,4,10,128]{3,0,2,1:T(8,128)}, f32[129,4,10,128]{3,0,2,1:T(8,128)S(1)}, u32[]{:S(2)}) copy-start(f32[129,4,10,128]{3,0,2,1:T(8,128)S(1)} %pad_maximum_fusion) | copy-start | bytes 7925764
  21.9 12.8 %collective-permute-start.4 = (f32[64,1,8,128]{3,0,2,1:T(8,128)S(1)}, f32[64,1,8,128]{3,0,2,1:T(8,128)S(1)}, u32[]{:S(2)}, u32[]{:S(2)}) collective-permute-start(f32[64,1,8,128]{3,0,2,1:T(8,128)S(1)} %get-tuple-element.30), channel_id=1, source_target_pairs={{32,0},{64,32},{96,64},{128,96},{160,128},{192,160},{224,192},{33,... | collective-permute-start | bytes 786440 | tf_op jit(solution)/shard_map/ppermute | solution.py:23
  23.2 11.5 %collective-permute-start.5 = (f32[64,1,8,128]{3,0,2,1:T(8,128)S(1)}, f32[64,1,8,128]{3,0,2,1:T(8,128)S(1)}, u32[]{:S(2)}, u32[]{:S(2)}) collective-permute-start(f32[64,1,8,128]{3,0,2,1:T(8,128)S(1)} %get-tuple-element.29), channel_id=1, source_target_pairs={{0,32},{32,64},{64,96},{96,128},{128,160},{160,192},{192,224},{1,3... | collective-permute-start | bytes 786440 | tf_op jit(solution)/shard_map/ppermute | solution.py:20
  26.3 6.9 %collective-permute-start.6 = (f32[64,2,1,128]{3,0,2,1:T(8,128)S(1)}, f32[64,2,1,128]{3,0,2,1:T(8,128)S(1)}, u32[]{:S(2)}, u32[]{:S(2)}) collective-permute-start(f32[64,2,1,128]{3,0,2,1:T(8,128)S(1)} %get-tuple-element.28), channel_id=1, source_target_pairs={{2,0},{4,2},{6,4},{8,6},{10,8},{12,10},{14,12},{16,14},{18,16},{20... | collective-permute-start | bytes 196616 | tf_op jit(solution)/shard_map/ppermute | solution.py:23
  27.6 7.1 %collective-permute-start.7 = (f32[64,2,1,128]{3,0,2,1:T(8,128)S(1)}, f32[64,2,1,128]{3,0,2,1:T(8,128)S(1)}, u32[]{:S(2)}, u32[]{:S(2)}) collective-permute-start(f32[64,2,1,128]{3,0,2,1:T(8,128)S(1)} %get-tuple-element.27), channel_id=1, source_target_pairs={{0,2},{2,4},{4,6},{6,8},{8,10},{10,12},{12,14},{14,16},{16,18},{18... | collective-permute-start | bytes 196616 | tf_op jit(solution)/shard_map/ppermute | solution.py:20
  33.2 2.0 %copy-start.9 = (f32[64,4,1,128]{3,0,2,1:T(8,128)}, f32[64,4,1,128]{3,0,2,1:T(8,128)S(1)}, u32[]{:S(2)}) copy-start(f32[64,4,1,128]{3,0,2,1:T(8,128)S(1)} %pad.44) | copy-start | bytes 393220
  34.7 0.7 copy-start.11
  34.7 0.7 copy-start.5
  34.8 0.8 copy-start.7
  36.0 11.8 %collective-permute-start.10 = (f32[64,2,1,128]{3,0,2,1:T(8,128)S(1)}, f32[64,2,1,128]{3,0,2,1:T(8,128)S(1)}, u32[]{:S(2)}, u32[]{:S(2)}) collective-permute-start(f32[64,2,1,128]{3,0,2,1:T(8,128)S(1)} %get-tuple-element.24), channel_id=1, source_target_pairs={{2,0},{4,2},{6,4},{8,6},{10,8},{12,10},{14,12},{16,14},{18,16},{20... | collective-permute-start | bytes 196616 | tf_op jit(solution)/shard_map/ppermute | solution.py:23
  37.3 11.4 %collective-permute-start.8 = (f32[64,1,8,128]{3,0,2,1:T(8,128)S(1)}, f32[64,1,8,128]{3,0,2,1:T(8,128)S(1)}, u32[]{:S(2)}, u32[]{:S(2)}) collective-permute-start(f32[64,1,8,128]{3,0,2,1:T(8,128)S(1)} %get-tuple-element.26), channel_id=1, source_target_pairs={{32,0},{64,32},{96,64},{128,96},{160,128},{192,160},{224,192},{33,... | collective-permute-start | bytes 786440 | tf_op jit(solution)/shard_map/ppermute | solution.py:23
  38.6 10.1 %collective-permute-start.9 = (f32[64,1,8,128]{3,0,2,1:T(8,128)S(1)}, f32[64,1,8,128]{3,0,2,1:T(8,128)S(1)}, u32[]{:S(2)}, u32[]{:S(2)}) collective-permute-start(f32[64,1,8,128]{3,0,2,1:T(8,128)S(1)} %get-tuple-element.25), channel_id=1, source_target_pairs={{0,32},{32,64},{64,96},{96,128},{128,160},{160,192},{192,224},{1,3... | collective-permute-start | bytes 786440 | tf_op jit(solution)/shard_map/ppermute | solution.py:20
  41.7 7.0 %collective-permute-start.11 = (f32[64,2,1,128]{3,0,2,1:T(8,128)S(1)}, f32[64,2,1,128]{3,0,2,1:T(8,128)S(1)}, u32[]{:S(2)}, u32[]{:S(2)}) collective-permute-start(f32[64,2,1,128]{3,0,2,1:T(8,128)S(1)} %get-tuple-element.23), channel_id=1, source_target_pairs={{0,2},{2,4},{4,6},{6,8},{8,10},{10,12},{12,14},{14,16},{16,18},{18... | collective-permute-start | bytes 196616 | tf_op jit(solution)/shard_map/ppermute | solution.py:20
  47.9 1.4 copy-start.17
  48.7 0.7 copy-start.13
  48.8 0.8 copy-start.15
  50.4 1.6 %collective-permute-start.12 = (f32[4,64,64]{2,1,0:T(8,128)S(1)}, f32[4,64,64]{2,1,0:T(8,128)S(1)}, u32[]{:S(2)}, u32[]{:S(2)}) collective-permute-start(f32[4,64,64]{2,1,0:T(8,128)S(1)} %pad_maximum_fusion.34), channel_id=1, source_target_pairs={{0,32},{32,0},{64,96},{96,64},{128,160},{160,128},{192,224},{224,1... | collective-permute-start | bytes 196616 | tf_op jit(solution)/shard_map/ppermute | solution.py:43
  52.1 7.4 %collective-permute-start.14 = (f32[4,64,64]{2,1,0:T(8,128)S(1)}, f32[4,64,64]{2,1,0:T(8,128)S(1)}, u32[]{:S(2)}, u32[]{:S(2)}) collective-permute-start(f32[4,64,64]{2,1,0:T(8,128)S(1)} %fusion.61), channel_id=1, source_target_pairs={{0,128},{32,160},{64,192},{96,224},{128,0},{160,32},{192,64},{224,... | collective-permute-start | bytes 196616 | tf_op jit(solution)/shard_map/ppermute | solution.py:47
  55.5 6.8 %collective-permute-start.15 = (f32[4,64,64]{2,1,0:T(8,128)S(1)}, f32[4,64,64]{2,1,0:T(8,128)S(1)}, u32[]{:S(2)}, u32[]{:S(2)}) collective-permute-start(f32[4,64,64]{2,1,0:T(8,128)S(1)} %fusion.61), channel_id=1, source_target_pairs={{0,192},{32,224},{64,128},{96,160},{128,64},{160,96},{192,0},{224,... | collective-permute-start | bytes 196616 | tf_op jit(solution)/shard_map/ppermute | solution.py:47
  56.3 6.1 %collective-permute-start.13 = (f32[4,64,64]{2,1,0:T(8,128)S(1)}, f32[4,64,64]{2,1,0:T(8,128)S(1)}, u32[]{:S(2)}, u32[]{:S(2)}) collective-permute-start(f32[4,64,64]{2,1,0:T(8,128)S(1)} %fusion.61), channel_id=1, source_target_pairs={{0,64},{32,96},{64,0},{96,32},{128,192},{160,224},{192,128},{224,1... | collective-permute-start | bytes 196616 | tf_op jit(solution)/shard_map/ppermute | solution.py:47
  63.0 8.8 %collective-permute-start.17 = (f32[4,64,64]{2,1,0:T(8,128)}, f32[4,64,64]{2,1,0:T(8,128)}, u32[]{:S(2)}, u32[]{:S(2)}) collective-permute-start(f32[4,64,64]{2,1,0:T(8,128)} %add_add_fusion.2), channel_id=1, source_target_pairs={{0,4},{2,6},{4,0},{6,2},{8,12},{10,14},{12,8},{14,10},{16,20},{18,... | collective-permute-start | bytes 196616 | tf_op jit(solution)/shard_map/ppermute | solution.py:47
  68.3 10.5 %collective-permute-start.18 = (f32[4,64,64]{2,1,0:T(8,128)}, f32[4,64,64]{2,1,0:T(8,128)}, u32[]{:S(2)}, u32[]{:S(2)}) collective-permute-start(f32[4,64,64]{2,1,0:T(8,128)} %add_add_fusion.2), channel_id=1, source_target_pairs={{0,6},{2,4},{4,2},{6,0},{8,14},{10,12},{12,10},{14,8},{16,22},{18,... | collective-permute-start | bytes 196616 | tf_op jit(solution)/shard_map/ppermute | solution.py:47
  71.3 7.6 %collective-permute-start.16 = (f32[4,64,64]{2,1,0:T(8,128)}, f32[4,64,64]{2,1,0:T(8,128)}, u32[]{:S(2)}, u32[]{:S(2)}) collective-permute-start(f32[4,64,64]{2,1,0:T(8,128)} %add_add_fusion.2), channel_id=1, source_target_pairs={{0,2},{2,0},{4,6},{6,4},{8,10},{10,8},{12,14},{14,12},{16,18},{18,... | collective-permute-start | bytes 196616 | tf_op jit(solution)/shard_map/ppermute | solution.py:47
  80.0 20.1 %collective-permute-start.20 = (f32[4,64,64]{2,1,0:T(8,128)S(1)}, f32[4,64,64]{2,1,0:T(8,128)S(1)}, u32[]{:S(2)}, u32[]{:S(2)}) collective-permute-start(f32[4,64,64]{2,1,0:T(8,128)S(1)} %add_add_fusion.1), channel_id=1, source_target_pairs={{0,16},{2,18},{4,20},{6,22},{8,24},{10,26},{12,28},{14,30},{16,0},... | collective-permute-start | bytes 196616 | tf_op jit(solution)/shard_map/ppermute | solution.py:47
  90.5 15.9 %collective-permute-start.21 = (f32[4,64,64]{2,1,0:T(8,128)S(1)}, f32[4,64,64]{2,1,0:T(8,128)S(1)}, u32[]{:S(2)}, u32[]{:S(2)}) collective-permute-start(f32[4,64,64]{2,1,0:T(8,128)S(1)} %add_add_fusion.1), channel_id=1, source_target_pairs={{0,24},{2,26},{4,28},{6,30},{8,16},{10,18},{12,20},{14,22},{16,8},... | collective-permute-start | bytes 196616 | tf_op jit(solution)/shard_map/ppermute | solution.py:47
  90.6 16.1 %collective-permute-start.19 = (f32[4,64,64]{2,1,0:T(8,128)S(1)}, f32[4,64,64]{2,1,0:T(8,128)S(1)}, u32[]{:S(2)}, u32[]{:S(2)}) collective-permute-start(f32[4,64,64]{2,1,0:T(8,128)S(1)} %add_add_fusion.1), channel_id=1, source_target_pairs={{0,8},{2,10},{4,12},{6,14},{8,0},{10,2},{12,4},{14,6},{16,24},{18,... | collective-permute-start | bytes 196616 | tf_op jit(solution)/shard_map/ppermute | solution.py:47
  130.6 2.6 %copy-start.6 = (f32[64,1,8,128]{3,0,2,1:T(8,128)S(1)}, f32[64,1,8,128]{3,0,2,1:T(8,128)}, u32[]{:S(2)}) copy-start(f32[64,1,8,128]{3,0,2,1:T(8,128)} %copy-done.5) | copy-start | bytes 786436
  130.6 2.6 %copy-start.8 = (f32[64,1,8,128]{3,0,2,1:T(8,128)S(1)}, f32[64,1,8,128]{3,0,2,1:T(8,128)}, u32[]{:S(2)}) copy-start(f32[64,1,8,128]{3,0,2,1:T(8,128)} %copy-done.7) | copy-start | bytes 786436
  130.6 2.6 %copy-start.10 = (f32[64,4,1,128]{3,0,2,1:T(8,128)S(1)}, f32[64,4,1,128]{3,0,2,1:T(8,128)}, u32[]{:S(2)}) copy-start(f32[64,4,1,128]{3,0,2,1:T(8,128)} %copy-done.9) | copy-start | bytes 393220
  130.6 2.6 %copy-start.12 = (f32[64,4,1,128]{3,0,2,1:T(8,128)S(1)}, f32[64,4,1,128]{3,0,2,1:T(8,128)}, u32[]{:S(2)}) copy-start(f32[64,4,1,128]{3,0,2,1:T(8,128)} %copy-done.11) | copy-start | bytes 393220
  130.6 2.6 %copy-start.14 = (f32[64,1,8,128]{3,0,2,1:T(8,128)S(1)}, f32[64,1,8,128]{3,0,2,1:T(8,128)}, u32[]{:S(2)}) copy-start(f32[64,1,8,128]{3,0,2,1:T(8,128)} %copy-done.13) | copy-start | bytes 786436
  130.6 2.6 %copy-start.16 = (f32[64,1,8,128]{3,0,2,1:T(8,128)S(1)}, f32[64,1,8,128]{3,0,2,1:T(8,128)}, u32[]{:S(2)}) copy-start(f32[64,1,8,128]{3,0,2,1:T(8,128)} %copy-done.15) | copy-start | bytes 786436
  130.6 2.6 %copy-start.18 = (f32[64,4,1,128]{3,0,2,1:T(8,128)S(1)}, f32[64,4,1,128]{3,0,2,1:T(8,128)}, u32[]{:S(2)}) copy-start(f32[64,4,1,128]{3,0,2,1:T(8,128)} %copy-done.17) | copy-start | bytes 393220
  130.6 2.6 %copy-start.20 = (f32[64,4,1,128]{3,0,2,1:T(8,128)S(1)}, f32[64,4,1,128]{3,0,2,1:T(8,128)}, u32[]{:S(2)}) copy-start(f32[64,4,1,128]{3,0,2,1:T(8,128)} %copy-done.19) | copy-start | bytes 393220
  130.6 2.6 %copy-start.23 = (f32[3,64,64]{2,1,0:T(8,128)S(1)}, f32[3,64,64]{2,1,0:T(8,128)}, u32[]{:S(2)}) copy-start(f32[3,64,64]{2,1,0:T(8,128)} %shard_map.68) | copy-start | bytes 147460
  135.9 3.0 %copy-start.3 = (f32[129,4,1,128]{3,0,2,1:T(8,128)S(1)}, f32[129,4,1,128]{3,0,2,1:T(8,128)}, u32[]{:S(2)}) copy-start(f32[129,4,1,128]{3,0,2,1:T(8,128)} %copy-done.2) | copy-start | bytes 792580
  138.8 1.1 copy-start
  139.0 2.1 %copy-start.4 = (f32[64,4,10,130]{3,0,2,1:T(8,128)S(1)}, f32[64,4,10,130]{3,0,2,1:T(8,128)}, u32[]{:S(2)}) copy-start(f32[64,4,10,130]{3,0,2,1:T(8,128)} %select_maximum_fusion) | copy-start | bytes 3993604
  141.9 5.2 %collective-permute-start.22 = (f32[2,8,64]{2,1,0:T(8,128)S(1)}, f32[2,8,64]{2,1,0:T(8,128)S(1)}, u32[]{:S(2)}, u32[]{:S(2)}) collective-permute-start(f32[2,8,64]{2,1,0:T(8,128)S(1)} %constant_dynamic-slice_fusion), channel_id=1, source_target_pairs={{0,1},{1,0},{2,3},{3,2},{4,5},{5,4},{6,7},{7,6},{8,9},{9,8},{10,11... | collective-permute-start | bytes 12296 | tf_op jit(solution)/shard_map/ppermute | solution.py:243
  (1 other events, 0.7 us)

commit v5 on v4

--- a/solution.py
+++ b/solution.py
@@ -122,27 +122,31 @@
 def _tr(a):
     return jnp.transpose(a)
 
-def _solve(matrix, right):
-    n = matrix.shape[0]
-    rows = lax.broadcasted_iota(jnp.int32, matrix.shape, 0)
-    lanes = lax.broadcasted_iota(jnp.int32, matrix.shape, 1)
+def _solve(pairs, unroll):
+    n = pairs[0][0].shape[0]
+    shape = pairs[0][0].shape
+    rows = lax.broadcasted_iota(jnp.int32, shape, 0)
+    lanes = lax.broadcasted_iota(jnp.int32, shape, 1)
     lane_r = lax.broadcasted_iota(jnp.int32, (1, n), 1)
 
     def step(j, carry):
-        m, r = carry
         pick = rows == j
-        row_m = jnp.sum(jnp.where(pick, m, 0.0), axis=0, keepdims=True)
-        row_r = jnp.sum(jnp.where(pick, r, 0.0), axis=0, keepdims=True)
-        pivot = jnp.sum(jnp.where(lane_r == j, row_m, 0.0), axis=1, keepdims=True)
-        col = jnp.sum(jnp.where(lanes == j, m, 0.0), axis=1, keepdims=True)
-        row_m = row_m / pivot
-        row_r = row_r / pivot
-        m = jnp.where(pick, row_m, m - col * row_m)
-        r = jnp.where(pick, row_r, r - col * row_r)
-        return m, r
-
-    _, out = lax.fori_loop(0, n, step, (matrix, right))
-    return out
+        out = []
+        for m, r in carry:
+            row_m = jnp.sum(jnp.where(pick, m, 0.0), axis=0, keepdims=True)
+            row_r = jnp.sum(jnp.where(pick, r, 0.0), axis=0, keepdims=True)
+            pivot = jnp.sum(jnp.where(lane_r == j, row_m, 0.0), axis=1, keepdims=True)
+            col = jnp.sum(jnp.where(lanes == j, m, 0.0), axis=1, keepdims=True)
+            row_m = row_m / pivot
+            row_r = row_r / pivot
+            m = jnp.where(pick, row_m, m - col * row_m)
+            r = jnp.where(pick, row_r, r - col * row_r)
+            out.append((m, r))
+        return tuple(out)
+
+    done = lax.fori_loop(0, n, step, tuple(pairs), unroll=unroll)
+    return [r for _, r in done]
+
 
 def steps_kernel(grams_ref, out_ref):
     g_rr = grams_ref[0]
@@ -150,20 +154,27 @@
     g_qq = grams_ref[2]
     g_qw = grams_ref[3]
     n = g_rr.shape[0]
-    step0 = _solve(g_rq, g_rr)
+    eye = (
+        lax.broadcasted_iota(jnp.int32, (n, n), 0) == lax.broadcasted_iota(jnp.int32, (n, n), 1)
+    ).astype(jnp.float32)
+    step0, rr_inv = _solve([(g_rq, g_rr), (g_rr, eye)], 2)
     cross = _mm(g_rq, step0)
     step0_t = _tr(step0)
     new_gram = g_rr - cross - _tr(cross) + _mm(step0_t, _mm(g_qq, step0))
-    turn = _solve(g_rr, new_gram)
-    eye = (lax.broadcasted_iota(jnp.int32, (n, n), 0) == lax.broadcasted_iota(jnp.int32, (n, n), 1)).astype(jnp.float32)
+    turn = _mm(rr_inv, new_gram)
     keep = eye + turn
     keep_t = _tr(keep)
-    curv = (_mm(keep_t, _mm(g_rq, keep)) - _mm(keep_t, _mm(g_qq, step0))
-            - _mm(step0_t, _mm(g_qq, keep)) + _mm(step0_t, _mm(g_qw, step0)))
-    step1 = _solve(curv, new_gram)
+    curv = (
+        _mm(keep_t, _mm(g_rq, keep))
+        - _mm(keep_t, _mm(g_qq, step0))
+        - _mm(step0_t, _mm(g_qq, keep))
+        + _mm(step0_t, _mm(g_qw, step0))
+    )
+    (step1,) = _solve([(curv, new_gram)], 4)
     out_ref[0] = step0
     out_ref[1] = turn
     out_ref[2] = step1
+
 
 def steps(grams):
     n = grams.shape[1]

time: 150 us -> 143 us (0.953)
  Pallas kernels: 23.2 us -> 16.9 us
    pallas_call x1, Pallas kernels: 23.2 us -> 16.9 us  [steps(): pl.pallas_call(steps_kernel, out_shape=jax.ShapeDtypeStruct((3, n, n), jn...]
where the time goes in v5:
time: 143 us; the launch traced here: 141 us
  starting transfers between devices  62.3 us (44%)
  waiting for transfers between devices  26.6 us (19%)
  Pallas kernels  16.9 us (12%)
  other arithmetic  12.7 us (9%)
  local copies, waits for them, and re-layouts  10.9 us (8%)
  matrix products  10.5 us (7%)
  between operations  1.52 us (1%)
    ppermute x9, starting transfers between devices, allsum(): lax.ppermute(value, axis, [(i, i ^ d << shift) for i in range(count)])  29 us
    ppermute x6, starting transfers between devices, padded_2(): lax.ppermute(lax.slice_in_dim(block, block.shape[dim] - width, None, axis...  24.4 us
    ppermute x9, waiting for transfers between devices, allsum(): lax.ppermute(value, axis, [(i, i ^ d << shift) for i in range(count)])  19.7 us
    pallas_call x1, Pallas kernels, steps(): pl.pallas_call(steps_kernel, out_shape=jax.ShapeDtypeStruct((3, n, n), jn...  16.9 us
    dot_general x4, matrix products, combine_cols(): jnp.einsum('axyz,ab->bxyz', field, matrix, precision=lax.Precision.HIGHEST)  8.07 us
    ppermute x6, starting transfers between devices, padded_2(): lax.ppermute(lax.slice_in_dim(block, 0, width, axis=dim), axis, backward)  7.74 us
    unnamed x56, local copies, waits for them, and re-layouts  6.49 us
    slice x1, other arithmetic, on_device(): adjoint_pad = padded[1 + columns:]  4.07 us
  transfers between devices with their start and end apart: 23, of which 11 were waited for; matrix products, arithmetic and copies ran while one was open for 8% of the time, Pallas kernels for 0%

profile of v5, /device:TPU:4, one launch (start us, length us, event | category | flops | bytes accessed | tf_op | source)
XLA Modules:
  0.0 141.4 jit_solution(12474931555778311264)
XLA Ops:
  0.6 1.3 copy.42
  2.1 0.7 pad_maximum_fusion.33
  2.8 1.3 collective-permute-start.3
  4.4 1.3 collective-permute-start.2
  5.8 3.1 %collective-permute-start.1 = (f32[129,1,8,128]{3,2,1,0:T(8,128)S(1)}, f32[129,1,8,128]{3,2,1,0:T(8,128)S(1)}, u32[]{:S(2)}, u32[]{:S(2)}) collective-permute-start(f32[129,1,8,128]{3,2,1,0:T(8,128)S(1)} %copy.43), channel_id=1, source_target_pairs={{0,32},{32,64},{64,96},{96,128},{128,160},{160,192},{192,224},{1,3... | collective-permute-start | bytes 1585160 | tf_op jit(solution)/shard_map/ppermute | solution.py:20
  8.9 5.2 %collective-permute-start = (f32[129,2,1,128]{3,0,2,1:T(8,128)}, f32[129,2,1,128]{3,0,2,1:T(8,128)}, u32[]{:S(2)}, u32[]{:S(2)}) collective-permute-start(f32[129,2,1,128]{3,0,2,1:T(8,128)} %get-tuple-element.21), channel_id=1, source_target_pairs={{0,2},{2,4},{4,6},{6,8},{8,10},{10,12},{12,14},{14,16},{16,18},{18... | collective-permute-start | bytes 396296 | tf_op jit(solution)/shard_map/ppermute | solution.py:20
  15.6 0.9 pad.41
  16.5 1.1 collective-permute-done
  17.6 0.9 pad.40
  19.1 1.4 %copy-done.1 = f32[129,4,10,128]{3,0,2,1:T(8,128)} copy-done((f32[129,4,10,128]{3,0,2,1:T(8,128)}, f32[129,4,10,128]{3,0,2,1:T(8,128)S(1)}, u32[]{:S(2)}) %copy-start.1) | copy-done | bytes 2641944
  21.9 1.3 collective-permute-start.4
  23.2 3.0 %collective-permute-start.5 = (f32[64,1,8,128]{3,0,2,1:T(8,128)S(1)}, f32[64,1,8,128]{3,0,2,1:T(8,128)S(1)}, u32[]{:S(2)}, u32[]{:S(2)}) collective-permute-start(f32[64,1,8,128]{3,0,2,1:T(8,128)S(1)} %get-tuple-element.29), channel_id=1, source_target_pairs={{0,32},{32,64},{64,96},{96,128},{128,160},{160,192},{192,224},{1,3... | collective-permute-start | bytes 786440 | tf_op jit(solution)/shard_map/ppermute | solution.py:20
  26.3 1.3 collective-permute-start.6
  27.6 5.0 %collective-permute-start.7 = (f32[64,2,1,128]{3,0,2,1:T(8,128)S(1)}, f32[64,2,1,128]{3,0,2,1:T(8,128)S(1)}, u32[]{:S(2)}, u32[]{:S(2)}) collective-permute-start(f32[64,2,1,128]{3,0,2,1:T(8,128)S(1)} %get-tuple-element.27), channel_id=1, source_target_pairs={{0,2},{2,4},{4,6},{6,8},{8,10},{10,12},{12,14},{14,16},{16,18},{18... | collective-permute-start | bytes 196616 | tf_op jit(solution)/shard_map/ppermute | solution.py:20
  33.2 1.5 %collective-permute-done.7 = f32[64,2,1,128]{3,0,2,1:T(8,128)S(1)} collective-permute-done((f32[64,2,1,128]{3,0,2,1:T(8,128)S(1)}, f32[64,2,1,128]{3,0,2,1:T(8,128)S(1)}, u32[]{:S(2)}, u32[]{:S(2)}) %collective-permute-start.7) | collective-permute-done | bytes 65568 | tf_op jit(solution)/shard_map/ppermute | solution.py:20
  36.0 1.3 collective-permute-start.10
  37.3 1.3 collective-permute-start.8
  38.6 3.0 %collective-permute-start.9 = (f32[64,1,8,128]{3,0,2,1:T(8,128)S(1)}, f32[64,1,8,128]{3,0,2,1:T(8,128)S(1)}, u32[]{:S(2)}, u32[]{:S(2)}) collective-permute-start(f32[64,1,8,128]{3,0,2,1:T(8,128)S(1)} %get-tuple-element.25), channel_id=1, source_target_pairs={{0,32},{32,64},{64,96},{96,128},{128,160},{160,192},{192,224},{1,3... | collective-permute-start | bytes 786440 | tf_op jit(solution)/shard_map/ppermute | solution.py:20
  41.7 5.0 %collective-permute-start.11 = (f32[64,2,1,128]{3,0,2,1:T(8,128)S(1)}, f32[64,2,1,128]{3,0,2,1:T(8,128)S(1)}, u32[]{:S(2)}, u32[]{:S(2)}) collective-permute-start(f32[64,2,1,128]{3,0,2,1:T(8,128)S(1)} %get-tuple-element.23), channel_id=1, source_target_pairs={{0,2},{2,4},{4,6},{6,8},{8,10},{10,12},{12,14},{14,16},{16,18},{18... | collective-permute-start | bytes 196616 | tf_op jit(solution)/shard_map/ppermute | solution.py:20
  47.9 0.8 collective-permute-done.11
  49.7 0.7 convolution_bitcast_fusion
  50.4 0.7 collective-permute-start.12
  51.1 1.0 collective-permute-done.12
  52.1 3.4 %collective-permute-start.14 = (f32[4,64,64]{2,1,0:T(8,128)S(1)}, f32[4,64,64]{2,1,0:T(8,128)S(1)}, u32[]{:S(2)}, u32[]{:S(2)}) collective-permute-start(f32[4,64,64]{2,1,0:T(8,128)S(1)} %fusion.61), channel_id=1, source_target_pairs={{0,128},{32,160},{64,192},{96,224},{128,0},{160,32},{192,64},{224,... | collective-permute-start | bytes 196616 | tf_op jit(solution)/shard_map/ppermute | solution.py:47
  55.5 0.8 collective-permute-start.15
  56.3 3.3 %collective-permute-done.14 = f32[4,64,64]{2,1,0:T(8,128)S(1)} collective-permute-done((f32[4,64,64]{2,1,0:T(8,128)S(1)}, f32[4,64,64]{2,1,0:T(8,128)S(1)}, u32[]{:S(2)}, u32[]{:S(2)}) %collective-permute-start.14) | collective-permute-done | bytes 65568 | tf_op jit(solution)/shard_map/ppermute | solution.py:47
  59.5 2.8 %collective-permute-done.15 = f32[4,64,64]{2,1,0:T(8,128)S(1)} collective-permute-done((f32[4,64,64]{2,1,0:T(8,128)S(1)}, f32[4,64,64]{2,1,0:T(8,128)S(1)}, u32[]{:S(2)}, u32[]{:S(2)}) %collective-permute-start.15) | collective-permute-done | bytes 65568 | tf_op jit(solution)/shard_map/ppermute | solution.py:47
  62.3 0.7 add_add_fusion.2
  63.0 5.3 %collective-permute-start.17 = (f32[4,64,64]{2,1,0:T(8,128)}, f32[4,64,64]{2,1,0:T(8,128)}, u32[]{:S(2)}, u32[]{:S(2)}) collective-permute-start(f32[4,64,64]{2,1,0:T(8,128)} %add_add_fusion.2), channel_id=1, source_target_pairs={{0,4},{2,6},{4,0},{6,2},{8,12},{10,14},{12,8},{14,10},{16,20},{18,... | collective-permute-start | bytes 196616 | tf_op jit(solution)/shard_map/ppermute | solution.py:47
  68.3 2.9 %collective-permute-start.18 = (f32[4,64,64]{2,1,0:T(8,128)}, f32[4,64,64]{2,1,0:T(8,128)}, u32[]{:S(2)}, u32[]{:S(2)}) collective-permute-start(f32[4,64,64]{2,1,0:T(8,128)} %add_add_fusion.2), channel_id=1, source_target_pairs={{0,6},{2,4},{4,2},{6,0},{8,14},{10,12},{12,10},{14,8},{16,22},{18,... | collective-permute-start | bytes 196616 | tf_op jit(solution)/shard_map/ppermute | solution.py:47
  71.9 6.9 %collective-permute-done.18 = f32[4,64,64]{2,1,0:T(8,128)} collective-permute-done((f32[4,64,64]{2,1,0:T(8,128)}, f32[4,64,64]{2,1,0:T(8,128)}, u32[]{:S(2)}, u32[]{:S(2)}) %collective-permute-start.18) | collective-permute-done | bytes 65568 | tf_op jit(solution)/shard_map/ppermute | solution.py:47
  78.9 1.1 add_add_fusion.1
  80.0 10.5 %collective-permute-start.20 = (f32[4,64,64]{2,1,0:T(8,128)S(1)}, f32[4,64,64]{2,1,0:T(8,128)S(1)}, u32[]{:S(2)}, u32[]{:S(2)}) collective-permute-start(f32[4,64,64]{2,1,0:T(8,128)S(1)} %add_add_fusion.1), channel_id=1, source_target_pairs={{0,16},{2,18},{4,20},{6,22},{8,24},{10,26},{12,28},{14,30},{16,0},... | collective-permute-start | bytes 196616 | tf_op jit(solution)/shard_map/ppermute | solution.py:47
  90.6 5.5 %collective-permute-start.19 = (f32[4,64,64]{2,1,0:T(8,128)S(1)}, f32[4,64,64]{2,1,0:T(8,128)S(1)}, u32[]{:S(2)}, u32[]{:S(2)}) collective-permute-start(f32[4,64,64]{2,1,0:T(8,128)S(1)} %add_add_fusion.1), channel_id=1, source_target_pairs={{0,8},{2,10},{4,12},{6,14},{8,0},{10,2},{12,4},{14,6},{16,24},{18,... | collective-permute-start | bytes 196616 | tf_op jit(solution)/shard_map/ppermute | solution.py:47
  96.0 4.1 %select_maximum_fusion = f32[64,4,10,130]{3,0,2,1:T(8,128)} fusion(f32[129,4,1,128]{3,0,2,1:T(8,128)S(1)} %pad.41, f32[129,4,1,128]{3,0,2,1:T(8,128)} %copy-done.2, f32[129,1,8,128]{3,0,2,1:T(8,128)S(1)} %copy.46, f32[129,1,8,128]{3,0,2,1:T(8,128)S(1)} %copy.45, f32[64,2,8,128]{3,0,2,1:T(8,128)S(1)} %copy.42, f32[64,2,8,128]{3,0,2,1:T(8,128)S(1)} %copy.41, ...), kind=kLoop, calls=%fused_computation.12 | loop fusion | flops 5324800 | bytes 3973120 | tf_op jit(solution)/shard_map/slice | solution.py:210
  100.1 6.4 %collective-permute-done.21 = f32[4,64,64]{2,1,0:T(8,128)S(1)} collective-permute-done((f32[4,64,64]{2,1,0:T(8,128)S(1)}, f32[4,64,64]{2,1,0:T(8,128)S(1)}, u32[]{:S(2)}, u32[]{:S(2)}) %collective-permute-start.21) | collective-permute-done | bytes 65568 | tf_op jit(solution)/shard_map/ppermute | solution.py:47
  106.7 0.7 add_add_fusion.grams_ref
  107.3 16.9 %shard_map.68 = f32[3,64,64]{2,1,0:T(8,128)} custom-call(f32[4,64,64]{2,1,0:T(8,128)} %add_add_fusion.grams_ref), custom_call_target="tpu_custom_call" | custom-call | tf_op jit(solution)/shard_map/pallas_call | solution.py:181
  124.3 2.5 %fusion.48 = f32[64,4,10,128]{3,0,2,1:T(8,128)S(1)} fusion(f32[3,64,64]{2,1,0:T(8,128)} %shard_map.68, f32[64,4,1,128]{3,0,2,1:T(8,128)} %copy-done.9, f32[64,1,8,128]{3,0,2,1:T(8,128)} %copy-done.5, f32[64,2,8,128]{3,0,2,1:T(8,128)S(1)} %fusion.36, f32[64,1,8,128]{3,0,2,1:T(8,128)} %copy-done.7, f32[64,4,1,128]{3,0,2,1:T(8,128)} %copy-done.11), kind=kOutput, calls=%fused_computation.148 | convolution fusion | flops 252968960 | bytes 2654208 | tf_op jit(solution)/shard_map/axyz,ab->bxyz/dot_general | solution.py:81
  126.9 1.4 fusion.1
  128.3 1.3 fusion.49
  129.6 2.9 %fusion.2 = f32[64,4,10,128]{3,0,2,1:T(8,128)S(1)} fusion(f32[64,4,10,128]{3,0,2,1:T(8,128)S(1)} %fusion.49, f32[3,64,64]{2,1,0:T(8,128)S(1)} %copy-done.23, f32[129,4,10,128]{3,0,2,1:T(8,128)} %copy-done.1, f32[64,4,1,128]{3,0,2,1:T(8,128)S(1)} %copy-done.10, f32[64,1,8,128]{3,0,2,1:T(8,128)S(1)} %copy-done.6, f32[64,2,8,128]{3,0,2,1:T(8,128)S(1)} %fusion.36, ...), kind=kOutput, calls=%fused_computation.22 | convolution fusion | flops 253624320 | bytes 5275648 | tf_op jit(solution)/shard_map/axyz,ab->bxyz/dot_general | solution.py:81
  132.9 0.7 copy-done
  133.6 1.1 copy-done.4
  136.1 1.1 slice.408
  137.2 1.1 copy.58
  138.3 2.4 %collective-permute-done.22 = f32[2,8,64]{2,1,0:T(8,128)S(1)} collective-permute-done((f32[2,8,64]{2,1,0:T(8,128)S(1)}, f32[2,8,64]{2,1,0:T(8,128)S(1)}, u32[]{:S(2)}, u32[]{:S(2)}) %collective-permute-start.22) | collective-permute-done | bytes 4128 | tf_op jit(solution)/shard_map/ppermute | solution.py:254
  140.7 0.7 dynamic-slice_add_fusion
  (129 shorter events, 10.2 us)
Async XLA Ops:
  0.6 1.3 copy-start.22
  0.6 1.5 %copy-start.21 = (f32[2,8,128]{2,1,0:T(8,128)S(1)}, f32[2,8,128]{2,1,0:T(8,128)}, u32[]{:S(2)}) copy-start(f32[2,8,128]{2,1,0:T(8,128)} %param.5) | copy-start | bytes 24580
  2.8 12.8 %collective-permute-start.3 = (f32[129,2,1,128]{3,0,2,1:T(8,128)S(1)}, f32[129,2,1,128]{3,0,2,1:T(8,128)}, u32[]{:S(2)}, u32[]{:S(2)}) collective-permute-start(f32[129,2,1,128]{3,0,2,1:T(8,128)S(1)} %get-tuple-element.22), channel_id=1, source_target_pairs={{2,0},{4,2},{6,4},{8,6},{10,8},{12,10},{14,12},{16,14},{18,16},{20... | collective-permute-start | bytes 396296 | tf_op jit(solution)/shard_map/ppermute | solution.py:23
  4.3 9.8 %copy-start.25 = (s32[64]{0:T(128)S(1)}, s32[64]{0:T(128)}, u32[]{:S(2)}) copy-start(s32[64]{0:T(128)} %param.7) | copy-start | bytes 772
  4.3 9.8 %copy-start.24 = (s32[128,2]{0,1:T(2,128)S(1)}, s32[128,2]{0,1:T(2,128)}, u32[]{:S(2)}) copy-start(s32[128,2]{0,1:T(2,128)} %param.6) | copy-start | bytes 3076
  4.4 14.2 %collective-permute-start.2 = (f32[129,1,8,128]{3,2,1,0:T(8,128)S(1)}, f32[129,1,8,128]{3,2,1,0:T(8,128)S(1)}, u32[]{:S(2)}, u32[]{:S(2)}) collective-permute-start(f32[129,1,8,128]{3,2,1,0:T(8,128)S(1)} %copy.44), channel_id=1, source_target_pairs={{32,0},{64,32},{96,64},{128,96},{160,128},{192,160},{224,192},{33,... | collective-permute-start | bytes 1585160 | tf_op jit(solution)/shard_map/ppermute | solution.py:23
  5.8 12.9 %collective-permute-start.1 = (f32[129,1,8,128]{3,2,1,0:T(8,128)S(1)}, f32[129,1,8,128]{3,2,1,0:T(8,128)S(1)}, u32[]{:S(2)}, u32[]{:S(2)}) collective-permute-start(f32[129,1,8,128]{3,2,1,0:T(8,128)S(1)} %copy.43), channel_id=1, source_target_pairs={{0,32},{32,64},{64,96},{96,128},{128,160},{160,192},{192,224},{1,3... | collective-permute-start | bytes 1585160 | tf_op jit(solution)/shard_map/ppermute | solution.py:20
  8.9 8.7 %collective-permute-start = (f32[129,2,1,128]{3,0,2,1:T(8,128)}, f32[129,2,1,128]{3,0,2,1:T(8,128)}, u32[]{:S(2)}, u32[]{:S(2)}) collective-permute-start(f32[129,2,1,128]{3,0,2,1:T(8,128)} %get-tuple-element.21), channel_id=1, source_target_pairs={{0,2},{2,4},{4,6},{6,8},{8,10},{10,12},{12,14},{14,16},{16,18},{18... | collective-permute-start | bytes 396296 | tf_op jit(solution)/shard_map/ppermute | solution.py:20
  18.5 2.2 %copy-start.2 = (f32[129,4,1,128]{3,0,2,1:T(8,128)}, f32[129,4,1,128]{3,0,2,1:T(8,128)S(1)}, u32[]{:S(2)}) copy-start(f32[129,4,1,128]{3,0,2,1:T(8,128)S(1)} %pad.40) | copy-start | bytes 792580
  19.0 1.5 %copy-start.1 = (f32[129,4,10,128]{3,0,2,1:T(8,128)}, f32[129,4,10,128]{3,0,2,1:T(8,128)S(1)}, u32[]{:S(2)}) copy-start(f32[129,4,10,128]{3,0,2,1:T(8,128)S(1)} %pad_maximum_fusion) | copy-start | bytes 7925764
  21.9 12.8 %collective-permute-start.4 = (f32[64,1,8,128]{3,0,2,1:T(8,128)S(1)}, f32[64,1,8,128]{3,0,2,1:T(8,128)S(1)}, u32[]{:S(2)}, u32[]{:S(2)}) collective-permute-start(f32[64,1,8,128]{3,0,2,1:T(8,128)S(1)} %get-tuple-element.30), channel_id=1, source_target_pairs={{32,0},{64,32},{96,64},{128,96},{160,128},{192,160},{224,192},{33,... | collective-permute-start | bytes 786440 | tf_op jit(solution)/shard_map/ppermute | solution.py:23
  23.2 11.5 %collective-permute-start.5 = (f32[64,1,8,128]{3,0,2,1:T(8,128)S(1)}, f32[64,1,8,128]{3,0,2,1:T(8,128)S(1)}, u32[]{:S(2)}, u32[]{:S(2)}) collective-permute-start(f32[64,1,8,128]{3,0,2,1:T(8,128)S(1)} %get-tuple-element.29), channel_id=1, source_target_pairs={{0,32},{32,64},{64,96},{96,128},{128,160},{160,192},{192,224},{1,3... | collective-permute-start | bytes 786440 | tf_op jit(solution)/shard_map/ppermute | solution.py:20
  26.3 6.9 %collective-permute-start.6 = (f32[64,2,1,128]{3,0,2,1:T(8,128)S(1)}, f32[64,2,1,128]{3,0,2,1:T(8,128)S(1)}, u32[]{:S(2)}, u32[]{:S(2)}) collective-permute-start(f32[64,2,1,128]{3,0,2,1:T(8,128)S(1)} %get-tuple-element.28), channel_id=1, source_target_pairs={{2,0},{4,2},{6,4},{8,6},{10,8},{12,10},{14,12},{16,14},{18,16},{20... | collective-permute-start | bytes 196616 | tf_op jit(solution)/shard_map/ppermute | solution.py:23
  27.6 7.1 %collective-permute-start.7 = (f32[64,2,1,128]{3,0,2,1:T(8,128)S(1)}, f32[64,2,1,128]{3,0,2,1:T(8,128)S(1)}, u32[]{:S(2)}, u32[]{:S(2)}) collective-permute-start(f32[64,2,1,128]{3,0,2,1:T(8,128)S(1)} %get-tuple-element.27), channel_id=1, source_target_pairs={{0,2},{2,4},{4,6},{6,8},{8,10},{10,12},{12,14},{14,16},{16,18},{18... | collective-permute-start | bytes 196616 | tf_op jit(solution)/shard_map/ppermute | solution.py:20
  33.2 2.0 %copy-start.9 = (f32[64,4,1,128]{3,0,2,1:T(8,128)}, f32[64,4,1,128]{3,0,2,1:T(8,128)S(1)}, u32[]{:S(2)}) copy-start(f32[64,4,1,128]{3,0,2,1:T(8,128)S(1)} %pad.44) | copy-start | bytes 393220
  34.7 0.7 copy-start.11
  34.7 0.7 copy-start.5
  34.8 0.8 copy-start.7
  36.0 11.8 %collective-permute-start.10 = (f32[64,2,1,128]{3,0,2,1:T(8,128)S(1)}, f32[64,2,1,128]{3,0,2,1:T(8,128)S(1)}, u32[]{:S(2)}, u32[]{:S(2)}) collective-permute-start(f32[64,2,1,128]{3,0,2,1:T(8,128)S(1)} %get-tuple-element.24), channel_id=1, source_target_pairs={{2,0},{4,2},{6,4},{8,6},{10,8},{12,10},{14,12},{16,14},{18,16},{20... | collective-permute-start | bytes 196616 | tf_op jit(solution)/shard_map/ppermute | solution.py:23
  37.3 11.4 %collective-permute-start.8 = (f32[64,1,8,128]{3,0,2,1:T(8,128)S(1)}, f32[64,1,8,128]{3,0,2,1:T(8,128)S(1)}, u32[]{:S(2)}, u32[]{:S(2)}) collective-permute-start(f32[64,1,8,128]{3,0,2,1:T(8,128)S(1)} %get-tuple-element.26), channel_id=1, source_target_pairs={{32,0},{64,32},{96,64},{128,96},{160,128},{192,160},{224,192},{33,... | collective-permute-start | bytes 786440 | tf_op jit(solution)/shard_map/ppermute | solution.py:23
  38.6 10.1 %collective-permute-start.9 = (f32[64,1,8,128]{3,0,2,1:T(8,128)S(1)}, f32[64,1,8,128]{3,0,2,1:T(8,128)S(1)}, u32[]{:S(2)}, u32[]{:S(2)}) collective-permute-start(f32[64,1,8,128]{3,0,2,1:T(8,128)S(1)} %get-tuple-element.25), channel_id=1, source_target_pairs={{0,32},{32,64},{64,96},{96,128},{128,160},{160,192},{192,224},{1,3... | collective-permute-start | bytes 786440 | tf_op jit(solution)/shard_map/ppermute | solution.py:20
  41.7 7.0 %collective-permute-start.11 = (f32[64,2,1,128]{3,0,2,1:T(8,128)S(1)}, f32[64,2,1,128]{3,0,2,1:T(8,128)S(1)}, u32[]{:S(2)}, u32[]{:S(2)}) collective-permute-start(f32[64,2,1,128]{3,0,2,1:T(8,128)S(1)} %get-tuple-element.23), channel_id=1, source_target_pairs={{0,2},{2,4},{4,6},{6,8},{8,10},{10,12},{12,14},{14,16},{16,18},{18... | collective-permute-start | bytes 196616 | tf_op jit(solution)/shard_map/ppermute | solution.py:20
  47.9 1.4 copy-start.17
  48.7 0.7 copy-start.13
  48.8 0.8 copy-start.15
  50.4 1.6 %collective-permute-start.12 = (f32[4,64,64]{2,1,0:T(8,128)S(1)}, f32[4,64,64]{2,1,0:T(8,128)S(1)}, u32[]{:S(2)}, u32[]{:S(2)}) collective-permute-start(f32[4,64,64]{2,1,0:T(8,128)S(1)} %pad_maximum_fusion.34), channel_id=1, source_target_pairs={{0,32},{32,0},{64,96},{96,64},{128,160},{160,128},{192,224},{224,1... | collective-permute-start | bytes 196616 | tf_op jit(solution)/shard_map/ppermute | solution.py:43
  52.1 7.4 %collective-permute-start.14 = (f32[4,64,64]{2,1,0:T(8,128)S(1)}, f32[4,64,64]{2,1,0:T(8,128)S(1)}, u32[]{:S(2)}, u32[]{:S(2)}) collective-permute-start(f32[4,64,64]{2,1,0:T(8,128)S(1)} %fusion.61), channel_id=1, source_target_pairs={{0,128},{32,160},{64,192},{96,224},{128,0},{160,32},{192,64},{224,... | collective-permute-start | bytes 196616 | tf_op jit(solution)/shard_map/ppermute | solution.py:47
  55.5 6.8 %collective-permute-start.15 = (f32[4,64,64]{2,1,0:T(8,128)S(1)}, f32[4,64,64]{2,1,0:T(8,128)S(1)}, u32[]{:S(2)}, u32[]{:S(2)}) collective-permute-start(f32[4,64,64]{2,1,0:T(8,128)S(1)} %fusion.61), channel_id=1, source_target_pairs={{0,192},{32,224},{64,128},{96,160},{128,64},{160,96},{192,0},{224,... | collective-permute-start | bytes 196616 | tf_op jit(solution)/shard_map/ppermute | solution.py:47
  56.3 6.1 %collective-permute-start.13 = (f32[4,64,64]{2,1,0:T(8,128)S(1)}, f32[4,64,64]{2,1,0:T(8,128)S(1)}, u32[]{:S(2)}, u32[]{:S(2)}) collective-permute-start(f32[4,64,64]{2,1,0:T(8,128)S(1)} %fusion.61), channel_id=1, source_target_pairs={{0,64},{32,96},{64,0},{96,32},{128,192},{160,224},{192,128},{224,1... | collective-permute-start | bytes 196616 | tf_op jit(solution)/shard_map/ppermute | solution.py:47
  63.0 8.8 %collective-permute-start.17 = (f32[4,64,64]{2,1,0:T(8,128)}, f32[4,64,64]{2,1,0:T(8,128)}, u32[]{:S(2)}, u32[]{:S(2)}) collective-permute-start(f32[4,64,64]{2,1,0:T(8,128)} %add_add_fusion.2), channel_id=1, source_target_pairs={{0,4},{2,6},{4,0},{6,2},{8,12},{10,14},{12,8},{14,10},{16,20},{18,... | collective-permute-start | bytes 196616 | tf_op jit(solution)/shard_map/ppermute | solution.py:47
  68.3 10.5 %collective-permute-start.18 = (f32[4,64,64]{2,1,0:T(8,128)}, f32[4,64,64]{2,1,0:T(8,128)}, u32[]{:S(2)}, u32[]{:S(2)}) collective-permute-start(f32[4,64,64]{2,1,0:T(8,128)} %add_add_fusion.2), channel_id=1, source_target_pairs={{0,6},{2,4},{4,2},{6,0},{8,14},{10,12},{12,10},{14,8},{16,22},{18,... | collective-permute-start | bytes 196616 | tf_op jit(solution)/shard_map/ppermute | solution.py:47
  71.3 7.6 %collective-permute-start.16 = (f32[4,64,64]{2,1,0:T(8,128)}, f32[4,64,64]{2,1,0:T(8,128)}, u32[]{:S(2)}, u32[]{:S(2)}) collective-permute-start(f32[4,64,64]{2,1,0:T(8,128)} %add_add_fusion.2), channel_id=1, source_target_pairs={{0,2},{2,0},{4,6},{6,4},{8,10},{10,8},{12,14},{14,12},{16,18},{18,... | collective-permute-start | bytes 196616 | tf_op jit(solution)/shard_map/ppermute | solution.py:47
  80.0 20.1 %collective-permute-start.20 = (f32[4,64,64]{2,1,0:T(8,128)S(1)}, f32[4,64,64]{2,1,0:T(8,128)S(1)}, u32[]{:S(2)}, u32[]{:S(2)}) collective-permute-start(f32[4,64,64]{2,1,0:T(8,128)S(1)} %add_add_fusion.1), channel_id=1, source_target_pairs={{0,16},{2,18},{4,20},{6,22},{8,24},{10,26},{12,28},{14,30},{16,0},... | collective-permute-start | bytes 196616 | tf_op jit(solution)/shard_map/ppermute | solution.py:47
  90.5 15.9 %collective-permute-start.21 = (f32[4,64,64]{2,1,0:T(8,128)S(1)}, f32[4,64,64]{2,1,0:T(8,128)S(1)}, u32[]{:S(2)}, u32[]{:S(2)}) collective-permute-start(f32[4,64,64]{2,1,0:T(8,128)S(1)} %add_add_fusion.1), channel_id=1, source_target_pairs={{0,24},{2,26},{4,28},{6,30},{8,16},{10,18},{12,20},{14,22},{16,8},... | collective-permute-start | bytes 196616 | tf_op jit(solution)/shard_map/ppermute | solution.py:47
  90.6 16.1 %collective-permute-start.19 = (f32[4,64,64]{2,1,0:T(8,128)S(1)}, f32[4,64,64]{2,1,0:T(8,128)S(1)}, u32[]{:S(2)}, u32[]{:S(2)}) collective-permute-start(f32[4,64,64]{2,1,0:T(8,128)S(1)} %add_add_fusion.1), channel_id=1, source_target_pairs={{0,8},{2,10},{4,12},{6,14},{8,0},{10,2},{12,4},{14,6},{16,24},{18,... | collective-permute-start | bytes 196616 | tf_op jit(solution)/shard_map/ppermute | solution.py:47
  124.3 2.6 %copy-start.6 = (f32[64,1,8,128]{3,0,2,1:T(8,128)S(1)}, f32[64,1,8,128]{3,0,2,1:T(8,128)}, u32[]{:S(2)}) copy-start(f32[64,1,8,128]{3,0,2,1:T(8,128)} %copy-done.5) | copy-start | bytes 786436
  124.3 2.6 %copy-start.8 = (f32[64,1,8,128]{3,0,2,1:T(8,128)S(1)}, f32[64,1,8,128]{3,0,2,1:T(8,128)}, u32[]{:S(2)}) copy-start(f32[64,1,8,128]{3,0,2,1:T(8,128)} %copy-done.7) | copy-start | bytes 786436
  124.3 2.6 %copy-start.10 = (f32[64,4,1,128]{3,0,2,1:T(8,128)S(1)}, f32[64,4,1,128]{3,0,2,1:T(8,128)}, u32[]{:S(2)}) copy-start(f32[64,4,1,128]{3,0,2,1:T(8,128)} %copy-done.9) | copy-start | bytes 393220
  124.3 2.6 %copy-start.12 = (f32[64,4,1,128]{3,0,2,1:T(8,128)S(1)}, f32[64,4,1,128]{3,0,2,1:T(8,128)}, u32[]{:S(2)}) copy-start(f32[64,4,1,128]{3,0,2,1:T(8,128)} %copy-done.11) | copy-start | bytes 393220
  124.3 2.6 %copy-start.14 = (f32[64,1,8,128]{3,0,2,1:T(8,128)S(1)}, f32[64,1,8,128]{3,0,2,1:T(8,128)}, u32[]{:S(2)}) copy-start(f32[64,1,8,128]{3,0,2,1:T(8,128)} %copy-done.13) | copy-start | bytes 786436
  124.3 2.6 %copy-start.16 = (f32[64,1,8,128]{3,0,2,1:T(8,128)S(1)}, f32[64,1,8,128]{3,0,2,1:T(8,128)}, u32[]{:S(2)}) copy-start(f32[64,1,8,128]{3,0,2,1:T(8,128)} %copy-done.15) | copy-start | bytes 786436
  124.3 2.6 %copy-start.18 = (f32[64,4,1,128]{3,0,2,1:T(8,128)S(1)}, f32[64,4,1,128]{3,0,2,1:T(8,128)}, u32[]{:S(2)}) copy-start(f32[64,4,1,128]{3,0,2,1:T(8,128)} %copy-done.17) | copy-start | bytes 393220
  124.3 2.6 %copy-start.20 = (f32[64,4,1,128]{3,0,2,1:T(8,128)S(1)}, f32[64,4,1,128]{3,0,2,1:T(8,128)}, u32[]{:S(2)}) copy-start(f32[64,4,1,128]{3,0,2,1:T(8,128)} %copy-done.19) | copy-start | bytes 393220
  124.3 2.6 %copy-start.23 = (f32[3,64,64]{2,1,0:T(8,128)S(1)}, f32[3,64,64]{2,1,0:T(8,128)}, u32[]{:S(2)}) copy-start(f32[3,64,64]{2,1,0:T(8,128)} %shard_map.68) | copy-start | bytes 147460
  129.6 3.0 %copy-start.3 = (f32[129,4,1,128]{3,0,2,1:T(8,128)S(1)}, f32[129,4,1,128]{3,0,2,1:T(8,128)}, u32[]{:S(2)}) copy-start(f32[129,4,1,128]{3,0,2,1:T(8,128)} %copy-done.2) | copy-start | bytes 792580
  132.5 1.1 copy-start
  132.7 2.1 %copy-start.4 = (f32[64,4,10,130]{3,0,2,1:T(8,128)S(1)}, f32[64,4,10,130]{3,0,2,1:T(8,128)}, u32[]{:S(2)}) copy-start(f32[64,4,10,130]{3,0,2,1:T(8,128)} %select_maximum_fusion) | copy-start | bytes 3993604
  135.6 5.2 %collective-permute-start.22 = (f32[2,8,64]{2,1,0:T(8,128)S(1)}, f32[2,8,64]{2,1,0:T(8,128)S(1)}, u32[]{:S(2)}, u32[]{:S(2)}) collective-permute-start(f32[2,8,64]{2,1,0:T(8,128)S(1)} %constant_dynamic-slice_fusion), channel_id=1, source_target_pairs={{0,1},{1,0},{2,3},{3,2},{4,5},{5,4},{6,7},{7,6},{8,9},{9,8},{10,11... | collective-permute-start | bytes 12296 | tf_op jit(solution)/shard_map/ppermute | solution.py:254
  (1 other events, 0.7 us)

commit v6 on v5

--- a/solution.py
+++ b/solution.py
@@ -15,12 +15,15 @@
     pieces = {}
     for axis, dim in sides:
         count = lax.axis_size(axis)
-        forward = [(i, i + 1) for i in range(count - 1)]
+        place = lax.axis_index(axis)
+        forward = [(i, (i + 1) % count) for i in range(count)]
         backward = [(target, source) for source, target in forward]
         low = lax.ppermute(
             lax.slice_in_dim(block, block.shape[dim] - width, None, axis=dim), axis, forward
         )
         high = lax.ppermute(lax.slice_in_dim(block, 0, width, axis=dim), axis, backward)
+        low = jnp.where(place == 0, jnp.zeros_like(low), low)
+        high = jnp.where(place == count - 1, jnp.zeros_like(high), high)
         pieces[axis] = (low, high)
     low_x, high_x = pieces[axis_x]
     low_y, high_y = pieces[axis_y]

time: 143 us -> 127 us (0.89); the launches traced: 141 us -> 127 us
  starting transfers between devices: 62.3 us -> 31.3 us
  waiting for transfers between devices: 26.6 us -> 42.8 us
  other arithmetic: 12.7 us -> 14.7 us
  local copies, waits for them, and re-layouts: 10.9 us -> 9.28 us
    ppermute x6, starting transfers between devices: 24.4 us -> 2.86 us  [padded_2(): lax.ppermute(lax.slice_in_dim(block, block.shape[dim] - width, None, axis...]
    ppermute x9, starting transfers between devices: 29 us -> 15.1 us  [allsum(): lax.ppermute(value, axis, [(i, i ^ d << shift) for i in range(count)])]
    ppermute x6, waiting for transfers between devices: 3.44 us -> 16.6 us  [padded_2(): lax.ppermute(lax.slice_in_dim(block, block.shape[dim] - width, None, axis...]
    ppermute x6, starting transfers between devices: 7.74 us -> 12.1 us  [padded_2(): lax.ppermute(lax.slice_in_dim(block, 0, width, axis=dim), axis, backward)]
    select_n x0 -> x12, other arithmetic: none -> 2.57 us  [the longest x6 1.34 us: padded_2(): high = jnp.where(place == count - 1, jnp.zeros_like(high), high)]
    ppermute x9, waiting for transfers between devices: 19.7 us -> 21.3 us  [allsum(): lax.ppermute(value, axis, [(i, i ^ d << shift) for i in range(count)])]
  transfers between devices with their start and end apart: 23 -> 23, of which waited for: 11 -> 16; matrix products, arithmetic and copies ran while one was open for 8% -> 8% of each run, Pallas kernels for 0% -> 0%
where the time goes in v6:
time: 127 us
  waiting for transfers between devices  42.8 us (34%)
  starting transfers between devices  31.3 us (25%)
  Pallas kernels  16.9 us (13%)
  other arithmetic  14.7 us (12%)
  matrix products  10.5 us (8%)
  local copies, waits for them, and re-layouts  9.28 us (7%)
  between operations  1.51 us (1%)
    ppermute x9, waiting for transfers between devices, allsum(): lax.ppermute(value, axis, [(i, i ^ d << shift) for i in range(count)])  21.3 us
    pallas_call x1, Pallas kernels, steps(): pl.pallas_call(steps_kernel, out_shape=jax.ShapeDtypeStruct((3, n, n), jn...  16.9 us
    ppermute x6, waiting for transfers between devices, padded_2(): lax.ppermute(lax.slice_in_dim(block, block.shape[dim] - width, None, axis...  16.6 us
    ppermute x9, starting transfers between devices, allsum(): lax.ppermute(value, axis, [(i, i ^ d << shift) for i in range(count)])  15.1 us
    ppermute x6, starting transfers between devices, padded_2(): lax.ppermute(lax.slice_in_dim(block, 0, width, axis=dim), axis, backward)  12.1 us
    dot_general x4, matrix products, combine_cols(): jnp.einsum('axyz,ab->bxyz', field, matrix, precision=lax.Precision.HIGHEST)  8.07 us
    unnamed x56, local copies, waits for them, and re-layouts  6.89 us
    slice x1, other arithmetic, on_device(): adjoint_pad = padded[1 + columns:]  4.07 us
  transfers between devices with their start and end apart: 23, of which 16 were waited for; matrix products, arithmetic and copies ran while one was open for 8% of the time, Pallas kernels for 0%

profile of v6, /device:TPU:4, one launch (start us, length us, event | category | flops | bytes accessed | tf_op | source)
XLA Modules:
  0.0 126.9 jit_solution(3242142873578415596)
XLA Ops:
  0.6 1.3 copy.40
  2.2 6.6 %collective-permute-start.3 = (f32[129,2,1,128]{3,0,2,1:T(8,128)S(1)}, f32[129,2,1,128]{3,0,2,1:T(8,128)S(1)}, u32[]{:S(2)}, u32[]{:S(2)}) collective-permute-start(f32[129,2,1,128]{3,0,2,1:T(8,128)S(1)} %get-tuple-element.22), channel_id=1, source_target_pairs={{2,0},{4,2},{6,4},{8,6},{10,8},{12,10},{14,12},{16,14},{18,16},{20... | collective-permute-start | bytes 396296 | tf_op jit(solution)/shard_map/ppermute | solution.py:24
  9.0 2.2 %collective-permute-start.2 = (f32[129,1,8,128]{3,2,1,0:T(8,128)S(1)}, f32[129,1,8,128]{3,2,1,0:T(8,128)}, u32[]{:S(2)}, u32[]{:S(2)}) collective-permute-start(f32[129,1,8,128]{3,2,1,0:T(8,128)S(1)} %copy.43), channel_id=1, source_target_pairs={{32,0},{64,32},{96,64},{128,96},{160,128},{192,160},{224,192},{0,2... | collective-permute-start | bytes 1585160 | tf_op jit(solution)/shard_map/ppermute | solution.py:24
  11.6 0.6 gather_fusion
  13.0 5.6 %collective-permute-done = f32[129,2,1,128]{3,0,2,1:T(8,128)S(1)} collective-permute-done((f32[129,2,1,128]{3,0,2,1:T(8,128)S(1)}, f32[129,2,1,128]{3,0,2,1:T(8,128)S(1)}, u32[]{:S(2)}, u32[]{:S(2)}) %collective-permute-start) | collective-permute-done | bytes 132128 | tf_op jit(solution)/shard_map/ppermute | solution.py:21
  18.7 1.3 copy_select_fusion
  19.9 1.4 %collective-permute-done.1 = f32[129,1,8,128]{3,2,1,0:T(8,128)} collective-permute-done((f32[129,1,8,128]{3,2,1,0:T(8,128)S(1)}, f32[129,1,8,128]{3,2,1,0:T(8,128)}, u32[]{:S(2)}, u32[]{:S(2)}) %collective-permute-start.1) | collective-permute-done | bytes 528416 | tf_op jit(solution)/shard_map/ppermute | solution.py:21
  21.3 1.2 copy_select_fusion.1
  22.8 1.4 %copy-done.1 = f32[129,4,10,128]{3,0,2,1:T(8,128)} copy-done((f32[129,4,10,128]{3,0,2,1:T(8,128)}, f32[129,4,10,128]{3,0,2,1:T(8,128)S(1)}, u32[]{:S(2)}) %copy-start.1) | copy-done | bytes 2641944
  25.6 1.1 collective-permute-start.6
  27.3 0.8 collective-permute-start.4
  28.1 1.0 collective-permute-start.7
  29.1 0.9 collective-permute-done.6
  30.0 4.5 %collective-permute-done.7 = f32[64,2,1,128]{3,0,2,1:T(8,128)S(1)} collective-permute-done((f32[64,2,1,128]{3,0,2,1:T(8,128)S(1)}, f32[64,2,1,128]{3,0,2,1:T(8,128)S(1)}, u32[]{:S(2)}, u32[]{:S(2)}) %collective-permute-start.7) | collective-permute-done | bytes 65568 | tf_op jit(solution)/shard_map/ppermute | solution.py:21
  37.1 1.1 collective-permute-start.10
  38.2 0.6 convolution_bitcast_fusion.2
  39.3 1.6 %collective-permute-start.11 = (f32[64,2,1,128]{3,0,2,1:T(8,128)S(1)}, f32[64,2,1,128]{3,0,2,1:T(8,128)S(1)}, u32[]{:S(2)}, u32[]{:S(2)}) collective-permute-start(f32[64,2,1,128]{3,0,2,1:T(8,128)S(1)} %get-tuple-element.23), channel_id=1, source_target_pairs={{0,2},{2,4},{4,6},{6,8},{8,10},{10,12},{12,14},{14,16},{16,18},{18... | collective-permute-start | bytes 196616 | tf_op jit(solution)/shard_map/ppermute | solution.py:21
  41.5 4.2 %collective-permute-done.11 = f32[64,2,1,128]{3,0,2,1:T(8,128)S(1)} collective-permute-done((f32[64,2,1,128]{3,0,2,1:T(8,128)S(1)}, f32[64,2,1,128]{3,0,2,1:T(8,128)S(1)}, u32[]{:S(2)}, u32[]{:S(2)}) %collective-permute-start.11) | collective-permute-done | bytes 65568 | tf_op jit(solution)/shard_map/ppermute | solution.py:21
  47.4 0.7 convolution_bitcast_fusion
  48.4 1.3 %collective-permute-done.12 = f32[4,64,64]{2,1,0:T(8,128)S(1)} collective-permute-done((f32[4,64,64]{2,1,0:T(8,128)S(1)}, f32[4,64,64]{2,1,0:T(8,128)S(1)}, u32[]{:S(2)}, u32[]{:S(2)}) %collective-permute-start.12) | collective-permute-done | bytes 65568 | tf_op jit(solution)/shard_map/ppermute | solution.py:46
  49.9 1.5 %collective-permute-start.15 = (f32[4,64,64]{2,1,0:T(8,128)S(1)}, f32[4,64,64]{2,1,0:T(8,128)S(1)}, u32[]{:S(2)}, u32[]{:S(2)}) collective-permute-start(f32[4,64,64]{2,1,0:T(8,128)S(1)} %fusion.61), channel_id=1, source_target_pairs={{0,192},{32,224},{64,128},{96,160},{128,64},{160,96},{192,0},{224,... | collective-permute-start | bytes 196616 | tf_op jit(solution)/shard_map/ppermute | solution.py:50
  51.4 2.0 %collective-permute-start.13 = (f32[4,64,64]{2,1,0:T(8,128)S(1)}, f32[4,64,64]{2,1,0:T(8,128)S(1)}, u32[]{:S(2)}, u32[]{:S(2)}) collective-permute-start(f32[4,64,64]{2,1,0:T(8,128)S(1)} %fusion.61), channel_id=1, source_target_pairs={{0,64},{32,96},{64,0},{96,32},{128,192},{160,224},{192,128},{224,1... | collective-permute-start | bytes 196616 | tf_op jit(solution)/shard_map/ppermute | solution.py:50
  53.4 4.4 %collective-permute-done.14 = f32[4,64,64]{2,1,0:T(8,128)S(1)} collective-permute-done((f32[4,64,64]{2,1,0:T(8,128)S(1)}, f32[4,64,64]{2,1,0:T(8,128)S(1)}, u32[]{:S(2)}, u32[]{:S(2)}) %collective-permute-start.14) | collective-permute-done | bytes 65568 | tf_op jit(solution)/shard_map/ppermute | solution.py:50
  57.8 1.7 %collective-permute-done.15 = f32[4,64,64]{2,1,0:T(8,128)S(1)} collective-permute-done((f32[4,64,64]{2,1,0:T(8,128)S(1)}, f32[4,64,64]{2,1,0:T(8,128)S(1)}, u32[]{:S(2)}, u32[]{:S(2)}) %collective-permute-start.15) | collective-permute-done | bytes 65568 | tf_op jit(solution)/shard_map/ppermute | solution.py:50
  59.5 0.7 add_add_fusion.2
  60.2 1.1 collective-permute-start.17
  61.4 3.0 %collective-permute-start.18 = (f32[4,64,64]{2,1,0:T(8,128)}, f32[4,64,64]{2,1,0:T(8,128)}, u32[]{:S(2)}, u32[]{:S(2)}) collective-permute-start(f32[4,64,64]{2,1,0:T(8,128)} %add_add_fusion.2), channel_id=1, source_target_pairs={{0,6},{2,4},{4,2},{6,0},{8,14},{10,12},{12,10},{14,8},{16,22},{18,... | collective-permute-start | bytes 196616 | tf_op jit(solution)/shard_map/ppermute | solution.py:50
  64.3 9.1 %collective-permute-done.17 = f32[4,64,64]{2,1,0:T(8,128)} collective-permute-done((f32[4,64,64]{2,1,0:T(8,128)}, f32[4,64,64]{2,1,0:T(8,128)}, u32[]{:S(2)}, u32[]{:S(2)}) %collective-permute-start.17) | collective-permute-done | bytes 65568 | tf_op jit(solution)/shard_map/ppermute | solution.py:50
  73.7 1.1 add_add_fusion.1
  74.8 0.9 collective-permute-start.20
  75.8 6.5 %collective-permute-start.19 = (f32[4,64,64]{2,1,0:T(8,128)S(1)}, f32[4,64,64]{2,1,0:T(8,128)S(1)}, u32[]{:S(2)}, u32[]{:S(2)}) collective-permute-start(f32[4,64,64]{2,1,0:T(8,128)S(1)} %add_add_fusion.1), channel_id=1, source_target_pairs={{0,8},{2,10},{4,12},{6,14},{8,0},{10,2},{12,4},{14,6},{16,24},{18,... | collective-permute-start | bytes 196616 | tf_op jit(solution)/shard_map/ppermute | solution.py:50
  82.3 4.1 %select_maximum_fusion = f32[64,4,10,130]{3,0,2,1:T(8,128)} fusion(f32[129,4,1,128]{3,0,2,1:T(8,128)S(1)} %pad.41, f32[129,4,1,128]{3,0,2,1:T(8,128)} %copy-done.2, f32[129,1,8,128]{3,0,2,1:T(8,128)S(1)} %copy_select_fusion, f32[129,1,8,128]{3,0,2,1:T(8,128)S(1)} %copy_select_fusion.1, f32[64,2,8,128]{3,0,2,1:T(8,128)S(1)} %copy.40, ...), kind=kLoop, calls=%fused_computation.12 | loop fusion | flops 5324800 | bytes 3973120 | tf_op jit(solution)/shard_map/slice | solution.py:213
  86.3 0.7 collective-permute-done.21
  87.0 5.1 %collective-permute-done.19 = f32[4,64,64]{2,1,0:T(8,128)S(1)} collective-permute-done((f32[4,64,64]{2,1,0:T(8,128)S(1)}, f32[4,64,64]{2,1,0:T(8,128)S(1)}, u32[]{:S(2)}, u32[]{:S(2)}) %collective-permute-start.19) | collective-permute-done | bytes 65568 | tf_op jit(solution)/shard_map/ppermute | solution.py:50
  92.2 0.7 add_add_fusion.grams_ref
  92.8 16.9 %shard_map.68 = f32[3,64,64]{2,1,0:T(8,128)} custom-call(f32[4,64,64]{2,1,0:T(8,128)} %add_add_fusion.grams_ref), custom_call_target="tpu_custom_call" | custom-call | tf_op jit(solution)/shard_map/pallas_call | solution.py:184
  109.8 2.5 %fusion.48 = f32[64,4,10,128]{3,0,2,1:T(8,128)S(1)} fusion(f32[3,64,64]{2,1,0:T(8,128)} %shard_map.68, f32[64,4,1,128]{3,0,2,1:T(8,128)} %copy-done.13, f32[64,1,8,128]{3,0,2,1:T(8,128)} %copy-done.4, f32[64,2,8,128]{3,0,2,1:T(8,128)S(1)} %fusion.36, f32[64,1,8,128]{3,0,2,1:T(8,128)} %copy-done.6, f32[64,4,1,128]{3,0,2,1:T(8,128)} %copy-done.15), kind=kOutput, calls=%fused_computation.156 | convolution fusion | flops 252968960 | bytes 2654208 | tf_op jit(solution)/shard_map/axyz,ab->bxyz/dot_general | solution.py:84
  112.4 1.4 %fusion.1 = f32[64,4,10,128]{3,0,2,1:T(8,128)S(1)} fusion(f32[64,4,10,128]{3,0,2,1:T(8,128)S(1)} %fusion.48, f32[3,64,64]{2,1,0:T(8,128)S(1)} %copy-done.23, f32[64,4,1,128]{3,0,2,1:T(8,128)S(1)} %copy-done.18, f32[64,1,8,128]{3,0,2,1:T(8,128)S(1)} %copy-done.10, f32[64,2,8,128]{3,0,2,1:T(8,128)S(1)} %fusion.33, f32[64,1,8,128]{3,0,2,1:T(8,128)S(1)} %copy-done.12, ...), kind=kOutput, calls=%fused_computation.20 | convolution fusion | flops 254935040 | bytes 5275648 | tf_op jit(solution)/shard_map/axyz,ab->bxyz/dot_general | solution.py:84
  113.8 1.3 fusion.49
  115.1 2.9 %fusion.2 = f32[64,4,10,128]{3,0,2,1:T(8,128)S(1)} fusion(f32[64,4,10,128]{3,0,2,1:T(8,128)S(1)} %fusion.49, f32[3,64,64]{2,1,0:T(8,128)S(1)} %copy-done.23, f32[129,4,10,128]{3,0,2,1:T(8,128)} %copy-done.1, f32[64,4,1,128]{3,0,2,1:T(8,128)S(1)} %copy-done.14, f32[64,1,8,128]{3,0,2,1:T(8,128)S(1)} %copy-done.5, f32[64,2,8,128]{3,0,2,1:T(8,128)S(1)} %fusion.36, ...), kind=kOutput, calls=%fused_computation.22 | convolution fusion | flops 253624320 | bytes 5275648 | tf_op jit(solution)/shard_map/axyz,ab->bxyz/dot_general | solution.py:84
  118.4 0.7 copy-done
  119.1 1.1 copy-done.8
  120.3 0.6 fusion.11
  121.1 0.9 collective-permute-start.22
  121.9 1.1 slice.408
  123.0 1.1 copy.54
  124.1 2.1 %collective-permute-done.22 = f32[2,8,64]{2,1,0:T(8,128)S(1)} collective-permute-done((f32[2,8,64]{2,1,0:T(8,128)S(1)}, f32[2,8,64]{2,1,0:T(8,128)S(1)}, u32[]{:S(2)}, u32[]{:S(2)}) %collective-permute-start.22) | collective-permute-done | bytes 4128 | tf_op jit(solution)/shard_map/ppermute | solution.py:257
  126.2 0.7 dynamic-slice_add_fusion
  (139 shorter events, 10.2 us)
Async XLA Ops:
  0.6 1.3 %copy-start.22 = (f32[64,2,8,128]{3,2,1,0:T(8,128)S(1)}, f32[64,2,8,128]{3,2,1,0:T(8,128)}, u32[]{:S(2)}) copy-start(f32[64,2,8,128]{3,2,1,0:T(8,128)} %param.8) | copy-start | bytes 1572868
  0.6 1.5 %copy-start.21 = (f32[2,8,128]{2,1,0:T(8,128)S(1)}, f32[2,8,128]{2,1,0:T(8,128)}, u32[]{:S(2)}) copy-start(f32[2,8,128]{2,1,0:T(8,128)} %param.5) | copy-start | bytes 24580
  2.2 10.8 %collective-permute-start.3 = (f32[129,2,1,128]{3,0,2,1:T(8,128)S(1)}, f32[129,2,1,128]{3,0,2,1:T(8,128)S(1)}, u32[]{:S(2)}, u32[]{:S(2)}) collective-permute-start(f32[129,2,1,128]{3,0,2,1:T(8,128)S(1)} %get-tuple-element.22), channel_id=1, source_target_pairs={{2,0},{4,2},{6,4},{8,6},{10,8},{12,10},{14,12},{16,14},{18,16},{20... | collective-permute-start | bytes 396296 | tf_op jit(solution)/shard_map/ppermute | solution.py:24
  8.9 2.6 %copy-start.25 = (s32[64]{0:T(128)S(1)}, s32[64]{0:T(128)}, u32[]{:S(2)}) copy-start(s32[64]{0:T(128)} %param.7) | copy-start | bytes 772
  8.9 2.6 %copy-start.24 = (s32[128,2]{0,1:T(2,128)S(1)}, s32[128,2]{0,1:T(2,128)}, u32[]{:S(2)}) copy-start(s32[128,2]{0,1:T(2,128)} %param.6) | copy-start | bytes 3076
  9.0 9.6 %collective-permute-start.2 = (f32[129,1,8,128]{3,2,1,0:T(8,128)S(1)}, f32[129,1,8,128]{3,2,1,0:T(8,128)}, u32[]{:S(2)}, u32[]{:S(2)}) collective-permute-start(f32[129,1,8,128]{3,2,1,0:T(8,128)S(1)} %copy.43), channel_id=1, source_target_pairs={{32,0},{64,32},{96,64},{128,96},{160,128},{192,160},{224,192},{0,2... | collective-permute-start | bytes 1585160 | tf_op jit(solution)/shard_map/ppermute | solution.py:24
  11.3 10.0 %collective-permute-start.1 = (f32[129,1,8,128]{3,2,1,0:T(8,128)S(1)}, f32[129,1,8,128]{3,2,1,0:T(8,128)}, u32[]{:S(2)}, u32[]{:S(2)}) collective-permute-start(f32[129,1,8,128]{3,2,1,0:T(8,128)S(1)} %copy.41), channel_id=1, source_target_pairs={{0,32},{32,64},{64,96},{96,128},{128,160},{160,192},{192,224},{224... | collective-permute-start | bytes 1585160 | tf_op jit(solution)/shard_map/ppermute | solution.py:21
  11.4 7.2 %collective-permute-start = (f32[129,2,1,128]{3,0,2,1:T(8,128)S(1)}, f32[129,2,1,128]{3,0,2,1:T(8,128)S(1)}, u32[]{:S(2)}, u32[]{:S(2)}) collective-permute-start(f32[129,2,1,128]{3,0,2,1:T(8,128)S(1)} %get-tuple-element.21), channel_id=1, source_target_pairs={{0,2},{2,4},{4,6},{6,8},{8,10},{10,12},{12,14},{14,16},{16,18},{18... | collective-permute-start | bytes 396296 | tf_op jit(solution)/shard_map/ppermute | solution.py:21
  18.6 5.8 %copy-start.2 = (f32[129,4,1,128]{3,0,2,1:T(8,128)}, f32[129,4,1,128]{3,0,2,1:T(8,128)S(1)}, u32[]{:S(2)}) copy-start(f32[129,4,1,128]{3,0,2,1:T(8,128)S(1)} %pad.40) | copy-start | bytes 792580
  22.7 1.5 %copy-start.1 = (f32[129,4,10,128]{3,0,2,1:T(8,128)}, f32[129,4,10,128]{3,0,2,1:T(8,128)S(1)}, u32[]{:S(2)}) copy-start(f32[129,4,10,128]{3,0,2,1:T(8,128)S(1)} %pad_maximum_fusion) | copy-start | bytes 7925764
  25.6 4.3 %collective-permute-start.6 = (f32[64,2,1,128]{3,0,2,1:T(8,128)S(1)}, f32[64,2,1,128]{3,0,2,1:T(8,128)S(1)}, u32[]{:S(2)}, u32[]{:S(2)}) collective-permute-start(f32[64,2,1,128]{3,0,2,1:T(8,128)S(1)} %get-tuple-element.28), channel_id=1, source_target_pairs={{2,0},{4,2},{6,4},{8,6},{10,8},{12,10},{14,12},{16,14},{18,16},{20... | collective-permute-start | bytes 196616 | tf_op jit(solution)/shard_map/ppermute | solution.py:24
  27.3 7.2 %collective-permute-start.4 = (f32[64,1,8,128]{3,0,2,1:T(8,128)S(1)}, f32[64,1,8,128]{3,0,2,1:T(8,128)S(1)}, u32[]{:S(2)}, u32[]{:S(2)}) collective-permute-start(f32[64,1,8,128]{3,0,2,1:T(8,128)S(1)} %get-tuple-element.30), channel_id=1, source_target_pairs={{32,0},{64,32},{96,64},{128,96},{160,128},{192,160},{224,192},{0,2... | collective-permute-start | bytes 786440 | tf_op jit(solution)/shard_map/ppermute | solution.py:24
  28.1 7.0 %collective-permute-start.5 = (f32[64,1,8,128]{3,0,2,1:T(8,128)S(1)}, f32[64,1,8,128]{3,0,2,1:T(8,128)S(1)}, u32[]{:S(2)}, u32[]{:S(2)}) collective-permute-start(f32[64,1,8,128]{3,0,2,1:T(8,128)S(1)} %get-tuple-element.29), channel_id=1, source_target_pairs={{0,32},{32,64},{64,96},{96,128},{128,160},{160,192},{192,224},{224... | collective-permute-start | bytes 786440 | tf_op jit(solution)/shard_map/ppermute | solution.py:21
  28.1 6.4 %collective-permute-start.7 = (f32[64,2,1,128]{3,0,2,1:T(8,128)S(1)}, f32[64,2,1,128]{3,0,2,1:T(8,128)S(1)}, u32[]{:S(2)}, u32[]{:S(2)}) collective-permute-start(f32[64,2,1,128]{3,0,2,1:T(8,128)S(1)} %get-tuple-element.27), channel_id=1, source_target_pairs={{0,2},{2,4},{4,6},{6,8},{8,10},{10,12},{12,14},{14,16},{16,18},{18... | collective-permute-start | bytes 196616 | tf_op jit(solution)/shard_map/ppermute | solution.py:21
  34.5 0.8 copy-start.13
  34.5 0.8 copy-start.15
  34.5 0.8 copy-start.4
  35.1 0.7 copy-start.6
  37.1 4.3 %collective-permute-start.10 = (f32[64,2,1,128]{3,0,2,1:T(8,128)S(1)}, f32[64,2,1,128]{3,0,2,1:T(8,128)S(1)}, u32[]{:S(2)}, u32[]{:S(2)}) collective-permute-start(f32[64,2,1,128]{3,0,2,1:T(8,128)S(1)} %get-tuple-element.24), channel_id=1, source_target_pairs={{2,0},{4,2},{6,4},{8,6},{10,8},{12,10},{14,12},{16,14},{18,16},{20... | collective-permute-start | bytes 196616 | tf_op jit(solution)/shard_map/ppermute | solution.py:24
  38.8 7.0 %collective-permute-start.8 = (f32[64,1,8,128]{3,0,2,1:T(8,128)S(1)}, f32[64,1,8,128]{3,0,2,1:T(8,128)S(1)}, u32[]{:S(2)}, u32[]{:S(2)}) collective-permute-start(f32[64,1,8,128]{3,0,2,1:T(8,128)S(1)} %get-tuple-element.26), channel_id=1, source_target_pairs={{32,0},{64,32},{96,64},{128,96},{160,128},{192,160},{224,192},{0,2... | collective-permute-start | bytes 786440 | tf_op jit(solution)/shard_map/ppermute | solution.py:24
  39.2 7.0 %collective-permute-start.9 = (f32[64,1,8,128]{3,0,2,1:T(8,128)S(1)}, f32[64,1,8,128]{3,0,2,1:T(8,128)S(1)}, u32[]{:S(2)}, u32[]{:S(2)}) collective-permute-start(f32[64,1,8,128]{3,0,2,1:T(8,128)S(1)} %get-tuple-element.25), channel_id=1, source_target_pairs={{0,32},{32,64},{64,96},{96,128},{128,160},{160,192},{192,224},{224... | collective-permute-start | bytes 786440 | tf_op jit(solution)/shard_map/ppermute | solution.py:21
  39.3 6.4 %collective-permute-start.11 = (f32[64,2,1,128]{3,0,2,1:T(8,128)S(1)}, f32[64,2,1,128]{3,0,2,1:T(8,128)S(1)}, u32[]{:S(2)}, u32[]{:S(2)}) collective-permute-start(f32[64,2,1,128]{3,0,2,1:T(8,128)S(1)} %get-tuple-element.23), channel_id=1, source_target_pairs={{0,2},{2,4},{4,6},{6,8},{8,10},{10,12},{12,14},{14,16},{16,18},{18... | collective-permute-start | bytes 196616 | tf_op jit(solution)/shard_map/ppermute | solution.py:21
  45.8 0.7 copy-start.19
  45.8 0.7 copy-start.9
  46.2 0.7 copy-start.11
  48.1 1.6 %collective-permute-start.12 = (f32[4,64,64]{2,1,0:T(8,128)S(1)}, f32[4,64,64]{2,1,0:T(8,128)S(1)}, u32[]{:S(2)}, u32[]{:S(2)}) collective-permute-start(f32[4,64,64]{2,1,0:T(8,128)S(1)} %pad_maximum_fusion.34), channel_id=1, source_target_pairs={{0,32},{32,0},{64,96},{96,64},{128,160},{160,128},{192,224},{224,1... | collective-permute-start | bytes 196616 | tf_op jit(solution)/shard_map/ppermute | solution.py:46
  49.8 8.0 %collective-permute-start.14 = (f32[4,64,64]{2,1,0:T(8,128)S(1)}, f32[4,64,64]{2,1,0:T(8,128)S(1)}, u32[]{:S(2)}, u32[]{:S(2)}) collective-permute-start(f32[4,64,64]{2,1,0:T(8,128)S(1)} %fusion.61), channel_id=1, source_target_pairs={{0,128},{32,160},{64,192},{96,224},{128,0},{160,32},{192,64},{224,... | collective-permute-start | bytes 196616 | tf_op jit(solution)/shard_map/ppermute | solution.py:50
  49.9 9.7 %collective-permute-start.15 = (f32[4,64,64]{2,1,0:T(8,128)S(1)}, f32[4,64,64]{2,1,0:T(8,128)S(1)}, u32[]{:S(2)}, u32[]{:S(2)}) collective-permute-start(f32[4,64,64]{2,1,0:T(8,128)S(1)} %fusion.61), channel_id=1, source_target_pairs={{0,192},{32,224},{64,128},{96,160},{128,64},{160,96},{192,0},{224,... | collective-permute-start | bytes 196616 | tf_op jit(solution)/shard_map/ppermute | solution.py:50
  51.4 8.2 %collective-permute-start.13 = (f32[4,64,64]{2,1,0:T(8,128)S(1)}, f32[4,64,64]{2,1,0:T(8,128)S(1)}, u32[]{:S(2)}, u32[]{:S(2)}) collective-permute-start(f32[4,64,64]{2,1,0:T(8,128)S(1)} %fusion.61), channel_id=1, source_target_pairs={{0,64},{32,96},{64,0},{96,32},{128,192},{160,224},{192,128},{224,1... | collective-permute-start | bytes 196616 | tf_op jit(solution)/shard_map/ppermute | solution.py:50
  60.2 13.2 %collective-permute-start.17 = (f32[4,64,64]{2,1,0:T(8,128)}, f32[4,64,64]{2,1,0:T(8,128)}, u32[]{:S(2)}, u32[]{:S(2)}) collective-permute-start(f32[4,64,64]{2,1,0:T(8,128)} %add_add_fusion.2), channel_id=1, source_target_pairs={{0,4},{2,6},{4,0},{6,2},{8,12},{10,14},{12,8},{14,10},{16,20},{18,... | collective-permute-start | bytes 196616 | tf_op jit(solution)/shard_map/ppermute | solution.py:50
  61.4 12.1 %collective-permute-start.18 = (f32[4,64,64]{2,1,0:T(8,128)}, f32[4,64,64]{2,1,0:T(8,128)}, u32[]{:S(2)}, u32[]{:S(2)}) collective-permute-start(f32[4,64,64]{2,1,0:T(8,128)} %add_add_fusion.2), channel_id=1, source_target_pairs={{0,6},{2,4},{4,2},{6,0},{8,14},{10,12},{12,10},{14,8},{16,22},{18,... | collective-permute-start | bytes 196616 | tf_op jit(solution)/shard_map/ppermute | solution.py:50
  64.3 9.3 %collective-permute-start.16 = (f32[4,64,64]{2,1,0:T(8,128)}, f32[4,64,64]{2,1,0:T(8,128)}, u32[]{:S(2)}, u32[]{:S(2)}) collective-permute-start(f32[4,64,64]{2,1,0:T(8,128)} %add_add_fusion.2), channel_id=1, source_target_pairs={{0,2},{2,0},{4,6},{6,4},{8,10},{10,8},{12,14},{14,12},{16,18},{18,... | collective-permute-start | bytes 196616 | tf_op jit(solution)/shard_map/ppermute | solution.py:50
  74.8 11.6 %collective-permute-start.20 = (f32[4,64,64]{2,1,0:T(8,128)S(1)}, f32[4,64,64]{2,1,0:T(8,128)S(1)}, u32[]{:S(2)}, u32[]{:S(2)}) collective-permute-start(f32[4,64,64]{2,1,0:T(8,128)S(1)} %add_add_fusion.1), channel_id=1, source_target_pairs={{0,16},{2,18},{4,20},{6,22},{8,24},{10,26},{12,28},{14,30},{16,0},... | collective-permute-start | bytes 196616 | tf_op jit(solution)/shard_map/ppermute | solution.py:50
  75.7 11.3 %collective-permute-start.21 = (f32[4,64,64]{2,1,0:T(8,128)S(1)}, f32[4,64,64]{2,1,0:T(8,128)S(1)}, u32[]{:S(2)}, u32[]{:S(2)}) collective-permute-start(f32[4,64,64]{2,1,0:T(8,128)S(1)} %add_add_fusion.1), channel_id=1, source_target_pairs={{0,24},{2,26},{4,28},{6,30},{8,16},{10,18},{12,20},{14,22},{16,8},... | collective-permute-start | bytes 196616 | tf_op jit(solution)/shard_map/ppermute | solution.py:50
  75.8 16.4 %collective-permute-start.19 = (f32[4,64,64]{2,1,0:T(8,128)S(1)}, f32[4,64,64]{2,1,0:T(8,128)S(1)}, u32[]{:S(2)}, u32[]{:S(2)}) collective-permute-start(f32[4,64,64]{2,1,0:T(8,128)S(1)} %add_add_fusion.1), channel_id=1, source_target_pairs={{0,8},{2,10},{4,12},{6,14},{8,0},{10,2},{12,4},{14,6},{16,24},{18,... | collective-permute-start | bytes 196616 | tf_op jit(solution)/shard_map/ppermute | solution.py:50
  109.8 2.6 %copy-start.5 = (f32[64,1,8,128]{3,0,2,1:T(8,128)S(1)}, f32[64,1,8,128]{3,0,2,1:T(8,128)}, u32[]{:S(2)}) copy-start(f32[64,1,8,128]{3,0,2,1:T(8,128)} %copy-done.4) | copy-start | bytes 786436
  109.8 2.6 %copy-start.7 = (f32[64,1,8,128]{3,0,2,1:T(8,128)S(1)}, f32[64,1,8,128]{3,0,2,1:T(8,128)}, u32[]{:S(2)}) copy-start(f32[64,1,8,128]{3,0,2,1:T(8,128)} %copy-done.6) | copy-start | bytes 786436
  109.8 2.6 %copy-start.10 = (f32[64,1,8,128]{3,0,2,1:T(8,128)S(1)}, f32[64,1,8,128]{3,0,2,1:T(8,128)}, u32[]{:S(2)}) copy-start(f32[64,1,8,128]{3,0,2,1:T(8,128)} %copy-done.9) | copy-start | bytes 786436
  109.8 2.6 %copy-start.12 = (f32[64,1,8,128]{3,0,2,1:T(8,128)S(1)}, f32[64,1,8,128]{3,0,2,1:T(8,128)}, u32[]{:S(2)}) copy-start(f32[64,1,8,128]{3,0,2,1:T(8,128)} %copy-done.11) | copy-start | bytes 786436
  109.8 2.6 %copy-start.14 = (f32[64,4,1,128]{3,0,2,1:T(8,128)S(1)}, f32[64,4,1,128]{3,0,2,1:T(8,128)}, u32[]{:S(2)}) copy-start(f32[64,4,1,128]{3,0,2,1:T(8,128)} %copy-done.13) | copy-start | bytes 393220
  109.8 2.6 %copy-start.16 = (f32[64,4,1,128]{3,0,2,1:T(8,128)S(1)}, f32[64,4,1,128]{3,0,2,1:T(8,128)}, u32[]{:S(2)}) copy-start(f32[64,4,1,128]{3,0,2,1:T(8,128)} %copy-done.15) | copy-start | bytes 393220
  109.8 2.6 %copy-start.18 = (f32[64,4,1,128]{3,0,2,1:T(8,128)S(1)}, f32[64,4,1,128]{3,0,2,1:T(8,128)}, u32[]{:S(2)}) copy-start(f32[64,4,1,128]{3,0,2,1:T(8,128)} %copy-done.17) | copy-start | bytes 393220
  109.8 2.6 %copy-start.20 = (f32[64,4,1,128]{3,0,2,1:T(8,128)S(1)}, f32[64,4,1,128]{3,0,2,1:T(8,128)}, u32[]{:S(2)}) copy-start(f32[64,4,1,128]{3,0,2,1:T(8,128)} %copy-done.19) | copy-start | bytes 393220
  109.8 2.6 %copy-start.23 = (f32[3,64,64]{2,1,0:T(8,128)S(1)}, f32[3,64,64]{2,1,0:T(8,128)}, u32[]{:S(2)}) copy-start(f32[3,64,64]{2,1,0:T(8,128)} %shard_map.68) | copy-start | bytes 147460
  115.1 3.0 %copy-start.3 = (f32[129,4,1,128]{3,0,2,1:T(8,128)S(1)}, f32[129,4,1,128]{3,0,2,1:T(8,128)}, u32[]{:S(2)}) copy-start(f32[129,4,1,128]{3,0,2,1:T(8,128)} %copy-done.2) | copy-start | bytes 792580
  118.0 1.1 copy-start
  118.2 2.1 %copy-start.8 = (f32[64,4,10,130]{3,0,2,1:T(8,128)S(1)}, f32[64,4,10,130]{3,0,2,1:T(8,128)}, u32[]{:S(2)}) copy-start(f32[64,4,10,130]{3,0,2,1:T(8,128)} %select_maximum_fusion) | copy-start | bytes 3993604
  121.1 5.2 %collective-permute-start.22 = (f32[2,8,64]{2,1,0:T(8,128)S(1)}, f32[2,8,64]{2,1,0:T(8,128)S(1)}, u32[]{:S(2)}, u32[]{:S(2)}) collective-permute-start(f32[2,8,64]{2,1,0:T(8,128)S(1)} %constant_dynamic-slice_fusion), channel_id=1, source_target_pairs={{0,1},{1,0},{2,3},{3,2},{4,5},{5,4},{6,7},{7,6},{8,9},{9,8},{10,11... | collective-permute-start | bytes 12296 | tf_op jit(solution)/shard_map/ppermute | solution.py:257
  (1 other events, 0.7 us)

commit v7 on v6

--- a/solution.py
+++ b/solution.py
@@ -18,12 +18,12 @@
         place = lax.axis_index(axis)
         forward = [(i, (i + 1) % count) for i in range(count)]
         backward = [(target, source) for source, target in forward]
-        low = lax.ppermute(
-            lax.slice_in_dim(block, block.shape[dim] - width, None, axis=dim), axis, forward
-        )
-        high = lax.ppermute(lax.slice_in_dim(block, 0, width, axis=dim), axis, backward)
-        low = jnp.where(place == 0, jnp.zeros_like(low), low)
-        high = jnp.where(place == count - 1, jnp.zeros_like(high), high)
+        top = lax.slice_in_dim(block, block.shape[dim] - width, None, axis=dim)
+        bottom = lax.slice_in_dim(block, 0, width, axis=dim)
+        top = jnp.where(place == count - 1, jnp.zeros_like(top), top)
+        bottom = jnp.where(place == 0, jnp.zeros_like(bottom), bottom)
+        low = lax.ppermute(top, axis, forward)
+        high = lax.ppermute(bottom, axis, backward)
         pieces[axis] = (low, high)
     low_x, high_x = pieces[axis_x]
     low_y, high_y = pieces[axis_y]
@@ -174,14 +174,13 @@
         + _mm(step0_t, _mm(g_qw, step0))
     )
     (step1,) = _solve([(curv, new_gram)], 4)
-    out_ref[0] = step0
-    out_ref[1] = turn
-    out_ref[2] = step1
+    out_ref[0] = step0 + _mm(keep, step1)
+    out_ref[1] = -_mm(step0, step1)
 
 
 def steps(grams):
     n = grams.shape[1]
-    return pl.pallas_call(steps_kernel, out_shape=jax.ShapeDtypeStruct((3, n, n), jnp.float32))(grams)
+    return pl.pallas_call(steps_kernel, out_shape=jax.ShapeDtypeStruct((2, n, n), jnp.float32))(grams)
 
 
 def on_device(conductivity, electrodes, pair_order, initial_fields, adjoint_fields):
@@ -229,11 +228,7 @@
     )
 
     solved = steps(grams)
-    step0, turn, step1 = solved[0], solved[1], solved[2]
-    res1_pad = res_pad - combine_cols(image_pad, step0)
-    dir1_pad = res1_pad + combine_cols(res_pad, turn)
-    it1_pad = iter_pad + combine_cols(res_pad, step0)
-    it2_pad = it1_pad + combine_cols(dir1_pad, step1)
+    it2_pad = iter_pad + combine_cols(res_pad, solved[0]) + combine_cols(image_pad, solved[1])
     iterate = it2_pad[:, 1:-1, 1:-1]
     term_x, term_y, term_z = face_terms(it2_pad, adjoint_pad)
     local_grad = (

time: 127 us -> 121 us (0.953)
  waiting for transfers between devices: 42.8 us -> 39.5 us
  matrix products: 10.5 us -> 7.8 us
  other arithmetic: 14.7 us -> 12.9 us
  local copies, waits for them, and re-layouts: 9.28 us -> 10.6 us
    ppermute x12, waiting for transfers between devices: 18 us -> 14.7 us  [the longest x6 13 us: padded_2(): low = lax.ppermute(top, axis, forward)]
    dot_general x4 -> x2, matrix products: 8.07 us -> 5.4 us  [combine_cols(): jnp.einsum('axyz,ab->bxyz', field, matrix, precision=lax.Precision.HIGHEST)]
    select_n x12 -> x6, other arithmetic: 2.57 us -> 0.92 us  [padded_2(): top = jnp.where(place == count - 1, jnp.zeros_like(top), top)]
    unnamed x56 -> x48, local copies, waits for them, and re-layouts: 6.89 us -> 6.36 us
  transfers between devices with their start and end apart: 23 -> 23, of which waited for: 16 -> 14; matrix products, arithmetic and copies ran while one was open for 8% -> 10% of each run, Pallas kernels for 0% -> 0%
where the time goes in v7:
time: 121 us
  waiting for transfers between devices  39.5 us (33%)
  starting transfers between devices  31.3 us (26%)
  Pallas kernels  17.1 us (14%)
  other arithmetic  12.9 us (11%)
  local copies, waits for them, and re-layouts  10.6 us (9%)
  matrix products  7.8 us (6%)
  between operations  1.38 us (1%)
    ppermute x9, waiting for transfers between devices, allsum(): lax.ppermute(value, axis, [(i, i ^ d << shift) for i in range(count)])  21.3 us
    pallas_call x1, Pallas kernels, steps(): pl.pallas_call(steps_kernel, out_shape=jax.ShapeDtypeStruct((2, n, n), jn...  17.1 us
    ppermute x9, starting transfers between devices, allsum(): lax.ppermute(value, axis, [(i, i ^ d << shift) for i in range(count)])  15.3 us
    ppermute x6, waiting for transfers between devices, padded_2(): low = lax.ppermute(top, axis, forward)  13 us
    ppermute x6, starting transfers between devices, padded_2(): high = lax.ppermute(bottom, axis, backward)  11.7 us
    unnamed x48, local copies, waits for them, and re-layouts  6.36 us
    dot_general x2, matrix products, combine_cols(): jnp.einsum('axyz,ab->bxyz', field, matrix, precision=lax.Precision.HIGHEST)  5.4 us
    slice x1, other arithmetic, on_device(): adjoint_pad = padded[1 + columns:]  4.08 us
  transfers between devices with their start and end apart: 23, of which 14 were waited for; matrix products, arithmetic and copies ran while one was open for 10% of the time, Pallas kernels for 0%

profile of v7, /device:TPU:4, one launch (start us, length us, event | category | flops | bytes accessed | tf_op | source)
XLA Modules:
  0.0 120.6 jit_solution(14700679826076102370)
XLA Ops:
  0.7 1.3 %copy.40 = f32[64,2,8,128]{3,0,2,1:T(8,128)S(1)} copy(f32[64,2,8,128]{3,2,1,0:T(8,128)} %param.9) | data formatting | bytes 1048576 | tf_op args[4]
  2.1 0.7 maximum_select_fusion.1
  2.9 6.5 %collective-permute-start.3 = (f32[129,2,1,128]{3,0,2,1:T(8,128)}, f32[129,2,1,128]{3,0,2,1:T(8,128)}, u32[]{:S(2)}, u32[]{:S(2)}) collective-permute-start(f32[129,2,1,128]{3,0,2,1:T(8,128)} %get-tuple-element.22), channel_id=1, source_target_pairs={{2,0},{4,2},{6,4},{8,6},{10,8},{12,10},{14,12},{16,14},{18,16},{20... | collective-permute-start | bytes 396296 | tf_op jit(solution)/shard_map/ppermute | solution.py:26
  9.7 2.2 %collective-permute-start.2 = (f32[129,1,8,128]{3,2,1,0:T(8,128)S(1)}, f32[129,1,8,128]{3,2,1,0:T(8,128)S(1)}, u32[]{:S(2)}, u32[]{:S(2)}) collective-permute-start(f32[129,1,8,128]{3,2,1,0:T(8,128)S(1)} %copy.42), channel_id=1, source_target_pairs={{32,0},{64,32},{96,64},{128,96},{160,128},{192,160},{224,192},{0,2... | collective-permute-start | bytes 1585160 | tf_op jit(solution)/shard_map/ppermute | solution.py:26
  12.3 0.6 gather_fusion
  13.6 0.9 pad.41
  14.5 5.1 %collective-permute-done = f32[129,2,1,128]{3,0,2,1:T(8,128)} collective-permute-done((f32[129,2,1,128]{3,0,2,1:T(8,128)}, f32[129,2,1,128]{3,0,2,1:T(8,128)}, u32[]{:S(2)}, u32[]{:S(2)}) %collective-permute-start) | collective-permute-done | bytes 132128 | tf_op jit(solution)/shard_map/ppermute | solution.py:25
  19.6 0.9 pad.40
  20.6 1.2 %collective-permute-done.1 = f32[129,1,8,128]{3,2,1,0:T(8,128)S(1)} collective-permute-done((f32[129,1,8,128]{3,2,1,0:T(8,128)S(1)}, f32[129,1,8,128]{3,2,1,0:T(8,128)S(1)}, u32[]{:S(2)}, u32[]{:S(2)}) %collective-permute-start.1) | collective-permute-done | bytes 528416 | tf_op jit(solution)/shard_map/ppermute | solution.py:25
  22.3 1.4 %copy-done.1 = f32[129,4,10,128]{3,0,2,1:T(8,128)} copy-done((f32[129,4,10,128]{3,0,2,1:T(8,128)}, f32[129,4,10,128]{3,0,2,1:T(8,128)S(1)}, u32[]{:S(2)}) %copy-start.1) | copy-done | bytes 2641944
  25.1 1.0 collective-permute-start.4
  26.1 0.6 collective-permute-start.6
  26.7 1.5 %collective-permute-start.7 = (f32[64,2,1,128]{3,0,2,1:T(8,128)S(1)}, f32[64,2,1,128]{3,0,2,1:T(8,128)S(1)}, u32[]{:S(2)}, u32[]{:S(2)}) collective-permute-start(f32[64,2,1,128]{3,0,2,1:T(8,128)S(1)} %get-tuple-element.27), channel_id=1, source_target_pairs={{0,2},{2,4},{4,6},{6,8},{8,10},{10,12},{12,14},{14,16},{16,18},{18... | collective-permute-start | bytes 196616 | tf_op jit(solution)/shard_map/ppermute | solution.py:25
  28.8 1.7 %collective-permute-done.6 = f32[64,2,1,128]{3,0,2,1:T(8,128)S(1)} collective-permute-done((f32[64,2,1,128]{3,0,2,1:T(8,128)S(1)}, f32[64,2,1,128]{3,0,2,1:T(8,128)S(1)}, u32[]{:S(2)}, u32[]{:S(2)}) %collective-permute-start.6) | collective-permute-done | bytes 65568 | tf_op jit(solution)/shard_map/ppermute | solution.py:26
  30.5 2.6 %collective-permute-done.7 = f32[64,2,1,128]{3,0,2,1:T(8,128)S(1)} collective-permute-done((f32[64,2,1,128]{3,0,2,1:T(8,128)S(1)}, f32[64,2,1,128]{3,0,2,1:T(8,128)S(1)}, u32[]{:S(2)}, u32[]{:S(2)}) %collective-permute-start.7) | collective-permute-done | bytes 65568 | tf_op jit(solution)/shard_map/ppermute | solution.py:25
  34.5 1.3 %collective-permute-start.8 = (f32[64,1,8,128]{3,0,2,1:T(8,128)S(1)}, f32[64,1,8,128]{3,0,2,1:T(8,128)S(1)}, u32[]{:S(2)}, u32[]{:S(2)}) collective-permute-start(f32[64,1,8,128]{3,0,2,1:T(8,128)S(1)} %get-tuple-element.26), channel_id=1, source_target_pairs={{32,0},{64,32},{96,64},{128,96},{160,128},{192,160},{224,192},{0,2... | collective-permute-start | bytes 786440 | tf_op jit(solution)/shard_map/ppermute | solution.py:26
  35.8 1.7 %collective-permute-start.11 = (f32[64,2,1,128]{3,0,2,1:T(8,128)S(1)}, f32[64,2,1,128]{3,0,2,1:T(8,128)S(1)}, u32[]{:S(2)}, u32[]{:S(2)}) collective-permute-start(f32[64,2,1,128]{3,0,2,1:T(8,128)S(1)} %get-tuple-element.23), channel_id=1, source_target_pairs={{0,2},{2,4},{4,6},{6,8},{8,10},{10,12},{12,14},{14,16},{16,18},{18... | collective-permute-start | bytes 196616 | tf_op jit(solution)/shard_map/ppermute | solution.py:25
  38.1 0.6 convolution_bitcast_fusion.2
  38.7 3.5 %collective-permute-done.11 = f32[64,2,1,128]{3,0,2,1:T(8,128)S(1)} collective-permute-done((f32[64,2,1,128]{3,0,2,1:T(8,128)S(1)}, f32[64,2,1,128]{3,0,2,1:T(8,128)S(1)}, u32[]{:S(2)}, u32[]{:S(2)}) %collective-permute-start.11) | collective-permute-done | bytes 65568 | tf_op jit(solution)/shard_map/ppermute | solution.py:25
  42.3 0.6 collective-permute-done.9
  43.7 0.7 convolution_bitcast_fusion
  44.5 1.3 %collective-permute-done.12 = f32[4,64,64]{2,1,0:T(8,128)S(1)} collective-permute-done((f32[4,64,64]{2,1,0:T(8,128)S(1)}, f32[4,64,64]{2,1,0:T(8,128)S(1)}, u32[]{:S(2)}, u32[]{:S(2)}) %collective-permute-start.12) | collective-permute-done | bytes 65568 | tf_op jit(solution)/shard_map/ppermute | solution.py:46
  46.2 1.6 %collective-permute-start.15 = (f32[4,64,64]{2,1,0:T(8,128)S(1)}, f32[4,64,64]{2,1,0:T(8,128)S(1)}, u32[]{:S(2)}, u32[]{:S(2)}) collective-permute-start(f32[4,64,64]{2,1,0:T(8,128)S(1)} %fusion.59), channel_id=1, source_target_pairs={{0,192},{32,224},{64,128},{96,160},{128,64},{160,96},{192,0},{224,... | collective-permute-start | bytes 196616 | tf_op jit(solution)/shard_map/ppermute | solution.py:50
  47.9 1.8 %collective-permute-start.13 = (f32[4,64,64]{2,1,0:T(8,128)S(1)}, f32[4,64,64]{2,1,0:T(8,128)S(1)}, u32[]{:S(2)}, u32[]{:S(2)}) collective-permute-start(f32[4,64,64]{2,1,0:T(8,128)S(1)} %fusion.59), channel_id=1, source_target_pairs={{0,64},{32,96},{64,0},{96,32},{128,192},{160,224},{192,128},{224,1... | collective-permute-start | bytes 196616 | tf_op jit(solution)/shard_map/ppermute | solution.py:50
  49.6 4.4 %collective-permute-done.14 = f32[4,64,64]{2,1,0:T(8,128)S(1)} collective-permute-done((f32[4,64,64]{2,1,0:T(8,128)S(1)}, f32[4,64,64]{2,1,0:T(8,128)S(1)}, u32[]{:S(2)}, u32[]{:S(2)}) %collective-permute-start.14) | collective-permute-done | bytes 65568 | tf_op jit(solution)/shard_map/ppermute | solution.py:50
  54.0 1.7 %collective-permute-done.15 = f32[4,64,64]{2,1,0:T(8,128)S(1)} collective-permute-done((f32[4,64,64]{2,1,0:T(8,128)S(1)}, f32[4,64,64]{2,1,0:T(8,128)S(1)}, u32[]{:S(2)}, u32[]{:S(2)}) %collective-permute-start.15) | collective-permute-done | bytes 65568 | tf_op jit(solution)/shard_map/ppermute | solution.py:50
  55.8 0.7 add_add_fusion.2
  56.5 0.7 collective-permute-start.17
  57.2 3.4 %collective-permute-start.18 = (f32[4,64,64]{2,1,0:T(8,128)}, f32[4,64,64]{2,1,0:T(8,128)}, u32[]{:S(2)}, u32[]{:S(2)}) collective-permute-start(f32[4,64,64]{2,1,0:T(8,128)} %add_add_fusion.2), channel_id=1, source_target_pairs={{0,6},{2,4},{4,2},{6,0},{8,14},{10,12},{12,10},{14,8},{16,22},{18,... | collective-permute-start | bytes 196616 | tf_op jit(solution)/shard_map/ppermute | solution.py:50
  60.6 9.2 %collective-permute-done.17 = f32[4,64,64]{2,1,0:T(8,128)} collective-permute-done((f32[4,64,64]{2,1,0:T(8,128)}, f32[4,64,64]{2,1,0:T(8,128)}, u32[]{:S(2)}, u32[]{:S(2)}) %collective-permute-start.17) | collective-permute-done | bytes 65568 | tf_op jit(solution)/shard_map/ppermute | solution.py:50
  69.9 1.1 add_add_fusion.1
  71.0 0.9 collective-permute-start.20
  72.0 6.6 %collective-permute-start.19 = (f32[4,64,64]{2,1,0:T(8,128)S(1)}, f32[4,64,64]{2,1,0:T(8,128)S(1)}, u32[]{:S(2)}, u32[]{:S(2)}) collective-permute-start(f32[4,64,64]{2,1,0:T(8,128)S(1)} %add_add_fusion.1), channel_id=1, source_target_pairs={{0,8},{2,10},{4,12},{6,14},{8,0},{10,2},{12,4},{14,6},{16,24},{18,... | collective-permute-start | bytes 196616 | tf_op jit(solution)/shard_map/ppermute | solution.py:50
  78.5 4.1 %select_maximum_fusion = f32[64,4,10,130]{3,0,2,1:T(8,128)} fusion(f32[129,4,1,128]{3,0,2,1:T(8,128)S(1)} %pad.41, f32[129,4,1,128]{3,0,2,1:T(8,128)} %copy-done.2, f32[129,1,8,128]{3,0,2,1:T(8,128)S(1)} %copy.44, f32[129,1,8,128]{3,0,2,1:T(8,128)S(1)} %copy.43, f32[64,2,8,128]{3,0,2,1:T(8,128)S(1)} %copy.40, f32[64,2,8,128]{3,0,2,1:T(8,128)S(1)} %copy.39, ...), kind=kLoop, calls=%fused_computation.12 | loop fusion | flops 5324800 | bytes 3973120 | tf_op jit(solution)/shard_map/slice | solution.py:212
  82.6 0.7 collective-permute-done.21
  83.3 5.1 %collective-permute-done.19 = f32[4,64,64]{2,1,0:T(8,128)S(1)} collective-permute-done((f32[4,64,64]{2,1,0:T(8,128)S(1)}, f32[4,64,64]{2,1,0:T(8,128)S(1)}, u32[]{:S(2)}, u32[]{:S(2)}) %collective-permute-start.19) | collective-permute-done | bytes 65568 | tf_op jit(solution)/shard_map/ppermute | solution.py:50
  88.4 0.7 add_add_fusion.grams_ref
  89.1 17.1 %shard_map.68 = f32[2,64,64]{2,1,0:T(8,128)} custom-call(f32[4,64,64]{2,1,0:T(8,128)} %add_add_fusion.grams_ref), custom_call_target="tpu_custom_call" | custom-call | tf_op jit(solution)/shard_map/pallas_call | solution.py:183
  106.2 2.5 %fusion.47 = f32[64,4,10,128]{3,0,2,1:T(8,128)S(1)} fusion(f32[2,64,64]{2,1,0:T(8,128)} %shard_map.68, f32[64,4,1,128]{3,0,2,1:T(8,128)} %copy-done.15, f32[64,1,8,128]{3,0,2,1:T(8,128)} %copy-done.9, f32[64,2,8,128]{3,0,2,1:T(8,128)S(1)} %fusion.32, f32[64,1,8,128]{3,0,2,1:T(8,128)} %copy-done.10, f32[64,4,1,128]{3,0,2,1:T(8,128)} %copy-done.16), kind=kOutput, calls=%fused_computation.156 | convolution fusion | flops 252968960 | bytes 2654208 | tf_op jit(solution)/shard_map/axyz,ab->bxyz/dot_general | solution.py:84
  108.8 2.9 %fusion.1 = f32[64,4,10,128]{3,0,2,1:T(8,128)S(1)} fusion(f32[64,4,10,128]{3,0,2,1:T(8,128)S(1)} %fusion.47, f32[2,64,64]{2,1,0:T(8,128)S(1)} %copy-done.19, f32[129,4,10,128]{3,0,2,1:T(8,128)} %copy-done.1, f32[64,4,1,128]{3,0,2,1:T(8,128)S(1)} %copy-done.12, f32[64,1,8,128]{3,0,2,1:T(8,128)S(1)} %copy-done.6, f32[64,2,8,128]{3,0,2,1:T(8,128)S(1)} %fusion.35, ...), kind=kOutput, calls=%fused_computation.20 | convolution fusion | flops 253624320 | bytes 5275648 | tf_op jit(solution)/shard_map/axyz,ab->bxyz/dot_general | solution.py:84
  112.1 0.7 copy-done
  112.8 1.1 copy-done.4
  114.0 0.6 fusion.10
  114.7 0.8 collective-permute-start.22
  115.6 1.1 slice.403
  116.7 1.1 copy.54
  117.8 2.2 %collective-permute-done.22 = f32[2,8,64]{2,1,0:T(8,128)S(1)} collective-permute-done((f32[2,8,64]{2,1,0:T(8,128)S(1)}, f32[2,8,64]{2,1,0:T(8,128)S(1)}, u32[]{:S(2)}, u32[]{:S(2)}) %collective-permute-start.22) | collective-permute-done | bytes 4128 | tf_op jit(solution)/shard_map/ppermute | solution.py:252
  119.9 0.7 dynamic-slice_add_fusion
  (119 shorter events, 7.8 us)
Async XLA Ops:
  0.6 1.3 %copy-start.18 = (f32[64,2,8,128]{3,2,1,0:T(8,128)S(1)}, f32[64,2,8,128]{3,2,1,0:T(8,128)}, u32[]{:S(2)}) copy-start(f32[64,2,8,128]{3,2,1,0:T(8,128)} %param.8) | copy-start | bytes 1572868
  0.6 1.5 %copy-start.17 = (f32[2,8,128]{2,1,0:T(8,128)S(1)}, f32[2,8,128]{2,1,0:T(8,128)}, u32[]{:S(2)}) copy-start(f32[2,8,128]{2,1,0:T(8,128)} %param.5) | copy-start | bytes 24580
  2.9 10.7 %collective-permute-start.3 = (f32[129,2,1,128]{3,0,2,1:T(8,128)}, f32[129,2,1,128]{3,0,2,1:T(8,128)}, u32[]{:S(2)}, u32[]{:S(2)}) collective-permute-start(f32[129,2,1,128]{3,0,2,1:T(8,128)} %get-tuple-element.22), channel_id=1, source_target_pairs={{2,0},{4,2},{6,4},{8,6},{10,8},{12,10},{14,12},{16,14},{18,16},{20... | collective-permute-start | bytes 396296 | tf_op jit(solution)/shard_map/ppermute | solution.py:26
  9.5 2.5 %copy-start.21 = (s32[64]{0:T(128)S(1)}, s32[64]{0:T(128)}, u32[]{:S(2)}) copy-start(s32[64]{0:T(128)} %param.7) | copy-start | bytes 772
  9.6 2.6 %copy-start.20 = (s32[128,2]{0,1:T(2,128)S(1)}, s32[128,2]{0,1:T(2,128)}, u32[]{:S(2)}) copy-start(s32[128,2]{0,1:T(2,128)} %param.6) | copy-start | bytes 3076
  9.7 10.8 %collective-permute-start.2 = (f32[129,1,8,128]{3,2,1,0:T(8,128)S(1)}, f32[129,1,8,128]{3,2,1,0:T(8,128)S(1)}, u32[]{:S(2)}, u32[]{:S(2)}) collective-permute-start(f32[129,1,8,128]{3,2,1,0:T(8,128)S(1)} %copy.42), channel_id=1, source_target_pairs={{32,0},{64,32},{96,64},{128,96},{160,128},{192,160},{224,192},{0,2... | collective-permute-start | bytes 1585160 | tf_op jit(solution)/shard_map/ppermute | solution.py:26
  12.0 9.9 %collective-permute-start.1 = (f32[129,1,8,128]{3,2,1,0:T(8,128)S(1)}, f32[129,1,8,128]{3,2,1,0:T(8,128)S(1)}, u32[]{:S(2)}, u32[]{:S(2)}) collective-permute-start(f32[129,1,8,128]{3,2,1,0:T(8,128)S(1)} %copy.41), channel_id=1, source_target_pairs={{0,32},{32,64},{64,96},{96,128},{128,160},{160,192},{192,224},{224... | collective-permute-start | bytes 1585160 | tf_op jit(solution)/shard_map/ppermute | solution.py:25
  12.0 7.6 %collective-permute-start = (f32[129,2,1,128]{3,0,2,1:T(8,128)}, f32[129,2,1,128]{3,0,2,1:T(8,128)}, u32[]{:S(2)}, u32[]{:S(2)}) collective-permute-start(f32[129,2,1,128]{3,0,2,1:T(8,128)} %get-tuple-element.21), channel_id=1, source_target_pairs={{0,2},{2,4},{4,6},{6,8},{8,10},{10,12},{12,14},{14,16},{16,18},{18... | collective-permute-start | bytes 396296 | tf_op jit(solution)/shard_map/ppermute | solution.py:25
  20.5 3.5 %copy-start.2 = (f32[129,4,1,128]{3,0,2,1:T(8,128)}, f32[129,4,1,128]{3,0,2,1:T(8,128)S(1)}, u32[]{:S(2)}) copy-start(f32[129,4,1,128]{3,0,2,1:T(8,128)S(1)} %pad.40) | copy-start | bytes 792580
  22.2 1.5 %copy-start.1 = (f32[129,4,10,128]{3,0,2,1:T(8,128)}, f32[129,4,10,128]{3,0,2,1:T(8,128)S(1)}, u32[]{:S(2)}) copy-start(f32[129,4,10,128]{3,0,2,1:T(8,128)S(1)} %pad_maximum_fusion) | copy-start | bytes 7925764
  25.1 8.0 %collective-permute-start.4 = (f32[64,1,8,128]{3,0,2,1:T(8,128)S(1)}, f32[64,1,8,128]{3,0,2,1:T(8,128)S(1)}, u32[]{:S(2)}, u32[]{:S(2)}) collective-permute-start(f32[64,1,8,128]{3,0,2,1:T(8,128)S(1)} %get-tuple-element.30), channel_id=1, source_target_pairs={{32,0},{64,32},{96,64},{128,96},{160,128},{192,160},{224,192},{0,2... | collective-permute-start | bytes 786440 | tf_op jit(solution)/shard_map/ppermute | solution.py:26
  26.1 7.1 %collective-permute-start.5 = (f32[64,1,8,128]{3,0,2,1:T(8,128)S(1)}, f32[64,1,8,128]{3,0,2,1:T(8,128)S(1)}, u32[]{:S(2)}, u32[]{:S(2)}) collective-permute-start(f32[64,1,8,128]{3,0,2,1:T(8,128)S(1)} %get-tuple-element.29), channel_id=1, source_target_pairs={{0,32},{32,64},{64,96},{96,128},{128,160},{160,192},{192,224},{224... | collective-permute-start | bytes 786440 | tf_op jit(solution)/shard_map/ppermute | solution.py:25
  26.1 4.3 %collective-permute-start.6 = (f32[64,2,1,128]{3,0,2,1:T(8,128)S(1)}, f32[64,2,1,128]{3,0,2,1:T(8,128)S(1)}, u32[]{:S(2)}, u32[]{:S(2)}) collective-permute-start(f32[64,2,1,128]{3,0,2,1:T(8,128)S(1)} %get-tuple-element.28), channel_id=1, source_target_pairs={{2,0},{4,2},{6,4},{8,6},{10,8},{12,10},{14,12},{16,14},{18,16},{20... | collective-permute-start | bytes 196616 | tf_op jit(solution)/shard_map/ppermute | solution.py:26
  26.7 6.4 %collective-permute-start.7 = (f32[64,2,1,128]{3,0,2,1:T(8,128)S(1)}, f32[64,2,1,128]{3,0,2,1:T(8,128)S(1)}, u32[]{:S(2)}, u32[]{:S(2)}) collective-permute-start(f32[64,2,1,128]{3,0,2,1:T(8,128)S(1)} %get-tuple-element.27), channel_id=1, source_target_pairs={{0,2},{2,4},{4,6},{6,8},{8,10},{10,12},{12,14},{14,16},{16,18},{18... | collective-permute-start | bytes 196616 | tf_op jit(solution)/shard_map/ppermute | solution.py:25
  30.5 3.2 %copy-start.11 = (f32[64,4,1,128]{3,0,2,1:T(8,128)}, f32[64,4,1,128]{3,0,2,1:T(8,128)S(1)}, u32[]{:S(2)}) copy-start(f32[64,4,1,128]{3,0,2,1:T(8,128)S(1)} %pad.44) | copy-start | bytes 393220
  33.1 0.7 copy-start.13
  33.1 0.7 copy-start.5
  33.1 0.8 copy-start.7
  34.4 4.3 %collective-permute-start.10 = (f32[64,2,1,128]{3,0,2,1:T(8,128)S(1)}, f32[64,2,1,128]{3,0,2,1:T(8,128)S(1)}, u32[]{:S(2)}, u32[]{:S(2)}) collective-permute-start(f32[64,2,1,128]{3,0,2,1:T(8,128)S(1)} %get-tuple-element.24), channel_id=1, source_target_pairs={{2,0},{4,2},{6,4},{8,6},{10,8},{12,10},{14,12},{16,14},{18,16},{20... | collective-permute-start | bytes 196616 | tf_op jit(solution)/shard_map/ppermute | solution.py:26
  34.5 7.7 %collective-permute-start.8 = (f32[64,1,8,128]{3,0,2,1:T(8,128)S(1)}, f32[64,1,8,128]{3,0,2,1:T(8,128)S(1)}, u32[]{:S(2)}, u32[]{:S(2)}) collective-permute-start(f32[64,1,8,128]{3,0,2,1:T(8,128)S(1)} %get-tuple-element.26), channel_id=1, source_target_pairs={{32,0},{64,32},{96,64},{128,96},{160,128},{192,160},{224,192},{0,2... | collective-permute-start | bytes 786440 | tf_op jit(solution)/shard_map/ppermute | solution.py:26
  35.8 7.0 %collective-permute-start.9 = (f32[64,1,8,128]{3,0,2,1:T(8,128)S(1)}, f32[64,1,8,128]{3,0,2,1:T(8,128)S(1)}, u32[]{:S(2)}, u32[]{:S(2)}) collective-permute-start(f32[64,1,8,128]{3,0,2,1:T(8,128)S(1)} %get-tuple-element.25), channel_id=1, source_target_pairs={{0,32},{32,64},{64,96},{96,128},{128,160},{160,192},{192,224},{224... | collective-permute-start | bytes 786440 | tf_op jit(solution)/shard_map/ppermute | solution.py:25
  35.8 6.4 %collective-permute-start.11 = (f32[64,2,1,128]{3,0,2,1:T(8,128)S(1)}, f32[64,2,1,128]{3,0,2,1:T(8,128)S(1)}, u32[]{:S(2)}, u32[]{:S(2)}) collective-permute-start(f32[64,2,1,128]{3,0,2,1:T(8,128)S(1)} %get-tuple-element.23), channel_id=1, source_target_pairs={{0,2},{2,4},{4,6},{6,8},{8,10},{10,12},{12,14},{14,16},{16,18},{18... | collective-permute-start | bytes 196616 | tf_op jit(solution)/shard_map/ppermute | solution.py:25
  38.7 4.6 %copy-start.15 = (f32[64,4,1,128]{3,0,2,1:T(8,128)}, f32[64,4,1,128]{3,0,2,1:T(8,128)S(1)}, u32[]{:S(2)}) copy-start(f32[64,4,1,128]{3,0,2,1:T(8,128)S(1)} %pad.47) | copy-start | bytes 393220
  42.2 1.1 copy-start.16
  42.2 1.2 copy-start.9
  42.8 0.7 copy-start.10
  44.4 1.4 %collective-permute-start.12 = (f32[4,64,64]{2,1,0:T(8,128)S(1)}, f32[4,64,64]{2,1,0:T(8,128)S(1)}, u32[]{:S(2)}, u32[]{:S(2)}) collective-permute-start(f32[4,64,64]{2,1,0:T(8,128)S(1)} %pad_maximum_fusion.32), channel_id=1, source_target_pairs={{0,32},{32,0},{64,96},{96,64},{128,160},{160,128},{192,224},{224,1... | collective-permute-start | bytes 196616 | tf_op jit(solution)/shard_map/ppermute | solution.py:46
  45.9 8.2 %collective-permute-start.14 = (f32[4,64,64]{2,1,0:T(8,128)S(1)}, f32[4,64,64]{2,1,0:T(8,128)S(1)}, u32[]{:S(2)}, u32[]{:S(2)}) collective-permute-start(f32[4,64,64]{2,1,0:T(8,128)S(1)} %fusion.59), channel_id=1, source_target_pairs={{0,128},{32,160},{64,192},{96,224},{128,0},{160,32},{192,64},{224,... | collective-permute-start | bytes 196616 | tf_op jit(solution)/shard_map/ppermute | solution.py:50
  46.2 9.6 %collective-permute-start.15 = (f32[4,64,64]{2,1,0:T(8,128)S(1)}, f32[4,64,64]{2,1,0:T(8,128)S(1)}, u32[]{:S(2)}, u32[]{:S(2)}) collective-permute-start(f32[4,64,64]{2,1,0:T(8,128)S(1)} %fusion.59), channel_id=1, source_target_pairs={{0,192},{32,224},{64,128},{96,160},{128,64},{160,96},{192,0},{224,... | collective-permute-start | bytes 196616 | tf_op jit(solution)/shard_map/ppermute | solution.py:50
  47.9 7.9 %collective-permute-start.13 = (f32[4,64,64]{2,1,0:T(8,128)S(1)}, f32[4,64,64]{2,1,0:T(8,128)S(1)}, u32[]{:S(2)}, u32[]{:S(2)}) collective-permute-start(f32[4,64,64]{2,1,0:T(8,128)S(1)} %fusion.59), channel_id=1, source_target_pairs={{0,64},{32,96},{64,0},{96,32},{128,192},{160,224},{192,128},{224,1... | collective-permute-start | bytes 196616 | tf_op jit(solution)/shard_map/ppermute | solution.py:50
  56.5 13.2 %collective-permute-start.17 = (f32[4,64,64]{2,1,0:T(8,128)}, f32[4,64,64]{2,1,0:T(8,128)}, u32[]{:S(2)}, u32[]{:S(2)}) collective-permute-start(f32[4,64,64]{2,1,0:T(8,128)} %add_add_fusion.2), channel_id=1, source_target_pairs={{0,4},{2,6},{4,0},{6,2},{8,12},{10,14},{12,8},{14,10},{16,20},{18,... | collective-permute-start | bytes 196616 | tf_op jit(solution)/shard_map/ppermute | solution.py:50
  57.2 12.5 %collective-permute-start.18 = (f32[4,64,64]{2,1,0:T(8,128)}, f32[4,64,64]{2,1,0:T(8,128)}, u32[]{:S(2)}, u32[]{:S(2)}) collective-permute-start(f32[4,64,64]{2,1,0:T(8,128)} %add_add_fusion.2), channel_id=1, source_target_pairs={{0,6},{2,4},{4,2},{6,0},{8,14},{10,12},{12,10},{14,8},{16,22},{18,... | collective-permute-start | bytes 196616 | tf_op jit(solution)/shard_map/ppermute | solution.py:50
  60.6 9.3 %collective-permute-start.16 = (f32[4,64,64]{2,1,0:T(8,128)}, f32[4,64,64]{2,1,0:T(8,128)}, u32[]{:S(2)}, u32[]{:S(2)}) collective-permute-start(f32[4,64,64]{2,1,0:T(8,128)} %add_add_fusion.2), channel_id=1, source_target_pairs={{0,2},{2,0},{4,6},{6,4},{8,10},{10,8},{12,14},{14,12},{16,18},{18,... | collective-permute-start | bytes 196616 | tf_op jit(solution)/shard_map/ppermute | solution.py:50
  71.0 11.6 %collective-permute-start.20 = (f32[4,64,64]{2,1,0:T(8,128)S(1)}, f32[4,64,64]{2,1,0:T(8,128)S(1)}, u32[]{:S(2)}, u32[]{:S(2)}) collective-permute-start(f32[4,64,64]{2,1,0:T(8,128)S(1)} %add_add_fusion.1), channel_id=1, source_target_pairs={{0,16},{2,18},{4,20},{6,22},{8,24},{10,26},{12,28},{14,30},{16,0},... | collective-permute-start | bytes 196616 | tf_op jit(solution)/shard_map/ppermute | solution.py:50
  72.0 11.4 %collective-permute-start.21 = (f32[4,64,64]{2,1,0:T(8,128)S(1)}, f32[4,64,64]{2,1,0:T(8,128)S(1)}, u32[]{:S(2)}, u32[]{:S(2)}) collective-permute-start(f32[4,64,64]{2,1,0:T(8,128)S(1)} %add_add_fusion.1), channel_id=1, source_target_pairs={{0,24},{2,26},{4,28},{6,30},{8,16},{10,18},{12,20},{14,22},{16,8},... | collective-permute-start | bytes 196616 | tf_op jit(solution)/shard_map/ppermute | solution.py:50
  72.0 16.5 %collective-permute-start.19 = (f32[4,64,64]{2,1,0:T(8,128)S(1)}, f32[4,64,64]{2,1,0:T(8,128)S(1)}, u32[]{:S(2)}, u32[]{:S(2)}) collective-permute-start(f32[4,64,64]{2,1,0:T(8,128)S(1)} %add_add_fusion.1), channel_id=1, source_target_pairs={{0,8},{2,10},{4,12},{6,14},{8,0},{10,2},{12,4},{14,6},{16,24},{18,... | collective-permute-start | bytes 196616 | tf_op jit(solution)/shard_map/ppermute | solution.py:50
  106.2 2.5 %copy-start.6 = (f32[64,1,8,128]{3,0,2,1:T(8,128)S(1)}, f32[64,1,8,128]{3,0,2,1:T(8,128)}, u32[]{:S(2)}) copy-start(f32[64,1,8,128]{3,0,2,1:T(8,128)} %copy-done.5) | copy-start | bytes 786436
  106.2 2.5 %copy-start.8 = (f32[64,1,8,128]{3,0,2,1:T(8,128)S(1)}, f32[64,1,8,128]{3,0,2,1:T(8,128)}, u32[]{:S(2)}) copy-start(f32[64,1,8,128]{3,0,2,1:T(8,128)} %copy-done.7) | copy-start | bytes 786436
  106.2 2.5 %copy-start.12 = (f32[64,4,1,128]{3,0,2,1:T(8,128)S(1)}, f32[64,4,1,128]{3,0,2,1:T(8,128)}, u32[]{:S(2)}) copy-start(f32[64,4,1,128]{3,0,2,1:T(8,128)} %copy-done.11) | copy-start | bytes 393220
  106.2 2.5 %copy-start.14 = (f32[64,4,1,128]{3,0,2,1:T(8,128)S(1)}, f32[64,4,1,128]{3,0,2,1:T(8,128)}, u32[]{:S(2)}) copy-start(f32[64,4,1,128]{3,0,2,1:T(8,128)} %copy-done.13) | copy-start | bytes 393220
  106.2 2.5 %copy-start.19 = (f32[2,64,64]{2,1,0:T(8,128)S(1)}, f32[2,64,64]{2,1,0:T(8,128)}, u32[]{:S(2)}) copy-start(f32[2,64,64]{2,1,0:T(8,128)} %shard_map.68) | copy-start | bytes 98308
  108.8 3.0 %copy-start.3 = (f32[129,4,1,128]{3,0,2,1:T(8,128)S(1)}, f32[129,4,1,128]{3,0,2,1:T(8,128)}, u32[]{:S(2)}) copy-start(f32[129,4,1,128]{3,0,2,1:T(8,128)} %copy-done.2) | copy-start | bytes 792580
  111.7 1.1 copy-start
  111.9 2.1 %copy-start.4 = (f32[64,4,10,130]{3,0,2,1:T(8,128)S(1)}, f32[64,4,10,130]{3,0,2,1:T(8,128)}, u32[]{:S(2)}) copy-start(f32[64,4,10,130]{3,0,2,1:T(8,128)} %select_maximum_fusion) | copy-start | bytes 3993604
  114.7 5.2 %collective-permute-start.22 = (f32[2,8,64]{2,1,0:T(8,128)S(1)}, f32[2,8,64]{2,1,0:T(8,128)S(1)}, u32[]{:S(2)}, u32[]{:S(2)}) collective-permute-start(f32[2,8,64]{2,1,0:T(8,128)S(1)} %constant_dynamic-slice_fusion), channel_id=1, source_target_pairs={{0,1},{1,0},{2,3},{3,2},{4,5},{5,4},{6,7},{7,6},{8,9},{9,8},{10,11... | collective-permute-start | bytes 12296 | tf_op jit(solution)/shard_map/ppermute | solution.py:252

commit v8 on v7

--- a/solution.py
+++ b/solution.py
@@ -180,7 +180,11 @@
 
 def steps(grams):
     n = grams.shape[1]
-    return pl.pallas_call(steps_kernel, out_shape=jax.ShapeDtypeStruct((2, n, n), jnp.float32))(grams)
+    return pl.pallas_call(
+        steps_kernel,
+        out_shape=jax.ShapeDtypeStruct((2, n, n), jnp.float32),
+        cost_estimate=pl.CostEstimate(flops=20_000_000_000, transcendentals=0, bytes_accessed=6 * n * n * 4),
+    )(grams)
 
 
 def on_device(conductivity, electrodes, pair_order, initial_fields, adjoint_fields):
@@ -205,16 +209,17 @@
     right = INJECT * (point_source(picked[:, 0]) - point_source(picked[:, 1]))
     sides = (("gx", 1), ("gy", 2))
     grid_axes = ("gx", "gy")
-    stacked = jnp.concatenate([conductivity[None], initial_fields, adjoint_fields], axis=0)
+    stacked = jnp.concatenate([conductivity[None], initial_fields], axis=0)
     padded = padded_2(stacked, sides, 1)
     conds = conductances(padded[0])
-    iter_pad = padded[1 : 1 + columns]
-    adjoint_pad = padded[1 + columns :]
+    iter_pad = padded[1:]
     residual = right - operator(iter_pad, conds)
     res_pad = padded_2(residual, sides, 1)
     image = operator(res_pad, conds)
     image_pad = padded_2(image, sides, 1)
     image2 = operator(image_pad, conds)
+    image2, adjoint_late = lax.optimization_barrier((image2, adjoint_fields))
+    adjoint_pad = padded_2(adjoint_late, sides, 1)
     grams = allsum(
         jnp.stack(
             [

time: 121 us -> 114 us (0.942)
  waiting for transfers between devices: 39.5 us -> 30.7 us
  starting transfers between devices: 31.3 us -> 36.1 us
  matrix products: 7.8 us -> 5.88 us
    ppermute x9, waiting for transfers between devices: 21.3 us -> 12.3 us  [allsum(): lax.ppermute(value, axis, [(i, i ^ d << shift) for i in range(count)])]
    slice x1 -> x0, other arithmetic: 4.08 us -> none  [on_device(): adjoint_pad = padded[1 + columns:]]
    ppermute x6 -> x8, starting transfers between devices: 11.7 us -> 15 us  [padded_2(): high = lax.ppermute(bottom, axis, backward)]
    concatenate x3 -> x4, other arithmetic: 0.41 us -> 2.64 us  [padded_2(): return jnp.concatenate([low_y, middle, high_y], axis=dim_y)]
    dot_general x2, matrix products: 5.4 us -> 3.64 us  [combine_cols(): jnp.einsum('axyz,ab->bxyz', field, matrix, precision=lax.Precision.HIGHEST)]
    add x3, other arithmetic: 2.49 us -> 0.75 us  [allsum(): value = value + got[0] + (got[1] + got[2])]
    ppermute x6 -> x8, starting transfers between devices: 3.31 us -> 5 us  [padded_2(): low = lax.ppermute(top, axis, forward)]
    unnamed x48 -> x53, local copies, waits for them, and re-layouts: 6.36 us -> 7.56 us
  transfers between devices with their start and end apart: 23 -> 27, of which waited for: 14 -> 14; matrix products, arithmetic and copies ran while one was open for 10% -> 11% of each run, Pallas kernels for 0% -> 0%
where the time goes in v8:
time: 114 us; the launch traced here: 113 us
  starting transfers between devices  36.1 us (32%)
  waiting for transfers between devices  30.7 us (27%)
  Pallas kernels  17.2 us (15%)
  other arithmetic  11.8 us (10%)
  local copies, waits for them, and re-layouts  10.4 us (9%)
  matrix products  5.88 us (5%)
  between operations  1.34 us (1%)
    pallas_call x1, Pallas kernels, steps(): pl.pallas_call(steps_kernel, out_shape=jax.ShapeDtypeStruct((2, n, n), jn...  17.2 us
    ppermute x9, starting transfers between devices, allsum(): lax.ppermute(value, axis, [(i, i ^ d << shift) for i in range(count)])  15.2 us
    ppermute x8, starting transfers between devices, padded_2(): high = lax.ppermute(bottom, axis, backward)  15 us
    ppermute x8, waiting for transfers between devices, padded_2(): low = lax.ppermute(top, axis, forward)  12.6 us
    ppermute x9, waiting for transfers between devices, allsum(): lax.ppermute(value, axis, [(i, i ^ d << shift) for i in range(count)])  12.3 us
    unnamed x53, local copies, waits for them, and re-layouts  7.56 us
    ppermute x8, starting transfers between devices, padded_2(): low = lax.ppermute(top, axis, forward)  5 us
    dot_general x2, matrix products, combine_cols(): jnp.einsum('axyz,ab->bxyz', field, matrix, precision=lax.Precision.HIGHEST)  3.64 us
  transfers between devices with their start and end apart: 27, of which 14 were waited for; matrix products, arithmetic and copies ran while one was open for 11% of the time, Pallas kernels for 0%

profile of v8, /device:TPU:4, one launch (start us, length us, event | category | flops | bytes accessed | tf_op | source)
XLA Modules:
  0.0 113.4 jit_solution(5630211009287459992)
XLA Ops:
  0.7 1.2 %copy.35 = f32[64,2,8,128]{3,0,2,1:T(8,128)S(1)} copy(f32[64,2,8,128]{3,2,1,0:T(8,128)} %param.8) | data formatting | bytes 1048576 | tf_op args[3]
  1.9 0.7 maximum_select_fusion
  2.6 6.6 %collective-permute-start.3 = (f32[65,2,1,128]{3,0,2,1:T(8,128)S(1)}, f32[65,2,1,128]{3,0,2,1:T(8,128)S(1)}, u32[]{:S(2)}, u32[]{:S(2)}) collective-permute-start(f32[65,2,1,128]{3,0,2,1:T(8,128)S(1)} %get-tuple-element.22), channel_id=1, source_target_pairs={{2,0},{4,2},{6,4},{8,6},{10,8},{12,10},{14,12},{16,14},{18,16},{20... | collective-permute-start | bytes 199688 | tf_op jit(solution)/shard_map/ppermute | solution.py:26
  9.3 2.2 %collective-permute-start.2 = (f32[65,1,8,128]{3,0,2,1:T(8,128)S(1)}, f32[65,1,8,128]{3,0,2,1:T(8,128)S(1)}, u32[]{:S(2)}, u32[]{:S(2)}) collective-permute-start(f32[65,1,8,128]{3,0,2,1:T(8,128)S(1)} %get-tuple-element.24), channel_id=1, source_target_pairs={{32,0},{64,32},{96,64},{128,96},{160,128},{192,160},{224,192},{0,2... | collective-permute-start | bytes 798728 | tf_op jit(solution)/shard_map/ppermute | solution.py:26
  11.6 0.6 gather_fusion
  12.9 5.0 %collective-permute-done = f32[65,2,1,128]{3,0,2,1:T(8,128)S(1)} collective-permute-done((f32[65,2,1,128]{3,0,2,1:T(8,128)S(1)}, f32[65,2,1,128]{3,0,2,1:T(8,128)S(1)}, u32[]{:S(2)}, u32[]{:S(2)}) %collective-permute-start) | collective-permute-done | bytes 66592 | tf_op jit(solution)/shard_map/ppermute | solution.py:25
  17.9 0.9 collective-permute-done.1
  19.3 0.9 copy-done
  21.2 1.0 collective-permute-start.4
  22.2 0.6 collective-permute-start.6
  22.9 1.5 %collective-permute-start.7 = (f32[64,2,1,128]{3,0,2,1:T(8,128)S(1)}, f32[64,2,1,128]{3,0,2,1:T(8,128)S(1)}, u32[]{:S(2)}, u32[]{:S(2)}) collective-permute-start(f32[64,2,1,128]{3,0,2,1:T(8,128)S(1)} %get-tuple-element.33), channel_id=1, source_target_pairs={{0,2},{2,4},{4,6},{6,8},{8,10},{10,12},{12,14},{14,16},{16,18},{18... | collective-permute-start | bytes 196616 | tf_op jit(solution)/shard_map/ppermute | solution.py:25
  24.9 1.7 %collective-permute-done.6 = f32[64,2,1,128]{3,0,2,1:T(8,128)S(1)} collective-permute-done((f32[64,2,1,128]{3,0,2,1:T(8,128)S(1)}, f32[64,2,1,128]{3,0,2,1:T(8,128)S(1)}, u32[]{:S(2)}, u32[]{:S(2)}) %collective-permute-start.6) | collective-permute-done | bytes 65568 | tf_op jit(solution)/shard_map/ppermute | solution.py:26
  26.6 2.7 %collective-permute-done.7 = f32[64,2,1,128]{3,0,2,1:T(8,128)S(1)} collective-permute-done((f32[64,2,1,128]{3,0,2,1:T(8,128)S(1)}, f32[64,2,1,128]{3,0,2,1:T(8,128)S(1)}, u32[]{:S(2)}, u32[]{:S(2)}) %collective-permute-start.7) | collective-permute-done | bytes 65568 | tf_op jit(solution)/shard_map/ppermute | solution.py:25
  30.5 1.3 %collective-permute-start.8 = (f32[64,1,8,128]{3,0,2,1:T(8,128)S(1)}, f32[64,1,8,128]{3,0,2,1:T(8,128)S(1)}, u32[]{:S(2)}, u32[]{:S(2)}) collective-permute-start(f32[64,1,8,128]{3,0,2,1:T(8,128)S(1)} %get-tuple-element.32), channel_id=1, source_target_pairs={{32,0},{64,32},{96,64},{128,96},{160,128},{192,160},{224,192},{0,2... | collective-permute-start | bytes 786440 | tf_op jit(solution)/shard_map/ppermute | solution.py:26
  31.9 1.7 %collective-permute-start.11 = (f32[64,2,1,128]{3,0,2,1:T(8,128)S(1)}, f32[64,2,1,128]{3,0,2,1:T(8,128)S(1)}, u32[]{:S(2)}, u32[]{:S(2)}) collective-permute-start(f32[64,2,1,128]{3,0,2,1:T(8,128)S(1)} %get-tuple-element.29), channel_id=1, source_target_pairs={{0,2},{2,4},{4,6},{6,8},{8,10},{10,12},{12,14},{14,16},{16,18},{18... | collective-permute-start | bytes 196616 | tf_op jit(solution)/shard_map/ppermute | solution.py:25
  34.8 3.4 %collective-permute-done.11 = f32[64,2,1,128]{3,0,2,1:T(8,128)S(1)} collective-permute-done((f32[64,2,1,128]{3,0,2,1:T(8,128)S(1)}, f32[64,2,1,128]{3,0,2,1:T(8,128)S(1)}, u32[]{:S(2)}, u32[]{:S(2)}) %collective-permute-start.11) | collective-permute-done | bytes 65568 | tf_op jit(solution)/shard_map/ppermute | solution.py:25
  38.3 0.6 collective-permute-done.9
  41.2 0.8 collective-permute-done.12
  42.1 1.5 %collective-permute-start.15 = (f32[4,64,64]{2,1,0:T(8,128)S(1)}, f32[4,64,64]{2,1,0:T(8,128)S(1)}, u32[]{:S(2)}, u32[]{:S(2)}) collective-permute-start(f32[4,64,64]{2,1,0:T(8,128)S(1)} %fusion.60), channel_id=1, source_target_pairs={{0,192},{32,224},{64,128},{96,160},{128,64},{160,96},{192,0},{224,... | collective-permute-start | bytes 196616 | tf_op jit(solution)/shard_map/ppermute | solution.py:50
  43.6 1.9 %collective-permute-start.13 = (f32[4,64,64]{2,1,0:T(8,128)S(1)}, f32[4,64,64]{2,1,0:T(8,128)S(1)}, u32[]{:S(2)}, u32[]{:S(2)}) collective-permute-start(f32[4,64,64]{2,1,0:T(8,128)S(1)} %fusion.60), channel_id=1, source_target_pairs={{0,64},{32,96},{64,0},{96,32},{128,192},{160,224},{192,128},{224,1... | collective-permute-start | bytes 196616 | tf_op jit(solution)/shard_map/ppermute | solution.py:50
  45.6 0.6 slice_select_fusion.6
  46.5 1.8 %collective-permute-start.25 = (f32[64,2,1,128]{3,0,2,1:T(8,128)}, f32[64,2,1,128]{3,0,2,1:T(8,128)}, u32[]{:S(2)}, u32[]{:S(2)}) collective-permute-start(f32[64,2,1,128]{3,0,2,1:T(8,128)} %get-tuple-element.25), channel_id=1, source_target_pairs={{0,2},{2,4},{4,6},{6,8},{8,10},{10,12},{12,14},{14,16},{16,18},{18... | collective-permute-start | bytes 196616 | tf_op jit(solution)/shard_map/ppermute | solution.py:25
  48.3 1.8 %collective-permute-done.14 = f32[4,64,64]{2,1,0:T(8,128)S(1)} collective-permute-done((f32[4,64,64]{2,1,0:T(8,128)S(1)}, f32[4,64,64]{2,1,0:T(8,128)S(1)}, u32[]{:S(2)}, u32[]{:S(2)}) %collective-permute-start.14) | collective-permute-done | bytes 65568 | tf_op jit(solution)/shard_map/ppermute | solution.py:50
  50.0 1.9 %collective-permute-done.15 = f32[4,64,64]{2,1,0:T(8,128)S(1)} collective-permute-done((f32[4,64,64]{2,1,0:T(8,128)S(1)}, f32[4,64,64]{2,1,0:T(8,128)S(1)}, u32[]{:S(2)}, u32[]{:S(2)}) %collective-permute-start.15) | collective-permute-done | bytes 65568 | tf_op jit(solution)/shard_map/ppermute | solution.py:50
  52.0 0.8 collective-permute-start.17
  52.8 3.4 %collective-permute-start.18 = (f32[4,64,64]{2,1,0:T(8,128)S(1)}, f32[4,64,64]{2,1,0:T(8,128)S(1)}, u32[]{:S(2)}, u32[]{:S(2)}) collective-permute-start(f32[4,64,64]{2,1,0:T(8,128)S(1)} %add_add_fusion.2), channel_id=1, source_target_pairs={{0,6},{2,4},{4,2},{6,0},{8,14},{10,12},{12,10},{14,8},{16,22},{18,... | collective-permute-start | bytes 196616 | tf_op jit(solution)/shard_map/ppermute | solution.py:50
  56.2 0.8 slice_select_fusion.1
  56.9 0.9 pad.56
  57.8 3.0 %collective-permute-start.22 = (f32[64,1,8,128]{3,0,2,1:T(8,128)}, f32[64,1,8,128]{3,0,2,1:T(8,128)S(1)}, u32[]{:S(2)}, u32[]{:S(2)}) collective-permute-start(f32[64,1,8,128]{3,0,2,1:T(8,128)} %get-tuple-element.27), channel_id=1, source_target_pairs={{32,0},{64,32},{96,64},{128,96},{160,128},{192,160},{224,192},{0,2... | collective-permute-start | bytes 786440 | tf_op jit(solution)/shard_map/ppermute | solution.py:26
  60.8 0.8 pad.57
  61.6 3.4 %collective-permute-done.17 = f32[4,64,64]{2,1,0:T(8,128)S(1)} collective-permute-done((f32[4,64,64]{2,1,0:T(8,128)S(1)}, f32[4,64,64]{2,1,0:T(8,128)S(1)}, u32[]{:S(2)}, u32[]{:S(2)}) %collective-permute-start.17) | collective-permute-done | bytes 65568 | tf_op jit(solution)/shard_map/ppermute | solution.py:50
  65.4 0.9 collective-permute-start.20
  66.3 6.6 %collective-permute-start.19 = (f32[4,64,64]{2,1,0:T(8,128)S(1)}, f32[4,64,64]{2,1,0:T(8,128)S(1)}, u32[]{:S(2)}, u32[]{:S(2)}) collective-permute-start(f32[4,64,64]{2,1,0:T(8,128)S(1)} %add_add_fusion.1), channel_id=1, source_target_pairs={{0,8},{2,10},{4,12},{6,14},{8,0},{10,2},{12,4},{14,6},{16,24},{18,... | collective-permute-start | bytes 196616 | tf_op jit(solution)/shard_map/ppermute | solution.py:50
  72.9 1.0 constant_dynamic-update-slice_fusion.2
  73.9 1.2 %constant_dynamic-update-slice_fusion.1 = f32[64,4,8,128]{3,0,2,1:T(8,128)S(1)} fusion(f32[64,4,8,128]{3,0,2,1:T(8,128)S(1)} %constant_dynamic-update-slice_fusion.2, f32[64,2,8,128]{3,2,1,0:T(8,128)} %param.9), kind=kLoop, calls=%fused_computation.186 | loop fusion | bytes 1048576
  75.1 0.7 copy-done.18
  75.8 2.2 %select_maximum_fusion = f32[64,4,10,130]{3,0,2,1:T(8,128)} fusion(f32[64,4,1,128]{3,0,2,1:T(8,128)S(1)} %pad.56, f32[64,4,8,128]{3,0,2,1:T(8,128)S(1)} %constant_dynamic-update-slice_fusion, f32[64,4,1,128]{3,0,2,1:T(8,128)S(1)} %pad.57), kind=kLoop, calls=%fused_computation.11 | loop fusion | flops 2662400 | bytes 2641920 | tf_op jit(solution)/shard_map/concatenate | solution.py:35
  78.2 4.8 %collective-permute-done.19 = f32[4,64,64]{2,1,0:T(8,128)S(1)} collective-permute-done((f32[4,64,64]{2,1,0:T(8,128)S(1)}, f32[4,64,64]{2,1,0:T(8,128)S(1)}, u32[]{:S(2)}, u32[]{:S(2)}) %collective-permute-start.19) | collective-permute-done | bytes 65568 | tf_op jit(solution)/shard_map/ppermute | solution.py:50
  83.0 0.7 add_add_fusion.grams_ref
  83.7 17.2 %shard_map.68 = f32[2,64,64]{2,1,0:T(8,128)} custom-call(f32[4,64,64]{2,1,0:T(8,128)} %add_add_fusion.grams_ref), custom_call_target="tpu_custom_call" | custom-call | flops 20000000000 | bytes 98304 | tf_op jit(solution)/shard_map/pallas_call | solution.py:183
  100.9 2.1 %fusion.48 = f32[64,4,10,128]{3,0,2,1:T(8,128)S(1)} fusion(f32[2,64,64]{2,1,0:T(8,128)} %shard_map.68, f32[64,4,1,128]{3,0,2,1:T(8,128)S(1)} %copy-done.11, f32[64,1,8,128]{3,0,2,1:T(8,128)S(1)} %collective-permute-done.8, f32[64,2,8,128]{3,0,2,1:T(8,128)S(1)} %fusion.28, f32[64,1,8,128]{3,0,2,1:T(8,128)S(1)} %copy-done.6, f32[64,4,1,128]{3,0,2,1:T(8,128)S(1)} %copy-done.13), kind=kOutput, calls=%fused_computation.157 | convolution fusion | flops 252968960 | bytes 2654208 | tf_op jit(solution)/shard_map/axyz,ab->bxyz/dot_general | solution.py:84
  103.1 1.5 %fusion.1 = f32[64,4,10,128]{3,0,2,1:T(8,128)S(1)} fusion(f32[64,4,10,128]{3,0,2,1:T(8,128)S(1)} %fusion.48, f32[2,64,64]{2,1,0:T(8,128)S(1)} %copy-done.21, f32[65,4,10,128]{3,0,2,1:T(8,128)S(1)} %copy-done.1, f32[64,4,1,128]{3,0,2,1:T(8,128)S(1)} %pad.50, f32[64,1,8,128]{3,0,2,1:T(8,128)S(1)} %collective-permute-done.4, ...), kind=kOutput, calls=%fused_computation.16 | convolution fusion | flops 253624320 | bytes 5275648 | tf_op jit(solution)/shard_map/axyz,ab->bxyz/dot_general | solution.py:84
  105.2 0.6 fusion.10
  106.2 1.2 %fusion.12 = f32[3,8,128]{2,1,0:T(8,128)S(1)} fusion(f32[64,4,10,128]{3,0,2,1:T(8,128)S(1)} %fusion.1, f32[64,1,8,128]{3,0,2,1:T(8,128)S(1)} %copy-done.19, f32[64,2,8,128]{3,0,2,1:T(8,128)S(1)} %copy.44, f32[64,1,8,128]{3,0,2,1:T(8,128)} %collective-permute-done.23), kind=kLoop, calls=%fused_computation.37 | loop fusion | flops 1176576 | bytes 2633728 | tf_op jit(solution)/shard_map/reduce_sum | solution.py:102
  107.5 0.8 collective-permute-start.26
  108.4 1.1 copy.50
  109.5 3.2 %collective-permute-done.26 = f32[2,8,64]{2,1,0:T(8,128)S(1)} collective-permute-done((f32[2,8,64]{2,1,0:T(8,128)S(1)}, f32[2,8,64]{2,1,0:T(8,128)S(1)}, u32[]{:S(2)}, u32[]{:S(2)}) %collective-permute-start.26) | collective-permute-done | bytes 4128 | tf_op jit(solution)/shard_map/ppermute | solution.py:257
  112.7 0.7 dynamic-slice_add_fusion
  (134 shorter events, 9.6 us)
Async XLA Ops:
  0.6 8.6 %copy-start.20 = (f32[2,8,128]{2,1,0:T(8,128)S(1)}, f32[2,8,128]{2,1,0:T(8,128)}, u32[]{:S(2)}) copy-start(f32[2,8,128]{2,1,0:T(8,128)} %param.5) | copy-start | bytes 24580
  0.6 10.8 %copy-start.23 = (s32[64]{0:T(128)S(1)}, s32[64]{0:T(128)}, u32[]{:S(2)}) copy-start(s32[64]{0:T(128)} %param.7) | copy-start | bytes 772
  0.7 10.8 %copy-start.22 = (s32[128,2]{0,1:T(2,128)S(1)}, s32[128,2]{0,1:T(2,128)}, u32[]{:S(2)}) copy-start(s32[128,2]{0,1:T(2,128)} %param.6) | copy-start | bytes 3076
  2.6 10.3 %collective-permute-start.3 = (f32[65,2,1,128]{3,0,2,1:T(8,128)S(1)}, f32[65,2,1,128]{3,0,2,1:T(8,128)S(1)}, u32[]{:S(2)}, u32[]{:S(2)}) collective-permute-start(f32[65,2,1,128]{3,0,2,1:T(8,128)S(1)} %get-tuple-element.22), channel_id=1, source_target_pairs={{2,0},{4,2},{6,4},{8,6},{10,8},{12,10},{14,12},{16,14},{18,16},{20... | collective-permute-start | bytes 199688 | tf_op jit(solution)/shard_map/ppermute | solution.py:26
  9.3 8.7 %collective-permute-start.2 = (f32[65,1,8,128]{3,0,2,1:T(8,128)S(1)}, f32[65,1,8,128]{3,0,2,1:T(8,128)S(1)}, u32[]{:S(2)}, u32[]{:S(2)}) collective-permute-start(f32[65,1,8,128]{3,0,2,1:T(8,128)S(1)} %get-tuple-element.24), channel_id=1, source_target_pairs={{32,0},{64,32},{96,64},{128,96},{160,128},{192,160},{224,192},{0,2... | collective-permute-start | bytes 798728 | tf_op jit(solution)/shard_map/ppermute | solution.py:26
  11.5 7.4 %collective-permute-start.1 = (f32[65,1,8,128]{3,0,2,1:T(8,128)S(1)}, f32[65,1,8,128]{3,0,2,1:T(8,128)S(1)}, u32[]{:S(2)}, u32[]{:S(2)}) collective-permute-start(f32[65,1,8,128]{3,0,2,1:T(8,128)S(1)} %get-tuple-element.23), channel_id=1, source_target_pairs={{0,32},{32,64},{64,96},{96,128},{128,160},{160,192},{192,224},{224... | collective-permute-start | bytes 798728 | tf_op jit(solution)/shard_map/ppermute | solution.py:25
  11.5 6.5 %collective-permute-start = (f32[65,2,1,128]{3,0,2,1:T(8,128)S(1)}, f32[65,2,1,128]{3,0,2,1:T(8,128)S(1)}, u32[]{:S(2)}, u32[]{:S(2)}) collective-permute-start(f32[65,2,1,128]{3,0,2,1:T(8,128)S(1)} %get-tuple-element.21), channel_id=1, source_target_pairs={{0,2},{2,4},{4,6},{6,8},{8,10},{10,12},{12,14},{14,16},{16,18},{18... | collective-permute-start | bytes 199688 | tf_op jit(solution)/shard_map/ppermute | solution.py:25
  19.0 1.1 copy-start
  21.2 8.0 %collective-permute-start.4 = (f32[64,1,8,128]{3,0,2,1:T(8,128)S(1)}, f32[64,1,8,128]{3,0,2,1:T(8,128)S(1)}, u32[]{:S(2)}, u32[]{:S(2)}) collective-permute-start(f32[64,1,8,128]{3,0,2,1:T(8,128)S(1)} %get-tuple-element.36), channel_id=1, source_target_pairs={{32,0},{64,32},{96,64},{128,96},{160,128},{192,160},{224,192},{0,2... | collective-permute-start | bytes 786440 | tf_op jit(solution)/shard_map/ppermute | solution.py:26
  22.2 7.1 %collective-permute-start.5 = (f32[64,1,8,128]{3,0,2,1:T(8,128)S(1)}, f32[64,1,8,128]{3,0,2,1:T(8,128)S(1)}, u32[]{:S(2)}, u32[]{:S(2)}) collective-permute-start(f32[64,1,8,128]{3,0,2,1:T(8,128)S(1)} %get-tuple-element.35), channel_id=1, source_target_pairs={{0,32},{32,64},{64,96},{96,128},{128,160},{160,192},{192,224},{224... | collective-permute-start | bytes 786440 | tf_op jit(solution)/shard_map/ppermute | solution.py:25
  22.2 4.3 %collective-permute-start.6 = (f32[64,2,1,128]{3,0,2,1:T(8,128)S(1)}, f32[64,2,1,128]{3,0,2,1:T(8,128)S(1)}, u32[]{:S(2)}, u32[]{:S(2)}) collective-permute-start(f32[64,2,1,128]{3,0,2,1:T(8,128)S(1)} %get-tuple-element.34), channel_id=1, source_target_pairs={{2,0},{4,2},{6,4},{8,6},{10,8},{12,10},{14,12},{16,14},{18,16},{20... | collective-permute-start | bytes 196616 | tf_op jit(solution)/shard_map/ppermute | solution.py:26
  22.9 6.4 %collective-permute-start.7 = (f32[64,2,1,128]{3,0,2,1:T(8,128)S(1)}, f32[64,2,1,128]{3,0,2,1:T(8,128)S(1)}, u32[]{:S(2)}, u32[]{:S(2)}) collective-permute-start(f32[64,2,1,128]{3,0,2,1:T(8,128)S(1)} %get-tuple-element.33), channel_id=1, source_target_pairs={{0,2},{2,4},{4,6},{6,8},{8,10},{10,12},{12,14},{14,16},{16,18},{18... | collective-permute-start | bytes 196616 | tf_op jit(solution)/shard_map/ppermute | solution.py:25
  30.4 4.3 %collective-permute-start.10 = (f32[64,2,1,128]{3,0,2,1:T(8,128)S(1)}, f32[64,2,1,128]{3,0,2,1:T(8,128)S(1)}, u32[]{:S(2)}, u32[]{:S(2)}) collective-permute-start(f32[64,2,1,128]{3,0,2,1:T(8,128)S(1)} %get-tuple-element.30), channel_id=1, source_target_pairs={{2,0},{4,2},{6,4},{8,6},{10,8},{12,10},{14,12},{16,14},{18,16},{20... | collective-permute-start | bytes 196616 | tf_op jit(solution)/shard_map/ppermute | solution.py:26
  30.5 7.7 %collective-permute-start.8 = (f32[64,1,8,128]{3,0,2,1:T(8,128)S(1)}, f32[64,1,8,128]{3,0,2,1:T(8,128)S(1)}, u32[]{:S(2)}, u32[]{:S(2)}) collective-permute-start(f32[64,1,8,128]{3,0,2,1:T(8,128)S(1)} %get-tuple-element.32), channel_id=1, source_target_pairs={{32,0},{64,32},{96,64},{128,96},{160,128},{192,160},{224,192},{0,2... | collective-permute-start | bytes 786440 | tf_op jit(solution)/shard_map/ppermute | solution.py:26
  31.9 7.0 %collective-permute-start.9 = (f32[64,1,8,128]{3,0,2,1:T(8,128)S(1)}, f32[64,1,8,128]{3,0,2,1:T(8,128)S(1)}, u32[]{:S(2)}, u32[]{:S(2)}) collective-permute-start(f32[64,1,8,128]{3,0,2,1:T(8,128)S(1)} %get-tuple-element.31), channel_id=1, source_target_pairs={{0,32},{32,64},{64,96},{96,128},{128,160},{160,192},{192,224},{224... | collective-permute-start | bytes 786440 | tf_op jit(solution)/shard_map/ppermute | solution.py:25
  31.9 6.4 %collective-permute-start.11 = (f32[64,2,1,128]{3,0,2,1:T(8,128)S(1)}, f32[64,2,1,128]{3,0,2,1:T(8,128)S(1)}, u32[]{:S(2)}, u32[]{:S(2)}) collective-permute-start(f32[64,2,1,128]{3,0,2,1:T(8,128)S(1)} %get-tuple-element.29), channel_id=1, source_target_pairs={{0,2},{2,4},{4,6},{6,8},{8,10},{10,12},{12,14},{14,16},{16,18},{18... | collective-permute-start | bytes 196616 | tf_op jit(solution)/shard_map/ppermute | solution.py:25
  34.8 4.6 %copy-start.10 = (f32[64,4,1,128]{3,0,2,1:T(8,128)}, f32[64,4,1,128]{3,0,2,1:T(8,128)S(1)}, u32[]{:S(2)}) copy-start(f32[64,4,1,128]{3,0,2,1:T(8,128)S(1)} %pad.53) | copy-start | bytes 393220
  38.3 1.1 copy-start.12
  39.9 1.0 copy-start.7
  40.6 1.4 %collective-permute-start.12 = (f32[4,64,64]{2,1,0:T(8,128)S(1)}, f32[4,64,64]{2,1,0:T(8,128)S(1)}, u32[]{:S(2)}, u32[]{:S(2)}) collective-permute-start(f32[4,64,64]{2,1,0:T(8,128)S(1)} %pad_maximum_fusion.29), channel_id=1, source_target_pairs={{0,32},{32,0},{64,96},{96,64},{128,160},{160,128},{192,224},{224,1... | collective-permute-start | bytes 196616 | tf_op jit(solution)/shard_map/ppermute | solution.py:46
  42.0 8.0 %collective-permute-start.14 = (f32[4,64,64]{2,1,0:T(8,128)S(1)}, f32[4,64,64]{2,1,0:T(8,128)S(1)}, u32[]{:S(2)}, u32[]{:S(2)}) collective-permute-start(f32[4,64,64]{2,1,0:T(8,128)S(1)} %fusion.60), channel_id=1, source_target_pairs={{0,128},{32,160},{64,192},{96,224},{128,0},{160,32},{192,64},{224,... | collective-permute-start | bytes 196616 | tf_op jit(solution)/shard_map/ppermute | solution.py:50
  42.1 9.8 %collective-permute-start.15 = (f32[4,64,64]{2,1,0:T(8,128)S(1)}, f32[4,64,64]{2,1,0:T(8,128)S(1)}, u32[]{:S(2)}, u32[]{:S(2)}) collective-permute-start(f32[4,64,64]{2,1,0:T(8,128)S(1)} %fusion.60), channel_id=1, source_target_pairs={{0,192},{32,224},{64,128},{96,160},{128,64},{160,96},{192,0},{224,... | collective-permute-start | bytes 196616 | tf_op jit(solution)/shard_map/ppermute | solution.py:50
  43.6 8.3 %collective-permute-start.13 = (f32[4,64,64]{2,1,0:T(8,128)S(1)}, f32[4,64,64]{2,1,0:T(8,128)S(1)}, u32[]{:S(2)}, u32[]{:S(2)}) collective-permute-start(f32[4,64,64]{2,1,0:T(8,128)S(1)} %fusion.60), channel_id=1, source_target_pairs={{0,64},{32,96},{64,0},{96,32},{128,192},{160,224},{192,128},{224,1... | collective-permute-start | bytes 196616 | tf_op jit(solution)/shard_map/ppermute | solution.py:50
  46.2 10.7 %collective-permute-start.24 = (f32[64,2,1,128]{3,0,2,1:T(8,128)S(1)}, f32[64,2,1,128]{3,0,2,1:T(8,128)}, u32[]{:S(2)}, u32[]{:S(2)}) collective-permute-start(f32[64,2,1,128]{3,0,2,1:T(8,128)S(1)} %get-tuple-element.26), channel_id=1, source_target_pairs={{2,0},{4,2},{6,4},{8,6},{10,8},{12,10},{14,12},{16,14},{18,16},{20... | collective-permute-start | bytes 196616 | tf_op jit(solution)/shard_map/ppermute | solution.py:26
  46.5 11.3 %collective-permute-start.25 = (f32[64,2,1,128]{3,0,2,1:T(8,128)}, f32[64,2,1,128]{3,0,2,1:T(8,128)}, u32[]{:S(2)}, u32[]{:S(2)}) collective-permute-start(f32[64,2,1,128]{3,0,2,1:T(8,128)} %get-tuple-element.25), channel_id=1, source_target_pairs={{0,2},{2,4},{4,6},{6,8},{8,10},{10,12},{12,14},{14,16},{16,18},{18... | collective-permute-start | bytes 196616 | tf_op jit(solution)/shard_map/ppermute | solution.py:25
  52.0 13.0 %collective-permute-start.17 = (f32[4,64,64]{2,1,0:T(8,128)S(1)}, f32[4,64,64]{2,1,0:T(8,128)S(1)}, u32[]{:S(2)}, u32[]{:S(2)}) collective-permute-start(f32[4,64,64]{2,1,0:T(8,128)S(1)} %add_add_fusion.2), channel_id=1, source_target_pairs={{0,4},{2,6},{4,0},{6,2},{8,12},{10,14},{12,8},{14,10},{16,20},{18,... | collective-permute-start | bytes 196616 | tf_op jit(solution)/shard_map/ppermute | solution.py:50
  52.8 12.2 %collective-permute-start.18 = (f32[4,64,64]{2,1,0:T(8,128)S(1)}, f32[4,64,64]{2,1,0:T(8,128)S(1)}, u32[]{:S(2)}, u32[]{:S(2)}) collective-permute-start(f32[4,64,64]{2,1,0:T(8,128)S(1)} %add_add_fusion.2), channel_id=1, source_target_pairs={{0,6},{2,4},{4,2},{6,0},{8,14},{10,12},{12,10},{14,8},{16,22},{18,... | collective-permute-start | bytes 196616 | tf_op jit(solution)/shard_map/ppermute | solution.py:50
  56.2 9.2 %collective-permute-start.16 = (f32[4,64,64]{2,1,0:T(8,128)S(1)}, f32[4,64,64]{2,1,0:T(8,128)S(1)}, u32[]{:S(2)}, u32[]{:S(2)}) collective-permute-start(f32[4,64,64]{2,1,0:T(8,128)S(1)} %add_add_fusion.2), channel_id=1, source_target_pairs={{0,2},{2,0},{4,6},{6,4},{8,10},{10,8},{12,14},{14,12},{16,18},{18,... | collective-permute-start | bytes 196616 | tf_op jit(solution)/shard_map/ppermute | solution.py:50
  56.9 16.0 %collective-permute-start.23 = (f32[64,1,8,128]{3,0,2,1:T(8,128)S(1)}, f32[64,1,8,128]{3,0,2,1:T(8,128)}, u32[]{:S(2)}, u32[]{:S(2)}) collective-permute-start(f32[64,1,8,128]{3,0,2,1:T(8,128)S(1)} %get-tuple-element.28), channel_id=1, source_target_pairs={{0,32},{32,64},{64,96},{96,128},{128,160},{160,192},{192,224},{224... | collective-permute-start | bytes 786440 | tf_op jit(solution)/shard_map/ppermute | solution.py:25
  57.8 18.0 %copy-start.14 = (f32[64,4,1,128]{3,0,2,1:T(8,128)}, f32[64,4,1,128]{3,0,2,1:T(8,128)S(1)}, u32[]{:S(2)}) copy-start(f32[64,4,1,128]{3,0,2,1:T(8,128)S(1)} %pad.56) | copy-start | bytes 393220
  57.8 17.3 %collective-permute-start.22 = (f32[64,1,8,128]{3,0,2,1:T(8,128)}, f32[64,1,8,128]{3,0,2,1:T(8,128)S(1)}, u32[]{:S(2)}, u32[]{:S(2)}) collective-permute-start(f32[64,1,8,128]{3,0,2,1:T(8,128)} %get-tuple-element.27), channel_id=1, source_target_pairs={{32,0},{64,32},{96,64},{128,96},{160,128},{192,160},{224,192},{0,2... | collective-permute-start | bytes 786440 | tf_op jit(solution)/shard_map/ppermute | solution.py:26
  61.6 14.2 %copy-start.16 = (f32[64,4,1,128]{3,0,2,1:T(8,128)}, f32[64,4,1,128]{3,0,2,1:T(8,128)S(1)}, u32[]{:S(2)}) copy-start(f32[64,4,1,128]{3,0,2,1:T(8,128)S(1)} %pad.57) | copy-start | bytes 393220
  65.4 12.7 %collective-permute-start.20 = (f32[4,64,64]{2,1,0:T(8,128)S(1)}, f32[4,64,64]{2,1,0:T(8,128)S(1)}, u32[]{:S(2)}, u32[]{:S(2)}) collective-permute-start(f32[4,64,64]{2,1,0:T(8,128)S(1)} %add_add_fusion.1), channel_id=1, source_target_pairs={{0,16},{2,18},{4,20},{6,22},{8,24},{10,26},{12,28},{14,30},{16,0},... | collective-permute-start | bytes 196616 | tf_op jit(solution)/shard_map/ppermute | solution.py:50
  66.3 11.9 %collective-permute-start.21 = (f32[4,64,64]{2,1,0:T(8,128)S(1)}, f32[4,64,64]{2,1,0:T(8,128)S(1)}, u32[]{:S(2)}, u32[]{:S(2)}) collective-permute-start(f32[4,64,64]{2,1,0:T(8,128)S(1)} %add_add_fusion.1), channel_id=1, source_target_pairs={{0,24},{2,26},{4,28},{6,30},{8,16},{10,18},{12,20},{14,22},{16,8},... | collective-permute-start | bytes 196616 | tf_op jit(solution)/shard_map/ppermute | solution.py:50
  66.3 16.7 %collective-permute-start.19 = (f32[4,64,64]{2,1,0:T(8,128)S(1)}, f32[4,64,64]{2,1,0:T(8,128)S(1)}, u32[]{:S(2)}, u32[]{:S(2)}) collective-permute-start(f32[4,64,64]{2,1,0:T(8,128)S(1)} %add_add_fusion.1), channel_id=1, source_target_pairs={{0,8},{2,10},{4,12},{6,14},{8,0},{10,2},{12,4},{14,6},{16,24},{18,... | collective-permute-start | bytes 196616 | tf_op jit(solution)/shard_map/ppermute | solution.py:50
  75.8 2.3 %copy-start.3 = (f32[64,4,8,128]{3,0,2,1:T(8,128)}, f32[64,4,8,128]{3,0,2,1:T(8,128)S(1)}, u32[]{:S(2)}) copy-start(f32[64,4,8,128]{3,0,2,1:T(8,128)S(1)} %constant_dynamic-update-slice_fusion) | copy-start | bytes 3145732
  83.7 17.2 %copy-start.6 = (f32[64,1,8,128]{3,0,2,1:T(8,128)S(1)}, f32[64,1,8,128]{3,0,2,1:T(8,128)}, u32[]{:S(2)}) copy-start(f32[64,1,8,128]{3,0,2,1:T(8,128)} %copy-done.5) | copy-start | bytes 786436
  83.7 17.2 %copy-start.11 = (f32[64,4,1,128]{3,0,2,1:T(8,128)S(1)}, f32[64,4,1,128]{3,0,2,1:T(8,128)}, u32[]{:S(2)}) copy-start(f32[64,4,1,128]{3,0,2,1:T(8,128)} %copy-done.10) | copy-start | bytes 393220
  83.7 17.2 %copy-start.13 = (f32[64,4,1,128]{3,0,2,1:T(8,128)S(1)}, f32[64,4,1,128]{3,0,2,1:T(8,128)}, u32[]{:S(2)}) copy-start(f32[64,4,1,128]{3,0,2,1:T(8,128)} %copy-done.12) | copy-start | bytes 393220
  100.9 2.2 %copy-start.1 = (f32[65,4,10,128]{3,0,2,1:T(8,128)S(1)}, f32[65,4,10,128]{3,0,2,1:T(8,128)}, u32[]{:S(2)}) copy-start(f32[65,4,10,128]{3,0,2,1:T(8,128)} %copy-done) | copy-start | bytes 3993604
  100.9 2.2 %copy-start.9 = (f32[64,4,1,128]{3,0,2,1:T(8,128)S(1)}, f32[64,4,1,128]{3,0,2,1:T(8,128)}, u32[]{:S(2)}) copy-start(f32[64,4,1,128]{3,0,2,1:T(8,128)} %copy-done.8) | copy-start | bytes 393220
  100.9 2.2 %copy-start.21 = (f32[2,64,64]{2,1,0:T(8,128)S(1)}, f32[2,64,64]{2,1,0:T(8,128)}, u32[]{:S(2)}) copy-start(f32[2,64,64]{2,1,0:T(8,128)} %shard_map.68) | copy-start | bytes 98308
  103.1 1.6 %copy-start.4 = (f32[64,4,8,128]{3,0,2,1:T(8,128)S(1)}, f32[64,4,8,128]{3,0,2,1:T(8,128)}, u32[]{:S(2)}) copy-start(f32[64,4,8,128]{3,0,2,1:T(8,128)} %copy-done.3) | copy-start | bytes 3145732
  103.1 1.6 %copy-start.15 = (f32[64,4,1,128]{3,0,2,1:T(8,128)S(1)}, f32[64,4,1,128]{3,0,2,1:T(8,128)}, u32[]{:S(2)}) copy-start(f32[64,4,1,128]{3,0,2,1:T(8,128)} %copy-done.14) | copy-start | bytes 393220
  103.1 1.6 %copy-start.17 = (f32[64,4,1,128]{3,0,2,1:T(8,128)S(1)}, f32[64,4,1,128]{3,0,2,1:T(8,128)}, u32[]{:S(2)}) copy-start(f32[64,4,1,128]{3,0,2,1:T(8,128)} %copy-done.16) | copy-start | bytes 393220
  103.1 2.1 %copy-start.2 = (f32[64,4,10,130]{3,0,2,1:T(8,128)S(1)}, f32[64,4,10,130]{3,0,2,1:T(8,128)}, u32[]{:S(2)}) copy-start(f32[64,4,10,130]{3,0,2,1:T(8,128)} %select_maximum_fusion) | copy-start | bytes 3993604
  105.2 0.9 copy-start.19
  107.5 5.2 %collective-permute-start.26 = (f32[2,8,64]{2,1,0:T(8,128)S(1)}, f32[2,8,64]{2,1,0:T(8,128)S(1)}, u32[]{:S(2)}, u32[]{:S(2)}) collective-permute-start(f32[2,8,64]{2,1,0:T(8,128)S(1)} %constant_dynamic-slice_fusion), channel_id=1, source_target_pairs={{0,1},{1,0},{2,3},{3,2},{4,5},{5,4},{6,7},{7,6},{8,9},{9,8},{10,11... | collective-permute-start | bytes 12296 | tf_op jit(solution)/shard_map/ppermute | solution.py:257
  (3 other events, 2.1 us)

commit v9 on v8

--- a/solution.py
+++ b/solution.py
@@ -140,8 +140,9 @@
             row_r = jnp.sum(jnp.where(pick, r, 0.0), axis=0, keepdims=True)
             pivot = jnp.sum(jnp.where(lane_r == j, row_m, 0.0), axis=1, keepdims=True)
             col = jnp.sum(jnp.where(lanes == j, m, 0.0), axis=1, keepdims=True)
-            row_m = row_m / pivot
-            row_r = row_r / pivot
+            scale = 1.0 / pivot
+            row_m = row_m * scale
+            row_r = row_r * scale
             m = jnp.where(pick, row_m, m - col * row_m)
             r = jnp.where(pick, row_r, r - col * row_r)
             out.append((m, r))
@@ -160,7 +161,7 @@
     eye = (
         lax.broadcasted_iota(jnp.int32, (n, n), 0) == lax.broadcasted_iota(jnp.int32, (n, n), 1)
     ).astype(jnp.float32)
-    step0, rr_inv = _solve([(g_rq, g_rr), (g_rr, eye)], 2)
+    step0, rr_inv = _solve([(g_rq, g_rr), (g_rr, eye)], True)
     cross = _mm(g_rq, step0)
     step0_t = _tr(step0)
     new_gram = g_rr - cross - _tr(cross) + _mm(step0_t, _mm(g_qq, step0))
@@ -173,7 +174,7 @@
         - _mm(step0_t, _mm(g_qq, keep))
         + _mm(step0_t, _mm(g_qw, step0))
     )
-    (step1,) = _solve([(curv, new_gram)], 4)
+    (step1,) = _solve([(curv, new_gram)], True)
     out_ref[0] = step0 + _mm(keep, step1)
     out_ref[1] = -_mm(step0, step1)
 

time: 114 us -> 113 us (level)
  no operation moved by 1% of the time
where the time goes in v9:
time: 113 us
  starting transfers between devices  36.1 us (32%)
  waiting for transfers between devices  30.7 us (27%)
  Pallas kernels  16.5 us (15%)
  other arithmetic  11.8 us (10%)
  local copies, waits for them, and re-layouts  10.4 us (9%)
  matrix products  5.88 us (5%)
  between operations  1.34 us (1%)
    pallas_call x1, Pallas kernels, steps(): pl.pallas_call(steps_kernel, out_shape=jax.ShapeDtypeStruct((2, n, n), jn...  16.5 us
    ppermute x9, starting transfers between devices, allsum(): lax.ppermute(value, axis, [(i, i ^ d << shift) for i in range(count)])  15.2 us
    ppermute x8, starting transfers between devices, padded_2(): high = lax.ppermute(bottom, axis, backward)  15 us
    ppermute x8, waiting for transfers between devices, padded_2(): low = lax.ppermute(top, axis, forward)  12.6 us
    ppermute x9, waiting for transfers between devices, allsum(): lax.ppermute(value, axis, [(i, i ^ d << shift) for i in range(count)])  12.3 us
    unnamed x53, local copies, waits for them, and re-layouts  7.56 us
    ppermute x8, starting transfers between devices, padded_2(): low = lax.ppermute(top, axis, forward)  5 us
    dot_general x2, matrix products, combine_cols(): jnp.einsum('axyz,ab->bxyz', field, matrix, precision=lax.Precision.HIGHEST)  3.64 us
  transfers between devices with their start and end apart: 27, of which 14 were waited for; matrix products, arithmetic and copies ran while one was open for 11% of the time, Pallas kernels for 0%

profile of v9, /device:TPU:4, one launch (start us, length us, event | category | flops | bytes accessed | tf_op | source)
XLA Modules:
  0.0 112.7 jit_solution(10274244494097314163)
XLA Ops:
  0.7 1.2 %copy.35 = f32[64,2,8,128]{3,0,2,1:T(8,128)S(1)} copy(f32[64,2,8,128]{3,2,1,0:T(8,128)} %param.8) | data formatting | bytes 1048576 | tf_op args[3]
  1.9 0.7 maximum_select_fusion
  2.6 6.6 %collective-permute-start.3 = (f32[65,2,1,128]{3,0,2,1:T(8,128)S(1)}, f32[65,2,1,128]{3,0,2,1:T(8,128)S(1)}, u32[]{:S(2)}, u32[]{:S(2)}) collective-permute-start(f32[65,2,1,128]{3,0,2,1:T(8,128)S(1)} %get-tuple-element.22), channel_id=1, source_target_pairs={{2,0},{4,2},{6,4},{8,6},{10,8},{12,10},{14,12},{16,14},{18,16},{20... | collective-permute-start | bytes 199688 | tf_op jit(solution)/shard_map/ppermute | solution.py:26
  9.3 2.2 %collective-permute-start.2 = (f32[65,1,8,128]{3,0,2,1:T(8,128)S(1)}, f32[65,1,8,128]{3,0,2,1:T(8,128)S(1)}, u32[]{:S(2)}, u32[]{:S(2)}) collective-permute-start(f32[65,1,8,128]{3,0,2,1:T(8,128)S(1)} %get-tuple-element.24), channel_id=1, source_target_pairs={{32,0},{64,32},{96,64},{128,96},{160,128},{192,160},{224,192},{0,2... | collective-permute-start | bytes 798728 | tf_op jit(solution)/shard_map/ppermute | solution.py:26
  11.6 0.6 gather_fusion
  12.9 5.0 %collective-permute-done = f32[65,2,1,128]{3,0,2,1:T(8,128)S(1)} collective-permute-done((f32[65,2,1,128]{3,0,2,1:T(8,128)S(1)}, f32[65,2,1,128]{3,0,2,1:T(8,128)S(1)}, u32[]{:S(2)}, u32[]{:S(2)}) %collective-permute-start) | collective-permute-done | bytes 66592 | tf_op jit(solution)/shard_map/ppermute | solution.py:25
  17.9 0.9 collective-permute-done.1
  19.3 0.9 copy-done
  21.2 1.0 collective-permute-start.4
  22.2 0.6 collective-permute-start.6
  22.9 1.5 %collective-permute-start.7 = (f32[64,2,1,128]{3,0,2,1:T(8,128)S(1)}, f32[64,2,1,128]{3,0,2,1:T(8,128)S(1)}, u32[]{:S(2)}, u32[]{:S(2)}) collective-permute-start(f32[64,2,1,128]{3,0,2,1:T(8,128)S(1)} %get-tuple-element.33), channel_id=1, source_target_pairs={{0,2},{2,4},{4,6},{6,8},{8,10},{10,12},{12,14},{14,16},{16,18},{18... | collective-permute-start | bytes 196616 | tf_op jit(solution)/shard_map/ppermute | solution.py:25
  24.9 1.7 %collective-permute-done.6 = f32[64,2,1,128]{3,0,2,1:T(8,128)S(1)} collective-permute-done((f32[64,2,1,128]{3,0,2,1:T(8,128)S(1)}, f32[64,2,1,128]{3,0,2,1:T(8,128)S(1)}, u32[]{:S(2)}, u32[]{:S(2)}) %collective-permute-start.6) | collective-permute-done | bytes 65568 | tf_op jit(solution)/shard_map/ppermute | solution.py:26
  26.6 2.7 %collective-permute-done.7 = f32[64,2,1,128]{3,0,2,1:T(8,128)S(1)} collective-permute-done((f32[64,2,1,128]{3,0,2,1:T(8,128)S(1)}, f32[64,2,1,128]{3,0,2,1:T(8,128)S(1)}, u32[]{:S(2)}, u32[]{:S(2)}) %collective-permute-start.7) | collective-permute-done | bytes 65568 | tf_op jit(solution)/shard_map/ppermute | solution.py:25
  30.5 1.3 %collective-permute-start.8 = (f32[64,1,8,128]{3,0,2,1:T(8,128)S(1)}, f32[64,1,8,128]{3,0,2,1:T(8,128)S(1)}, u32[]{:S(2)}, u32[]{:S(2)}) collective-permute-start(f32[64,1,8,128]{3,0,2,1:T(8,128)S(1)} %get-tuple-element.32), channel_id=1, source_target_pairs={{32,0},{64,32},{96,64},{128,96},{160,128},{192,160},{224,192},{0,2... | collective-permute-start | bytes 786440 | tf_op jit(solution)/shard_map/ppermute | solution.py:26
  31.9 1.7 %collective-permute-start.11 = (f32[64,2,1,128]{3,0,2,1:T(8,128)S(1)}, f32[64,2,1,128]{3,0,2,1:T(8,128)S(1)}, u32[]{:S(2)}, u32[]{:S(2)}) collective-permute-start(f32[64,2,1,128]{3,0,2,1:T(8,128)S(1)} %get-tuple-element.29), channel_id=1, source_target_pairs={{0,2},{2,4},{4,6},{6,8},{8,10},{10,12},{12,14},{14,16},{16,18},{18... | collective-permute-start | bytes 196616 | tf_op jit(solution)/shard_map/ppermute | solution.py:25
  34.8 3.4 %collective-permute-done.11 = f32[64,2,1,128]{3,0,2,1:T(8,128)S(1)} collective-permute-done((f32[64,2,1,128]{3,0,2,1:T(8,128)S(1)}, f32[64,2,1,128]{3,0,2,1:T(8,128)S(1)}, u32[]{:S(2)}, u32[]{:S(2)}) %collective-permute-start.11) | collective-permute-done | bytes 65568 | tf_op jit(solution)/shard_map/ppermute | solution.py:25
  38.3 0.6 collective-permute-done.9
  41.2 0.8 collective-permute-done.12
  42.1 1.5 %collective-permute-start.15 = (f32[4,64,64]{2,1,0:T(8,128)S(1)}, f32[4,64,64]{2,1,0:T(8,128)S(1)}, u32[]{:S(2)}, u32[]{:S(2)}) collective-permute-start(f32[4,64,64]{2,1,0:T(8,128)S(1)} %fusion.60), channel_id=1, source_target_pairs={{0,192},{32,224},{64,128},{96,160},{128,64},{160,96},{192,0},{224,... | collective-permute-start | bytes 196616 | tf_op jit(solution)/shard_map/ppermute | solution.py:50
  43.6 1.9 %collective-permute-start.13 = (f32[4,64,64]{2,1,0:T(8,128)S(1)}, f32[4,64,64]{2,1,0:T(8,128)S(1)}, u32[]{:S(2)}, u32[]{:S(2)}) collective-permute-start(f32[4,64,64]{2,1,0:T(8,128)S(1)} %fusion.60), channel_id=1, source_target_pairs={{0,64},{32,96},{64,0},{96,32},{128,192},{160,224},{192,128},{224,1... | collective-permute-start | bytes 196616 | tf_op jit(solution)/shard_map/ppermute | solution.py:50
  45.6 0.6 slice_select_fusion.6
  46.5 1.8 %collective-permute-start.25 = (f32[64,2,1,128]{3,0,2,1:T(8,128)}, f32[64,2,1,128]{3,0,2,1:T(8,128)}, u32[]{:S(2)}, u32[]{:S(2)}) collective-permute-start(f32[64,2,1,128]{3,0,2,1:T(8,128)} %get-tuple-element.25), channel_id=1, source_target_pairs={{0,2},{2,4},{4,6},{6,8},{8,10},{10,12},{12,14},{14,16},{16,18},{18... | collective-permute-start | bytes 196616 | tf_op jit(solution)/shard_map/ppermute | solution.py:25
  48.3 1.8 %collective-permute-done.14 = f32[4,64,64]{2,1,0:T(8,128)S(1)} collective-permute-done((f32[4,64,64]{2,1,0:T(8,128)S(1)}, f32[4,64,64]{2,1,0:T(8,128)S(1)}, u32[]{:S(2)}, u32[]{:S(2)}) %collective-permute-start.14) | collective-permute-done | bytes 65568 | tf_op jit(solution)/shard_map/ppermute | solution.py:50
  50.0 1.9 %collective-permute-done.15 = f32[4,64,64]{2,1,0:T(8,128)S(1)} collective-permute-done((f32[4,64,64]{2,1,0:T(8,128)S(1)}, f32[4,64,64]{2,1,0:T(8,128)S(1)}, u32[]{:S(2)}, u32[]{:S(2)}) %collective-permute-start.15) | collective-permute-done | bytes 65568 | tf_op jit(solution)/shard_map/ppermute | solution.py:50
  52.0 0.8 collective-permute-start.17
  52.8 3.4 %collective-permute-start.18 = (f32[4,64,64]{2,1,0:T(8,128)S(1)}, f32[4,64,64]{2,1,0:T(8,128)S(1)}, u32[]{:S(2)}, u32[]{:S(2)}) collective-permute-start(f32[4,64,64]{2,1,0:T(8,128)S(1)} %add_add_fusion.2), channel_id=1, source_target_pairs={{0,6},{2,4},{4,2},{6,0},{8,14},{10,12},{12,10},{14,8},{16,22},{18,... | collective-permute-start | bytes 196616 | tf_op jit(solution)/shard_map/ppermute | solution.py:50
  56.2 0.8 slice_select_fusion.1
  56.9 0.9 pad.56
  57.8 3.0 %collective-permute-start.22 = (f32[64,1,8,128]{3,0,2,1:T(8,128)}, f32[64,1,8,128]{3,0,2,1:T(8,128)S(1)}, u32[]{:S(2)}, u32[]{:S(2)}) collective-permute-start(f32[64,1,8,128]{3,0,2,1:T(8,128)} %get-tuple-element.27), channel_id=1, source_target_pairs={{32,0},{64,32},{96,64},{128,96},{160,128},{192,160},{224,192},{0,2... | collective-permute-start | bytes 786440 | tf_op jit(solution)/shard_map/ppermute | solution.py:26
  60.8 0.8 pad.57
  61.6 3.4 %collective-permute-done.17 = f32[4,64,64]{2,1,0:T(8,128)S(1)} collective-permute-done((f32[4,64,64]{2,1,0:T(8,128)S(1)}, f32[4,64,64]{2,1,0:T(8,128)S(1)}, u32[]{:S(2)}, u32[]{:S(2)}) %collective-permute-start.17) | collective-permute-done | bytes 65568 | tf_op jit(solution)/shard_map/ppermute | solution.py:50
  65.4 0.9 collective-permute-start.20
  66.3 6.6 %collective-permute-start.19 = (f32[4,64,64]{2,1,0:T(8,128)S(1)}, f32[4,64,64]{2,1,0:T(8,128)S(1)}, u32[]{:S(2)}, u32[]{:S(2)}) collective-permute-start(f32[4,64,64]{2,1,0:T(8,128)S(1)} %add_add_fusion.1), channel_id=1, source_target_pairs={{0,8},{2,10},{4,12},{6,14},{8,0},{10,2},{12,4},{14,6},{16,24},{18,... | collective-permute-start | bytes 196616 | tf_op jit(solution)/shard_map/ppermute | solution.py:50
  72.9 1.0 constant_dynamic-update-slice_fusion.2
  73.9 1.2 %constant_dynamic-update-slice_fusion.1 = f32[64,4,8,128]{3,0,2,1:T(8,128)S(1)} fusion(f32[64,4,8,128]{3,0,2,1:T(8,128)S(1)} %constant_dynamic-update-slice_fusion.2, f32[64,2,8,128]{3,2,1,0:T(8,128)} %param.9), kind=kLoop, calls=%fused_computation.186 | loop fusion | bytes 1048576
  75.1 0.7 copy-done.18
  75.8 2.2 %select_maximum_fusion = f32[64,4,10,130]{3,0,2,1:T(8,128)} fusion(f32[64,4,1,128]{3,0,2,1:T(8,128)S(1)} %pad.56, f32[64,4,8,128]{3,0,2,1:T(8,128)S(1)} %constant_dynamic-update-slice_fusion, f32[64,4,1,128]{3,0,2,1:T(8,128)S(1)} %pad.57), kind=kLoop, calls=%fused_computation.11 | loop fusion | flops 2662400 | bytes 2641920 | tf_op jit(solution)/shard_map/concatenate | solution.py:35
  78.2 4.8 %collective-permute-done.19 = f32[4,64,64]{2,1,0:T(8,128)S(1)} collective-permute-done((f32[4,64,64]{2,1,0:T(8,128)S(1)}, f32[4,64,64]{2,1,0:T(8,128)S(1)}, u32[]{:S(2)}, u32[]{:S(2)}) %collective-permute-start.19) | collective-permute-done | bytes 65568 | tf_op jit(solution)/shard_map/ppermute | solution.py:50
  83.0 0.7 add_add_fusion.grams_ref
  83.7 16.5 %shard_map.68 = f32[2,64,64]{2,1,0:T(8,128)} custom-call(f32[4,64,64]{2,1,0:T(8,128)} %add_add_fusion.grams_ref), custom_call_target="tpu_custom_call" | custom-call | flops 20000000000 | bytes 98304 | tf_op jit(solution)/shard_map/pallas_call | solution.py:184
  100.3 2.1 %fusion.48 = f32[64,4,10,128]{3,0,2,1:T(8,128)S(1)} fusion(f32[2,64,64]{2,1,0:T(8,128)} %shard_map.68, f32[64,4,1,128]{3,0,2,1:T(8,128)S(1)} %copy-done.11, f32[64,1,8,128]{3,0,2,1:T(8,128)S(1)} %collective-permute-done.8, f32[64,2,8,128]{3,0,2,1:T(8,128)S(1)} %fusion.28, f32[64,1,8,128]{3,0,2,1:T(8,128)S(1)} %copy-done.6, f32[64,4,1,128]{3,0,2,1:T(8,128)S(1)} %copy-done.13), kind=kOutput, calls=%fused_computation.157 | convolution fusion | flops 252968960 | bytes 2654208 | tf_op jit(solution)/shard_map/axyz,ab->bxyz/dot_general | solution.py:84
  102.5 1.5 %fusion.1 = f32[64,4,10,128]{3,0,2,1:T(8,128)S(1)} fusion(f32[64,4,10,128]{3,0,2,1:T(8,128)S(1)} %fusion.48, f32[2,64,64]{2,1,0:T(8,128)S(1)} %copy-done.21, f32[65,4,10,128]{3,0,2,1:T(8,128)S(1)} %copy-done.1, f32[64,4,1,128]{3,0,2,1:T(8,128)S(1)} %pad.50, f32[64,1,8,128]{3,0,2,1:T(8,128)S(1)} %collective-permute-done.4, ...), kind=kOutput, calls=%fused_computation.16 | convolution fusion | flops 253624320 | bytes 5275648 | tf_op jit(solution)/shard_map/axyz,ab->bxyz/dot_general | solution.py:84
  104.6 0.6 fusion.10
  105.5 1.2 %fusion.12 = f32[3,8,128]{2,1,0:T(8,128)S(1)} fusion(f32[64,4,10,128]{3,0,2,1:T(8,128)S(1)} %fusion.1, f32[64,1,8,128]{3,0,2,1:T(8,128)S(1)} %copy-done.19, f32[64,2,8,128]{3,0,2,1:T(8,128)S(1)} %copy.44, f32[64,1,8,128]{3,0,2,1:T(8,128)} %collective-permute-done.23), kind=kLoop, calls=%fused_computation.37 | loop fusion | flops 1176576 | bytes 2633728 | tf_op jit(solution)/shard_map/reduce_sum | solution.py:102
  106.9 0.8 collective-permute-start.26
  107.8 1.1 copy.50
  108.9 3.2 %collective-permute-done.26 = f32[2,8,64]{2,1,0:T(8,128)S(1)} collective-permute-done((f32[2,8,64]{2,1,0:T(8,128)S(1)}, f32[2,8,64]{2,1,0:T(8,128)S(1)}, u32[]{:S(2)}, u32[]{:S(2)}) %collective-permute-start.26) | collective-permute-done | bytes 4128 | tf_op jit(solution)/shard_map/ppermute | solution.py:258
  112.1 0.7 dynamic-slice_add_fusion
  (134 shorter events, 9.6 us)
Async XLA Ops:
  0.6 8.6 %copy-start.20 = (f32[2,8,128]{2,1,0:T(8,128)S(1)}, f32[2,8,128]{2,1,0:T(8,128)}, u32[]{:S(2)}) copy-start(f32[2,8,128]{2,1,0:T(8,128)} %param.5) | copy-start | bytes 24580
  0.6 10.8 %copy-start.23 = (s32[64]{0:T(128)S(1)}, s32[64]{0:T(128)}, u32[]{:S(2)}) copy-start(s32[64]{0:T(128)} %param.7) | copy-start | bytes 772
  0.7 10.8 %copy-start.22 = (s32[128,2]{0,1:T(2,128)S(1)}, s32[128,2]{0,1:T(2,128)}, u32[]{:S(2)}) copy-start(s32[128,2]{0,1:T(2,128)} %param.6) | copy-start | bytes 3076
  2.6 10.3 %collective-permute-start.3 = (f32[65,2,1,128]{3,0,2,1:T(8,128)S(1)}, f32[65,2,1,128]{3,0,2,1:T(8,128)S(1)}, u32[]{:S(2)}, u32[]{:S(2)}) collective-permute-start(f32[65,2,1,128]{3,0,2,1:T(8,128)S(1)} %get-tuple-element.22), channel_id=1, source_target_pairs={{2,0},{4,2},{6,4},{8,6},{10,8},{12,10},{14,12},{16,14},{18,16},{20... | collective-permute-start | bytes 199688 | tf_op jit(solution)/shard_map/ppermute | solution.py:26
  9.3 8.7 %collective-permute-start.2 = (f32[65,1,8,128]{3,0,2,1:T(8,128)S(1)}, f32[65,1,8,128]{3,0,2,1:T(8,128)S(1)}, u32[]{:S(2)}, u32[]{:S(2)}) collective-permute-start(f32[65,1,8,128]{3,0,2,1:T(8,128)S(1)} %get-tuple-element.24), channel_id=1, source_target_pairs={{32,0},{64,32},{96,64},{128,96},{160,128},{192,160},{224,192},{0,2... | collective-permute-start | bytes 798728 | tf_op jit(solution)/shard_map/ppermute | solution.py:26
  11.5 7.4 %collective-permute-start.1 = (f32[65,1,8,128]{3,0,2,1:T(8,128)S(1)}, f32[65,1,8,128]{3,0,2,1:T(8,128)S(1)}, u32[]{:S(2)}, u32[]{:S(2)}) collective-permute-start(f32[65,1,8,128]{3,0,2,1:T(8,128)S(1)} %get-tuple-element.23), channel_id=1, source_target_pairs={{0,32},{32,64},{64,96},{96,128},{128,160},{160,192},{192,224},{224... | collective-permute-start | bytes 798728 | tf_op jit(solution)/shard_map/ppermute | solution.py:25
  11.5 6.5 %collective-permute-start = (f32[65,2,1,128]{3,0,2,1:T(8,128)S(1)}, f32[65,2,1,128]{3,0,2,1:T(8,128)S(1)}, u32[]{:S(2)}, u32[]{:S(2)}) collective-permute-start(f32[65,2,1,128]{3,0,2,1:T(8,128)S(1)} %get-tuple-element.21), channel_id=1, source_target_pairs={{0,2},{2,4},{4,6},{6,8},{8,10},{10,12},{12,14},{14,16},{16,18},{18... | collective-permute-start | bytes 199688 | tf_op jit(solution)/shard_map/ppermute | solution.py:25
  19.0 1.1 copy-start
  21.2 8.0 %collective-permute-start.4 = (f32[64,1,8,128]{3,0,2,1:T(8,128)S(1)}, f32[64,1,8,128]{3,0,2,1:T(8,128)S(1)}, u32[]{:S(2)}, u32[]{:S(2)}) collective-permute-start(f32[64,1,8,128]{3,0,2,1:T(8,128)S(1)} %get-tuple-element.36), channel_id=1, source_target_pairs={{32,0},{64,32},{96,64},{128,96},{160,128},{192,160},{224,192},{0,2... | collective-permute-start | bytes 786440 | tf_op jit(solution)/shard_map/ppermute | solution.py:26
  22.2 7.1 %collective-permute-start.5 = (f32[64,1,8,128]{3,0,2,1:T(8,128)S(1)}, f32[64,1,8,128]{3,0,2,1:T(8,128)S(1)}, u32[]{:S(2)}, u32[]{:S(2)}) collective-permute-start(f32[64,1,8,128]{3,0,2,1:T(8,128)S(1)} %get-tuple-element.35), channel_id=1, source_target_pairs={{0,32},{32,64},{64,96},{96,128},{128,160},{160,192},{192,224},{224... | collective-permute-start | bytes 786440 | tf_op jit(solution)/shard_map/ppermute | solution.py:25
  22.2 4.3 %collective-permute-start.6 = (f32[64,2,1,128]{3,0,2,1:T(8,128)S(1)}, f32[64,2,1,128]{3,0,2,1:T(8,128)S(1)}, u32[]{:S(2)}, u32[]{:S(2)}) collective-permute-start(f32[64,2,1,128]{3,0,2,1:T(8,128)S(1)} %get-tuple-element.34), channel_id=1, source_target_pairs={{2,0},{4,2},{6,4},{8,6},{10,8},{12,10},{14,12},{16,14},{18,16},{20... | collective-permute-start | bytes 196616 | tf_op jit(solution)/shard_map/ppermute | solution.py:26
  22.9 6.4 %collective-permute-start.7 = (f32[64,2,1,128]{3,0,2,1:T(8,128)S(1)}, f32[64,2,1,128]{3,0,2,1:T(8,128)S(1)}, u32[]{:S(2)}, u32[]{:S(2)}) collective-permute-start(f32[64,2,1,128]{3,0,2,1:T(8,128)S(1)} %get-tuple-element.33), channel_id=1, source_target_pairs={{0,2},{2,4},{4,6},{6,8},{8,10},{10,12},{12,14},{14,16},{16,18},{18... | collective-permute-start | bytes 196616 | tf_op jit(solution)/shard_map/ppermute | solution.py:25
  30.4 4.3 %collective-permute-start.10 = (f32[64,2,1,128]{3,0,2,1:T(8,128)S(1)}, f32[64,2,1,128]{3,0,2,1:T(8,128)S(1)}, u32[]{:S(2)}, u32[]{:S(2)}) collective-permute-start(f32[64,2,1,128]{3,0,2,1:T(8,128)S(1)} %get-tuple-element.30), channel_id=1, source_target_pairs={{2,0},{4,2},{6,4},{8,6},{10,8},{12,10},{14,12},{16,14},{18,16},{20... | collective-permute-start | bytes 196616 | tf_op jit(solution)/shard_map/ppermute | solution.py:26
  30.5 7.7 %collective-permute-start.8 = (f32[64,1,8,128]{3,0,2,1:T(8,128)S(1)}, f32[64,1,8,128]{3,0,2,1:T(8,128)S(1)}, u32[]{:S(2)}, u32[]{:S(2)}) collective-permute-start(f32[64,1,8,128]{3,0,2,1:T(8,128)S(1)} %get-tuple-element.32), channel_id=1, source_target_pairs={{32,0},{64,32},{96,64},{128,96},{160,128},{192,160},{224,192},{0,2... | collective-permute-start | bytes 786440 | tf_op jit(solution)/shard_map/ppermute | solution.py:26
  31.9 7.0 %collective-permute-start.9 = (f32[64,1,8,128]{3,0,2,1:T(8,128)S(1)}, f32[64,1,8,128]{3,0,2,1:T(8,128)S(1)}, u32[]{:S(2)}, u32[]{:S(2)}) collective-permute-start(f32[64,1,8,128]{3,0,2,1:T(8,128)S(1)} %get-tuple-element.31), channel_id=1, source_target_pairs={{0,32},{32,64},{64,96},{96,128},{128,160},{160,192},{192,224},{224... | collective-permute-start | bytes 786440 | tf_op jit(solution)/shard_map/ppermute | solution.py:25
  31.9 6.4 %collective-permute-start.11 = (f32[64,2,1,128]{3,0,2,1:T(8,128)S(1)}, f32[64,2,1,128]{3,0,2,1:T(8,128)S(1)}, u32[]{:S(2)}, u32[]{:S(2)}) collective-permute-start(f32[64,2,1,128]{3,0,2,1:T(8,128)S(1)} %get-tuple-element.29), channel_id=1, source_target_pairs={{0,2},{2,4},{4,6},{6,8},{8,10},{10,12},{12,14},{14,16},{16,18},{18... | collective-permute-start | bytes 196616 | tf_op jit(solution)/shard_map/ppermute | solution.py:25
  34.8 4.6 %copy-start.10 = (f32[64,4,1,128]{3,0,2,1:T(8,128)}, f32[64,4,1,128]{3,0,2,1:T(8,128)S(1)}, u32[]{:S(2)}) copy-start(f32[64,4,1,128]{3,0,2,1:T(8,128)S(1)} %pad.53) | copy-start | bytes 393220
  38.3 1.1 copy-start.12
  39.9 1.0 copy-start.7
  40.6 1.4 %collective-permute-start.12 = (f32[4,64,64]{2,1,0:T(8,128)S(1)}, f32[4,64,64]{2,1,0:T(8,128)S(1)}, u32[]{:S(2)}, u32[]{:S(2)}) collective-permute-start(f32[4,64,64]{2,1,0:T(8,128)S(1)} %pad_maximum_fusion.29), channel_id=1, source_target_pairs={{0,32},{32,0},{64,96},{96,64},{128,160},{160,128},{192,224},{224,1... | collective-permute-start | bytes 196616 | tf_op jit(solution)/shard_map/ppermute | solution.py:46
  42.0 8.0 %collective-permute-start.14 = (f32[4,64,64]{2,1,0:T(8,128)S(1)}, f32[4,64,64]{2,1,0:T(8,128)S(1)}, u32[]{:S(2)}, u32[]{:S(2)}) collective-permute-start(f32[4,64,64]{2,1,0:T(8,128)S(1)} %fusion.60), channel_id=1, source_target_pairs={{0,128},{32,160},{64,192},{96,224},{128,0},{160,32},{192,64},{224,... | collective-permute-start | bytes 196616 | tf_op jit(solution)/shard_map/ppermute | solution.py:50
  42.1 9.8 %collective-permute-start.15 = (f32[4,64,64]{2,1,0:T(8,128)S(1)}, f32[4,64,64]{2,1,0:T(8,128)S(1)}, u32[]{:S(2)}, u32[]{:S(2)}) collective-permute-start(f32[4,64,64]{2,1,0:T(8,128)S(1)} %fusion.60), channel_id=1, source_target_pairs={{0,192},{32,224},{64,128},{96,160},{128,64},{160,96},{192,0},{224,... | collective-permute-start | bytes 196616 | tf_op jit(solution)/shard_map/ppermute | solution.py:50
  43.6 8.3 %collective-permute-start.13 = (f32[4,64,64]{2,1,0:T(8,128)S(1)}, f32[4,64,64]{2,1,0:T(8,128)S(1)}, u32[]{:S(2)}, u32[]{:S(2)}) collective-permute-start(f32[4,64,64]{2,1,0:T(8,128)S(1)} %fusion.60), channel_id=1, source_target_pairs={{0,64},{32,96},{64,0},{96,32},{128,192},{160,224},{192,128},{224,1... | collective-permute-start | bytes 196616 | tf_op jit(solution)/shard_map/ppermute | solution.py:50
  46.2 10.7 %collective-permute-start.24 = (f32[64,2,1,128]{3,0,2,1:T(8,128)S(1)}, f32[64,2,1,128]{3,0,2,1:T(8,128)}, u32[]{:S(2)}, u32[]{:S(2)}) collective-permute-start(f32[64,2,1,128]{3,0,2,1:T(8,128)S(1)} %get-tuple-element.26), channel_id=1, source_target_pairs={{2,0},{4,2},{6,4},{8,6},{10,8},{12,10},{14,12},{16,14},{18,16},{20... | collective-permute-start | bytes 196616 | tf_op jit(solution)/shard_map/ppermute | solution.py:26
  46.5 11.3 %collective-permute-start.25 = (f32[64,2,1,128]{3,0,2,1:T(8,128)}, f32[64,2,1,128]{3,0,2,1:T(8,128)}, u32[]{:S(2)}, u32[]{:S(2)}) collective-permute-start(f32[64,2,1,128]{3,0,2,1:T(8,128)} %get-tuple-element.25), channel_id=1, source_target_pairs={{0,2},{2,4},{4,6},{6,8},{8,10},{10,12},{12,14},{14,16},{16,18},{18... | collective-permute-start | bytes 196616 | tf_op jit(solution)/shard_map/ppermute | solution.py:25
  52.0 13.0 %collective-permute-start.17 = (f32[4,64,64]{2,1,0:T(8,128)S(1)}, f32[4,64,64]{2,1,0:T(8,128)S(1)}, u32[]{:S(2)}, u32[]{:S(2)}) collective-permute-start(f32[4,64,64]{2,1,0:T(8,128)S(1)} %add_add_fusion.2), channel_id=1, source_target_pairs={{0,4},{2,6},{4,0},{6,2},{8,12},{10,14},{12,8},{14,10},{16,20},{18,... | collective-permute-start | bytes 196616 | tf_op jit(solution)/shard_map/ppermute | solution.py:50
  52.8 12.2 %collective-permute-start.18 = (f32[4,64,64]{2,1,0:T(8,128)S(1)}, f32[4,64,64]{2,1,0:T(8,128)S(1)}, u32[]{:S(2)}, u32[]{:S(2)}) collective-permute-start(f32[4,64,64]{2,1,0:T(8,128)S(1)} %add_add_fusion.2), channel_id=1, source_target_pairs={{0,6},{2,4},{4,2},{6,0},{8,14},{10,12},{12,10},{14,8},{16,22},{18,... | collective-permute-start | bytes 196616 | tf_op jit(solution)/shard_map/ppermute | solution.py:50
  56.2 9.2 %collective-permute-start.16 = (f32[4,64,64]{2,1,0:T(8,128)S(1)}, f32[4,64,64]{2,1,0:T(8,128)S(1)}, u32[]{:S(2)}, u32[]{:S(2)}) collective-permute-start(f32[4,64,64]{2,1,0:T(8,128)S(1)} %add_add_fusion.2), channel_id=1, source_target_pairs={{0,2},{2,0},{4,6},{6,4},{8,10},{10,8},{12,14},{14,12},{16,18},{18,... | collective-permute-start | bytes 196616 | tf_op jit(solution)/shard_map/ppermute | solution.py:50
  56.9 16.0 %collective-permute-start.23 = (f32[64,1,8,128]{3,0,2,1:T(8,128)S(1)}, f32[64,1,8,128]{3,0,2,1:T(8,128)}, u32[]{:S(2)}, u32[]{:S(2)}) collective-permute-start(f32[64,1,8,128]{3,0,2,1:T(8,128)S(1)} %get-tuple-element.28), channel_id=1, source_target_pairs={{0,32},{32,64},{64,96},{96,128},{128,160},{160,192},{192,224},{224... | collective-permute-start | bytes 786440 | tf_op jit(solution)/shard_map/ppermute | solution.py:25
  57.8 18.0 %copy-start.14 = (f32[64,4,1,128]{3,0,2,1:T(8,128)}, f32[64,4,1,128]{3,0,2,1:T(8,128)S(1)}, u32[]{:S(2)}) copy-start(f32[64,4,1,128]{3,0,2,1:T(8,128)S(1)} %pad.56) | copy-start | bytes 393220
  57.8 17.3 %collective-permute-start.22 = (f32[64,1,8,128]{3,0,2,1:T(8,128)}, f32[64,1,8,128]{3,0,2,1:T(8,128)S(1)}, u32[]{:S(2)}, u32[]{:S(2)}) collective-permute-start(f32[64,1,8,128]{3,0,2,1:T(8,128)} %get-tuple-element.27), channel_id=1, source_target_pairs={{32,0},{64,32},{96,64},{128,96},{160,128},{192,160},{224,192},{0,2... | collective-permute-start | bytes 786440 | tf_op jit(solution)/shard_map/ppermute | solution.py:26
  61.6 14.2 %copy-start.16 = (f32[64,4,1,128]{3,0,2,1:T(8,128)}, f32[64,4,1,128]{3,0,2,1:T(8,128)S(1)}, u32[]{:S(2)}) copy-start(f32[64,4,1,128]{3,0,2,1:T(8,128)S(1)} %pad.57) | copy-start | bytes 393220
  65.4 12.7 %collective-permute-start.20 = (f32[4,64,64]{2,1,0:T(8,128)S(1)}, f32[4,64,64]{2,1,0:T(8,128)S(1)}, u32[]{:S(2)}, u32[]{:S(2)}) collective-permute-start(f32[4,64,64]{2,1,0:T(8,128)S(1)} %add_add_fusion.1), channel_id=1, source_target_pairs={{0,16},{2,18},{4,20},{6,22},{8,24},{10,26},{12,28},{14,30},{16,0},... | collective-permute-start | bytes 196616 | tf_op jit(solution)/shard_map/ppermute | solution.py:50
  66.3 11.9 %collective-permute-start.21 = (f32[4,64,64]{2,1,0:T(8,128)S(1)}, f32[4,64,64]{2,1,0:T(8,128)S(1)}, u32[]{:S(2)}, u32[]{:S(2)}) collective-permute-start(f32[4,64,64]{2,1,0:T(8,128)S(1)} %add_add_fusion.1), channel_id=1, source_target_pairs={{0,24},{2,26},{4,28},{6,30},{8,16},{10,18},{12,20},{14,22},{16,8},... | collective-permute-start | bytes 196616 | tf_op jit(solution)/shard_map/ppermute | solution.py:50
  66.3 16.7 %collective-permute-start.19 = (f32[4,64,64]{2,1,0:T(8,128)S(1)}, f32[4,64,64]{2,1,0:T(8,128)S(1)}, u32[]{:S(2)}, u32[]{:S(2)}) collective-permute-start(f32[4,64,64]{2,1,0:T(8,128)S(1)} %add_add_fusion.1), channel_id=1, source_target_pairs={{0,8},{2,10},{4,12},{6,14},{8,0},{10,2},{12,4},{14,6},{16,24},{18,... | collective-permute-start | bytes 196616 | tf_op jit(solution)/shard_map/ppermute | solution.py:50
  75.8 2.3 %copy-start.3 = (f32[64,4,8,128]{3,0,2,1:T(8,128)}, f32[64,4,8,128]{3,0,2,1:T(8,128)S(1)}, u32[]{:S(2)}) copy-start(f32[64,4,8,128]{3,0,2,1:T(8,128)S(1)} %constant_dynamic-update-slice_fusion) | copy-start | bytes 3145732
  83.7 16.5 %copy-start.6 = (f32[64,1,8,128]{3,0,2,1:T(8,128)S(1)}, f32[64,1,8,128]{3,0,2,1:T(8,128)}, u32[]{:S(2)}) copy-start(f32[64,1,8,128]{3,0,2,1:T(8,128)} %copy-done.5) | copy-start | bytes 786436
  83.7 16.5 %copy-start.11 = (f32[64,4,1,128]{3,0,2,1:T(8,128)S(1)}, f32[64,4,1,128]{3,0,2,1:T(8,128)}, u32[]{:S(2)}) copy-start(f32[64,4,1,128]{3,0,2,1:T(8,128)} %copy-done.10) | copy-start | bytes 393220
  83.7 16.5 %copy-start.13 = (f32[64,4,1,128]{3,0,2,1:T(8,128)S(1)}, f32[64,4,1,128]{3,0,2,1:T(8,128)}, u32[]{:S(2)}) copy-start(f32[64,4,1,128]{3,0,2,1:T(8,128)} %copy-done.12) | copy-start | bytes 393220
  100.2 2.2 %copy-start.1 = (f32[65,4,10,128]{3,0,2,1:T(8,128)S(1)}, f32[65,4,10,128]{3,0,2,1:T(8,128)}, u32[]{:S(2)}) copy-start(f32[65,4,10,128]{3,0,2,1:T(8,128)} %copy-done) | copy-start | bytes 3993604
  100.3 2.2 %copy-start.9 = (f32[64,4,1,128]{3,0,2,1:T(8,128)S(1)}, f32[64,4,1,128]{3,0,2,1:T(8,128)}, u32[]{:S(2)}) copy-start(f32[64,4,1,128]{3,0,2,1:T(8,128)} %copy-done.8) | copy-start | bytes 393220
  100.3 2.2 %copy-start.21 = (f32[2,64,64]{2,1,0:T(8,128)S(1)}, f32[2,64,64]{2,1,0:T(8,128)}, u32[]{:S(2)}) copy-start(f32[2,64,64]{2,1,0:T(8,128)} %shard_map.68) | copy-start | bytes 98308
  102.4 1.6 %copy-start.4 = (f32[64,4,8,128]{3,0,2,1:T(8,128)S(1)}, f32[64,4,8,128]{3,0,2,1:T(8,128)}, u32[]{:S(2)}) copy-start(f32[64,4,8,128]{3,0,2,1:T(8,128)} %copy-done.3) | copy-start | bytes 3145732
  102.4 1.6 %copy-start.15 = (f32[64,4,1,128]{3,0,2,1:T(8,128)S(1)}, f32[64,4,1,128]{3,0,2,1:T(8,128)}, u32[]{:S(2)}) copy-start(f32[64,4,1,128]{3,0,2,1:T(8,128)} %copy-done.14) | copy-start | bytes 393220
  102.5 1.6 %copy-start.17 = (f32[64,4,1,128]{3,0,2,1:T(8,128)S(1)}, f32[64,4,1,128]{3,0,2,1:T(8,128)}, u32[]{:S(2)}) copy-start(f32[64,4,1,128]{3,0,2,1:T(8,128)} %copy-done.16) | copy-start | bytes 393220
  102.5 2.1 %copy-start.2 = (f32[64,4,10,130]{3,0,2,1:T(8,128)S(1)}, f32[64,4,10,130]{3,0,2,1:T(8,128)}, u32[]{:S(2)}) copy-start(f32[64,4,10,130]{3,0,2,1:T(8,128)} %select_maximum_fusion) | copy-start | bytes 3993604
  104.6 0.9 copy-start.19
  106.9 5.2 %collective-permute-start.26 = (f32[2,8,64]{2,1,0:T(8,128)S(1)}, f32[2,8,64]{2,1,0:T(8,128)S(1)}, u32[]{:S(2)}, u32[]{:S(2)}) collective-permute-start(f32[2,8,64]{2,1,0:T(8,128)S(1)} %constant_dynamic-slice_fusion), channel_id=1, source_target_pairs={{0,1},{1,0},{2,3},{3,2},{4,5},{5,4},{6,7},{7,6},{8,9},{9,8},{10,11... | collective-permute-start | bytes 12296 | tf_op jit(solution)/shard_map/ppermute | solution.py:258
  (3 other events, 2.1 us)

commit v10 on v9

--- a/solution.py
+++ b/solution.py
@@ -152,20 +152,34 @@
     return [r for _, r in done]
 
 
-def steps_kernel(grams_ref, out_ref):
+def first_kernel(grams_ref, out_ref):
     g_rr = grams_ref[0]
     g_rq = grams_ref[1]
     g_qq = grams_ref[2]
-    g_qw = grams_ref[3]
     n = g_rr.shape[0]
     eye = (
         lax.broadcasted_iota(jnp.int32, (n, n), 0) == lax.broadcasted_iota(jnp.int32, (n, n), 1)
     ).astype(jnp.float32)
     step0, rr_inv = _solve([(g_rq, g_rr), (g_rr, eye)], True)
     cross = _mm(g_rq, step0)
+    new_gram = g_rr - cross - _tr(cross) + _mm(_tr(step0), _mm(g_qq, step0))
+    out_ref[0] = step0
+    out_ref[1] = _mm(rr_inv, new_gram)
+    out_ref[2] = new_gram
+
+
+def second_kernel(grams_ref, first_ref, last_ref, out_ref):
+    g_rq = grams_ref[1]
+    g_qq = grams_ref[2]
+    g_qw = last_ref[0]
+    step0 = first_ref[0]
+    turn = first_ref[1]
+    new_gram = first_ref[2]
+    n = g_rq.shape[0]
+    eye = (
+        lax.broadcasted_iota(jnp.int32, (n, n), 0) == lax.broadcasted_iota(jnp.int32, (n, n), 1)
+    ).astype(jnp.float32)
     step0_t = _tr(step0)
-    new_gram = g_rr - cross - _tr(cross) + _mm(step0_t, _mm(g_qq, step0))
-    turn = _mm(rr_inv, new_gram)
     keep = eye + turn
     keep_t = _tr(keep)
     curv = (
@@ -179,13 +193,18 @@
     out_ref[1] = -_mm(step0, step1)
 
 
-def steps(grams):
+def steps(grams, last):
     n = grams.shape[1]
+    first = pl.pallas_call(
+        first_kernel,
+        out_shape=jax.ShapeDtypeStruct((3, n, n), jnp.float32),
+        cost_estimate=pl.CostEstimate(flops=10_000_000_000, transcendentals=0, bytes_accessed=6 * n * n * 4),
+    )(grams)
     return pl.pallas_call(
-        steps_kernel,
+        second_kernel,
         out_shape=jax.ShapeDtypeStruct((2, n, n), jnp.float32),
-        cost_estimate=pl.CostEstimate(flops=20_000_000_000, transcendentals=0, bytes_accessed=6 * n * n * 4),
-    )(grams)
+        cost_estimate=pl.CostEstimate(flops=10_000_000_000, transcendentals=0, bytes_accessed=9 * n * n * 4),
+    )(grams, first, last)
 
 
 def on_device(conductivity, electrodes, pair_order, initial_fields, adjoint_fields):
@@ -217,23 +236,22 @@
     residual = right - operator(iter_pad, conds)
     res_pad = padded_2(residual, sides, 1)
     image = operator(res_pad, conds)
-    image_pad = padded_2(image, sides, 1)
-    image2 = operator(image_pad, conds)
-    image2, adjoint_late = lax.optimization_barrier((image2, adjoint_fields))
-    adjoint_pad = padded_2(adjoint_late, sides, 1)
     grams = allsum(
         jnp.stack(
             [
                 gram_of(residual, residual),
                 gram_of(residual, image),
                 gram_of(image, image),
-                gram_of(image, image2),
             ]
         ),
         grid_axes,
     )
-
-    solved = steps(grams)
+    image_pad = padded_2(image, sides, 1)
+    image2 = operator(image_pad, conds)
+    image2, adjoint_late = lax.optimization_barrier((image2, adjoint_fields))
+    adjoint_pad = padded_2(adjoint_late, sides, 1)
+    last = allsum(gram_of(image, image2)[None], grid_axes)
+    solved = steps(grams, last)
     it2_pad = iter_pad + combine_cols(res_pad, solved[0]) + combine_cols(image_pad, solved[1])
     iterate = it2_pad[:, 1:-1, 1:-1]
     term_x, term_y, term_z = face_terms(it2_pad, adjoint_pad)

time: 113 us -> 128 us (1.13)
  starting transfers between devices: 36.1 us -> 50 us
  local copies, waits for them, and re-layouts: 10.4 us -> 6.72 us
  waiting for transfers between devices: 30.7 us -> 32.7 us
  Pallas kernels: 16.5 us -> 17.9 us
    ppermute x9 -> x18, starting transfers between devices: 15.2 us -> 29.4 us  [allsum(): lax.ppermute(value, axis, [(i, i ^ d << shift) for i in range(count)])]
    ppermute x9 -> x18, waiting for transfers between devices: 12.3 us -> 18.1 us  [allsum(): lax.ppermute(value, axis, [(i, i ^ d << shift) for i in range(count)])]
    ppermute x8, waiting for transfers between devices: 12.6 us -> 8.52 us  [padded_2(): low = lax.ppermute(top, axis, forward)]
    unnamed x53 -> x25, local copies, waits for them, and re-layouts: 7.56 us -> 4.61 us
    add x3 -> x6, other arithmetic: 0.75 us -> 3.06 us  [allsum(): value = value + got[0] + (got[1] + got[2])]
    concatenate x4, other arithmetic: 2.64 us -> 1.14 us  [padded_2(): return jnp.concatenate([low_y, middle, high_y], axis=dim_y)]
    pallas_call x1 -> x2, Pallas kernels: 16.5 us -> 17.9 us  [the longest x1 9.05 us: steps(): pl.pallas_call(first_kernel, out_shape=jax.ShapeDtypeStruct((3, n, n), jn...]
  transfers between devices with their start and end apart: 27 -> 37, of which waited for: 14 -> 15; matrix products, arithmetic and copies ran while one was open for 11% -> 10% of each run, Pallas kernels for 0% -> 14%
where the time goes in v10:
time: 128 us; the launch traced here: 127 us
  starting transfers between devices  50 us (39%)
  waiting for transfers between devices  32.7 us (26%)
  Pallas kernels  17.9 us (14%)
  other arithmetic  12.8 us (10%)
  local copies, waits for them, and re-layouts  6.72 us (5%)
  matrix products  5.89 us (5%)
  between operations  1.29 us (1%)
    ppermute x18, starting transfers between devices, allsum(): lax.ppermute(value, axis, [(i, i ^ d << shift) for i in range(count)])  29.4 us
    ppermute x18, waiting for transfers between devices, allsum(): lax.ppermute(value, axis, [(i, i ^ d << shift) for i in range(count)])  18.1 us
    ppermute x8, starting transfers between devices, padded_2(): high = lax.ppermute(bottom, axis, backward)  14.7 us
    pallas_call x1, Pallas kernels, steps(): pl.pallas_call(first_kernel, out_shape=jax.ShapeDtypeStruct((3, n, n), jn...  9.05 us
    pallas_call x1, Pallas kernels, steps(): pl.pallas_call(second_kernel, out_shape=jax.ShapeDtypeStruct((2, n, n), j...  8.88 us
    ppermute x8, waiting for transfers between devices, padded_2(): low = lax.ppermute(top, axis, forward)  8.52 us
    ppermute x8, starting transfers between devices, padded_2(): low = lax.ppermute(top, axis, forward)  4.77 us
    unnamed x25, local copies, waits for them, and re-layouts  4.61 us
  transfers between devices with their start and end apart: 37, of which 15 were waited for; matrix products, arithmetic and copies ran while one was open for 10% of the time, Pallas kernels for 14%

profile of v10, /device:TPU:4, one launch (start us, length us, event | category | flops | bytes accessed | tf_op | source)
XLA Modules:
  0.0 127.3 jit_solution(16550814140760206145)
XLA Ops:
  0.7 1.2 copy.35
  2.6 6.6 %collective-permute-start.3 = (f32[65,2,1,128]{3,0,2,1:T(8,128)S(1)}, f32[65,2,1,128]{3,0,2,1:T(8,128)S(1)}, u32[]{:S(2)}, u32[]{:S(2)}) collective-permute-start(f32[65,2,1,128]{3,0,2,1:T(8,128)S(1)} %get-tuple-element.22), channel_id=1, source_target_pairs={{2,0},{4,2},{6,4},{8,6},{10,8},{12,10},{14,12},{16,14},{18,16},{20... | collective-permute-start | bytes 199688 | tf_op jit(solution)/shard_map/ppermute | solution.py:26
  9.3 2.2 %collective-permute-start.2 = (f32[65,1,8,128]{3,0,2,1:T(8,128)S(1)}, f32[65,1,8,128]{3,0,2,1:T(8,128)S(1)}, u32[]{:S(2)}, u32[]{:S(2)}) collective-permute-start(f32[65,1,8,128]{3,0,2,1:T(8,128)S(1)} %get-tuple-element.24), channel_id=1, source_target_pairs={{32,0},{64,32},{96,64},{128,96},{160,128},{192,160},{224,192},{0,2... | collective-permute-start | bytes 798728 | tf_op jit(solution)/shard_map/ppermute | solution.py:26
  12.9 5.0 %collective-permute-done = f32[65,2,1,128]{3,0,2,1:T(8,128)S(1)} collective-permute-done((f32[65,2,1,128]{3,0,2,1:T(8,128)S(1)}, f32[65,2,1,128]{3,0,2,1:T(8,128)S(1)}, u32[]{:S(2)}, u32[]{:S(2)}) %collective-permute-start) | collective-permute-done | bytes 66592 | tf_op jit(solution)/shard_map/ppermute | solution.py:25
  17.9 0.9 collective-permute-done.1
  19.3 0.9 copy-done
  21.3 1.0 collective-permute-start.4
  22.9 1.5 %collective-permute-start.7 = (f32[64,2,1,128]{3,0,2,1:T(8,128)S(1)}, f32[64,2,1,128]{3,0,2,1:T(8,128)S(1)}, u32[]{:S(2)}, u32[]{:S(2)}) collective-permute-start(f32[64,2,1,128]{3,0,2,1:T(8,128)S(1)} %get-tuple-element.33), channel_id=1, source_target_pairs={{0,2},{2,4},{4,6},{6,8},{8,10},{10,12},{12,14},{14,16},{16,18},{18... | collective-permute-start | bytes 196616 | tf_op jit(solution)/shard_map/ppermute | solution.py:25
  24.9 1.7 %collective-permute-done.6 = f32[64,2,1,128]{3,0,2,1:T(8,128)S(1)} collective-permute-done((f32[64,2,1,128]{3,0,2,1:T(8,128)S(1)}, f32[64,2,1,128]{3,0,2,1:T(8,128)S(1)}, u32[]{:S(2)}, u32[]{:S(2)}) %collective-permute-start.6) | collective-permute-done | bytes 65568 | tf_op jit(solution)/shard_map/ppermute | solution.py:26
  26.6 2.7 %collective-permute-done.7 = f32[64,2,1,128]{3,0,2,1:T(8,128)S(1)} collective-permute-done((f32[64,2,1,128]{3,0,2,1:T(8,128)S(1)}, f32[64,2,1,128]{3,0,2,1:T(8,128)S(1)}, u32[]{:S(2)}, u32[]{:S(2)}) %collective-permute-start.7) | collective-permute-done | bytes 65568 | tf_op jit(solution)/shard_map/ppermute | solution.py:25
  31.6 1.3 %collective-permute-done.8 = f32[3,64,64]{2,1,0:T(8,128)S(1)} collective-permute-done((f32[3,64,64]{2,1,0:T(8,128)S(1)}, f32[3,64,64]{2,1,0:T(8,128)S(1)}, u32[]{:S(2)}, u32[]{:S(2)}) %collective-permute-start.8) | collective-permute-done | bytes 49184 | tf_op jit(solution)/shard_map/ppermute | solution.py:46
  32.9 1.0 collective-permute-start.10
  34.7 1.8 %collective-permute-start.9 = (f32[3,64,64]{2,1,0:T(8,128)S(1)}, f32[3,64,64]{2,1,0:T(8,128)S(1)}, u32[]{:S(2)}, u32[]{:S(2)}) collective-permute-start(f32[3,64,64]{2,1,0:T(8,128)S(1)} %fusion.60), channel_id=1, source_target_pairs={{0,64},{32,96},{64,0},{96,32},{128,192},{160,224},{192,128},{224,1... | collective-permute-start | bytes 147464 | tf_op jit(solution)/shard_map/ppermute | solution.py:50
  36.6 2.0 %collective-permute-start.21 = (f32[64,2,1,128]{3,0,2,1:T(8,128)S(1)}, f32[64,2,1,128]{3,0,2,1:T(8,128)S(1)}, u32[]{:S(2)}, u32[]{:S(2)}) collective-permute-start(f32[64,2,1,128]{3,0,2,1:T(8,128)S(1)} %get-tuple-element.29), channel_id=1, source_target_pairs={{0,2},{2,4},{4,6},{6,8},{8,10},{10,12},{12,14},{14,16},{16,18},{18... | collective-permute-start | bytes 196616 | tf_op jit(solution)/shard_map/ppermute | solution.py:25
  38.6 1.4 %collective-permute-done.10 = f32[3,64,64]{2,1,0:T(8,128)S(1)} collective-permute-done((f32[3,64,64]{2,1,0:T(8,128)S(1)}, f32[3,64,64]{2,1,0:T(8,128)S(1)}, u32[]{:S(2)}, u32[]{:S(2)}) %collective-permute-start.10) | collective-permute-done | bytes 49184 | tf_op jit(solution)/shard_map/ppermute | solution.py:50
  40.0 1.5 %collective-permute-done.11 = f32[3,64,64]{2,1,0:T(8,128)S(1)} collective-permute-done((f32[3,64,64]{2,1,0:T(8,128)S(1)}, f32[3,64,64]{2,1,0:T(8,128)S(1)}, u32[]{:S(2)}, u32[]{:S(2)}) %collective-permute-start.11) | collective-permute-done | bytes 49184 | tf_op jit(solution)/shard_map/ppermute | solution.py:50
  41.6 1.7 %collective-permute-start.14 = (f32[3,64,64]{2,1,0:T(8,128)S(1)}, f32[3,64,64]{2,1,0:T(8,128)S(1)}, u32[]{:S(2)}, u32[]{:S(2)}) collective-permute-start(f32[3,64,64]{2,1,0:T(8,128)S(1)} %add_add_fusion.2), channel_id=1, source_target_pairs={{0,6},{2,4},{4,2},{6,0},{8,14},{10,12},{12,10},{14,8},{16,22},{18,... | collective-permute-start | bytes 147464 | tf_op jit(solution)/shard_map/ppermute | solution.py:50
  43.3 1.8 %collective-permute-start.12 = (f32[3,64,64]{2,1,0:T(8,128)S(1)}, f32[3,64,64]{2,1,0:T(8,128)}, u32[]{:S(2)}, u32[]{:S(2)}) collective-permute-start(f32[3,64,64]{2,1,0:T(8,128)S(1)} %add_add_fusion.2), channel_id=1, source_target_pairs={{0,2},{2,0},{4,6},{6,4},{8,10},{10,8},{12,14},{14,12},{16,18},{18,... | collective-permute-start | bytes 147464 | tf_op jit(solution)/shard_map/ppermute | solution.py:50
  45.7 4.6 %collective-permute-done.13 = f32[3,64,64]{2,1,0:T(8,128)S(1)} collective-permute-done((f32[3,64,64]{2,1,0:T(8,128)S(1)}, f32[3,64,64]{2,1,0:T(8,128)S(1)}, u32[]{:S(2)}, u32[]{:S(2)}) %collective-permute-start.13) | collective-permute-done | bytes 49184 | tf_op jit(solution)/shard_map/ppermute | solution.py:50
  50.4 1.4 %collective-permute-done.12 = f32[3,64,64]{2,1,0:T(8,128)} collective-permute-done((f32[3,64,64]{2,1,0:T(8,128)S(1)}, f32[3,64,64]{2,1,0:T(8,128)}, u32[]{:S(2)}, u32[]{:S(2)}) %collective-permute-start.12) | collective-permute-done | bytes 49184 | tf_op jit(solution)/shard_map/ppermute | solution.py:50
  51.8 0.9 add_add_fusion.1
  52.7 0.9 collective-permute-start.16
  53.6 1.4 %collective-permute-start.17 = (f32[3,64,64]{2,1,0:T(8,128)S(1)}, f32[3,64,64]{2,1,0:T(8,128)S(1)}, u32[]{:S(2)}, u32[]{:S(2)}) collective-permute-start(f32[3,64,64]{2,1,0:T(8,128)S(1)} %add_add_fusion.1), channel_id=1, source_target_pairs={{0,24},{2,26},{4,28},{6,30},{8,16},{10,18},{12,20},{14,22},{16,8},... | collective-permute-start | bytes 147464 | tf_op jit(solution)/shard_map/ppermute | solution.py:50
  55.0 5.2 %collective-permute-start.15 = (f32[3,64,64]{2,1,0:T(8,128)S(1)}, f32[3,64,64]{2,1,0:T(8,128)S(1)}, u32[]{:S(2)}, u32[]{:S(2)}) collective-permute-start(f32[3,64,64]{2,1,0:T(8,128)S(1)} %add_add_fusion.1), channel_id=1, source_target_pairs={{0,8},{2,10},{4,12},{6,14},{8,0},{10,2},{12,4},{14,6},{16,24},{18,... | collective-permute-start | bytes 147464 | tf_op jit(solution)/shard_map/ppermute | solution.py:50
  61.8 4.0 %collective-permute-done.17 = f32[3,64,64]{2,1,0:T(8,128)S(1)} collective-permute-done((f32[3,64,64]{2,1,0:T(8,128)S(1)}, f32[3,64,64]{2,1,0:T(8,128)S(1)}, u32[]{:S(2)}, u32[]{:S(2)}) %collective-permute-start.17) | collective-permute-done | bytes 49184 | tf_op jit(solution)/shard_map/ppermute | solution.py:50
  65.8 2.4 %collective-permute-done.15 = f32[3,64,64]{2,1,0:T(8,128)S(1)} collective-permute-done((f32[3,64,64]{2,1,0:T(8,128)S(1)}, f32[3,64,64]{2,1,0:T(8,128)S(1)}, u32[]{:S(2)}, u32[]{:S(2)}) %collective-permute-start.15) | collective-permute-done | bytes 49184 | tf_op jit(solution)/shard_map/ppermute | solution.py:50
  69.5 1.5 %collective-permute-start.24 = (f32[1,64,64]{2,1,0:T(8,128)}, f32[1,64,64]{2,1,0:T(8,128)}, u32[]{:S(2)}, u32[]{:S(2)}) collective-permute-start(f32[1,64,64]{2,1,0:T(8,128)} %add.238), channel_id=1, source_target_pairs={{0,128},{32,160},{64,192},{96,224},{128,0},{160,32},{192,64},{224,... | collective-permute-start | bytes 49160 | tf_op jit(solution)/shard_map/ppermute | solution.py:50
  71.3 1.7 %collective-permute-start.23 = (f32[1,64,64]{2,1,0:T(8,128)}, f32[1,64,64]{2,1,0:T(8,128)}, u32[]{:S(2)}, u32[]{:S(2)}) collective-permute-start(f32[1,64,64]{2,1,0:T(8,128)} %add.238), channel_id=1, source_target_pairs={{0,64},{32,96},{64,0},{96,32},{128,192},{160,224},{192,128},{224,1... | collective-permute-start | bytes 49160 | tf_op jit(solution)/shard_map/ppermute | solution.py:50
  73.0 9.0 %shard_map.68.first_ref = f32[3,64,64]{2,1,0:T(8,128)} custom-call(f32[3,64,64]{2,1,0:T(8,128)} %add_add_fusion.grams_ref), custom_call_target="tpu_custom_call" | custom-call | flops 10000000000 | bytes 98304 | tf_op jit(solution)/shard_map/pallas_call | solution.py:198
  82.2 0.8 add_add_fusion.5
  83.2 3.2 %collective-permute-start.28 = (f32[1,64,64]{2,1,0:T(8,128)S(1)}, f32[1,64,64]{2,1,0:T(8,128)S(1)}, u32[]{:S(2)}, u32[]{:S(2)}) collective-permute-start(f32[1,64,64]{2,1,0:T(8,128)S(1)} %add_add_fusion.5), channel_id=1, source_target_pairs={{0,6},{2,4},{4,2},{6,0},{8,14},{10,12},{12,10},{14,8},{16,22},{18,... | collective-permute-start | bytes 49160 | tf_op jit(solution)/shard_map/ppermute | solution.py:50
  86.6 0.9 slice_select_fusion.1
  88.1 0.9 collective-permute-done.28
  89.0 1.3 %collective-permute-done.26 = f32[1,64,64]{2,1,0:T(8,128)S(1)} collective-permute-done((f32[1,64,64]{2,1,0:T(8,128)S(1)}, f32[1,64,64]{2,1,0:T(8,128)S(1)}, u32[]{:S(2)}, u32[]{:S(2)}) %collective-permute-start.26) | collective-permute-done | bytes 16416 | tf_op jit(solution)/shard_map/ppermute | solution.py:50
  90.3 1.1 collective-permute-start.30
  91.4 2.8 %collective-permute-start.31 = (f32[1,64,64]{2,1,0:T(8,128)S(1)}, f32[1,64,64]{2,1,0:T(8,128)S(1)}, u32[]{:S(2)}, u32[]{:S(2)}) collective-permute-start(f32[1,64,64]{2,1,0:T(8,128)S(1)} %add_add_fusion.4), channel_id=1, source_target_pairs={{0,24},{2,26},{4,28},{6,30},{8,16},{10,18},{12,20},{14,22},{16,8},... | collective-permute-start | bytes 49160 | tf_op jit(solution)/shard_map/ppermute | solution.py:50
  94.2 3.8 %collective-permute-start.29 = (f32[1,64,64]{2,1,0:T(8,128)S(1)}, f32[1,64,64]{2,1,0:T(8,128)S(1)}, u32[]{:S(2)}, u32[]{:S(2)}) collective-permute-start(f32[1,64,64]{2,1,0:T(8,128)S(1)} %add_add_fusion.4), channel_id=1, source_target_pairs={{0,8},{2,10},{4,12},{6,14},{8,0},{10,2},{12,4},{14,6},{16,24},{18,... | collective-permute-start | bytes 49160 | tf_op jit(solution)/shard_map/ppermute | solution.py:50
  98.0 1.3 %collective-permute-start.34 = (f32[64,2,1,128]{3,0,2,1:T(8,128)S(1)}, f32[64,2,1,128]{3,0,2,1:T(8,128)S(1)}, u32[]{:S(2)}, u32[]{:S(2)}) collective-permute-start(f32[64,2,1,128]{3,0,2,1:T(8,128)S(1)} %get-tuple-element.26), channel_id=1, source_target_pairs={{2,0},{4,2},{6,4},{8,6},{10,8},{12,10},{14,12},{16,14},{18,16},{20... | collective-permute-start | bytes 196616 | tf_op jit(solution)/shard_map/ppermute | solution.py:26
  99.3 3.0 %collective-permute-start.32 = (f32[64,1,8,128]{3,0,2,1:T(8,128)}, f32[64,1,8,128]{3,0,2,1:T(8,128)}, u32[]{:S(2)}, u32[]{:S(2)}) collective-permute-start(f32[64,1,8,128]{3,0,2,1:T(8,128)} %get-tuple-element.27), channel_id=1, source_target_pairs={{32,0},{64,32},{96,64},{128,96},{160,128},{192,160},{224,192},{0,2... | collective-permute-start | bytes 786440 | tf_op jit(solution)/shard_map/ppermute | solution.py:26
  103.7 8.9 %shard_map.69 = f32[2,64,64]{2,1,0:T(8,128)} custom-call(f32[3,64,64]{2,1,0:T(8,128)} %add_add_fusion.grams_ref, f32[3,64,64]{2,1,0:T(8,128)} %shard_map.68.first_ref, f32[1,64,64]{2,1,0:T(8,128)} %add_add_fusion.3.last_ref), custom_call_target="tpu_custom_call" | custom-call | flops 10000000000 | bytes 147456 | tf_op jit(solution)/shard_map/pallas_call | solution.py:203
  112.6 2.1 %fusion.48 = f32[64,4,10,128]{3,0,2,1:T(8,128)S(1)} fusion(f32[2,64,64]{2,1,0:T(8,128)} %shard_map.69, f32[64,4,1,128]{3,0,2,1:T(8,128)S(1)} %pad.53, f32[64,1,8,128]{3,0,2,1:T(8,128)S(1)} %collective-permute-done.18, f32[64,2,8,128]{3,0,2,1:T(8,128)S(1)} %fusion.28, f32[64,1,8,128]{3,0,2,1:T(8,128)S(1)} %collective-permute-done.19, ...), kind=kOutput, calls=%fused_computation.157 | convolution fusion | flops 252968960 | bytes 2654208 | tf_op jit(solution)/shard_map/axyz,ab->bxyz/dot_general | solution.py:84
  114.8 1.5 %fusion.1 = f32[64,4,10,128]{3,0,2,1:T(8,128)S(1)} fusion(f32[64,4,10,128]{3,0,2,1:T(8,128)S(1)} %fusion.48, f32[2,64,64]{2,1,0:T(8,128)S(1)} %copy-done.7, f32[65,4,10,128]{3,0,2,1:T(8,128)S(1)} %copy-done.1, f32[64,4,1,128]{3,0,2,1:T(8,128)S(1)} %pad.50, f32[64,1,8,128]{3,0,2,1:T(8,128)S(1)} %collective-permute-done.4, f32[64,2,8,128]{3,0,2,1:T(8,128)S(1)} %fusion.31, ...), kind=kOutput, calls=%fused_computation.16 | convolution fusion | flops 253624320 | bytes 5275648 | tf_op jit(solution)/shard_map/axyz,ab->bxyz/dot_general | solution.py:84
  116.3 1.0 constant_dynamic-update-slice_fusion.2
  117.5 1.0 constant_dynamic-update-slice_fusion
  120.0 1.3 fusion.12
  121.4 0.9 collective-permute-start.36
  122.4 1.1 copy.50
  123.5 3.1 %collective-permute-done.36 = f32[2,8,64]{2,1,0:T(8,128)S(1)} collective-permute-done((f32[2,8,64]{2,1,0:T(8,128)S(1)}, f32[2,8,64]{2,1,0:T(8,128)S(1)}, u32[]{:S(2)}, u32[]{:S(2)}) %collective-permute-start.36) | collective-permute-done | bytes 4128 | tf_op jit(solution)/shard_map/ppermute | solution.py:276
  (131 shorter events, 17.1 us)
Async XLA Ops:
  0.6 8.6 %copy-start.6 = (f32[2,8,128]{2,1,0:T(8,128)S(1)}, f32[2,8,128]{2,1,0:T(8,128)}, u32[]{:S(2)}) copy-start(f32[2,8,128]{2,1,0:T(8,128)} %param.5) | copy-start | bytes 24580
  0.6 10.8 %copy-start.9 = (s32[64]{0:T(128)S(1)}, s32[64]{0:T(128)}, u32[]{:S(2)}) copy-start(s32[64]{0:T(128)} %param.7) | copy-start | bytes 772
  0.7 10.8 %copy-start.8 = (s32[128,2]{0,1:T(2,128)S(1)}, s32[128,2]{0,1:T(2,128)}, u32[]{:S(2)}) copy-start(s32[128,2]{0,1:T(2,128)} %param.6) | copy-start | bytes 3076
  2.6 10.3 %collective-permute-start.3 = (f32[65,2,1,128]{3,0,2,1:T(8,128)S(1)}, f32[65,2,1,128]{3,0,2,1:T(8,128)S(1)}, u32[]{:S(2)}, u32[]{:S(2)}) collective-permute-start(f32[65,2,1,128]{3,0,2,1:T(8,128)S(1)} %get-tuple-element.22), channel_id=1, source_target_pairs={{2,0},{4,2},{6,4},{8,6},{10,8},{12,10},{14,12},{16,14},{18,16},{20... | collective-permute-start | bytes 199688 | tf_op jit(solution)/shard_map/ppermute | solution.py:26
  9.3 8.7 %collective-permute-start.2 = (f32[65,1,8,128]{3,0,2,1:T(8,128)S(1)}, f32[65,1,8,128]{3,0,2,1:T(8,128)S(1)}, u32[]{:S(2)}, u32[]{:S(2)}) collective-permute-start(f32[65,1,8,128]{3,0,2,1:T(8,128)S(1)} %get-tuple-element.24), channel_id=1, source_target_pairs={{32,0},{64,32},{96,64},{128,96},{160,128},{192,160},{224,192},{0,2... | collective-permute-start | bytes 798728 | tf_op jit(solution)/shard_map/ppermute | solution.py:26
  11.5 7.4 %collective-permute-start.1 = (f32[65,1,8,128]{3,0,2,1:T(8,128)S(1)}, f32[65,1,8,128]{3,0,2,1:T(8,128)S(1)}, u32[]{:S(2)}, u32[]{:S(2)}) collective-permute-start(f32[65,1,8,128]{3,0,2,1:T(8,128)S(1)} %get-tuple-element.23), channel_id=1, source_target_pairs={{0,32},{32,64},{64,96},{96,128},{128,160},{160,192},{192,224},{224... | collective-permute-start | bytes 798728 | tf_op jit(solution)/shard_map/ppermute | solution.py:25
  11.5 6.5 %collective-permute-start = (f32[65,2,1,128]{3,0,2,1:T(8,128)S(1)}, f32[65,2,1,128]{3,0,2,1:T(8,128)S(1)}, u32[]{:S(2)}, u32[]{:S(2)}) collective-permute-start(f32[65,2,1,128]{3,0,2,1:T(8,128)S(1)} %get-tuple-element.21), channel_id=1, source_target_pairs={{0,2},{2,4},{4,6},{6,8},{8,10},{10,12},{12,14},{14,16},{16,18},{18... | collective-permute-start | bytes 199688 | tf_op jit(solution)/shard_map/ppermute | solution.py:25
  19.0 1.1 copy-start
  21.3 8.0 %collective-permute-start.4 = (f32[64,1,8,128]{3,0,2,1:T(8,128)S(1)}, f32[64,1,8,128]{3,0,2,1:T(8,128)S(1)}, u32[]{:S(2)}, u32[]{:S(2)}) collective-permute-start(f32[64,1,8,128]{3,0,2,1:T(8,128)S(1)} %get-tuple-element.36), channel_id=1, source_target_pairs={{32,0},{64,32},{96,64},{128,96},{160,128},{192,160},{224,192},{0,2... | collective-permute-start | bytes 786440 | tf_op jit(solution)/shard_map/ppermute | solution.py:26
  22.2 7.1 %collective-permute-start.5 = (f32[64,1,8,128]{3,0,2,1:T(8,128)S(1)}, f32[64,1,8,128]{3,0,2,1:T(8,128)S(1)}, u32[]{:S(2)}, u32[]{:S(2)}) collective-permute-start(f32[64,1,8,128]{3,0,2,1:T(8,128)S(1)} %get-tuple-element.35), channel_id=1, source_target_pairs={{0,32},{32,64},{64,96},{96,128},{128,160},{160,192},{192,224},{224... | collective-permute-start | bytes 786440 | tf_op jit(solution)/shard_map/ppermute | solution.py:25
  22.2 4.3 %collective-permute-start.6 = (f32[64,2,1,128]{3,0,2,1:T(8,128)S(1)}, f32[64,2,1,128]{3,0,2,1:T(8,128)S(1)}, u32[]{:S(2)}, u32[]{:S(2)}) collective-permute-start(f32[64,2,1,128]{3,0,2,1:T(8,128)S(1)} %get-tuple-element.34), channel_id=1, source_target_pairs={{2,0},{4,2},{6,4},{8,6},{10,8},{12,10},{14,12},{16,14},{18,16},{20... | collective-permute-start | bytes 196616 | tf_op jit(solution)/shard_map/ppermute | solution.py:26
  22.9 6.4 %collective-permute-start.7 = (f32[64,2,1,128]{3,0,2,1:T(8,128)S(1)}, f32[64,2,1,128]{3,0,2,1:T(8,128)S(1)}, u32[]{:S(2)}, u32[]{:S(2)}) collective-permute-start(f32[64,2,1,128]{3,0,2,1:T(8,128)S(1)} %get-tuple-element.33), channel_id=1, source_target_pairs={{0,2},{2,4},{4,6},{6,8},{8,10},{10,12},{12,14},{14,16},{16,18},{18... | collective-permute-start | bytes 196616 | tf_op jit(solution)/shard_map/ppermute | solution.py:25
  29.3 0.6 copy-start.4
  31.5 1.4 %collective-permute-start.8 = (f32[3,64,64]{2,1,0:T(8,128)S(1)}, f32[3,64,64]{2,1,0:T(8,128)S(1)}, u32[]{:S(2)}, u32[]{:S(2)}) collective-permute-start(f32[3,64,64]{2,1,0:T(8,128)S(1)} %pad_maximum_fusion.29), channel_id=1, source_target_pairs={{0,32},{32,0},{64,96},{96,64},{128,160},{160,128},{192,224},{224,1... | collective-permute-start | bytes 147464 | tf_op jit(solution)/shard_map/ppermute | solution.py:46
  32.9 7.1 %collective-permute-start.10 = (f32[3,64,64]{2,1,0:T(8,128)S(1)}, f32[3,64,64]{2,1,0:T(8,128)S(1)}, u32[]{:S(2)}, u32[]{:S(2)}) collective-permute-start(f32[3,64,64]{2,1,0:T(8,128)S(1)} %fusion.60), channel_id=1, source_target_pairs={{0,128},{32,160},{64,192},{96,224},{128,0},{160,32},{192,64},{224,... | collective-permute-start | bytes 147464 | tf_op jit(solution)/shard_map/ppermute | solution.py:50
  33.9 7.6 %collective-permute-start.11 = (f32[3,64,64]{2,1,0:T(8,128)S(1)}, f32[3,64,64]{2,1,0:T(8,128)S(1)}, u32[]{:S(2)}, u32[]{:S(2)}) collective-permute-start(f32[3,64,64]{2,1,0:T(8,128)S(1)} %fusion.60), channel_id=1, source_target_pairs={{0,192},{32,224},{64,128},{96,160},{128,64},{160,96},{192,0},{224,... | collective-permute-start | bytes 147464 | tf_op jit(solution)/shard_map/ppermute | solution.py:50
  34.7 6.8 %collective-permute-start.9 = (f32[3,64,64]{2,1,0:T(8,128)S(1)}, f32[3,64,64]{2,1,0:T(8,128)S(1)}, u32[]{:S(2)}, u32[]{:S(2)}) collective-permute-start(f32[3,64,64]{2,1,0:T(8,128)S(1)} %fusion.60), channel_id=1, source_target_pairs={{0,64},{32,96},{64,0},{96,32},{128,192},{160,224},{192,128},{224,1... | collective-permute-start | bytes 147464 | tf_op jit(solution)/shard_map/ppermute | solution.py:50
  36.5 8.6 %collective-permute-start.20 = (f32[64,2,1,128]{3,0,2,1:T(8,128)S(1)}, f32[64,2,1,128]{3,0,2,1:T(8,128)S(1)}, u32[]{:S(2)}, u32[]{:S(2)}) collective-permute-start(f32[64,2,1,128]{3,0,2,1:T(8,128)S(1)} %get-tuple-element.30), channel_id=1, source_target_pairs={{2,0},{4,2},{6,4},{8,6},{10,8},{12,10},{14,12},{16,14},{18,16},{20... | collective-permute-start | bytes 196616 | tf_op jit(solution)/shard_map/ppermute | solution.py:26
  36.6 8.6 %collective-permute-start.21 = (f32[64,2,1,128]{3,0,2,1:T(8,128)S(1)}, f32[64,2,1,128]{3,0,2,1:T(8,128)S(1)}, u32[]{:S(2)}, u32[]{:S(2)}) collective-permute-start(f32[64,2,1,128]{3,0,2,1:T(8,128)S(1)} %get-tuple-element.29), channel_id=1, source_target_pairs={{0,2},{2,4},{4,6},{6,8},{8,10},{10,12},{12,14},{14,16},{16,18},{18... | collective-permute-start | bytes 196616 | tf_op jit(solution)/shard_map/ppermute | solution.py:25
  41.5 8.8 %collective-permute-start.13 = (f32[3,64,64]{2,1,0:T(8,128)S(1)}, f32[3,64,64]{2,1,0:T(8,128)S(1)}, u32[]{:S(2)}, u32[]{:S(2)}) collective-permute-start(f32[3,64,64]{2,1,0:T(8,128)S(1)} %add_add_fusion.2), channel_id=1, source_target_pairs={{0,4},{2,6},{4,0},{6,2},{8,12},{10,14},{12,8},{14,10},{16,20},{18,... | collective-permute-start | bytes 147464 | tf_op jit(solution)/shard_map/ppermute | solution.py:50
  41.6 8.7 %collective-permute-start.14 = (f32[3,64,64]{2,1,0:T(8,128)S(1)}, f32[3,64,64]{2,1,0:T(8,128)S(1)}, u32[]{:S(2)}, u32[]{:S(2)}) collective-permute-start(f32[3,64,64]{2,1,0:T(8,128)S(1)} %add_add_fusion.2), channel_id=1, source_target_pairs={{0,6},{2,4},{4,2},{6,0},{8,14},{10,12},{12,10},{14,8},{16,22},{18,... | collective-permute-start | bytes 147464 | tf_op jit(solution)/shard_map/ppermute | solution.py:50
  43.3 8.5 %collective-permute-start.12 = (f32[3,64,64]{2,1,0:T(8,128)S(1)}, f32[3,64,64]{2,1,0:T(8,128)}, u32[]{:S(2)}, u32[]{:S(2)}) collective-permute-start(f32[3,64,64]{2,1,0:T(8,128)S(1)} %add_add_fusion.2), channel_id=1, source_target_pairs={{0,2},{2,0},{4,6},{6,4},{8,10},{10,8},{12,14},{14,12},{16,18},{18,... | collective-permute-start | bytes 147464 | tf_op jit(solution)/shard_map/ppermute | solution.py:50
  45.2 15.1 %collective-permute-start.18 = (f32[64,1,8,128]{3,0,2,1:T(8,128)S(1)}, f32[64,1,8,128]{3,0,2,1:T(8,128)S(1)}, u32[]{:S(2)}, u32[]{:S(2)}) collective-permute-start(f32[64,1,8,128]{3,0,2,1:T(8,128)S(1)} %get-tuple-element.32), channel_id=1, source_target_pairs={{32,0},{64,32},{96,64},{128,96},{160,128},{192,160},{224,192},{0,2... | collective-permute-start | bytes 786440 | tf_op jit(solution)/shard_map/ppermute | solution.py:26
  45.2 15.0 %collective-permute-start.19 = (f32[64,1,8,128]{3,0,2,1:T(8,128)S(1)}, f32[64,1,8,128]{3,0,2,1:T(8,128)S(1)}, u32[]{:S(2)}, u32[]{:S(2)}) collective-permute-start(f32[64,1,8,128]{3,0,2,1:T(8,128)S(1)} %get-tuple-element.31), channel_id=1, source_target_pairs={{0,32},{32,64},{64,96},{96,128},{128,160},{160,192},{192,224},{224... | collective-permute-start | bytes 786440 | tf_op jit(solution)/shard_map/ppermute | solution.py:25
  52.7 9.1 %collective-permute-start.16 = (f32[3,64,64]{2,1,0:T(8,128)S(1)}, f32[3,64,64]{2,1,0:T(8,128)S(1)}, u32[]{:S(2)}, u32[]{:S(2)}) collective-permute-start(f32[3,64,64]{2,1,0:T(8,128)S(1)} %add_add_fusion.1), channel_id=1, source_target_pairs={{0,16},{2,18},{4,20},{6,22},{8,24},{10,26},{12,28},{14,30},{16,0},... | collective-permute-start | bytes 147464 | tf_op jit(solution)/shard_map/ppermute | solution.py:50
  53.6 12.2 %collective-permute-start.17 = (f32[3,64,64]{2,1,0:T(8,128)S(1)}, f32[3,64,64]{2,1,0:T(8,128)S(1)}, u32[]{:S(2)}, u32[]{:S(2)}) collective-permute-start(f32[3,64,64]{2,1,0:T(8,128)S(1)} %add_add_fusion.1), channel_id=1, source_target_pairs={{0,24},{2,26},{4,28},{6,30},{8,16},{10,18},{12,20},{14,22},{16,8},... | collective-permute-start | bytes 147464 | tf_op jit(solution)/shard_map/ppermute | solution.py:50
  55.0 13.2 %collective-permute-start.15 = (f32[3,64,64]{2,1,0:T(8,128)S(1)}, f32[3,64,64]{2,1,0:T(8,128)S(1)}, u32[]{:S(2)}, u32[]{:S(2)}) collective-permute-start(f32[3,64,64]{2,1,0:T(8,128)S(1)} %add_add_fusion.1), channel_id=1, source_target_pairs={{0,8},{2,10},{4,12},{6,14},{8,0},{10,2},{12,4},{14,6},{16,24},{18,... | collective-permute-start | bytes 147464 | tf_op jit(solution)/shard_map/ppermute | solution.py:50
  61.7 7.1 %collective-permute-start.22 = (f32[1,64,64]{2,1,0:T(8,128)S(1)}, f32[1,64,64]{2,1,0:T(8,128)S(1)}, u32[]{:S(2)}, u32[]{:S(2)}) collective-permute-start(f32[1,64,64]{2,1,0:T(8,128)S(1)} %convolution_bitcast_fusion), channel_id=1, source_target_pairs={{0,32},{32,0},{64,96},{96,64},{128,160},{160,128},{192,224},{224,1... | collective-permute-start | bytes 49160 | tf_op jit(solution)/shard_map/ppermute | solution.py:46
  69.5 12.5 %copy-start.2 = (f32[64,2,8,128]{3,2,1,0:T(8,128)S(1)}, f32[64,2,8,128]{3,2,1,0:T(8,128)}, u32[]{:S(2)}) copy-start(f32[64,2,8,128]{3,2,1,0:T(8,128)} %param.9) | copy-start | bytes 1572868
  69.5 12.7 %collective-permute-start.24 = (f32[1,64,64]{2,1,0:T(8,128)}, f32[1,64,64]{2,1,0:T(8,128)}, u32[]{:S(2)}, u32[]{:S(2)}) collective-permute-start(f32[1,64,64]{2,1,0:T(8,128)} %add.238), channel_id=1, source_target_pairs={{0,128},{32,160},{64,192},{96,224},{128,0},{160,32},{192,64},{224,... | collective-permute-start | bytes 49160 | tf_op jit(solution)/shard_map/ppermute | solution.py:50
  71.0 11.2 %collective-permute-start.25 = (f32[1,64,64]{2,1,0:T(8,128)}, f32[1,64,64]{2,1,0:T(8,128)}, u32[]{:S(2)}, u32[]{:S(2)}) collective-permute-start(f32[1,64,64]{2,1,0:T(8,128)} %add.238), channel_id=1, source_target_pairs={{0,192},{32,224},{64,128},{96,160},{128,64},{160,96},{192,0},{224,... | collective-permute-start | bytes 49160 | tf_op jit(solution)/shard_map/ppermute | solution.py:50
  71.3 11.0 %collective-permute-start.23 = (f32[1,64,64]{2,1,0:T(8,128)}, f32[1,64,64]{2,1,0:T(8,128)}, u32[]{:S(2)}, u32[]{:S(2)}) collective-permute-start(f32[1,64,64]{2,1,0:T(8,128)} %add.238), channel_id=1, source_target_pairs={{0,64},{32,96},{64,0},{96,32},{128,192},{160,224},{192,128},{224,1... | collective-permute-start | bytes 49160 | tf_op jit(solution)/shard_map/ppermute | solution.py:50
  83.1 5.0 %collective-permute-start.27 = (f32[1,64,64]{2,1,0:T(8,128)S(1)}, f32[1,64,64]{2,1,0:T(8,128)S(1)}, u32[]{:S(2)}, u32[]{:S(2)}) collective-permute-start(f32[1,64,64]{2,1,0:T(8,128)S(1)} %add_add_fusion.5), channel_id=1, source_target_pairs={{0,4},{2,6},{4,0},{6,2},{8,12},{10,14},{12,8},{14,10},{16,20},{18,... | collective-permute-start | bytes 49160 | tf_op jit(solution)/shard_map/ppermute | solution.py:50
  83.2 5.8 %collective-permute-start.28 = (f32[1,64,64]{2,1,0:T(8,128)S(1)}, f32[1,64,64]{2,1,0:T(8,128)S(1)}, u32[]{:S(2)}, u32[]{:S(2)}) collective-permute-start(f32[1,64,64]{2,1,0:T(8,128)S(1)} %add_add_fusion.5), channel_id=1, source_target_pairs={{0,6},{2,4},{4,2},{6,0},{8,14},{10,12},{12,10},{14,8},{16,22},{18,... | collective-permute-start | bytes 49160 | tf_op jit(solution)/shard_map/ppermute | solution.py:50
  86.3 3.9 %collective-permute-start.26 = (f32[1,64,64]{2,1,0:T(8,128)S(1)}, f32[1,64,64]{2,1,0:T(8,128)S(1)}, u32[]{:S(2)}, u32[]{:S(2)}) collective-permute-start(f32[1,64,64]{2,1,0:T(8,128)S(1)} %add_add_fusion.5), channel_id=1, source_target_pairs={{0,2},{2,0},{4,6},{6,4},{8,10},{10,8},{12,14},{14,12},{16,18},{18,... | collective-permute-start | bytes 49160 | tf_op jit(solution)/shard_map/ppermute | solution.py:50
  90.3 9.0 %collective-permute-start.30 = (f32[1,64,64]{2,1,0:T(8,128)S(1)}, f32[1,64,64]{2,1,0:T(8,128)S(1)}, u32[]{:S(2)}, u32[]{:S(2)}) collective-permute-start(f32[1,64,64]{2,1,0:T(8,128)S(1)} %add_add_fusion.4), channel_id=1, source_target_pairs={{0,16},{2,18},{4,20},{6,22},{8,24},{10,26},{12,28},{14,30},{16,0},... | collective-permute-start | bytes 49160 | tf_op jit(solution)/shard_map/ppermute | solution.py:50
  91.4 10.8 %collective-permute-start.31 = (f32[1,64,64]{2,1,0:T(8,128)S(1)}, f32[1,64,64]{2,1,0:T(8,128)S(1)}, u32[]{:S(2)}, u32[]{:S(2)}) collective-permute-start(f32[1,64,64]{2,1,0:T(8,128)S(1)} %add_add_fusion.4), channel_id=1, source_target_pairs={{0,24},{2,26},{4,28},{6,30},{8,16},{10,18},{12,20},{14,22},{16,8},... | collective-permute-start | bytes 49160 | tf_op jit(solution)/shard_map/ppermute | solution.py:50
  94.2 8.9 %collective-permute-start.29 = (f32[1,64,64]{2,1,0:T(8,128)S(1)}, f32[1,64,64]{2,1,0:T(8,128)S(1)}, u32[]{:S(2)}, u32[]{:S(2)}) collective-permute-start(f32[1,64,64]{2,1,0:T(8,128)S(1)} %add_add_fusion.4), channel_id=1, source_target_pairs={{0,8},{2,10},{4,12},{6,14},{8,0},{10,2},{12,4},{14,6},{16,24},{18,... | collective-permute-start | bytes 49160 | tf_op jit(solution)/shard_map/ppermute | solution.py:50
  98.0 16.7 %collective-permute-start.34 = (f32[64,2,1,128]{3,0,2,1:T(8,128)S(1)}, f32[64,2,1,128]{3,0,2,1:T(8,128)S(1)}, u32[]{:S(2)}, u32[]{:S(2)}) collective-permute-start(f32[64,2,1,128]{3,0,2,1:T(8,128)S(1)} %get-tuple-element.26), channel_id=1, source_target_pairs={{2,0},{4,2},{6,4},{8,6},{10,8},{12,10},{14,12},{16,14},{18,16},{20... | collective-permute-start | bytes 196616 | tf_op jit(solution)/shard_map/ppermute | solution.py:26
  99.3 17.0 %collective-permute-start.33 = (f32[64,1,8,128]{3,0,2,1:T(8,128)}, f32[64,1,8,128]{3,0,2,1:T(8,128)}, u32[]{:S(2)}, u32[]{:S(2)}) collective-permute-start(f32[64,1,8,128]{3,0,2,1:T(8,128)} %get-tuple-element.28), channel_id=1, source_target_pairs={{0,32},{32,64},{64,96},{96,128},{128,160},{160,192},{192,224},{224... | collective-permute-start | bytes 786440 | tf_op jit(solution)/shard_map/ppermute | solution.py:25
  99.3 18.2 %collective-permute-start.32 = (f32[64,1,8,128]{3,0,2,1:T(8,128)}, f32[64,1,8,128]{3,0,2,1:T(8,128)}, u32[]{:S(2)}, u32[]{:S(2)}) collective-permute-start(f32[64,1,8,128]{3,0,2,1:T(8,128)} %get-tuple-element.27), channel_id=1, source_target_pairs={{32,0},{64,32},{96,64},{128,96},{160,128},{192,160},{224,192},{0,2... | collective-permute-start | bytes 786440 | tf_op jit(solution)/shard_map/ppermute | solution.py:26
  102.3 12.5 %collective-permute-start.35 = (f32[64,2,1,128]{3,0,2,1:T(8,128)S(1)}, f32[64,2,1,128]{3,0,2,1:T(8,128)S(1)}, u32[]{:S(2)}, u32[]{:S(2)}) collective-permute-start(f32[64,2,1,128]{3,0,2,1:T(8,128)S(1)} %get-tuple-element.25), channel_id=1, source_target_pairs={{0,2},{2,4},{4,6},{6,8},{8,10},{10,12},{12,14},{14,16},{16,18},{18... | collective-permute-start | bytes 196616 | tf_op jit(solution)/shard_map/ppermute | solution.py:25
  112.6 2.2 %copy-start.1 = (f32[65,4,10,128]{3,0,2,1:T(8,128)S(1)}, f32[65,4,10,128]{3,0,2,1:T(8,128)}, u32[]{:S(2)}) copy-start(f32[65,4,10,128]{3,0,2,1:T(8,128)} %copy-done) | copy-start | bytes 3993604
  112.6 2.2 %copy-start.5 = (f32[64,4,1,128]{3,0,2,1:T(8,128)S(1)}, f32[64,4,1,128]{3,0,2,1:T(8,128)}, u32[]{:S(2)}) copy-start(f32[64,4,1,128]{3,0,2,1:T(8,128)} %copy-done.4) | copy-start | bytes 393220
  112.6 2.2 %copy-start.7 = (f32[2,64,64]{2,1,0:T(8,128)S(1)}, f32[2,64,64]{2,1,0:T(8,128)}, u32[]{:S(2)}) copy-start(f32[2,64,64]{2,1,0:T(8,128)} %shard_map.69) | copy-start | bytes 98308
  114.8 2.5 %copy-start.3 = (f32[64,2,8,128]{3,2,1,0:T(8,128)S(1)}, f32[64,2,8,128]{3,2,1,0:T(8,128)}, u32[]{:S(2)}) copy-start(f32[64,2,8,128]{3,2,1,0:T(8,128)} %param.9) | copy-start | bytes 1572868
  121.4 5.2 %collective-permute-start.36 = (f32[2,8,64]{2,1,0:T(8,128)S(1)}, f32[2,8,64]{2,1,0:T(8,128)S(1)}, u32[]{:S(2)}, u32[]{:S(2)}) collective-permute-start(f32[2,8,64]{2,1,0:T(8,128)S(1)} %constant_dynamic-slice_fusion), channel_id=1, source_target_pairs={{0,1},{1,0},{2,3},{3,2},{4,5},{5,4},{6,7},{7,6},{8,9},{9,8},{10,11... | collective-permute-start | bytes 12296 | tf_op jit(solution)/shard_map/ppermute | solution.py:276

commit v11 on v9

--- a/solution.py
+++ b/solution.py
@@ -132,23 +132,39 @@
     lanes = lax.broadcasted_iota(jnp.int32, shape, 1)
     lane_r = lax.broadcasted_iota(jnp.int32, (1, n), 1)
 
-    def step(j, carry):
-        pick = rows == j
+    def pick_row(x, i):
+        return jnp.sum(jnp.where(rows == i, x, 0.0), axis=0, keepdims=True)
+
+    def pick_col(x, i):
+        return jnp.sum(jnp.where(lanes == i, x, 0.0), axis=1, keepdims=True)
+
+    def entry(row, i):
+        return jnp.sum(jnp.where(lane_r == i, row, 0.0), axis=1, keepdims=True)
+
+    def step(k, carry):
+        p = 2 * k
+        q = p + 1
         out = []
         for m, r in carry:
-            row_m = jnp.sum(jnp.where(pick, m, 0.0), axis=0, keepdims=True)
-            row_r = jnp.sum(jnp.where(pick, r, 0.0), axis=0, keepdims=True)
-            pivot = jnp.sum(jnp.where(lane_r == j, row_m, 0.0), axis=1, keepdims=True)
-            col = jnp.sum(jnp.where(lanes == j, m, 0.0), axis=1, keepdims=True)
-            scale = 1.0 / pivot
-            row_m = row_m * scale
-            row_r = row_r * scale
-            m = jnp.where(pick, row_m, m - col * row_m)
-            r = jnp.where(pick, row_r, r - col * row_r)
+            row_p = pick_row(m, p)
+            row_q = pick_row(m, q)
+            res_p = pick_row(r, p)
+            res_q = pick_row(r, q)
+            col_p = pick_col(m, p)
+            col_q = pick_col(m, q)
+            a, b = entry(row_p, p), entry(row_p, q)
+            c, d = entry(row_q, p), entry(row_q, q)
+            scale = 1.0 / (a * d - b * c)
+            new_p = (d * row_p - b * row_q) * scale
+            new_q = (a * row_q - c * row_p) * scale
+            got_p = (d * res_p - b * res_q) * scale
+            got_q = (a * res_q - c * res_p) * scale
+            m = jnp.where(rows == p, new_p, jnp.where(rows == q, new_q, m - col_p * new_p - col_q * new_q))
+            r = jnp.where(rows == p, got_p, jnp.where(rows == q, got_q, r - col_p * got_p - col_q * got_q))
             out.append((m, r))
         return tuple(out)
 
-    done = lax.fori_loop(0, n, step, tuple(pairs), unroll=unroll)
+    done = lax.fori_loop(0, n // 2, step, tuple(pairs), unroll=unroll)
     return [r for _, r in done]
 
 

time: 113 us -> 107 us (0.947)
  Pallas kernels: 16.5 us -> 10.4 us
    pallas_call x1, Pallas kernels: 16.5 us -> 10.4 us  [steps(): pl.pallas_call(steps_kernel, out_shape=jax.ShapeDtypeStruct((2, n, n), jn...]
where the time goes in v11:
time: 107 us
  starting transfers between devices  36.1 us (34%)
  waiting for transfers between devices  30.7 us (29%)
  other arithmetic  11.8 us (11%)
  local copies, waits for them, and re-layouts  10.4 us (10%)
  Pallas kernels  10.4 us (10%)
  matrix products  5.88 us (5%)
  between operations  1.34 us (1%)
    ppermute x9, starting transfers between devices, allsum(): lax.ppermute(value, axis, [(i, i ^ d << shift) for i in range(count)])  15.2 us
    ppermute x8, starting transfers between devices, padded_2(): high = lax.ppermute(bottom, axis, backward)  15 us
    ppermute x8, waiting for transfers between devices, padded_2(): low = lax.ppermute(top, axis, forward)  12.6 us
    ppermute x9, waiting for transfers between devices, allsum(): lax.ppermute(value, axis, [(i, i ^ d << shift) for i in range(count)])  12.3 us
    pallas_call x1, Pallas kernels, steps(): pl.pallas_call(steps_kernel, out_shape=jax.ShapeDtypeStruct((2, n, n), jn...  10.4 us
    unnamed x53, local copies, waits for them, and re-layouts  7.56 us
    ppermute x8, starting transfers between devices, padded_2(): low = lax.ppermute(top, axis, forward)  5 us
    dot_general x2, matrix products, combine_cols(): jnp.einsum('axyz,ab->bxyz', field, matrix, precision=lax.Precision.HIGHEST)  3.64 us
  transfers between devices with their start and end apart: 27, of which 14 were waited for; matrix products, arithmetic and copies ran while one was open for 11% of the time, Pallas kernels for 0%

profile of v11, /device:TPU:4, one launch (start us, length us, event | category | flops | bytes accessed | tf_op | source)
XLA Modules:
  0.0 106.6 jit_solution(5950118786828634356)
XLA Ops:
  0.7 1.2 %copy.35 = f32[64,2,8,128]{3,0,2,1:T(8,128)S(1)} copy(f32[64,2,8,128]{3,2,1,0:T(8,128)} %param.8) | data formatting | bytes 1048576 | tf_op args[3]
  1.9 0.7 maximum_select_fusion
  2.6 6.6 %collective-permute-start.3 = (f32[65,2,1,128]{3,0,2,1:T(8,128)S(1)}, f32[65,2,1,128]{3,0,2,1:T(8,128)S(1)}, u32[]{:S(2)}, u32[]{:S(2)}) collective-permute-start(f32[65,2,1,128]{3,0,2,1:T(8,128)S(1)} %get-tuple-element.22), channel_id=1, source_target_pairs={{2,0},{4,2},{6,4},{8,6},{10,8},{12,10},{14,12},{16,14},{18,16},{20... | collective-permute-start | bytes 199688 | tf_op jit(solution)/shard_map/ppermute | solution.py:26
  9.3 2.2 %collective-permute-start.2 = (f32[65,1,8,128]{3,0,2,1:T(8,128)S(1)}, f32[65,1,8,128]{3,0,2,1:T(8,128)S(1)}, u32[]{:S(2)}, u32[]{:S(2)}) collective-permute-start(f32[65,1,8,128]{3,0,2,1:T(8,128)S(1)} %get-tuple-element.24), channel_id=1, source_target_pairs={{32,0},{64,32},{96,64},{128,96},{160,128},{192,160},{224,192},{0,2... | collective-permute-start | bytes 798728 | tf_op jit(solution)/shard_map/ppermute | solution.py:26
  11.6 0.6 gather_fusion
  12.9 5.0 %collective-permute-done = f32[65,2,1,128]{3,0,2,1:T(8,128)S(1)} collective-permute-done((f32[65,2,1,128]{3,0,2,1:T(8,128)S(1)}, f32[65,2,1,128]{3,0,2,1:T(8,128)S(1)}, u32[]{:S(2)}, u32[]{:S(2)}) %collective-permute-start) | collective-permute-done | bytes 66592 | tf_op jit(solution)/shard_map/ppermute | solution.py:25
  17.9 0.9 collective-permute-done.1
  19.3 0.9 copy-done
  21.2 1.0 collective-permute-start.4
  22.2 0.6 collective-permute-start.6
  22.9 1.5 %collective-permute-start.7 = (f32[64,2,1,128]{3,0,2,1:T(8,128)S(1)}, f32[64,2,1,128]{3,0,2,1:T(8,128)S(1)}, u32[]{:S(2)}, u32[]{:S(2)}) collective-permute-start(f32[64,2,1,128]{3,0,2,1:T(8,128)S(1)} %get-tuple-element.33), channel_id=1, source_target_pairs={{0,2},{2,4},{4,6},{6,8},{8,10},{10,12},{12,14},{14,16},{16,18},{18... | collective-permute-start | bytes 196616 | tf_op jit(solution)/shard_map/ppermute | solution.py:25
  24.9 1.7 %collective-permute-done.6 = f32[64,2,1,128]{3,0,2,1:T(8,128)S(1)} collective-permute-done((f32[64,2,1,128]{3,0,2,1:T(8,128)S(1)}, f32[64,2,1,128]{3,0,2,1:T(8,128)S(1)}, u32[]{:S(2)}, u32[]{:S(2)}) %collective-permute-start.6) | collective-permute-done | bytes 65568 | tf_op jit(solution)/shard_map/ppermute | solution.py:26
  26.6 2.7 %collective-permute-done.7 = f32[64,2,1,128]{3,0,2,1:T(8,128)S(1)} collective-permute-done((f32[64,2,1,128]{3,0,2,1:T(8,128)S(1)}, f32[64,2,1,128]{3,0,2,1:T(8,128)S(1)}, u32[]{:S(2)}, u32[]{:S(2)}) %collective-permute-start.7) | collective-permute-done | bytes 65568 | tf_op jit(solution)/shard_map/ppermute | solution.py:25
  30.5 1.3 %collective-permute-start.8 = (f32[64,1,8,128]{3,0,2,1:T(8,128)S(1)}, f32[64,1,8,128]{3,0,2,1:T(8,128)S(1)}, u32[]{:S(2)}, u32[]{:S(2)}) collective-permute-start(f32[64,1,8,128]{3,0,2,1:T(8,128)S(1)} %get-tuple-element.32), channel_id=1, source_target_pairs={{32,0},{64,32},{96,64},{128,96},{160,128},{192,160},{224,192},{0,2... | collective-permute-start | bytes 786440 | tf_op jit(solution)/shard_map/ppermute | solution.py:26
  31.9 1.7 %collective-permute-start.11 = (f32[64,2,1,128]{3,0,2,1:T(8,128)S(1)}, f32[64,2,1,128]{3,0,2,1:T(8,128)S(1)}, u32[]{:S(2)}, u32[]{:S(2)}) collective-permute-start(f32[64,2,1,128]{3,0,2,1:T(8,128)S(1)} %get-tuple-element.29), channel_id=1, source_target_pairs={{0,2},{2,4},{4,6},{6,8},{8,10},{10,12},{12,14},{14,16},{16,18},{18... | collective-permute-start | bytes 196616 | tf_op jit(solution)/shard_map/ppermute | solution.py:25
  34.8 3.4 %collective-permute-done.11 = f32[64,2,1,128]{3,0,2,1:T(8,128)S(1)} collective-permute-done((f32[64,2,1,128]{3,0,2,1:T(8,128)S(1)}, f32[64,2,1,128]{3,0,2,1:T(8,128)S(1)}, u32[]{:S(2)}, u32[]{:S(2)}) %collective-permute-start.11) | collective-permute-done | bytes 65568 | tf_op jit(solution)/shard_map/ppermute | solution.py:25
  38.3 0.6 collective-permute-done.9
  41.2 0.8 collective-permute-done.12
  42.1 1.5 %collective-permute-start.15 = (f32[4,64,64]{2,1,0:T(8,128)S(1)}, f32[4,64,64]{2,1,0:T(8,128)S(1)}, u32[]{:S(2)}, u32[]{:S(2)}) collective-permute-start(f32[4,64,64]{2,1,0:T(8,128)S(1)} %fusion.60), channel_id=1, source_target_pairs={{0,192},{32,224},{64,128},{96,160},{128,64},{160,96},{192,0},{224,... | collective-permute-start | bytes 196616 | tf_op jit(solution)/shard_map/ppermute | solution.py:50
  43.6 1.9 %collective-permute-start.13 = (f32[4,64,64]{2,1,0:T(8,128)S(1)}, f32[4,64,64]{2,1,0:T(8,128)S(1)}, u32[]{:S(2)}, u32[]{:S(2)}) collective-permute-start(f32[4,64,64]{2,1,0:T(8,128)S(1)} %fusion.60), channel_id=1, source_target_pairs={{0,64},{32,96},{64,0},{96,32},{128,192},{160,224},{192,128},{224,1... | collective-permute-start | bytes 196616 | tf_op jit(solution)/shard_map/ppermute | solution.py:50
  45.6 0.6 slice_select_fusion.6
  46.5 1.8 %collective-permute-start.25 = (f32[64,2,1,128]{3,0,2,1:T(8,128)}, f32[64,2,1,128]{3,0,2,1:T(8,128)}, u32[]{:S(2)}, u32[]{:S(2)}) collective-permute-start(f32[64,2,1,128]{3,0,2,1:T(8,128)} %get-tuple-element.25), channel_id=1, source_target_pairs={{0,2},{2,4},{4,6},{6,8},{8,10},{10,12},{12,14},{14,16},{16,18},{18... | collective-permute-start | bytes 196616 | tf_op jit(solution)/shard_map/ppermute | solution.py:25
  48.3 1.8 %collective-permute-done.14 = f32[4,64,64]{2,1,0:T(8,128)S(1)} collective-permute-done((f32[4,64,64]{2,1,0:T(8,128)S(1)}, f32[4,64,64]{2,1,0:T(8,128)S(1)}, u32[]{:S(2)}, u32[]{:S(2)}) %collective-permute-start.14) | collective-permute-done | bytes 65568 | tf_op jit(solution)/shard_map/ppermute | solution.py:50
  50.0 1.9 %collective-permute-done.15 = f32[4,64,64]{2,1,0:T(8,128)S(1)} collective-permute-done((f32[4,64,64]{2,1,0:T(8,128)S(1)}, f32[4,64,64]{2,1,0:T(8,128)S(1)}, u32[]{:S(2)}, u32[]{:S(2)}) %collective-permute-start.15) | collective-permute-done | bytes 65568 | tf_op jit(solution)/shard_map/ppermute | solution.py:50
  52.0 0.8 collective-permute-start.17
  52.8 3.4 %collective-permute-start.18 = (f32[4,64,64]{2,1,0:T(8,128)S(1)}, f32[4,64,64]{2,1,0:T(8,128)S(1)}, u32[]{:S(2)}, u32[]{:S(2)}) collective-permute-start(f32[4,64,64]{2,1,0:T(8,128)S(1)} %add_add_fusion.2), channel_id=1, source_target_pairs={{0,6},{2,4},{4,2},{6,0},{8,14},{10,12},{12,10},{14,8},{16,22},{18,... | collective-permute-start | bytes 196616 | tf_op jit(solution)/shard_map/ppermute | solution.py:50
  56.2 0.8 slice_select_fusion.1
  56.9 0.9 pad.56
  57.8 3.0 %collective-permute-start.22 = (f32[64,1,8,128]{3,0,2,1:T(8,128)}, f32[64,1,8,128]{3,0,2,1:T(8,128)S(1)}, u32[]{:S(2)}, u32[]{:S(2)}) collective-permute-start(f32[64,1,8,128]{3,0,2,1:T(8,128)} %get-tuple-element.27), channel_id=1, source_target_pairs={{32,0},{64,32},{96,64},{128,96},{160,128},{192,160},{224,192},{0,2... | collective-permute-start | bytes 786440 | tf_op jit(solution)/shard_map/ppermute | solution.py:26
  60.8 0.8 pad.57
  61.6 3.4 %collective-permute-done.17 = f32[4,64,64]{2,1,0:T(8,128)S(1)} collective-permute-done((f32[4,64,64]{2,1,0:T(8,128)S(1)}, f32[4,64,64]{2,1,0:T(8,128)S(1)}, u32[]{:S(2)}, u32[]{:S(2)}) %collective-permute-start.17) | collective-permute-done | bytes 65568 | tf_op jit(solution)/shard_map/ppermute | solution.py:50
  65.4 0.9 collective-permute-start.20
  66.3 6.6 %collective-permute-start.19 = (f32[4,64,64]{2,1,0:T(8,128)S(1)}, f32[4,64,64]{2,1,0:T(8,128)S(1)}, u32[]{:S(2)}, u32[]{:S(2)}) collective-permute-start(f32[4,64,64]{2,1,0:T(8,128)S(1)} %add_add_fusion.1), channel_id=1, source_target_pairs={{0,8},{2,10},{4,12},{6,14},{8,0},{10,2},{12,4},{14,6},{16,24},{18,... | collective-permute-start | bytes 196616 | tf_op jit(solution)/shard_map/ppermute | solution.py:50
  72.9 1.0 constant_dynamic-update-slice_fusion.2
  73.9 1.2 %constant_dynamic-update-slice_fusion.1 = f32[64,4,8,128]{3,0,2,1:T(8,128)S(1)} fusion(f32[64,4,8,128]{3,0,2,1:T(8,128)S(1)} %constant_dynamic-update-slice_fusion.2, f32[64,2,8,128]{3,2,1,0:T(8,128)} %param.9), kind=kLoop, calls=%fused_computation.186 | loop fusion | bytes 1048576
  75.1 0.7 copy-done.18
  75.8 2.2 %select_maximum_fusion = f32[64,4,10,130]{3,0,2,1:T(8,128)} fusion(f32[64,4,1,128]{3,0,2,1:T(8,128)S(1)} %pad.56, f32[64,4,8,128]{3,0,2,1:T(8,128)S(1)} %constant_dynamic-update-slice_fusion, f32[64,4,1,128]{3,0,2,1:T(8,128)S(1)} %pad.57), kind=kLoop, calls=%fused_computation.11 | loop fusion | flops 2662400 | bytes 2641920 | tf_op jit(solution)/shard_map/concatenate | solution.py:35
  78.2 4.8 %collective-permute-done.19 = f32[4,64,64]{2,1,0:T(8,128)S(1)} collective-permute-done((f32[4,64,64]{2,1,0:T(8,128)S(1)}, f32[4,64,64]{2,1,0:T(8,128)S(1)}, u32[]{:S(2)}, u32[]{:S(2)}) %collective-permute-start.19) | collective-permute-done | bytes 65568 | tf_op jit(solution)/shard_map/ppermute | solution.py:50
  83.0 0.7 add_add_fusion.grams_ref
  83.7 10.4 %shard_map.68 = f32[2,64,64]{2,1,0:T(8,128)} custom-call(f32[4,64,64]{2,1,0:T(8,128)} %add_add_fusion.grams_ref), custom_call_target="tpu_custom_call" | custom-call | flops 20000000000 | bytes 98304 | tf_op jit(solution)/shard_map/pallas_call | solution.py:200
  94.2 2.1 %fusion.48 = f32[64,4,10,128]{3,0,2,1:T(8,128)S(1)} fusion(f32[2,64,64]{2,1,0:T(8,128)} %shard_map.68, f32[64,4,1,128]{3,0,2,1:T(8,128)S(1)} %copy-done.11, f32[64,1,8,128]{3,0,2,1:T(8,128)S(1)} %collective-permute-done.8, f32[64,2,8,128]{3,0,2,1:T(8,128)S(1)} %fusion.28, f32[64,1,8,128]{3,0,2,1:T(8,128)S(1)} %copy-done.6, f32[64,4,1,128]{3,0,2,1:T(8,128)S(1)} %copy-done.13), kind=kOutput, calls=%fused_computation.157 | convolution fusion | flops 252968960 | bytes 2654208 | tf_op jit(solution)/shard_map/axyz,ab->bxyz/dot_general | solution.py:84
  96.4 1.5 %fusion.1 = f32[64,4,10,128]{3,0,2,1:T(8,128)S(1)} fusion(f32[64,4,10,128]{3,0,2,1:T(8,128)S(1)} %fusion.48, f32[2,64,64]{2,1,0:T(8,128)S(1)} %copy-done.21, f32[65,4,10,128]{3,0,2,1:T(8,128)S(1)} %copy-done.1, f32[64,4,1,128]{3,0,2,1:T(8,128)S(1)} %pad.50, f32[64,1,8,128]{3,0,2,1:T(8,128)S(1)} %collective-permute-done.4, ...), kind=kOutput, calls=%fused_computation.16 | convolution fusion | flops 253624320 | bytes 5275648 | tf_op jit(solution)/shard_map/axyz,ab->bxyz/dot_general | solution.py:84
  98.5 0.6 fusion.10
  99.5 1.2 %fusion.12 = f32[3,8,128]{2,1,0:T(8,128)S(1)} fusion(f32[64,4,10,128]{3,0,2,1:T(8,128)S(1)} %fusion.1, f32[64,1,8,128]{3,0,2,1:T(8,128)S(1)} %copy-done.19, f32[64,2,8,128]{3,0,2,1:T(8,128)S(1)} %copy.44, f32[64,1,8,128]{3,0,2,1:T(8,128)} %collective-permute-done.23), kind=kLoop, calls=%fused_computation.37 | loop fusion | flops 1176576 | bytes 2633728 | tf_op jit(solution)/shard_map/reduce_sum | solution.py:102
  100.8 0.8 collective-permute-start.26
  101.7 1.1 %copy.50 = f32[64,2,8,128]{3,2,1,0:T(8,128)} copy(f32[64,2,8,128]{3,0,2,1:T(8,128)S(1)} %slice.407) | data formatting | bytes 1048576
  102.8 3.2 %collective-permute-done.26 = f32[2,8,64]{2,1,0:T(8,128)S(1)} collective-permute-done((f32[2,8,64]{2,1,0:T(8,128)S(1)}, f32[2,8,64]{2,1,0:T(8,128)S(1)}, u32[]{:S(2)}, u32[]{:S(2)}) %collective-permute-start.26) | collective-permute-done | bytes 4128 | tf_op jit(solution)/shard_map/ppermute | solution.py:274
  106.0 0.7 dynamic-slice_add_fusion
  (134 shorter events, 9.6 us)
Async XLA Ops:
  0.6 8.6 %copy-start.20 = (f32[2,8,128]{2,1,0:T(8,128)S(1)}, f32[2,8,128]{2,1,0:T(8,128)}, u32[]{:S(2)}) copy-start(f32[2,8,128]{2,1,0:T(8,128)} %param.5) | copy-start | bytes 24580
  0.6 10.8 %copy-start.23 = (s32[64]{0:T(128)S(1)}, s32[64]{0:T(128)}, u32[]{:S(2)}) copy-start(s32[64]{0:T(128)} %param.7) | copy-start | bytes 772
  0.7 10.8 %copy-start.22 = (s32[128,2]{0,1:T(2,128)S(1)}, s32[128,2]{0,1:T(2,128)}, u32[]{:S(2)}) copy-start(s32[128,2]{0,1:T(2,128)} %param.6) | copy-start | bytes 3076
  2.6 10.3 %collective-permute-start.3 = (f32[65,2,1,128]{3,0,2,1:T(8,128)S(1)}, f32[65,2,1,128]{3,0,2,1:T(8,128)S(1)}, u32[]{:S(2)}, u32[]{:S(2)}) collective-permute-start(f32[65,2,1,128]{3,0,2,1:T(8,128)S(1)} %get-tuple-element.22), channel_id=1, source_target_pairs={{2,0},{4,2},{6,4},{8,6},{10,8},{12,10},{14,12},{16,14},{18,16},{20... | collective-permute-start | bytes 199688 | tf_op jit(solution)/shard_map/ppermute | solution.py:26
  9.3 8.7 %collective-permute-start.2 = (f32[65,1,8,128]{3,0,2,1:T(8,128)S(1)}, f32[65,1,8,128]{3,0,2,1:T(8,128)S(1)}, u32[]{:S(2)}, u32[]{:S(2)}) collective-permute-start(f32[65,1,8,128]{3,0,2,1:T(8,128)S(1)} %get-tuple-element.24), channel_id=1, source_target_pairs={{32,0},{64,32},{96,64},{128,96},{160,128},{192,160},{224,192},{0,2... | collective-permute-start | bytes 798728 | tf_op jit(solution)/shard_map/ppermute | solution.py:26
  11.5 7.4 %collective-permute-start.1 = (f32[65,1,8,128]{3,0,2,1:T(8,128)S(1)}, f32[65,1,8,128]{3,0,2,1:T(8,128)S(1)}, u32[]{:S(2)}, u32[]{:S(2)}) collective-permute-start(f32[65,1,8,128]{3,0,2,1:T(8,128)S(1)} %get-tuple-element.23), channel_id=1, source_target_pairs={{0,32},{32,64},{64,96},{96,128},{128,160},{160,192},{192,224},{224... | collective-permute-start | bytes 798728 | tf_op jit(solution)/shard_map/ppermute | solution.py:25
  11.5 6.5 %collective-permute-start = (f32[65,2,1,128]{3,0,2,1:T(8,128)S(1)}, f32[65,2,1,128]{3,0,2,1:T(8,128)S(1)}, u32[]{:S(2)}, u32[]{:S(2)}) collective-permute-start(f32[65,2,1,128]{3,0,2,1:T(8,128)S(1)} %get-tuple-element.21), channel_id=1, source_target_pairs={{0,2},{2,4},{4,6},{6,8},{8,10},{10,12},{12,14},{14,16},{16,18},{18... | collective-permute-start | bytes 199688 | tf_op jit(solution)/shard_map/ppermute | solution.py:25
  19.0 1.1 %copy-start = (f32[65,4,10,128]{3,0,2,1:T(8,128)}, f32[65,4,10,128]{3,0,2,1:T(8,128)S(1)}, u32[]{:S(2)}) copy-start(f32[65,4,10,128]{3,0,2,1:T(8,128)S(1)} %pad_maximum_fusion) | copy-start | bytes 3993604
  21.2 8.0 %collective-permute-start.4 = (f32[64,1,8,128]{3,0,2,1:T(8,128)S(1)}, f32[64,1,8,128]{3,0,2,1:T(8,128)S(1)}, u32[]{:S(2)}, u32[]{:S(2)}) collective-permute-start(f32[64,1,8,128]{3,0,2,1:T(8,128)S(1)} %get-tuple-element.36), channel_id=1, source_target_pairs={{32,0},{64,32},{96,64},{128,96},{160,128},{192,160},{224,192},{0,2... | collective-permute-start | bytes 786440 | tf_op jit(solution)/shard_map/ppermute | solution.py:26
  22.2 7.1 %collective-permute-start.5 = (f32[64,1,8,128]{3,0,2,1:T(8,128)S(1)}, f32[64,1,8,128]{3,0,2,1:T(8,128)S(1)}, u32[]{:S(2)}, u32[]{:S(2)}) collective-permute-start(f32[64,1,8,128]{3,0,2,1:T(8,128)S(1)} %get-tuple-element.35), channel_id=1, source_target_pairs={{0,32},{32,64},{64,96},{96,128},{128,160},{160,192},{192,224},{224... | collective-permute-start | bytes 786440 | tf_op jit(solution)/shard_map/ppermute | solution.py:25
  22.2 4.3 %collective-permute-start.6 = (f32[64,2,1,128]{3,0,2,1:T(8,128)S(1)}, f32[64,2,1,128]{3,0,2,1:T(8,128)S(1)}, u32[]{:S(2)}, u32[]{:S(2)}) collective-permute-start(f32[64,2,1,128]{3,0,2,1:T(8,128)S(1)} %get-tuple-element.34), channel_id=1, source_target_pairs={{2,0},{4,2},{6,4},{8,6},{10,8},{12,10},{14,12},{16,14},{18,16},{20... | collective-permute-start | bytes 196616 | tf_op jit(solution)/shard_map/ppermute | solution.py:26
  22.9 6.4 %collective-permute-start.7 = (f32[64,2,1,128]{3,0,2,1:T(8,128)S(1)}, f32[64,2,1,128]{3,0,2,1:T(8,128)S(1)}, u32[]{:S(2)}, u32[]{:S(2)}) collective-permute-start(f32[64,2,1,128]{3,0,2,1:T(8,128)S(1)} %get-tuple-element.33), channel_id=1, source_target_pairs={{0,2},{2,4},{4,6},{6,8},{8,10},{10,12},{12,14},{14,16},{16,18},{18... | collective-permute-start | bytes 196616 | tf_op jit(solution)/shard_map/ppermute | solution.py:25
  30.4 4.3 %collective-permute-start.10 = (f32[64,2,1,128]{3,0,2,1:T(8,128)S(1)}, f32[64,2,1,128]{3,0,2,1:T(8,128)S(1)}, u32[]{:S(2)}, u32[]{:S(2)}) collective-permute-start(f32[64,2,1,128]{3,0,2,1:T(8,128)S(1)} %get-tuple-element.30), channel_id=1, source_target_pairs={{2,0},{4,2},{6,4},{8,6},{10,8},{12,10},{14,12},{16,14},{18,16},{20... | collective-permute-start | bytes 196616 | tf_op jit(solution)/shard_map/ppermute | solution.py:26
  30.5 7.7 %collective-permute-start.8 = (f32[64,1,8,128]{3,0,2,1:T(8,128)S(1)}, f32[64,1,8,128]{3,0,2,1:T(8,128)S(1)}, u32[]{:S(2)}, u32[]{:S(2)}) collective-permute-start(f32[64,1,8,128]{3,0,2,1:T(8,128)S(1)} %get-tuple-element.32), channel_id=1, source_target_pairs={{32,0},{64,32},{96,64},{128,96},{160,128},{192,160},{224,192},{0,2... | collective-permute-start | bytes 786440 | tf_op jit(solution)/shard_map/ppermute | solution.py:26
  31.9 7.0 %collective-permute-start.9 = (f32[64,1,8,128]{3,0,2,1:T(8,128)S(1)}, f32[64,1,8,128]{3,0,2,1:T(8,128)S(1)}, u32[]{:S(2)}, u32[]{:S(2)}) collective-permute-start(f32[64,1,8,128]{3,0,2,1:T(8,128)S(1)} %get-tuple-element.31), channel_id=1, source_target_pairs={{0,32},{32,64},{64,96},{96,128},{128,160},{160,192},{192,224},{224... | collective-permute-start | bytes 786440 | tf_op jit(solution)/shard_map/ppermute | solution.py:25
  31.9 6.4 %collective-permute-start.11 = (f32[64,2,1,128]{3,0,2,1:T(8,128)S(1)}, f32[64,2,1,128]{3,0,2,1:T(8,128)S(1)}, u32[]{:S(2)}, u32[]{:S(2)}) collective-permute-start(f32[64,2,1,128]{3,0,2,1:T(8,128)S(1)} %get-tuple-element.29), channel_id=1, source_target_pairs={{0,2},{2,4},{4,6},{6,8},{8,10},{10,12},{12,14},{14,16},{16,18},{18... | collective-permute-start | bytes 196616 | tf_op jit(solution)/shard_map/ppermute | solution.py:25
  34.8 4.6 %copy-start.10 = (f32[64,4,1,128]{3,0,2,1:T(8,128)}, f32[64,4,1,128]{3,0,2,1:T(8,128)S(1)}, u32[]{:S(2)}) copy-start(f32[64,4,1,128]{3,0,2,1:T(8,128)S(1)} %pad.53) | copy-start | bytes 393220
  38.3 1.1 %copy-start.12 = (f32[64,4,1,128]{3,0,2,1:T(8,128)}, f32[64,4,1,128]{3,0,2,1:T(8,128)S(1)}, u32[]{:S(2)}) copy-start(f32[64,4,1,128]{3,0,2,1:T(8,128)S(1)} %pad.54) | copy-start | bytes 393220
  39.9 1.0 copy-start.7
  40.6 1.4 %collective-permute-start.12 = (f32[4,64,64]{2,1,0:T(8,128)S(1)}, f32[4,64,64]{2,1,0:T(8,128)S(1)}, u32[]{:S(2)}, u32[]{:S(2)}) collective-permute-start(f32[4,64,64]{2,1,0:T(8,128)S(1)} %pad_maximum_fusion.29), channel_id=1, source_target_pairs={{0,32},{32,0},{64,96},{96,64},{128,160},{160,128},{192,224},{224,1... | collective-permute-start | bytes 196616 | tf_op jit(solution)/shard_map/ppermute | solution.py:46
  42.0 8.0 %collective-permute-start.14 = (f32[4,64,64]{2,1,0:T(8,128)S(1)}, f32[4,64,64]{2,1,0:T(8,128)S(1)}, u32[]{:S(2)}, u32[]{:S(2)}) collective-permute-start(f32[4,64,64]{2,1,0:T(8,128)S(1)} %fusion.60), channel_id=1, source_target_pairs={{0,128},{32,160},{64,192},{96,224},{128,0},{160,32},{192,64},{224,... | collective-permute-start | bytes 196616 | tf_op jit(solution)/shard_map/ppermute | solution.py:50
  42.1 9.8 %collective-permute-start.15 = (f32[4,64,64]{2,1,0:T(8,128)S(1)}, f32[4,64,64]{2,1,0:T(8,128)S(1)}, u32[]{:S(2)}, u32[]{:S(2)}) collective-permute-start(f32[4,64,64]{2,1,0:T(8,128)S(1)} %fusion.60), channel_id=1, source_target_pairs={{0,192},{32,224},{64,128},{96,160},{128,64},{160,96},{192,0},{224,... | collective-permute-start | bytes 196616 | tf_op jit(solution)/shard_map/ppermute | solution.py:50
  43.6 8.3 %collective-permute-start.13 = (f32[4,64,64]{2,1,0:T(8,128)S(1)}, f32[4,64,64]{2,1,0:T(8,128)S(1)}, u32[]{:S(2)}, u32[]{:S(2)}) collective-permute-start(f32[4,64,64]{2,1,0:T(8,128)S(1)} %fusion.60), channel_id=1, source_target_pairs={{0,64},{32,96},{64,0},{96,32},{128,192},{160,224},{192,128},{224,1... | collective-permute-start | bytes 196616 | tf_op jit(solution)/shard_map/ppermute | solution.py:50
  46.2 10.7 %collective-permute-start.24 = (f32[64,2,1,128]{3,0,2,1:T(8,128)S(1)}, f32[64,2,1,128]{3,0,2,1:T(8,128)}, u32[]{:S(2)}, u32[]{:S(2)}) collective-permute-start(f32[64,2,1,128]{3,0,2,1:T(8,128)S(1)} %get-tuple-element.26), channel_id=1, source_target_pairs={{2,0},{4,2},{6,4},{8,6},{10,8},{12,10},{14,12},{16,14},{18,16},{20... | collective-permute-start | bytes 196616 | tf_op jit(solution)/shard_map/ppermute | solution.py:26
  46.5 11.3 %collective-permute-start.25 = (f32[64,2,1,128]{3,0,2,1:T(8,128)}, f32[64,2,1,128]{3,0,2,1:T(8,128)}, u32[]{:S(2)}, u32[]{:S(2)}) collective-permute-start(f32[64,2,1,128]{3,0,2,1:T(8,128)} %get-tuple-element.25), channel_id=1, source_target_pairs={{0,2},{2,4},{4,6},{6,8},{8,10},{10,12},{12,14},{14,16},{16,18},{18... | collective-permute-start | bytes 196616 | tf_op jit(solution)/shard_map/ppermute | solution.py:25
  52.0 13.0 %collective-permute-start.17 = (f32[4,64,64]{2,1,0:T(8,128)S(1)}, f32[4,64,64]{2,1,0:T(8,128)S(1)}, u32[]{:S(2)}, u32[]{:S(2)}) collective-permute-start(f32[4,64,64]{2,1,0:T(8,128)S(1)} %add_add_fusion.2), channel_id=1, source_target_pairs={{0,4},{2,6},{4,0},{6,2},{8,12},{10,14},{12,8},{14,10},{16,20},{18,... | collective-permute-start | bytes 196616 | tf_op jit(solution)/shard_map/ppermute | solution.py:50
  52.8 12.2 %collective-permute-start.18 = (f32[4,64,64]{2,1,0:T(8,128)S(1)}, f32[4,64,64]{2,1,0:T(8,128)S(1)}, u32[]{:S(2)}, u32[]{:S(2)}) collective-permute-start(f32[4,64,64]{2,1,0:T(8,128)S(1)} %add_add_fusion.2), channel_id=1, source_target_pairs={{0,6},{2,4},{4,2},{6,0},{8,14},{10,12},{12,10},{14,8},{16,22},{18,... | collective-permute-start | bytes 196616 | tf_op jit(solution)/shard_map/ppermute | solution.py:50
  56.2 9.2 %collective-permute-start.16 = (f32[4,64,64]{2,1,0:T(8,128)S(1)}, f32[4,64,64]{2,1,0:T(8,128)S(1)}, u32[]{:S(2)}, u32[]{:S(2)}) collective-permute-start(f32[4,64,64]{2,1,0:T(8,128)S(1)} %add_add_fusion.2), channel_id=1, source_target_pairs={{0,2},{2,0},{4,6},{6,4},{8,10},{10,8},{12,14},{14,12},{16,18},{18,... | collective-permute-start | bytes 196616 | tf_op jit(solution)/shard_map/ppermute | solution.py:50
  56.9 16.0 %collective-permute-start.23 = (f32[64,1,8,128]{3,0,2,1:T(8,128)S(1)}, f32[64,1,8,128]{3,0,2,1:T(8,128)}, u32[]{:S(2)}, u32[]{:S(2)}) collective-permute-start(f32[64,1,8,128]{3,0,2,1:T(8,128)S(1)} %get-tuple-element.28), channel_id=1, source_target_pairs={{0,32},{32,64},{64,96},{96,128},{128,160},{160,192},{192,224},{224... | collective-permute-start | bytes 786440 | tf_op jit(solution)/shard_map/ppermute | solution.py:25
  57.8 18.0 %copy-start.14 = (f32[64,4,1,128]{3,0,2,1:T(8,128)}, f32[64,4,1,128]{3,0,2,1:T(8,128)S(1)}, u32[]{:S(2)}) copy-start(f32[64,4,1,128]{3,0,2,1:T(8,128)S(1)} %pad.56) | copy-start | bytes 393220
  57.8 17.3 %collective-permute-start.22 = (f32[64,1,8,128]{3,0,2,1:T(8,128)}, f32[64,1,8,128]{3,0,2,1:T(8,128)S(1)}, u32[]{:S(2)}, u32[]{:S(2)}) collective-permute-start(f32[64,1,8,128]{3,0,2,1:T(8,128)} %get-tuple-element.27), channel_id=1, source_target_pairs={{32,0},{64,32},{96,64},{128,96},{160,128},{192,160},{224,192},{0,2... | collective-permute-start | bytes 786440 | tf_op jit(solution)/shard_map/ppermute | solution.py:26
  61.6 14.2 %copy-start.16 = (f32[64,4,1,128]{3,0,2,1:T(8,128)}, f32[64,4,1,128]{3,0,2,1:T(8,128)S(1)}, u32[]{:S(2)}) copy-start(f32[64,4,1,128]{3,0,2,1:T(8,128)S(1)} %pad.57) | copy-start | bytes 393220
  65.4 12.7 %collective-permute-start.20 = (f32[4,64,64]{2,1,0:T(8,128)S(1)}, f32[4,64,64]{2,1,0:T(8,128)S(1)}, u32[]{:S(2)}, u32[]{:S(2)}) collective-permute-start(f32[4,64,64]{2,1,0:T(8,128)S(1)} %add_add_fusion.1), channel_id=1, source_target_pairs={{0,16},{2,18},{4,20},{6,22},{8,24},{10,26},{12,28},{14,30},{16,0},... | collective-permute-start | bytes 196616 | tf_op jit(solution)/shard_map/ppermute | solution.py:50
  66.3 11.9 %collective-permute-start.21 = (f32[4,64,64]{2,1,0:T(8,128)S(1)}, f32[4,64,64]{2,1,0:T(8,128)S(1)}, u32[]{:S(2)}, u32[]{:S(2)}) collective-permute-start(f32[4,64,64]{2,1,0:T(8,128)S(1)} %add_add_fusion.1), channel_id=1, source_target_pairs={{0,24},{2,26},{4,28},{6,30},{8,16},{10,18},{12,20},{14,22},{16,8},... | collective-permute-start | bytes 196616 | tf_op jit(solution)/shard_map/ppermute | solution.py:50
  66.3 16.7 %collective-permute-start.19 = (f32[4,64,64]{2,1,0:T(8,128)S(1)}, f32[4,64,64]{2,1,0:T(8,128)S(1)}, u32[]{:S(2)}, u32[]{:S(2)}) collective-permute-start(f32[4,64,64]{2,1,0:T(8,128)S(1)} %add_add_fusion.1), channel_id=1, source_target_pairs={{0,8},{2,10},{4,12},{6,14},{8,0},{10,2},{12,4},{14,6},{16,24},{18,... | collective-permute-start | bytes 196616 | tf_op jit(solution)/shard_map/ppermute | solution.py:50
  75.8 2.3 %copy-start.3 = (f32[64,4,8,128]{3,0,2,1:T(8,128)}, f32[64,4,8,128]{3,0,2,1:T(8,128)S(1)}, u32[]{:S(2)}) copy-start(f32[64,4,8,128]{3,0,2,1:T(8,128)S(1)} %constant_dynamic-update-slice_fusion) | copy-start | bytes 3145732
  83.7 10.5 %copy-start.6 = (f32[64,1,8,128]{3,0,2,1:T(8,128)S(1)}, f32[64,1,8,128]{3,0,2,1:T(8,128)}, u32[]{:S(2)}) copy-start(f32[64,1,8,128]{3,0,2,1:T(8,128)} %copy-done.5) | copy-start | bytes 786436
  83.7 10.5 %copy-start.11 = (f32[64,4,1,128]{3,0,2,1:T(8,128)S(1)}, f32[64,4,1,128]{3,0,2,1:T(8,128)}, u32[]{:S(2)}) copy-start(f32[64,4,1,128]{3,0,2,1:T(8,128)} %copy-done.10) | copy-start | bytes 393220
  83.7 10.5 %copy-start.13 = (f32[64,4,1,128]{3,0,2,1:T(8,128)S(1)}, f32[64,4,1,128]{3,0,2,1:T(8,128)}, u32[]{:S(2)}) copy-start(f32[64,4,1,128]{3,0,2,1:T(8,128)} %copy-done.12) | copy-start | bytes 393220
  94.2 2.2 %copy-start.1 = (f32[65,4,10,128]{3,0,2,1:T(8,128)S(1)}, f32[65,4,10,128]{3,0,2,1:T(8,128)}, u32[]{:S(2)}) copy-start(f32[65,4,10,128]{3,0,2,1:T(8,128)} %copy-done) | copy-start | bytes 3993604
  94.2 2.2 %copy-start.9 = (f32[64,4,1,128]{3,0,2,1:T(8,128)S(1)}, f32[64,4,1,128]{3,0,2,1:T(8,128)}, u32[]{:S(2)}) copy-start(f32[64,4,1,128]{3,0,2,1:T(8,128)} %copy-done.8) | copy-start | bytes 393220
  94.2 2.2 %copy-start.21 = (f32[2,64,64]{2,1,0:T(8,128)S(1)}, f32[2,64,64]{2,1,0:T(8,128)}, u32[]{:S(2)}) copy-start(f32[2,64,64]{2,1,0:T(8,128)} %shard_map.68) | copy-start | bytes 98308
  96.4 1.6 %copy-start.4 = (f32[64,4,8,128]{3,0,2,1:T(8,128)S(1)}, f32[64,4,8,128]{3,0,2,1:T(8,128)}, u32[]{:S(2)}) copy-start(f32[64,4,8,128]{3,0,2,1:T(8,128)} %copy-done.3) | copy-start | bytes 3145732
  96.4 1.6 %copy-start.15 = (f32[64,4,1,128]{3,0,2,1:T(8,128)S(1)}, f32[64,4,1,128]{3,0,2,1:T(8,128)}, u32[]{:S(2)}) copy-start(f32[64,4,1,128]{3,0,2,1:T(8,128)} %copy-done.14) | copy-start | bytes 393220
  96.4 1.6 %copy-start.17 = (f32[64,4,1,128]{3,0,2,1:T(8,128)S(1)}, f32[64,4,1,128]{3,0,2,1:T(8,128)}, u32[]{:S(2)}) copy-start(f32[64,4,1,128]{3,0,2,1:T(8,128)} %copy-done.16) | copy-start | bytes 393220
  96.4 2.1 %copy-start.2 = (f32[64,4,10,130]{3,0,2,1:T(8,128)S(1)}, f32[64,4,10,130]{3,0,2,1:T(8,128)}, u32[]{:S(2)}) copy-start(f32[64,4,10,130]{3,0,2,1:T(8,128)} %select_maximum_fusion) | copy-start | bytes 3993604
  98.5 0.9 copy-start.19
  100.8 5.2 %collective-permute-start.26 = (f32[2,8,64]{2,1,0:T(8,128)S(1)}, f32[2,8,64]{2,1,0:T(8,128)S(1)}, u32[]{:S(2)}, u32[]{:S(2)}) collective-permute-start(f32[2,8,64]{2,1,0:T(8,128)S(1)} %constant_dynamic-slice_fusion), channel_id=1, source_target_pairs={{0,1},{1,0},{2,3},{3,2},{4,5},{5,4},{6,7},{7,6},{8,9},{9,8},{10,11... | collective-permute-start | bytes 12296 | tf_op jit(solution)/shard_map/ppermute | solution.py:274
  (3 other events, 2.1 us)

commit v12 on v11

--- a/solution.py
+++ b/solution.py
@@ -141,30 +141,52 @@
     def entry(row, i):
         return jnp.sum(jnp.where(lane_r == i, row, 0.0), axis=1, keepdims=True)
 
+    def pair_inverse(a, b, c, d):
+        scale = 1.0 / (a * d - b * c)
+        return d * scale, -b * scale, -c * scale, a * scale
+
     def step(k, carry):
-        p = 2 * k
-        q = p + 1
+        piv = [4 * k + i for i in range(4)]
         out = []
         for m, r in carry:
-            row_p = pick_row(m, p)
-            row_q = pick_row(m, q)
-            res_p = pick_row(r, p)
-            res_q = pick_row(r, q)
-            col_p = pick_col(m, p)
-            col_q = pick_col(m, q)
-            a, b = entry(row_p, p), entry(row_p, q)
-            c, d = entry(row_q, p), entry(row_q, q)
-            scale = 1.0 / (a * d - b * c)
-            new_p = (d * row_p - b * row_q) * scale
-            new_q = (a * row_q - c * row_p) * scale
-            got_p = (d * res_p - b * res_q) * scale
-            got_q = (a * res_q - c * res_p) * scale
-            m = jnp.where(rows == p, new_p, jnp.where(rows == q, new_q, m - col_p * new_p - col_q * new_q))
-            r = jnp.where(rows == p, got_p, jnp.where(rows == q, got_q, r - col_p * got_p - col_q * got_q))
-            out.append((m, r))
+            row = [pick_row(m, i) for i in piv]
+            res = [pick_row(r, i) for i in piv]
+            col = [pick_col(m, i) for i in piv]
+            ent = [[entry(row[i], piv[j]) for j in range(4)] for i in range(4)]
+            w00, w01, w10, w11 = pair_inverse(ent[0][0], ent[0][1], ent[1][0], ent[1][1])
+
+            def lead(x0, x1):
+                return w00 * x0 + w01 * x1, w10 * x0 + w11 * x1
+
+            e02, e12 = lead(ent[0][2], ent[1][2])
+            e03, e13 = lead(ent[0][3], ent[1][3])
+            t22 = ent[2][2] - ent[2][0] * e02 - ent[2][1] * e12
+            t23 = ent[2][3] - ent[2][0] * e03 - ent[2][1] * e13
+            t32 = ent[3][2] - ent[3][0] * e02 - ent[3][1] * e12
+            t33 = ent[3][3] - ent[3][0] * e03 - ent[3][1] * e13
+            v00, v01, v10, v11 = pair_inverse(t22, t23, t32, t33)
+
+            def reduce(x):
+                x0, x1 = lead(x[0], x[1])
+                x2 = x[2] - ent[2][0] * x0 - ent[2][1] * x1
+                x3 = x[3] - ent[3][0] * x0 - ent[3][1] * x1
+                y2 = v00 * x2 + v01 * x3
+                y3 = v10 * x2 + v11 * x3
+                y0 = x0 - e02 * y2 - e03 * y3
+                y1 = x1 - e12 * y2 - e13 * y3
+                return [y0, y1, y2, y3]
+
+            new_m = reduce(row)
+            new_r = reduce(res)
+            rest_m = m - col[0] * new_m[0] - col[1] * new_m[1] - col[2] * new_m[2] - col[3] * new_m[3]
+            rest_r = r - col[0] * new_r[0] - col[1] * new_r[1] - col[2] * new_r[2] - col[3] * new_r[3]
+            for i in range(4):
+                rest_m = jnp.where(rows == piv[i], new_m[i], rest_m)
+                rest_r = jnp.where(rows == piv[i], new_r[i], rest_r)
+            out.append((rest_m, rest_r))
         return tuple(out)
 
-    done = lax.fori_loop(0, n // 2, step, tuple(pairs), unroll=unroll)
+    done = lax.fori_loop(0, n // 4, step, tuple(pairs), unroll=unroll)
     return [r for _, r in done]
 
 

time: 107 us -> 106 us (level)
  Pallas kernels: 10.4 us -> 8.74 us
    pallas_call x1, Pallas kernels: 10.4 us -> 8.74 us  [steps(): pl.pallas_call(steps_kernel, out_shape=jax.ShapeDtypeStruct((2, n, n), jn...]
  transfers between devices with their start and end apart: 27 -> 27, of which waited for: 14 -> 14; matrix products, arithmetic and copies ran while one was open for 11% -> 12% of each run, Pallas kernels for 0% -> 0%
where the time goes in v12:
time: 106 us; the launch traced here: 105 us
  starting transfers between devices  36.1 us (34%)
  waiting for transfers between devices  30.7 us (29%)
  other arithmetic  11.8 us (11%)
  local copies, waits for them, and re-layouts  10.4 us (10%)
  Pallas kernels  8.74 us (8%)
  matrix products  5.88 us (6%)
  between operations  1.34 us (1%)
    ppermute x9, starting transfers between devices, allsum(): lax.ppermute(value, axis, [(i, i ^ d << shift) for i in range(count)])  15.2 us
    ppermute x8, starting transfers between devices, padded_2(): high = lax.ppermute(bottom, axis, backward)  15 us
    ppermute x8, waiting for transfers between devices, padded_2(): low = lax.ppermute(top, axis, forward)  12.6 us
    ppermute x9, waiting for transfers between devices, allsum(): lax.ppermute(value, axis, [(i, i ^ d << shift) for i in range(count)])  12.3 us
    pallas_call x1, Pallas kernels, steps(): pl.pallas_call(steps_kernel, out_shape=jax.ShapeDtypeStruct((2, n, n), jn...  8.74 us
    unnamed x53, local copies, waits for them, and re-layouts  7.56 us
    ppermute x8, starting transfers between devices, padded_2(): low = lax.ppermute(top, axis, forward)  5 us
    dot_general x2, matrix products, combine_cols(): jnp.einsum('axyz,ab->bxyz', field, matrix, precision=lax.Precision.HIGHEST)  3.64 us
  transfers between devices with their start and end apart: 27, of which 14 were waited for; matrix products, arithmetic and copies ran while one was open for 12% of the time, Pallas kernels for 0%

profile of v12, /device:TPU:4, one launch (start us, length us, event | category | flops | bytes accessed | tf_op | source)
XLA Modules:
  0.0 104.9 jit_solution(1460311174014205565)
XLA Ops:
  0.7 1.2 %copy.35 = f32[64,2,8,128]{3,0,2,1:T(8,128)S(1)} copy(f32[64,2,8,128]{3,2,1,0:T(8,128)} %param.8) | data formatting | bytes 1048576 | tf_op args[3]
  1.9 0.7 maximum_select_fusion
  2.6 6.6 %collective-permute-start.3 = (f32[65,2,1,128]{3,0,2,1:T(8,128)S(1)}, f32[65,2,1,128]{3,0,2,1:T(8,128)S(1)}, u32[]{:S(2)}, u32[]{:S(2)}) collective-permute-start(f32[65,2,1,128]{3,0,2,1:T(8,128)S(1)} %get-tuple-element.22), channel_id=1, source_target_pairs={{2,0},{4,2},{6,4},{8,6},{10,8},{12,10},{14,12},{16,14},{18,16},{20... | collective-permute-start | bytes 199688 | tf_op jit(solution)/shard_map/ppermute | solution.py:26
  9.3 2.2 %collective-permute-start.2 = (f32[65,1,8,128]{3,0,2,1:T(8,128)S(1)}, f32[65,1,8,128]{3,0,2,1:T(8,128)S(1)}, u32[]{:S(2)}, u32[]{:S(2)}) collective-permute-start(f32[65,1,8,128]{3,0,2,1:T(8,128)S(1)} %get-tuple-element.24), channel_id=1, source_target_pairs={{32,0},{64,32},{96,64},{128,96},{160,128},{192,160},{224,192},{0,2... | collective-permute-start | bytes 798728 | tf_op jit(solution)/shard_map/ppermute | solution.py:26
  11.6 0.6 gather_fusion
  12.9 5.0 %collective-permute-done = f32[65,2,1,128]{3,0,2,1:T(8,128)S(1)} collective-permute-done((f32[65,2,1,128]{3,0,2,1:T(8,128)S(1)}, f32[65,2,1,128]{3,0,2,1:T(8,128)S(1)}, u32[]{:S(2)}, u32[]{:S(2)}) %collective-permute-start) | collective-permute-done | bytes 66592 | tf_op jit(solution)/shard_map/ppermute | solution.py:25
  17.9 0.9 collective-permute-done.1
  19.3 0.9 copy-done
  21.2 1.0 collective-permute-start.4
  22.2 0.6 collective-permute-start.6
  22.9 1.5 %collective-permute-start.7 = (f32[64,2,1,128]{3,0,2,1:T(8,128)S(1)}, f32[64,2,1,128]{3,0,2,1:T(8,128)S(1)}, u32[]{:S(2)}, u32[]{:S(2)}) collective-permute-start(f32[64,2,1,128]{3,0,2,1:T(8,128)S(1)} %get-tuple-element.33), channel_id=1, source_target_pairs={{0,2},{2,4},{4,6},{6,8},{8,10},{10,12},{12,14},{14,16},{16,18},{18... | collective-permute-start | bytes 196616 | tf_op jit(solution)/shard_map/ppermute | solution.py:25
  24.9 1.7 %collective-permute-done.6 = f32[64,2,1,128]{3,0,2,1:T(8,128)S(1)} collective-permute-done((f32[64,2,1,128]{3,0,2,1:T(8,128)S(1)}, f32[64,2,1,128]{3,0,2,1:T(8,128)S(1)}, u32[]{:S(2)}, u32[]{:S(2)}) %collective-permute-start.6) | collective-permute-done | bytes 65568 | tf_op jit(solution)/shard_map/ppermute | solution.py:26
  26.6 2.7 %collective-permute-done.7 = f32[64,2,1,128]{3,0,2,1:T(8,128)S(1)} collective-permute-done((f32[64,2,1,128]{3,0,2,1:T(8,128)S(1)}, f32[64,2,1,128]{3,0,2,1:T(8,128)S(1)}, u32[]{:S(2)}, u32[]{:S(2)}) %collective-permute-start.7) | collective-permute-done | bytes 65568 | tf_op jit(solution)/shard_map/ppermute | solution.py:25
  30.5 1.3 %collective-permute-start.8 = (f32[64,1,8,128]{3,0,2,1:T(8,128)S(1)}, f32[64,1,8,128]{3,0,2,1:T(8,128)S(1)}, u32[]{:S(2)}, u32[]{:S(2)}) collective-permute-start(f32[64,1,8,128]{3,0,2,1:T(8,128)S(1)} %get-tuple-element.32), channel_id=1, source_target_pairs={{32,0},{64,32},{96,64},{128,96},{160,128},{192,160},{224,192},{0,2... | collective-permute-start | bytes 786440 | tf_op jit(solution)/shard_map/ppermute | solution.py:26
  31.9 1.7 %collective-permute-start.11 = (f32[64,2,1,128]{3,0,2,1:T(8,128)S(1)}, f32[64,2,1,128]{3,0,2,1:T(8,128)S(1)}, u32[]{:S(2)}, u32[]{:S(2)}) collective-permute-start(f32[64,2,1,128]{3,0,2,1:T(8,128)S(1)} %get-tuple-element.29), channel_id=1, source_target_pairs={{0,2},{2,4},{4,6},{6,8},{8,10},{10,12},{12,14},{14,16},{16,18},{18... | collective-permute-start | bytes 196616 | tf_op jit(solution)/shard_map/ppermute | solution.py:25
  34.8 3.4 %collective-permute-done.11 = f32[64,2,1,128]{3,0,2,1:T(8,128)S(1)} collective-permute-done((f32[64,2,1,128]{3,0,2,1:T(8,128)S(1)}, f32[64,2,1,128]{3,0,2,1:T(8,128)S(1)}, u32[]{:S(2)}, u32[]{:S(2)}) %collective-permute-start.11) | collective-permute-done | bytes 65568 | tf_op jit(solution)/shard_map/ppermute | solution.py:25
  38.3 0.6 collective-permute-done.9
  41.2 0.8 collective-permute-done.12
  42.1 1.5 %collective-permute-start.15 = (f32[4,64,64]{2,1,0:T(8,128)S(1)}, f32[4,64,64]{2,1,0:T(8,128)S(1)}, u32[]{:S(2)}, u32[]{:S(2)}) collective-permute-start(f32[4,64,64]{2,1,0:T(8,128)S(1)} %fusion.60), channel_id=1, source_target_pairs={{0,192},{32,224},{64,128},{96,160},{128,64},{160,96},{192,0},{224,... | collective-permute-start | bytes 196616 | tf_op jit(solution)/shard_map/ppermute | solution.py:50
  43.6 1.9 %collective-permute-start.13 = (f32[4,64,64]{2,1,0:T(8,128)S(1)}, f32[4,64,64]{2,1,0:T(8,128)S(1)}, u32[]{:S(2)}, u32[]{:S(2)}) collective-permute-start(f32[4,64,64]{2,1,0:T(8,128)S(1)} %fusion.60), channel_id=1, source_target_pairs={{0,64},{32,96},{64,0},{96,32},{128,192},{160,224},{192,128},{224,1... | collective-permute-start | bytes 196616 | tf_op jit(solution)/shard_map/ppermute | solution.py:50
  45.6 0.6 slice_select_fusion.6
  46.5 1.8 %collective-permute-start.25 = (f32[64,2,1,128]{3,0,2,1:T(8,128)}, f32[64,2,1,128]{3,0,2,1:T(8,128)}, u32[]{:S(2)}, u32[]{:S(2)}) collective-permute-start(f32[64,2,1,128]{3,0,2,1:T(8,128)} %get-tuple-element.25), channel_id=1, source_target_pairs={{0,2},{2,4},{4,6},{6,8},{8,10},{10,12},{12,14},{14,16},{16,18},{18... | collective-permute-start | bytes 196616 | tf_op jit(solution)/shard_map/ppermute | solution.py:25
  48.3 1.8 %collective-permute-done.14 = f32[4,64,64]{2,1,0:T(8,128)S(1)} collective-permute-done((f32[4,64,64]{2,1,0:T(8,128)S(1)}, f32[4,64,64]{2,1,0:T(8,128)S(1)}, u32[]{:S(2)}, u32[]{:S(2)}) %collective-permute-start.14) | collective-permute-done | bytes 65568 | tf_op jit(solution)/shard_map/ppermute | solution.py:50
  50.0 1.9 %collective-permute-done.15 = f32[4,64,64]{2,1,0:T(8,128)S(1)} collective-permute-done((f32[4,64,64]{2,1,0:T(8,128)S(1)}, f32[4,64,64]{2,1,0:T(8,128)S(1)}, u32[]{:S(2)}, u32[]{:S(2)}) %collective-permute-start.15) | collective-permute-done | bytes 65568 | tf_op jit(solution)/shard_map/ppermute | solution.py:50
  52.0 0.8 collective-permute-start.17
  52.8 3.4 %collective-permute-start.18 = (f32[4,64,64]{2,1,0:T(8,128)S(1)}, f32[4,64,64]{2,1,0:T(8,128)S(1)}, u32[]{:S(2)}, u32[]{:S(2)}) collective-permute-start(f32[4,64,64]{2,1,0:T(8,128)S(1)} %add_add_fusion.2), channel_id=1, source_target_pairs={{0,6},{2,4},{4,2},{6,0},{8,14},{10,12},{12,10},{14,8},{16,22},{18,... | collective-permute-start | bytes 196616 | tf_op jit(solution)/shard_map/ppermute | solution.py:50
  56.2 0.8 slice_select_fusion.1
  56.9 0.9 pad.56
  57.8 3.0 %collective-permute-start.22 = (f32[64,1,8,128]{3,0,2,1:T(8,128)}, f32[64,1,8,128]{3,0,2,1:T(8,128)S(1)}, u32[]{:S(2)}, u32[]{:S(2)}) collective-permute-start(f32[64,1,8,128]{3,0,2,1:T(8,128)} %get-tuple-element.27), channel_id=1, source_target_pairs={{32,0},{64,32},{96,64},{128,96},{160,128},{192,160},{224,192},{0,2... | collective-permute-start | bytes 786440 | tf_op jit(solution)/shard_map/ppermute | solution.py:26
  60.8 0.8 pad.57
  61.6 3.4 %collective-permute-done.17 = f32[4,64,64]{2,1,0:T(8,128)S(1)} collective-permute-done((f32[4,64,64]{2,1,0:T(8,128)S(1)}, f32[4,64,64]{2,1,0:T(8,128)S(1)}, u32[]{:S(2)}, u32[]{:S(2)}) %collective-permute-start.17) | collective-permute-done | bytes 65568 | tf_op jit(solution)/shard_map/ppermute | solution.py:50
  65.4 0.9 collective-permute-start.20
  66.3 6.6 %collective-permute-start.19 = (f32[4,64,64]{2,1,0:T(8,128)S(1)}, f32[4,64,64]{2,1,0:T(8,128)S(1)}, u32[]{:S(2)}, u32[]{:S(2)}) collective-permute-start(f32[4,64,64]{2,1,0:T(8,128)S(1)} %add_add_fusion.1), channel_id=1, source_target_pairs={{0,8},{2,10},{4,12},{6,14},{8,0},{10,2},{12,4},{14,6},{16,24},{18,... | collective-permute-start | bytes 196616 | tf_op jit(solution)/shard_map/ppermute | solution.py:50
  72.9 1.0 constant_dynamic-update-slice_fusion.2
  73.9 1.2 %constant_dynamic-update-slice_fusion.1 = f32[64,4,8,128]{3,0,2,1:T(8,128)S(1)} fusion(f32[64,4,8,128]{3,0,2,1:T(8,128)S(1)} %constant_dynamic-update-slice_fusion.2, f32[64,2,8,128]{3,2,1,0:T(8,128)} %param.9), kind=kLoop, calls=%fused_computation.186 | loop fusion | bytes 1048576
  75.1 0.7 copy-done.18
  75.8 2.2 %select_maximum_fusion = f32[64,4,10,130]{3,0,2,1:T(8,128)} fusion(f32[64,4,1,128]{3,0,2,1:T(8,128)S(1)} %pad.56, f32[64,4,8,128]{3,0,2,1:T(8,128)S(1)} %constant_dynamic-update-slice_fusion, f32[64,4,1,128]{3,0,2,1:T(8,128)S(1)} %pad.57), kind=kLoop, calls=%fused_computation.11 | loop fusion | flops 2662400 | bytes 2641920 | tf_op jit(solution)/shard_map/concatenate | solution.py:35
  78.2 4.8 %collective-permute-done.19 = f32[4,64,64]{2,1,0:T(8,128)S(1)} collective-permute-done((f32[4,64,64]{2,1,0:T(8,128)S(1)}, f32[4,64,64]{2,1,0:T(8,128)S(1)}, u32[]{:S(2)}, u32[]{:S(2)}) %collective-permute-start.19) | collective-permute-done | bytes 65568 | tf_op jit(solution)/shard_map/ppermute | solution.py:50
  83.0 0.7 add_add_fusion.grams_ref
  83.7 8.7 %shard_map.68 = f32[2,64,64]{2,1,0:T(8,128)} custom-call(f32[4,64,64]{2,1,0:T(8,128)} %add_add_fusion.grams_ref), custom_call_target="tpu_custom_call" | custom-call | flops 20000000000 | bytes 98304 | tf_op jit(solution)/shard_map/pallas_call | solution.py:222
  92.5 2.1 %fusion.48 = f32[64,4,10,128]{3,0,2,1:T(8,128)S(1)} fusion(f32[2,64,64]{2,1,0:T(8,128)} %shard_map.68, f32[64,4,1,128]{3,0,2,1:T(8,128)S(1)} %copy-done.11, f32[64,1,8,128]{3,0,2,1:T(8,128)S(1)} %collective-permute-done.8, f32[64,2,8,128]{3,0,2,1:T(8,128)S(1)} %fusion.28, f32[64,1,8,128]{3,0,2,1:T(8,128)S(1)} %copy-done.6, f32[64,4,1,128]{3,0,2,1:T(8,128)S(1)} %copy-done.13), kind=kOutput, calls=%fused_computation.157 | convolution fusion | flops 252968960 | bytes 2654208 | tf_op jit(solution)/shard_map/axyz,ab->bxyz/dot_general | solution.py:84
  94.7 1.5 %fusion.1 = f32[64,4,10,128]{3,0,2,1:T(8,128)S(1)} fusion(f32[64,4,10,128]{3,0,2,1:T(8,128)S(1)} %fusion.48, f32[2,64,64]{2,1,0:T(8,128)S(1)} %copy-done.21, f32[65,4,10,128]{3,0,2,1:T(8,128)S(1)} %copy-done.1, f32[64,4,1,128]{3,0,2,1:T(8,128)S(1)} %pad.50, f32[64,1,8,128]{3,0,2,1:T(8,128)S(1)} %collective-permute-done.4, ...), kind=kOutput, calls=%fused_computation.16 | convolution fusion | flops 253624320 | bytes 5275648 | tf_op jit(solution)/shard_map/axyz,ab->bxyz/dot_general | solution.py:84
  96.8 0.6 fusion.10
  97.7 1.2 %fusion.12 = f32[3,8,128]{2,1,0:T(8,128)S(1)} fusion(f32[64,4,10,128]{3,0,2,1:T(8,128)S(1)} %fusion.1, f32[64,1,8,128]{3,0,2,1:T(8,128)S(1)} %copy-done.19, f32[64,2,8,128]{3,0,2,1:T(8,128)S(1)} %copy.44, f32[64,1,8,128]{3,0,2,1:T(8,128)} %collective-permute-done.23), kind=kLoop, calls=%fused_computation.37 | loop fusion | flops 1176576 | bytes 2633728 | tf_op jit(solution)/shard_map/reduce_sum | solution.py:102
  99.1 0.8 collective-permute-start.26
  100.0 1.1 %copy.50 = f32[64,2,8,128]{3,2,1,0:T(8,128)} copy(f32[64,2,8,128]{3,0,2,1:T(8,128)S(1)} %slice.407) | data formatting | bytes 1048576
  101.1 3.2 %collective-permute-done.26 = f32[2,8,64]{2,1,0:T(8,128)S(1)} collective-permute-done((f32[2,8,64]{2,1,0:T(8,128)S(1)}, f32[2,8,64]{2,1,0:T(8,128)S(1)}, u32[]{:S(2)}, u32[]{:S(2)}) %collective-permute-start.26) | collective-permute-done | bytes 4128 | tf_op jit(solution)/shard_map/ppermute | solution.py:296
  104.3 0.7 dynamic-slice_add_fusion
  (134 shorter events, 9.6 us)
Async XLA Ops:
  0.6 8.6 %copy-start.20 = (f32[2,8,128]{2,1,0:T(8,128)S(1)}, f32[2,8,128]{2,1,0:T(8,128)}, u32[]{:S(2)}) copy-start(f32[2,8,128]{2,1,0:T(8,128)} %param.5) | copy-start | bytes 24580
  0.6 10.8 %copy-start.23 = (s32[64]{0:T(128)S(1)}, s32[64]{0:T(128)}, u32[]{:S(2)}) copy-start(s32[64]{0:T(128)} %param.7) | copy-start | bytes 772
  0.7 10.8 %copy-start.22 = (s32[128,2]{0,1:T(2,128)S(1)}, s32[128,2]{0,1:T(2,128)}, u32[]{:S(2)}) copy-start(s32[128,2]{0,1:T(2,128)} %param.6) | copy-start | bytes 3076
  2.6 10.3 %collective-permute-start.3 = (f32[65,2,1,128]{3,0,2,1:T(8,128)S(1)}, f32[65,2,1,128]{3,0,2,1:T(8,128)S(1)}, u32[]{:S(2)}, u32[]{:S(2)}) collective-permute-start(f32[65,2,1,128]{3,0,2,1:T(8,128)S(1)} %get-tuple-element.22), channel_id=1, source_target_pairs={{2,0},{4,2},{6,4},{8,6},{10,8},{12,10},{14,12},{16,14},{18,16},{20... | collective-permute-start | bytes 199688 | tf_op jit(solution)/shard_map/ppermute | solution.py:26
  9.3 8.7 %collective-permute-start.2 = (f32[65,1,8,128]{3,0,2,1:T(8,128)S(1)}, f32[65,1,8,128]{3,0,2,1:T(8,128)S(1)}, u32[]{:S(2)}, u32[]{:S(2)}) collective-permute-start(f32[65,1,8,128]{3,0,2,1:T(8,128)S(1)} %get-tuple-element.24), channel_id=1, source_target_pairs={{32,0},{64,32},{96,64},{128,96},{160,128},{192,160},{224,192},{0,2... | collective-permute-start | bytes 798728 | tf_op jit(solution)/shard_map/ppermute | solution.py:26
  11.5 7.4 %collective-permute-start.1 = (f32[65,1,8,128]{3,0,2,1:T(8,128)S(1)}, f32[65,1,8,128]{3,0,2,1:T(8,128)S(1)}, u32[]{:S(2)}, u32[]{:S(2)}) collective-permute-start(f32[65,1,8,128]{3,0,2,1:T(8,128)S(1)} %get-tuple-element.23), channel_id=1, source_target_pairs={{0,32},{32,64},{64,96},{96,128},{128,160},{160,192},{192,224},{224... | collective-permute-start | bytes 798728 | tf_op jit(solution)/shard_map/ppermute | solution.py:25
  11.5 6.5 %collective-permute-start = (f32[65,2,1,128]{3,0,2,1:T(8,128)S(1)}, f32[65,2,1,128]{3,0,2,1:T(8,128)S(1)}, u32[]{:S(2)}, u32[]{:S(2)}) collective-permute-start(f32[65,2,1,128]{3,0,2,1:T(8,128)S(1)} %get-tuple-element.21), channel_id=1, source_target_pairs={{0,2},{2,4},{4,6},{6,8},{8,10},{10,12},{12,14},{14,16},{16,18},{18... | collective-permute-start | bytes 199688 | tf_op jit(solution)/shard_map/ppermute | solution.py:25
  19.0 1.1 %copy-start = (f32[65,4,10,128]{3,0,2,1:T(8,128)}, f32[65,4,10,128]{3,0,2,1:T(8,128)S(1)}, u32[]{:S(2)}) copy-start(f32[65,4,10,128]{3,0,2,1:T(8,128)S(1)} %pad_maximum_fusion) | copy-start | bytes 3993604
  21.2 8.0 %collective-permute-start.4 = (f32[64,1,8,128]{3,0,2,1:T(8,128)S(1)}, f32[64,1,8,128]{3,0,2,1:T(8,128)S(1)}, u32[]{:S(2)}, u32[]{:S(2)}) collective-permute-start(f32[64,1,8,128]{3,0,2,1:T(8,128)S(1)} %get-tuple-element.36), channel_id=1, source_target_pairs={{32,0},{64,32},{96,64},{128,96},{160,128},{192,160},{224,192},{0,2... | collective-permute-start | bytes 786440 | tf_op jit(solution)/shard_map/ppermute | solution.py:26
  22.2 7.1 %collective-permute-start.5 = (f32[64,1,8,128]{3,0,2,1:T(8,128)S(1)}, f32[64,1,8,128]{3,0,2,1:T(8,128)S(1)}, u32[]{:S(2)}, u32[]{:S(2)}) collective-permute-start(f32[64,1,8,128]{3,0,2,1:T(8,128)S(1)} %get-tuple-element.35), channel_id=1, source_target_pairs={{0,32},{32,64},{64,96},{96,128},{128,160},{160,192},{192,224},{224... | collective-permute-start | bytes 786440 | tf_op jit(solution)/shard_map/ppermute | solution.py:25
  22.2 4.3 %collective-permute-start.6 = (f32[64,2,1,128]{3,0,2,1:T(8,128)S(1)}, f32[64,2,1,128]{3,0,2,1:T(8,128)S(1)}, u32[]{:S(2)}, u32[]{:S(2)}) collective-permute-start(f32[64,2,1,128]{3,0,2,1:T(8,128)S(1)} %get-tuple-element.34), channel_id=1, source_target_pairs={{2,0},{4,2},{6,4},{8,6},{10,8},{12,10},{14,12},{16,14},{18,16},{20... | collective-permute-start | bytes 196616 | tf_op jit(solution)/shard_map/ppermute | solution.py:26
  22.9 6.4 %collective-permute-start.7 = (f32[64,2,1,128]{3,0,2,1:T(8,128)S(1)}, f32[64,2,1,128]{3,0,2,1:T(8,128)S(1)}, u32[]{:S(2)}, u32[]{:S(2)}) collective-permute-start(f32[64,2,1,128]{3,0,2,1:T(8,128)S(1)} %get-tuple-element.33), channel_id=1, source_target_pairs={{0,2},{2,4},{4,6},{6,8},{8,10},{10,12},{12,14},{14,16},{16,18},{18... | collective-permute-start | bytes 196616 | tf_op jit(solution)/shard_map/ppermute | solution.py:25
  30.4 4.3 %collective-permute-start.10 = (f32[64,2,1,128]{3,0,2,1:T(8,128)S(1)}, f32[64,2,1,128]{3,0,2,1:T(8,128)S(1)}, u32[]{:S(2)}, u32[]{:S(2)}) collective-permute-start(f32[64,2,1,128]{3,0,2,1:T(8,128)S(1)} %get-tuple-element.30), channel_id=1, source_target_pairs={{2,0},{4,2},{6,4},{8,6},{10,8},{12,10},{14,12},{16,14},{18,16},{20... | collective-permute-start | bytes 196616 | tf_op jit(solution)/shard_map/ppermute | solution.py:26
  30.5 7.7 %collective-permute-start.8 = (f32[64,1,8,128]{3,0,2,1:T(8,128)S(1)}, f32[64,1,8,128]{3,0,2,1:T(8,128)S(1)}, u32[]{:S(2)}, u32[]{:S(2)}) collective-permute-start(f32[64,1,8,128]{3,0,2,1:T(8,128)S(1)} %get-tuple-element.32), channel_id=1, source_target_pairs={{32,0},{64,32},{96,64},{128,96},{160,128},{192,160},{224,192},{0,2... | collective-permute-start | bytes 786440 | tf_op jit(solution)/shard_map/ppermute | solution.py:26
  31.9 7.0 %collective-permute-start.9 = (f32[64,1,8,128]{3,0,2,1:T(8,128)S(1)}, f32[64,1,8,128]{3,0,2,1:T(8,128)S(1)}, u32[]{:S(2)}, u32[]{:S(2)}) collective-permute-start(f32[64,1,8,128]{3,0,2,1:T(8,128)S(1)} %get-tuple-element.31), channel_id=1, source_target_pairs={{0,32},{32,64},{64,96},{96,128},{128,160},{160,192},{192,224},{224... | collective-permute-start | bytes 786440 | tf_op jit(solution)/shard_map/ppermute | solution.py:25
  31.9 6.4 %collective-permute-start.11 = (f32[64,2,1,128]{3,0,2,1:T(8,128)S(1)}, f32[64,2,1,128]{3,0,2,1:T(8,128)S(1)}, u32[]{:S(2)}, u32[]{:S(2)}) collective-permute-start(f32[64,2,1,128]{3,0,2,1:T(8,128)S(1)} %get-tuple-element.29), channel_id=1, source_target_pairs={{0,2},{2,4},{4,6},{6,8},{8,10},{10,12},{12,14},{14,16},{16,18},{18... | collective-permute-start | bytes 196616 | tf_op jit(solution)/shard_map/ppermute | solution.py:25
  34.8 4.6 %copy-start.10 = (f32[64,4,1,128]{3,0,2,1:T(8,128)}, f32[64,4,1,128]{3,0,2,1:T(8,128)S(1)}, u32[]{:S(2)}) copy-start(f32[64,4,1,128]{3,0,2,1:T(8,128)S(1)} %pad.53) | copy-start | bytes 393220
  38.3 1.1 %copy-start.12 = (f32[64,4,1,128]{3,0,2,1:T(8,128)}, f32[64,4,1,128]{3,0,2,1:T(8,128)S(1)}, u32[]{:S(2)}) copy-start(f32[64,4,1,128]{3,0,2,1:T(8,128)S(1)} %pad.54) | copy-start | bytes 393220
  39.9 1.0 copy-start.7
  40.6 1.4 %collective-permute-start.12 = (f32[4,64,64]{2,1,0:T(8,128)S(1)}, f32[4,64,64]{2,1,0:T(8,128)S(1)}, u32[]{:S(2)}, u32[]{:S(2)}) collective-permute-start(f32[4,64,64]{2,1,0:T(8,128)S(1)} %pad_maximum_fusion.29), channel_id=1, source_target_pairs={{0,32},{32,0},{64,96},{96,64},{128,160},{160,128},{192,224},{224,1... | collective-permute-start | bytes 196616 | tf_op jit(solution)/shard_map/ppermute | solution.py:46
  42.0 8.0 %collective-permute-start.14 = (f32[4,64,64]{2,1,0:T(8,128)S(1)}, f32[4,64,64]{2,1,0:T(8,128)S(1)}, u32[]{:S(2)}, u32[]{:S(2)}) collective-permute-start(f32[4,64,64]{2,1,0:T(8,128)S(1)} %fusion.60), channel_id=1, source_target_pairs={{0,128},{32,160},{64,192},{96,224},{128,0},{160,32},{192,64},{224,... | collective-permute-start | bytes 196616 | tf_op jit(solution)/shard_map/ppermute | solution.py:50
  42.1 9.8 %collective-permute-start.15 = (f32[4,64,64]{2,1,0:T(8,128)S(1)}, f32[4,64,64]{2,1,0:T(8,128)S(1)}, u32[]{:S(2)}, u32[]{:S(2)}) collective-permute-start(f32[4,64,64]{2,1,0:T(8,128)S(1)} %fusion.60), channel_id=1, source_target_pairs={{0,192},{32,224},{64,128},{96,160},{128,64},{160,96},{192,0},{224,... | collective-permute-start | bytes 196616 | tf_op jit(solution)/shard_map/ppermute | solution.py:50
  43.6 8.3 %collective-permute-start.13 = (f32[4,64,64]{2,1,0:T(8,128)S(1)}, f32[4,64,64]{2,1,0:T(8,128)S(1)}, u32[]{:S(2)}, u32[]{:S(2)}) collective-permute-start(f32[4,64,64]{2,1,0:T(8,128)S(1)} %fusion.60), channel_id=1, source_target_pairs={{0,64},{32,96},{64,0},{96,32},{128,192},{160,224},{192,128},{224,1... | collective-permute-start | bytes 196616 | tf_op jit(solution)/shard_map/ppermute | solution.py:50
  46.2 10.7 %collective-permute-start.24 = (f32[64,2,1,128]{3,0,2,1:T(8,128)S(1)}, f32[64,2,1,128]{3,0,2,1:T(8,128)}, u32[]{:S(2)}, u32[]{:S(2)}) collective-permute-start(f32[64,2,1,128]{3,0,2,1:T(8,128)S(1)} %get-tuple-element.26), channel_id=1, source_target_pairs={{2,0},{4,2},{6,4},{8,6},{10,8},{12,10},{14,12},{16,14},{18,16},{20... | collective-permute-start | bytes 196616 | tf_op jit(solution)/shard_map/ppermute | solution.py:26
  46.5 11.3 %collective-permute-start.25 = (f32[64,2,1,128]{3,0,2,1:T(8,128)}, f32[64,2,1,128]{3,0,2,1:T(8,128)}, u32[]{:S(2)}, u32[]{:S(2)}) collective-permute-start(f32[64,2,1,128]{3,0,2,1:T(8,128)} %get-tuple-element.25), channel_id=1, source_target_pairs={{0,2},{2,4},{4,6},{6,8},{8,10},{10,12},{12,14},{14,16},{16,18},{18... | collective-permute-start | bytes 196616 | tf_op jit(solution)/shard_map/ppermute | solution.py:25
  52.0 13.0 %collective-permute-start.17 = (f32[4,64,64]{2,1,0:T(8,128)S(1)}, f32[4,64,64]{2,1,0:T(8,128)S(1)}, u32[]{:S(2)}, u32[]{:S(2)}) collective-permute-start(f32[4,64,64]{2,1,0:T(8,128)S(1)} %add_add_fusion.2), channel_id=1, source_target_pairs={{0,4},{2,6},{4,0},{6,2},{8,12},{10,14},{12,8},{14,10},{16,20},{18,... | collective-permute-start | bytes 196616 | tf_op jit(solution)/shard_map/ppermute | solution.py:50
  52.8 12.2 %collective-permute-start.18 = (f32[4,64,64]{2,1,0:T(8,128)S(1)}, f32[4,64,64]{2,1,0:T(8,128)S(1)}, u32[]{:S(2)}, u32[]{:S(2)}) collective-permute-start(f32[4,64,64]{2,1,0:T(8,128)S(1)} %add_add_fusion.2), channel_id=1, source_target_pairs={{0,6},{2,4},{4,2},{6,0},{8,14},{10,12},{12,10},{14,8},{16,22},{18,... | collective-permute-start | bytes 196616 | tf_op jit(solution)/shard_map/ppermute | solution.py:50
  56.2 9.2 %collective-permute-start.16 = (f32[4,64,64]{2,1,0:T(8,128)S(1)}, f32[4,64,64]{2,1,0:T(8,128)S(1)}, u32[]{:S(2)}, u32[]{:S(2)}) collective-permute-start(f32[4,64,64]{2,1,0:T(8,128)S(1)} %add_add_fusion.2), channel_id=1, source_target_pairs={{0,2},{2,0},{4,6},{6,4},{8,10},{10,8},{12,14},{14,12},{16,18},{18,... | collective-permute-start | bytes 196616 | tf_op jit(solution)/shard_map/ppermute | solution.py:50
  56.9 16.0 %collective-permute-start.23 = (f32[64,1,8,128]{3,0,2,1:T(8,128)S(1)}, f32[64,1,8,128]{3,0,2,1:T(8,128)}, u32[]{:S(2)}, u32[]{:S(2)}) collective-permute-start(f32[64,1,8,128]{3,0,2,1:T(8,128)S(1)} %get-tuple-element.28), channel_id=1, source_target_pairs={{0,32},{32,64},{64,96},{96,128},{128,160},{160,192},{192,224},{224... | collective-permute-start | bytes 786440 | tf_op jit(solution)/shard_map/ppermute | solution.py:25
  57.8 18.0 %copy-start.14 = (f32[64,4,1,128]{3,0,2,1:T(8,128)}, f32[64,4,1,128]{3,0,2,1:T(8,128)S(1)}, u32[]{:S(2)}) copy-start(f32[64,4,1,128]{3,0,2,1:T(8,128)S(1)} %pad.56) | copy-start | bytes 393220
  57.8 17.3 %collective-permute-start.22 = (f32[64,1,8,128]{3,0,2,1:T(8,128)}, f32[64,1,8,128]{3,0,2,1:T(8,128)S(1)}, u32[]{:S(2)}, u32[]{:S(2)}) collective-permute-start(f32[64,1,8,128]{3,0,2,1:T(8,128)} %get-tuple-element.27), channel_id=1, source_target_pairs={{32,0},{64,32},{96,64},{128,96},{160,128},{192,160},{224,192},{0,2... | collective-permute-start | bytes 786440 | tf_op jit(solution)/shard_map/ppermute | solution.py:26
  61.6 14.2 %copy-start.16 = (f32[64,4,1,128]{3,0,2,1:T(8,128)}, f32[64,4,1,128]{3,0,2,1:T(8,128)S(1)}, u32[]{:S(2)}) copy-start(f32[64,4,1,128]{3,0,2,1:T(8,128)S(1)} %pad.57) | copy-start | bytes 393220
  65.4 12.7 %collective-permute-start.20 = (f32[4,64,64]{2,1,0:T(8,128)S(1)}, f32[4,64,64]{2,1,0:T(8,128)S(1)}, u32[]{:S(2)}, u32[]{:S(2)}) collective-permute-start(f32[4,64,64]{2,1,0:T(8,128)S(1)} %add_add_fusion.1), channel_id=1, source_target_pairs={{0,16},{2,18},{4,20},{6,22},{8,24},{10,26},{12,28},{14,30},{16,0},... | collective-permute-start | bytes 196616 | tf_op jit(solution)/shard_map/ppermute | solution.py:50
  66.3 11.9 %collective-permute-start.21 = (f32[4,64,64]{2,1,0:T(8,128)S(1)}, f32[4,64,64]{2,1,0:T(8,128)S(1)}, u32[]{:S(2)}, u32[]{:S(2)}) collective-permute-start(f32[4,64,64]{2,1,0:T(8,128)S(1)} %add_add_fusion.1), channel_id=1, source_target_pairs={{0,24},{2,26},{4,28},{6,30},{8,16},{10,18},{12,20},{14,22},{16,8},... | collective-permute-start | bytes 196616 | tf_op jit(solution)/shard_map/ppermute | solution.py:50
  66.3 16.7 %collective-permute-start.19 = (f32[4,64,64]{2,1,0:T(8,128)S(1)}, f32[4,64,64]{2,1,0:T(8,128)S(1)}, u32[]{:S(2)}, u32[]{:S(2)}) collective-permute-start(f32[4,64,64]{2,1,0:T(8,128)S(1)} %add_add_fusion.1), channel_id=1, source_target_pairs={{0,8},{2,10},{4,12},{6,14},{8,0},{10,2},{12,4},{14,6},{16,24},{18,... | collective-permute-start | bytes 196616 | tf_op jit(solution)/shard_map/ppermute | solution.py:50
  75.8 2.3 %copy-start.3 = (f32[64,4,8,128]{3,0,2,1:T(8,128)}, f32[64,4,8,128]{3,0,2,1:T(8,128)S(1)}, u32[]{:S(2)}) copy-start(f32[64,4,8,128]{3,0,2,1:T(8,128)S(1)} %constant_dynamic-update-slice_fusion) | copy-start | bytes 3145732
  83.7 8.7 %copy-start.6 = (f32[64,1,8,128]{3,0,2,1:T(8,128)S(1)}, f32[64,1,8,128]{3,0,2,1:T(8,128)}, u32[]{:S(2)}) copy-start(f32[64,1,8,128]{3,0,2,1:T(8,128)} %copy-done.5) | copy-start | bytes 786436
  83.7 8.7 %copy-start.11 = (f32[64,4,1,128]{3,0,2,1:T(8,128)S(1)}, f32[64,4,1,128]{3,0,2,1:T(8,128)}, u32[]{:S(2)}) copy-start(f32[64,4,1,128]{3,0,2,1:T(8,128)} %copy-done.10) | copy-start | bytes 393220
  83.7 8.7 %copy-start.13 = (f32[64,4,1,128]{3,0,2,1:T(8,128)S(1)}, f32[64,4,1,128]{3,0,2,1:T(8,128)}, u32[]{:S(2)}) copy-start(f32[64,4,1,128]{3,0,2,1:T(8,128)} %copy-done.12) | copy-start | bytes 393220
  92.4 2.2 %copy-start.1 = (f32[65,4,10,128]{3,0,2,1:T(8,128)S(1)}, f32[65,4,10,128]{3,0,2,1:T(8,128)}, u32[]{:S(2)}) copy-start(f32[65,4,10,128]{3,0,2,1:T(8,128)} %copy-done) | copy-start | bytes 3993604
  92.5 2.2 %copy-start.9 = (f32[64,4,1,128]{3,0,2,1:T(8,128)S(1)}, f32[64,4,1,128]{3,0,2,1:T(8,128)}, u32[]{:S(2)}) copy-start(f32[64,4,1,128]{3,0,2,1:T(8,128)} %copy-done.8) | copy-start | bytes 393220
  92.5 2.2 %copy-start.21 = (f32[2,64,64]{2,1,0:T(8,128)S(1)}, f32[2,64,64]{2,1,0:T(8,128)}, u32[]{:S(2)}) copy-start(f32[2,64,64]{2,1,0:T(8,128)} %shard_map.68) | copy-start | bytes 98308
  94.6 1.6 %copy-start.4 = (f32[64,4,8,128]{3,0,2,1:T(8,128)S(1)}, f32[64,4,8,128]{3,0,2,1:T(8,128)}, u32[]{:S(2)}) copy-start(f32[64,4,8,128]{3,0,2,1:T(8,128)} %copy-done.3) | copy-start | bytes 3145732
  94.6 1.6 %copy-start.15 = (f32[64,4,1,128]{3,0,2,1:T(8,128)S(1)}, f32[64,4,1,128]{3,0,2,1:T(8,128)}, u32[]{:S(2)}) copy-start(f32[64,4,1,128]{3,0,2,1:T(8,128)} %copy-done.14) | copy-start | bytes 393220
  94.7 1.6 %copy-start.17 = (f32[64,4,1,128]{3,0,2,1:T(8,128)S(1)}, f32[64,4,1,128]{3,0,2,1:T(8,128)}, u32[]{:S(2)}) copy-start(f32[64,4,1,128]{3,0,2,1:T(8,128)} %copy-done.16) | copy-start | bytes 393220
  94.7 2.1 %copy-start.2 = (f32[64,4,10,130]{3,0,2,1:T(8,128)S(1)}, f32[64,4,10,130]{3,0,2,1:T(8,128)}, u32[]{:S(2)}) copy-start(f32[64,4,10,130]{3,0,2,1:T(8,128)} %select_maximum_fusion) | copy-start | bytes 3993604
  96.8 0.9 copy-start.19
  99.1 5.2 %collective-permute-start.26 = (f32[2,8,64]{2,1,0:T(8,128)S(1)}, f32[2,8,64]{2,1,0:T(8,128)S(1)}, u32[]{:S(2)}, u32[]{:S(2)}) collective-permute-start(f32[2,8,64]{2,1,0:T(8,128)S(1)} %constant_dynamic-slice_fusion), channel_id=1, source_target_pairs={{0,1},{1,0},{2,3},{3,2},{4,5},{5,4},{6,7},{7,6},{8,9},{9,8},{10,11... | collective-permute-start | bytes 12296 | tf_op jit(solution)/shard_map/ppermute | solution.py:296
  (3 other events, 2.1 us)

commit v13 on v12

--- a/solution.py
+++ b/solution.py
@@ -206,11 +206,8 @@
     turn = _mm(rr_inv, new_gram)
     keep = eye + turn
     keep_t = _tr(keep)
-    curv = (
-        _mm(keep_t, _mm(g_rq, keep))
-        - _mm(keep_t, _mm(g_qq, step0))
-        - _mm(step0_t, _mm(g_qq, keep))
-        + _mm(step0_t, _mm(g_qw, step0))
+    curv = _mm(keep_t, _mm(g_rq, keep) - _mm(g_qq, step0)) + _mm(
+        step0_t, _mm(g_qw, step0) - _mm(g_qq, keep)
     )
     (step1,) = _solve([(curv, new_gram)], True)
     out_ref[0] = step0 + _mm(keep, step1)

time: 106 us -> 106 us (level)
  no operation moved by 1% of the time
where the time goes in v13:
time: 106 us; the launch traced here: 105 us
  starting transfers between devices  36.1 us (34%)
  waiting for transfers between devices  30.7 us (29%)
  other arithmetic  11.8 us (11%)
  local copies, waits for them, and re-layouts  10.4 us (10%)
  Pallas kernels  8.6 us (8%)
  matrix products  5.88 us (6%)
  between operations  1.34 us (1%)
    ppermute x9, starting transfers between devices, allsum(): lax.ppermute(value, axis, [(i, i ^ d << shift) for i in range(count)])  15.2 us
    ppermute x8, starting transfers between devices, padded_2(): high = lax.ppermute(bottom, axis, backward)  15 us
    ppermute x8, waiting for transfers between devices, padded_2(): low = lax.ppermute(top, axis, forward)  12.6 us
    ppermute x9, waiting for transfers between devices, allsum(): lax.ppermute(value, axis, [(i, i ^ d << shift) for i in range(count)])  12.3 us
    pallas_call x1, Pallas kernels, steps(): pl.pallas_call(steps_kernel, out_shape=jax.ShapeDtypeStruct((2, n, n), jn...  8.6 us
    unnamed x53, local copies, waits for them, and re-layouts  7.56 us
    ppermute x8, starting transfers between devices, padded_2(): low = lax.ppermute(top, axis, forward)  5 us
    dot_general x2, matrix products, combine_cols(): jnp.einsum('axyz,ab->bxyz', field, matrix, precision=lax.Precision.HIGHEST)  3.64 us
  transfers between devices with their start and end apart: 27, of which 14 were waited for; matrix products, arithmetic and copies ran while one was open for 12% of the time, Pallas kernels for 0%

profile of v13, /device:TPU:4, one launch (start us, length us, event | category | flops | bytes accessed | tf_op | source)
XLA Modules:
  0.0 104.8 jit_solution(8596970678076314479)
XLA Ops:
  0.7 1.2 %copy.35 = f32[64,2,8,128]{3,0,2,1:T(8,128)S(1)} copy(f32[64,2,8,128]{3,2,1,0:T(8,128)} %param.8) | data formatting | bytes 1048576 | tf_op args[3]
  1.9 0.7 maximum_select_fusion
  2.6 6.6 %collective-permute-start.3 = (f32[65,2,1,128]{3,0,2,1:T(8,128)S(1)}, f32[65,2,1,128]{3,0,2,1:T(8,128)S(1)}, u32[]{:S(2)}, u32[]{:S(2)}) collective-permute-start(f32[65,2,1,128]{3,0,2,1:T(8,128)S(1)} %get-tuple-element.22), channel_id=1, source_target_pairs={{2,0},{4,2},{6,4},{8,6},{10,8},{12,10},{14,12},{16,14},{18,16},{20... | collective-permute-start | bytes 199688 | tf_op jit(solution)/shard_map/ppermute | solution.py:26
  9.3 2.2 %collective-permute-start.2 = (f32[65,1,8,128]{3,0,2,1:T(8,128)S(1)}, f32[65,1,8,128]{3,0,2,1:T(8,128)S(1)}, u32[]{:S(2)}, u32[]{:S(2)}) collective-permute-start(f32[65,1,8,128]{3,0,2,1:T(8,128)S(1)} %get-tuple-element.24), channel_id=1, source_target_pairs={{32,0},{64,32},{96,64},{128,96},{160,128},{192,160},{224,192},{0,2... | collective-permute-start | bytes 798728 | tf_op jit(solution)/shard_map/ppermute | solution.py:26
  11.6 0.6 gather_fusion
  12.9 5.0 %collective-permute-done = f32[65,2,1,128]{3,0,2,1:T(8,128)S(1)} collective-permute-done((f32[65,2,1,128]{3,0,2,1:T(8,128)S(1)}, f32[65,2,1,128]{3,0,2,1:T(8,128)S(1)}, u32[]{:S(2)}, u32[]{:S(2)}) %collective-permute-start) | collective-permute-done | bytes 66592 | tf_op jit(solution)/shard_map/ppermute | solution.py:25
  17.9 0.9 collective-permute-done.1
  19.3 0.9 copy-done
  21.2 1.0 collective-permute-start.4
  22.2 0.6 collective-permute-start.6
  22.9 1.5 %collective-permute-start.7 = (f32[64,2,1,128]{3,0,2,1:T(8,128)S(1)}, f32[64,2,1,128]{3,0,2,1:T(8,128)S(1)}, u32[]{:S(2)}, u32[]{:S(2)}) collective-permute-start(f32[64,2,1,128]{3,0,2,1:T(8,128)S(1)} %get-tuple-element.33), channel_id=1, source_target_pairs={{0,2},{2,4},{4,6},{6,8},{8,10},{10,12},{12,14},{14,16},{16,18},{18... | collective-permute-start | bytes 196616 | tf_op jit(solution)/shard_map/ppermute | solution.py:25
  24.9 1.7 %collective-permute-done.6 = f32[64,2,1,128]{3,0,2,1:T(8,128)S(1)} collective-permute-done((f32[64,2,1,128]{3,0,2,1:T(8,128)S(1)}, f32[64,2,1,128]{3,0,2,1:T(8,128)S(1)}, u32[]{:S(2)}, u32[]{:S(2)}) %collective-permute-start.6) | collective-permute-done | bytes 65568 | tf_op jit(solution)/shard_map/ppermute | solution.py:26
  26.6 2.7 %collective-permute-done.7 = f32[64,2,1,128]{3,0,2,1:T(8,128)S(1)} collective-permute-done((f32[64,2,1,128]{3,0,2,1:T(8,128)S(1)}, f32[64,2,1,128]{3,0,2,1:T(8,128)S(1)}, u32[]{:S(2)}, u32[]{:S(2)}) %collective-permute-start.7) | collective-permute-done | bytes 65568 | tf_op jit(solution)/shard_map/ppermute | solution.py:25
  30.5 1.3 %collective-permute-start.8 = (f32[64,1,8,128]{3,0,2,1:T(8,128)S(1)}, f32[64,1,8,128]{3,0,2,1:T(8,128)S(1)}, u32[]{:S(2)}, u32[]{:S(2)}) collective-permute-start(f32[64,1,8,128]{3,0,2,1:T(8,128)S(1)} %get-tuple-element.32), channel_id=1, source_target_pairs={{32,0},{64,32},{96,64},{128,96},{160,128},{192,160},{224,192},{0,2... | collective-permute-start | bytes 786440 | tf_op jit(solution)/shard_map/ppermute | solution.py:26
  31.9 1.7 %collective-permute-start.11 = (f32[64,2,1,128]{3,0,2,1:T(8,128)S(1)}, f32[64,2,1,128]{3,0,2,1:T(8,128)S(1)}, u32[]{:S(2)}, u32[]{:S(2)}) collective-permute-start(f32[64,2,1,128]{3,0,2,1:T(8,128)S(1)} %get-tuple-element.29), channel_id=1, source_target_pairs={{0,2},{2,4},{4,6},{6,8},{8,10},{10,12},{12,14},{14,16},{16,18},{18... | collective-permute-start | bytes 196616 | tf_op jit(solution)/shard_map/ppermute | solution.py:25
  34.8 3.4 %collective-permute-done.11 = f32[64,2,1,128]{3,0,2,1:T(8,128)S(1)} collective-permute-done((f32[64,2,1,128]{3,0,2,1:T(8,128)S(1)}, f32[64,2,1,128]{3,0,2,1:T(8,128)S(1)}, u32[]{:S(2)}, u32[]{:S(2)}) %collective-permute-start.11) | collective-permute-done | bytes 65568 | tf_op jit(solution)/shard_map/ppermute | solution.py:25
  38.3 0.6 collective-permute-done.9
  41.2 0.8 collective-permute-done.12
  42.1 1.5 %collective-permute-start.15 = (f32[4,64,64]{2,1,0:T(8,128)S(1)}, f32[4,64,64]{2,1,0:T(8,128)S(1)}, u32[]{:S(2)}, u32[]{:S(2)}) collective-permute-start(f32[4,64,64]{2,1,0:T(8,128)S(1)} %fusion.60), channel_id=1, source_target_pairs={{0,192},{32,224},{64,128},{96,160},{128,64},{160,96},{192,0},{224,... | collective-permute-start | bytes 196616 | tf_op jit(solution)/shard_map/ppermute | solution.py:50
  43.6 1.9 %collective-permute-start.13 = (f32[4,64,64]{2,1,0:T(8,128)S(1)}, f32[4,64,64]{2,1,0:T(8,128)S(1)}, u32[]{:S(2)}, u32[]{:S(2)}) collective-permute-start(f32[4,64,64]{2,1,0:T(8,128)S(1)} %fusion.60), channel_id=1, source_target_pairs={{0,64},{32,96},{64,0},{96,32},{128,192},{160,224},{192,128},{224,1... | collective-permute-start | bytes 196616 | tf_op jit(solution)/shard_map/ppermute | solution.py:50
  45.6 0.6 slice_select_fusion.6
  46.5 1.8 %collective-permute-start.25 = (f32[64,2,1,128]{3,0,2,1:T(8,128)}, f32[64,2,1,128]{3,0,2,1:T(8,128)}, u32[]{:S(2)}, u32[]{:S(2)}) collective-permute-start(f32[64,2,1,128]{3,0,2,1:T(8,128)} %get-tuple-element.25), channel_id=1, source_target_pairs={{0,2},{2,4},{4,6},{6,8},{8,10},{10,12},{12,14},{14,16},{16,18},{18... | collective-permute-start | bytes 196616 | tf_op jit(solution)/shard_map/ppermute | solution.py:25
  48.3 1.8 %collective-permute-done.14 = f32[4,64,64]{2,1,0:T(8,128)S(1)} collective-permute-done((f32[4,64,64]{2,1,0:T(8,128)S(1)}, f32[4,64,64]{2,1,0:T(8,128)S(1)}, u32[]{:S(2)}, u32[]{:S(2)}) %collective-permute-start.14) | collective-permute-done | bytes 65568 | tf_op jit(solution)/shard_map/ppermute | solution.py:50
  50.0 1.9 %collective-permute-done.15 = f32[4,64,64]{2,1,0:T(8,128)S(1)} collective-permute-done((f32[4,64,64]{2,1,0:T(8,128)S(1)}, f32[4,64,64]{2,1,0:T(8,128)S(1)}, u32[]{:S(2)}, u32[]{:S(2)}) %collective-permute-start.15) | collective-permute-done | bytes 65568 | tf_op jit(solution)/shard_map/ppermute | solution.py:50
  52.0 0.8 collective-permute-start.17
  52.8 3.4 %collective-permute-start.18 = (f32[4,64,64]{2,1,0:T(8,128)S(1)}, f32[4,64,64]{2,1,0:T(8,128)S(1)}, u32[]{:S(2)}, u32[]{:S(2)}) collective-permute-start(f32[4,64,64]{2,1,0:T(8,128)S(1)} %add_add_fusion.2), channel_id=1, source_target_pairs={{0,6},{2,4},{4,2},{6,0},{8,14},{10,12},{12,10},{14,8},{16,22},{18,... | collective-permute-start | bytes 196616 | tf_op jit(solution)/shard_map/ppermute | solution.py:50
  56.2 0.8 slice_select_fusion.1
  56.9 0.9 pad.56
  57.8 3.0 %collective-permute-start.22 = (f32[64,1,8,128]{3,0,2,1:T(8,128)}, f32[64,1,8,128]{3,0,2,1:T(8,128)S(1)}, u32[]{:S(2)}, u32[]{:S(2)}) collective-permute-start(f32[64,1,8,128]{3,0,2,1:T(8,128)} %get-tuple-element.27), channel_id=1, source_target_pairs={{32,0},{64,32},{96,64},{128,96},{160,128},{192,160},{224,192},{0,2... | collective-permute-start | bytes 786440 | tf_op jit(solution)/shard_map/ppermute | solution.py:26
  60.8 0.8 pad.57
  61.6 3.4 %collective-permute-done.17 = f32[4,64,64]{2,1,0:T(8,128)S(1)} collective-permute-done((f32[4,64,64]{2,1,0:T(8,128)S(1)}, f32[4,64,64]{2,1,0:T(8,128)S(1)}, u32[]{:S(2)}, u32[]{:S(2)}) %collective-permute-start.17) | collective-permute-done | bytes 65568 | tf_op jit(solution)/shard_map/ppermute | solution.py:50
  65.4 0.9 collective-permute-start.20
  66.3 6.6 %collective-permute-start.19 = (f32[4,64,64]{2,1,0:T(8,128)S(1)}, f32[4,64,64]{2,1,0:T(8,128)S(1)}, u32[]{:S(2)}, u32[]{:S(2)}) collective-permute-start(f32[4,64,64]{2,1,0:T(8,128)S(1)} %add_add_fusion.1), channel_id=1, source_target_pairs={{0,8},{2,10},{4,12},{6,14},{8,0},{10,2},{12,4},{14,6},{16,24},{18,... | collective-permute-start | bytes 196616 | tf_op jit(solution)/shard_map/ppermute | solution.py:50
  72.9 1.0 constant_dynamic-update-slice_fusion.2
  73.9 1.2 %constant_dynamic-update-slice_fusion.1 = f32[64,4,8,128]{3,0,2,1:T(8,128)S(1)} fusion(f32[64,4,8,128]{3,0,2,1:T(8,128)S(1)} %constant_dynamic-update-slice_fusion.2, f32[64,2,8,128]{3,2,1,0:T(8,128)} %param.9), kind=kLoop, calls=%fused_computation.186 | loop fusion | bytes 1048576
  75.1 0.7 copy-done.18
  75.8 2.2 %select_maximum_fusion = f32[64,4,10,130]{3,0,2,1:T(8,128)} fusion(f32[64,4,1,128]{3,0,2,1:T(8,128)S(1)} %pad.56, f32[64,4,8,128]{3,0,2,1:T(8,128)S(1)} %constant_dynamic-update-slice_fusion, f32[64,4,1,128]{3,0,2,1:T(8,128)S(1)} %pad.57), kind=kLoop, calls=%fused_computation.11 | loop fusion | flops 2662400 | bytes 2641920 | tf_op jit(solution)/shard_map/concatenate | solution.py:35
  78.2 4.8 %collective-permute-done.19 = f32[4,64,64]{2,1,0:T(8,128)S(1)} collective-permute-done((f32[4,64,64]{2,1,0:T(8,128)S(1)}, f32[4,64,64]{2,1,0:T(8,128)S(1)}, u32[]{:S(2)}, u32[]{:S(2)}) %collective-permute-start.19) | collective-permute-done | bytes 65568 | tf_op jit(solution)/shard_map/ppermute | solution.py:50
  83.0 0.7 add_add_fusion.grams_ref
  83.7 8.6 %shard_map.68 = f32[2,64,64]{2,1,0:T(8,128)} custom-call(f32[4,64,64]{2,1,0:T(8,128)} %add_add_fusion.grams_ref), custom_call_target="tpu_custom_call" | custom-call | flops 20000000000 | bytes 98304 | tf_op jit(solution)/shard_map/pallas_call | solution.py:219
  92.3 2.1 %fusion.48 = f32[64,4,10,128]{3,0,2,1:T(8,128)S(1)} fusion(f32[2,64,64]{2,1,0:T(8,128)} %shard_map.68, f32[64,4,1,128]{3,0,2,1:T(8,128)S(1)} %copy-done.11, f32[64,1,8,128]{3,0,2,1:T(8,128)S(1)} %collective-permute-done.8, f32[64,2,8,128]{3,0,2,1:T(8,128)S(1)} %fusion.28, f32[64,1,8,128]{3,0,2,1:T(8,128)S(1)} %copy-done.6, f32[64,4,1,128]{3,0,2,1:T(8,128)S(1)} %copy-done.13), kind=kOutput, calls=%fused_computation.157 | convolution fusion | flops 252968960 | bytes 2654208 | tf_op jit(solution)/shard_map/axyz,ab->bxyz/dot_general | solution.py:84
  94.5 1.5 %fusion.1 = f32[64,4,10,128]{3,0,2,1:T(8,128)S(1)} fusion(f32[64,4,10,128]{3,0,2,1:T(8,128)S(1)} %fusion.48, f32[2,64,64]{2,1,0:T(8,128)S(1)} %copy-done.21, f32[65,4,10,128]{3,0,2,1:T(8,128)S(1)} %copy-done.1, f32[64,4,1,128]{3,0,2,1:T(8,128)S(1)} %pad.50, f32[64,1,8,128]{3,0,2,1:T(8,128)S(1)} %collective-permute-done.4, ...), kind=kOutput, calls=%fused_computation.16 | convolution fusion | flops 253624320 | bytes 5275648 | tf_op jit(solution)/shard_map/axyz,ab->bxyz/dot_general | solution.py:84
  96.7 0.6 fusion.10
  97.6 1.2 %fusion.12 = f32[3,8,128]{2,1,0:T(8,128)S(1)} fusion(f32[64,4,10,128]{3,0,2,1:T(8,128)S(1)} %fusion.1, f32[64,1,8,128]{3,0,2,1:T(8,128)S(1)} %copy-done.19, f32[64,2,8,128]{3,0,2,1:T(8,128)S(1)} %copy.44, f32[64,1,8,128]{3,0,2,1:T(8,128)} %collective-permute-done.23), kind=kLoop, calls=%fused_computation.37 | loop fusion | flops 1176576 | bytes 2633728 | tf_op jit(solution)/shard_map/reduce_sum | solution.py:102
  98.9 0.8 collective-permute-start.26
  99.8 1.1 %copy.50 = f32[64,2,8,128]{3,2,1,0:T(8,128)} copy(f32[64,2,8,128]{3,0,2,1:T(8,128)S(1)} %slice.407) | data formatting | bytes 1048576
  100.9 3.2 %collective-permute-done.26 = f32[2,8,64]{2,1,0:T(8,128)S(1)} collective-permute-done((f32[2,8,64]{2,1,0:T(8,128)S(1)}, f32[2,8,64]{2,1,0:T(8,128)S(1)}, u32[]{:S(2)}, u32[]{:S(2)}) %collective-permute-start.26) | collective-permute-done | bytes 4128 | tf_op jit(solution)/shard_map/ppermute | solution.py:293
  104.1 0.7 dynamic-slice_add_fusion
  (134 shorter events, 9.6 us)
Async XLA Ops:
  0.6 8.6 %copy-start.20 = (f32[2,8,128]{2,1,0:T(8,128)S(1)}, f32[2,8,128]{2,1,0:T(8,128)}, u32[]{:S(2)}) copy-start(f32[2,8,128]{2,1,0:T(8,128)} %param.5) | copy-start | bytes 24580
  0.6 10.8 %copy-start.23 = (s32[64]{0:T(128)S(1)}, s32[64]{0:T(128)}, u32[]{:S(2)}) copy-start(s32[64]{0:T(128)} %param.7) | copy-start | bytes 772
  0.7 10.8 %copy-start.22 = (s32[128,2]{0,1:T(2,128)S(1)}, s32[128,2]{0,1:T(2,128)}, u32[]{:S(2)}) copy-start(s32[128,2]{0,1:T(2,128)} %param.6) | copy-start | bytes 3076
  2.6 10.3 %collective-permute-start.3 = (f32[65,2,1,128]{3,0,2,1:T(8,128)S(1)}, f32[65,2,1,128]{3,0,2,1:T(8,128)S(1)}, u32[]{:S(2)}, u32[]{:S(2)}) collective-permute-start(f32[65,2,1,128]{3,0,2,1:T(8,128)S(1)} %get-tuple-element.22), channel_id=1, source_target_pairs={{2,0},{4,2},{6,4},{8,6},{10,8},{12,10},{14,12},{16,14},{18,16},{20... | collective-permute-start | bytes 199688 | tf_op jit(solution)/shard_map/ppermute | solution.py:26
  9.3 8.7 %collective-permute-start.2 = (f32[65,1,8,128]{3,0,2,1:T(8,128)S(1)}, f32[65,1,8,128]{3,0,2,1:T(8,128)S(1)}, u32[]{:S(2)}, u32[]{:S(2)}) collective-permute-start(f32[65,1,8,128]{3,0,2,1:T(8,128)S(1)} %get-tuple-element.24), channel_id=1, source_target_pairs={{32,0},{64,32},{96,64},{128,96},{160,128},{192,160},{224,192},{0,2... | collective-permute-start | bytes 798728 | tf_op jit(solution)/shard_map/ppermute | solution.py:26
  11.5 7.4 %collective-permute-start.1 = (f32[65,1,8,128]{3,0,2,1:T(8,128)S(1)}, f32[65,1,8,128]{3,0,2,1:T(8,128)S(1)}, u32[]{:S(2)}, u32[]{:S(2)}) collective-permute-start(f32[65,1,8,128]{3,0,2,1:T(8,128)S(1)} %get-tuple-element.23), channel_id=1, source_target_pairs={{0,32},{32,64},{64,96},{96,128},{128,160},{160,192},{192,224},{224... | collective-permute-start | bytes 798728 | tf_op jit(solution)/shard_map/ppermute | solution.py:25
  11.5 6.5 %collective-permute-start = (f32[65,2,1,128]{3,0,2,1:T(8,128)S(1)}, f32[65,2,1,128]{3,0,2,1:T(8,128)S(1)}, u32[]{:S(2)}, u32[]{:S(2)}) collective-permute-start(f32[65,2,1,128]{3,0,2,1:T(8,128)S(1)} %get-tuple-element.21), channel_id=1, source_target_pairs={{0,2},{2,4},{4,6},{6,8},{8,10},{10,12},{12,14},{14,16},{16,18},{18... | collective-permute-start | bytes 199688 | tf_op jit(solution)/shard_map/ppermute | solution.py:25
  19.0 1.1 %copy-start = (f32[65,4,10,128]{3,0,2,1:T(8,128)}, f32[65,4,10,128]{3,0,2,1:T(8,128)S(1)}, u32[]{:S(2)}) copy-start(f32[65,4,10,128]{3,0,2,1:T(8,128)S(1)} %pad_maximum_fusion) | copy-start | bytes 3993604
  21.2 8.0 %collective-permute-start.4 = (f32[64,1,8,128]{3,0,2,1:T(8,128)S(1)}, f32[64,1,8,128]{3,0,2,1:T(8,128)S(1)}, u32[]{:S(2)}, u32[]{:S(2)}) collective-permute-start(f32[64,1,8,128]{3,0,2,1:T(8,128)S(1)} %get-tuple-element.36), channel_id=1, source_target_pairs={{32,0},{64,32},{96,64},{128,96},{160,128},{192,160},{224,192},{0,2... | collective-permute-start | bytes 786440 | tf_op jit(solution)/shard_map/ppermute | solution.py:26
  22.2 7.1 %collective-permute-start.5 = (f32[64,1,8,128]{3,0,2,1:T(8,128)S(1)}, f32[64,1,8,128]{3,0,2,1:T(8,128)S(1)}, u32[]{:S(2)}, u32[]{:S(2)}) collective-permute-start(f32[64,1,8,128]{3,0,2,1:T(8,128)S(1)} %get-tuple-element.35), channel_id=1, source_target_pairs={{0,32},{32,64},{64,96},{96,128},{128,160},{160,192},{192,224},{224... | collective-permute-start | bytes 786440 | tf_op jit(solution)/shard_map/ppermute | solution.py:25
  22.2 4.3 %collective-permute-start.6 = (f32[64,2,1,128]{3,0,2,1:T(8,128)S(1)}, f32[64,2,1,128]{3,0,2,1:T(8,128)S(1)}, u32[]{:S(2)}, u32[]{:S(2)}) collective-permute-start(f32[64,2,1,128]{3,0,2,1:T(8,128)S(1)} %get-tuple-element.34), channel_id=1, source_target_pairs={{2,0},{4,2},{6,4},{8,6},{10,8},{12,10},{14,12},{16,14},{18,16},{20... | collective-permute-start | bytes 196616 | tf_op jit(solution)/shard_map/ppermute | solution.py:26
  22.9 6.4 %collective-permute-start.7 = (f32[64,2,1,128]{3,0,2,1:T(8,128)S(1)}, f32[64,2,1,128]{3,0,2,1:T(8,128)S(1)}, u32[]{:S(2)}, u32[]{:S(2)}) collective-permute-start(f32[64,2,1,128]{3,0,2,1:T(8,128)S(1)} %get-tuple-element.33), channel_id=1, source_target_pairs={{0,2},{2,4},{4,6},{6,8},{8,10},{10,12},{12,14},{14,16},{16,18},{18... | collective-permute-start | bytes 196616 | tf_op jit(solution)/shard_map/ppermute | solution.py:25
  30.4 4.3 %collective-permute-start.10 = (f32[64,2,1,128]{3,0,2,1:T(8,128)S(1)}, f32[64,2,1,128]{3,0,2,1:T(8,128)S(1)}, u32[]{:S(2)}, u32[]{:S(2)}) collective-permute-start(f32[64,2,1,128]{3,0,2,1:T(8,128)S(1)} %get-tuple-element.30), channel_id=1, source_target_pairs={{2,0},{4,2},{6,4},{8,6},{10,8},{12,10},{14,12},{16,14},{18,16},{20... | collective-permute-start | bytes 196616 | tf_op jit(solution)/shard_map/ppermute | solution.py:26
  30.5 7.7 %collective-permute-start.8 = (f32[64,1,8,128]{3,0,2,1:T(8,128)S(1)}, f32[64,1,8,128]{3,0,2,1:T(8,128)S(1)}, u32[]{:S(2)}, u32[]{:S(2)}) collective-permute-start(f32[64,1,8,128]{3,0,2,1:T(8,128)S(1)} %get-tuple-element.32), channel_id=1, source_target_pairs={{32,0},{64,32},{96,64},{128,96},{160,128},{192,160},{224,192},{0,2... | collective-permute-start | bytes 786440 | tf_op jit(solution)/shard_map/ppermute | solution.py:26
  31.9 7.0 %collective-permute-start.9 = (f32[64,1,8,128]{3,0,2,1:T(8,128)S(1)}, f32[64,1,8,128]{3,0,2,1:T(8,128)S(1)}, u32[]{:S(2)}, u32[]{:S(2)}) collective-permute-start(f32[64,1,8,128]{3,0,2,1:T(8,128)S(1)} %get-tuple-element.31), channel_id=1, source_target_pairs={{0,32},{32,64},{64,96},{96,128},{128,160},{160,192},{192,224},{224... | collective-permute-start | bytes 786440 | tf_op jit(solution)/shard_map/ppermute | solution.py:25
  31.9 6.4 %collective-permute-start.11 = (f32[64,2,1,128]{3,0,2,1:T(8,128)S(1)}, f32[64,2,1,128]{3,0,2,1:T(8,128)S(1)}, u32[]{:S(2)}, u32[]{:S(2)}) collective-permute-start(f32[64,2,1,128]{3,0,2,1:T(8,128)S(1)} %get-tuple-element.29), channel_id=1, source_target_pairs={{0,2},{2,4},{4,6},{6,8},{8,10},{10,12},{12,14},{14,16},{16,18},{18... | collective-permute-start | bytes 196616 | tf_op jit(solution)/shard_map/ppermute | solution.py:25
  34.8 4.6 %copy-start.10 = (f32[64,4,1,128]{3,0,2,1:T(8,128)}, f32[64,4,1,128]{3,0,2,1:T(8,128)S(1)}, u32[]{:S(2)}) copy-start(f32[64,4,1,128]{3,0,2,1:T(8,128)S(1)} %pad.53) | copy-start | bytes 393220
  38.3 1.1 %copy-start.12 = (f32[64,4,1,128]{3,0,2,1:T(8,128)}, f32[64,4,1,128]{3,0,2,1:T(8,128)S(1)}, u32[]{:S(2)}) copy-start(f32[64,4,1,128]{3,0,2,1:T(8,128)S(1)} %pad.54) | copy-start | bytes 393220
  39.9 1.0 copy-start.7
  40.6 1.4 %collective-permute-start.12 = (f32[4,64,64]{2,1,0:T(8,128)S(1)}, f32[4,64,64]{2,1,0:T(8,128)S(1)}, u32[]{:S(2)}, u32[]{:S(2)}) collective-permute-start(f32[4,64,64]{2,1,0:T(8,128)S(1)} %pad_maximum_fusion.29), channel_id=1, source_target_pairs={{0,32},{32,0},{64,96},{96,64},{128,160},{160,128},{192,224},{224,1... | collective-permute-start | bytes 196616 | tf_op jit(solution)/shard_map/ppermute | solution.py:46
  42.0 8.0 %collective-permute-start.14 = (f32[4,64,64]{2,1,0:T(8,128)S(1)}, f32[4,64,64]{2,1,0:T(8,128)S(1)}, u32[]{:S(2)}, u32[]{:S(2)}) collective-permute-start(f32[4,64,64]{2,1,0:T(8,128)S(1)} %fusion.60), channel_id=1, source_target_pairs={{0,128},{32,160},{64,192},{96,224},{128,0},{160,32},{192,64},{224,... | collective-permute-start | bytes 196616 | tf_op jit(solution)/shard_map/ppermute | solution.py:50
  42.1 9.8 %collective-permute-start.15 = (f32[4,64,64]{2,1,0:T(8,128)S(1)}, f32[4,64,64]{2,1,0:T(8,128)S(1)}, u32[]{:S(2)}, u32[]{:S(2)}) collective-permute-start(f32[4,64,64]{2,1,0:T(8,128)S(1)} %fusion.60), channel_id=1, source_target_pairs={{0,192},{32,224},{64,128},{96,160},{128,64},{160,96},{192,0},{224,... | collective-permute-start | bytes 196616 | tf_op jit(solution)/shard_map/ppermute | solution.py:50
  43.6 8.3 %collective-permute-start.13 = (f32[4,64,64]{2,1,0:T(8,128)S(1)}, f32[4,64,64]{2,1,0:T(8,128)S(1)}, u32[]{:S(2)}, u32[]{:S(2)}) collective-permute-start(f32[4,64,64]{2,1,0:T(8,128)S(1)} %fusion.60), channel_id=1, source_target_pairs={{0,64},{32,96},{64,0},{96,32},{128,192},{160,224},{192,128},{224,1... | collective-permute-start | bytes 196616 | tf_op jit(solution)/shard_map/ppermute | solution.py:50
  46.2 10.7 %collective-permute-start.24 = (f32[64,2,1,128]{3,0,2,1:T(8,128)S(1)}, f32[64,2,1,128]{3,0,2,1:T(8,128)}, u32[]{:S(2)}, u32[]{:S(2)}) collective-permute-start(f32[64,2,1,128]{3,0,2,1:T(8,128)S(1)} %get-tuple-element.26), channel_id=1, source_target_pairs={{2,0},{4,2},{6,4},{8,6},{10,8},{12,10},{14,12},{16,14},{18,16},{20... | collective-permute-start | bytes 196616 | tf_op jit(solution)/shard_map/ppermute | solution.py:26
  46.5 11.3 %collective-permute-start.25 = (f32[64,2,1,128]{3,0,2,1:T(8,128)}, f32[64,2,1,128]{3,0,2,1:T(8,128)}, u32[]{:S(2)}, u32[]{:S(2)}) collective-permute-start(f32[64,2,1,128]{3,0,2,1:T(8,128)} %get-tuple-element.25), channel_id=1, source_target_pairs={{0,2},{2,4},{4,6},{6,8},{8,10},{10,12},{12,14},{14,16},{16,18},{18... | collective-permute-start | bytes 196616 | tf_op jit(solution)/shard_map/ppermute | solution.py:25
  52.0 13.0 %collective-permute-start.17 = (f32[4,64,64]{2,1,0:T(8,128)S(1)}, f32[4,64,64]{2,1,0:T(8,128)S(1)}, u32[]{:S(2)}, u32[]{:S(2)}) collective-permute-start(f32[4,64,64]{2,1,0:T(8,128)S(1)} %add_add_fusion.2), channel_id=1, source_target_pairs={{0,4},{2,6},{4,0},{6,2},{8,12},{10,14},{12,8},{14,10},{16,20},{18,... | collective-permute-start | bytes 196616 | tf_op jit(solution)/shard_map/ppermute | solution.py:50
  52.8 12.2 %collective-permute-start.18 = (f32[4,64,64]{2,1,0:T(8,128)S(1)}, f32[4,64,64]{2,1,0:T(8,128)S(1)}, u32[]{:S(2)}, u32[]{:S(2)}) collective-permute-start(f32[4,64,64]{2,1,0:T(8,128)S(1)} %add_add_fusion.2), channel_id=1, source_target_pairs={{0,6},{2,4},{4,2},{6,0},{8,14},{10,12},{12,10},{14,8},{16,22},{18,... | collective-permute-start | bytes 196616 | tf_op jit(solution)/shard_map/ppermute | solution.py:50
  56.2 9.2 %collective-permute-start.16 = (f32[4,64,64]{2,1,0:T(8,128)S(1)}, f32[4,64,64]{2,1,0:T(8,128)S(1)}, u32[]{:S(2)}, u32[]{:S(2)}) collective-permute-start(f32[4,64,64]{2,1,0:T(8,128)S(1)} %add_add_fusion.2), channel_id=1, source_target_pairs={{0,2},{2,0},{4,6},{6,4},{8,10},{10,8},{12,14},{14,12},{16,18},{18,... | collective-permute-start | bytes 196616 | tf_op jit(solution)/shard_map/ppermute | solution.py:50
  56.9 16.0 %collective-permute-start.23 = (f32[64,1,8,128]{3,0,2,1:T(8,128)S(1)}, f32[64,1,8,128]{3,0,2,1:T(8,128)}, u32[]{:S(2)}, u32[]{:S(2)}) collective-permute-start(f32[64,1,8,128]{3,0,2,1:T(8,128)S(1)} %get-tuple-element.28), channel_id=1, source_target_pairs={{0,32},{32,64},{64,96},{96,128},{128,160},{160,192},{192,224},{224... | collective-permute-start | bytes 786440 | tf_op jit(solution)/shard_map/ppermute | solution.py:25
  57.8 18.0 %copy-start.14 = (f32[64,4,1,128]{3,0,2,1:T(8,128)}, f32[64,4,1,128]{3,0,2,1:T(8,128)S(1)}, u32[]{:S(2)}) copy-start(f32[64,4,1,128]{3,0,2,1:T(8,128)S(1)} %pad.56) | copy-start | bytes 393220
  57.8 17.3 %collective-permute-start.22 = (f32[64,1,8,128]{3,0,2,1:T(8,128)}, f32[64,1,8,128]{3,0,2,1:T(8,128)S(1)}, u32[]{:S(2)}, u32[]{:S(2)}) collective-permute-start(f32[64,1,8,128]{3,0,2,1:T(8,128)} %get-tuple-element.27), channel_id=1, source_target_pairs={{32,0},{64,32},{96,64},{128,96},{160,128},{192,160},{224,192},{0,2... | collective-permute-start | bytes 786440 | tf_op jit(solution)/shard_map/ppermute | solution.py:26
  61.6 14.2 %copy-start.16 = (f32[64,4,1,128]{3,0,2,1:T(8,128)}, f32[64,4,1,128]{3,0,2,1:T(8,128)S(1)}, u32[]{:S(2)}) copy-start(f32[64,4,1,128]{3,0,2,1:T(8,128)S(1)} %pad.57) | copy-start | bytes 393220
  65.4 12.7 %collective-permute-start.20 = (f32[4,64,64]{2,1,0:T(8,128)S(1)}, f32[4,64,64]{2,1,0:T(8,128)S(1)}, u32[]{:S(2)}, u32[]{:S(2)}) collective-permute-start(f32[4,64,64]{2,1,0:T(8,128)S(1)} %add_add_fusion.1), channel_id=1, source_target_pairs={{0,16},{2,18},{4,20},{6,22},{8,24},{10,26},{12,28},{14,30},{16,0},... | collective-permute-start | bytes 196616 | tf_op jit(solution)/shard_map/ppermute | solution.py:50
  66.3 11.9 %collective-permute-start.21 = (f32[4,64,64]{2,1,0:T(8,128)S(1)}, f32[4,64,64]{2,1,0:T(8,128)S(1)}, u32[]{:S(2)}, u32[]{:S(2)}) collective-permute-start(f32[4,64,64]{2,1,0:T(8,128)S(1)} %add_add_fusion.1), channel_id=1, source_target_pairs={{0,24},{2,26},{4,28},{6,30},{8,16},{10,18},{12,20},{14,22},{16,8},... | collective-permute-start | bytes 196616 | tf_op jit(solution)/shard_map/ppermute | solution.py:50
  66.3 16.7 %collective-permute-start.19 = (f32[4,64,64]{2,1,0:T(8,128)S(1)}, f32[4,64,64]{2,1,0:T(8,128)S(1)}, u32[]{:S(2)}, u32[]{:S(2)}) collective-permute-start(f32[4,64,64]{2,1,0:T(8,128)S(1)} %add_add_fusion.1), channel_id=1, source_target_pairs={{0,8},{2,10},{4,12},{6,14},{8,0},{10,2},{12,4},{14,6},{16,24},{18,... | collective-permute-start | bytes 196616 | tf_op jit(solution)/shard_map/ppermute | solution.py:50
  75.8 2.3 %copy-start.3 = (f32[64,4,8,128]{3,0,2,1:T(8,128)}, f32[64,4,8,128]{3,0,2,1:T(8,128)S(1)}, u32[]{:S(2)}) copy-start(f32[64,4,8,128]{3,0,2,1:T(8,128)S(1)} %constant_dynamic-update-slice_fusion) | copy-start | bytes 3145732
  83.7 8.6 %copy-start.6 = (f32[64,1,8,128]{3,0,2,1:T(8,128)S(1)}, f32[64,1,8,128]{3,0,2,1:T(8,128)}, u32[]{:S(2)}) copy-start(f32[64,1,8,128]{3,0,2,1:T(8,128)} %copy-done.5) | copy-start | bytes 786436
  83.7 8.6 %copy-start.11 = (f32[64,4,1,128]{3,0,2,1:T(8,128)S(1)}, f32[64,4,1,128]{3,0,2,1:T(8,128)}, u32[]{:S(2)}) copy-start(f32[64,4,1,128]{3,0,2,1:T(8,128)} %copy-done.10) | copy-start | bytes 393220
  83.7 8.6 %copy-start.13 = (f32[64,4,1,128]{3,0,2,1:T(8,128)S(1)}, f32[64,4,1,128]{3,0,2,1:T(8,128)}, u32[]{:S(2)}) copy-start(f32[64,4,1,128]{3,0,2,1:T(8,128)} %copy-done.12) | copy-start | bytes 393220
  92.3 2.2 %copy-start.1 = (f32[65,4,10,128]{3,0,2,1:T(8,128)S(1)}, f32[65,4,10,128]{3,0,2,1:T(8,128)}, u32[]{:S(2)}) copy-start(f32[65,4,10,128]{3,0,2,1:T(8,128)} %copy-done) | copy-start | bytes 3993604
  92.3 2.2 %copy-start.9 = (f32[64,4,1,128]{3,0,2,1:T(8,128)S(1)}, f32[64,4,1,128]{3,0,2,1:T(8,128)}, u32[]{:S(2)}) copy-start(f32[64,4,1,128]{3,0,2,1:T(8,128)} %copy-done.8) | copy-start | bytes 393220
  92.3 2.2 %copy-start.21 = (f32[2,64,64]{2,1,0:T(8,128)S(1)}, f32[2,64,64]{2,1,0:T(8,128)}, u32[]{:S(2)}) copy-start(f32[2,64,64]{2,1,0:T(8,128)} %shard_map.68) | copy-start | bytes 98308
  94.5 1.6 %copy-start.4 = (f32[64,4,8,128]{3,0,2,1:T(8,128)S(1)}, f32[64,4,8,128]{3,0,2,1:T(8,128)}, u32[]{:S(2)}) copy-start(f32[64,4,8,128]{3,0,2,1:T(8,128)} %copy-done.3) | copy-start | bytes 3145732
  94.5 1.6 %copy-start.15 = (f32[64,4,1,128]{3,0,2,1:T(8,128)S(1)}, f32[64,4,1,128]{3,0,2,1:T(8,128)}, u32[]{:S(2)}) copy-start(f32[64,4,1,128]{3,0,2,1:T(8,128)} %copy-done.14) | copy-start | bytes 393220
  94.5 1.6 %copy-start.17 = (f32[64,4,1,128]{3,0,2,1:T(8,128)S(1)}, f32[64,4,1,128]{3,0,2,1:T(8,128)}, u32[]{:S(2)}) copy-start(f32[64,4,1,128]{3,0,2,1:T(8,128)} %copy-done.16) | copy-start | bytes 393220
  94.5 2.1 %copy-start.2 = (f32[64,4,10,130]{3,0,2,1:T(8,128)S(1)}, f32[64,4,10,130]{3,0,2,1:T(8,128)}, u32[]{:S(2)}) copy-start(f32[64,4,10,130]{3,0,2,1:T(8,128)} %select_maximum_fusion) | copy-start | bytes 3993604
  96.7 0.9 copy-start.19
  98.9 5.2 %collective-permute-start.26 = (f32[2,8,64]{2,1,0:T(8,128)S(1)}, f32[2,8,64]{2,1,0:T(8,128)S(1)}, u32[]{:S(2)}, u32[]{:S(2)}) collective-permute-start(f32[2,8,64]{2,1,0:T(8,128)S(1)} %constant_dynamic-slice_fusion), channel_id=1, source_target_pairs={{0,1},{1,0},{2,3},{3,2},{4,5},{5,4},{6,7},{7,6},{8,9},{9,8},{10,11... | collective-permute-start | bytes 12296 | tf_op jit(solution)/shard_map/ppermute | solution.py:293
  (3 other events, 2.1 us)

commit v14 on v13

--- a/solution.py
+++ b/solution.py
@@ -269,7 +269,10 @@
     )
 
     solved = steps(grams)
-    it2_pad = iter_pad + combine_cols(res_pad, solved[0]) + combine_cols(image_pad, solved[1])
+    def combine_high(field, matrix):
+        return jnp.einsum("axyz,ab->bxyz", field, matrix, precision=lax.Precision.HIGH)
+
+    it2_pad = iter_pad + combine_high(res_pad, solved[0]) + combine_high(image_pad, solved[1])
     iterate = it2_pad[:, 1:-1, 1:-1]
     term_x, term_y, term_z = face_terms(it2_pad, adjoint_pad)
     local_grad = (

time: 106 us -> 105 us (level)
  no operation moved by 1% of the time
where the time goes in v14:
time: 105 us; the launch traced here: 104 us
  starting transfers between devices  36.1 us (34%)
  waiting for transfers between devices  30.7 us (29%)
  other arithmetic  11.8 us (11%)
  local copies, waits for them, and re-layouts  10.9 us (10%)
  Pallas kernels  8.6 us (8%)
  matrix products  4.84 us (5%)
  between operations  1.31 us (1%)
    ppermute x9, starting transfers between devices, allsum(): lax.ppermute(value, axis, [(i, i ^ d << shift) for i in range(count)])  15.2 us
    ppermute x8, starting transfers between devices, padded_2(): high = lax.ppermute(bottom, axis, backward)  15 us
    ppermute x8, waiting for transfers between devices, padded_2(): low = lax.ppermute(top, axis, forward)  12.6 us
    ppermute x9, waiting for transfers between devices, allsum(): lax.ppermute(value, axis, [(i, i ^ d << shift) for i in range(count)])  12.3 us
    pallas_call x1, Pallas kernels, steps(): pl.pallas_call(steps_kernel, out_shape=jax.ShapeDtypeStruct((2, n, n), jn...  8.6 us
    unnamed x53, local copies, waits for them, and re-layouts  8.1 us
    ppermute x8, starting transfers between devices, padded_2(): low = lax.ppermute(top, axis, forward)  5 us
    ppermute x1, waiting for transfers between devices, on_device(): got = lax.ppermute(sent, 'src', [(0, 1), (1, 0)])  3.2 us
  transfers between devices with their start and end apart: 27, of which 14 were waited for; matrix products, arithmetic and copies ran while one was open for 12% of the time, Pallas kernels for 0%

profile of v14, /device:TPU:4, one launch (start us, length us, event | category | flops | bytes accessed | tf_op | source)
XLA Modules:
  0.0 104.3 jit_solution(12593863627184461708)
XLA Ops:
  0.7 1.2 %copy.35 = f32[64,2,8,128]{3,0,2,1:T(8,128)S(1)} copy(f32[64,2,8,128]{3,2,1,0:T(8,128)} %param.8) | data formatting | bytes 1048576 | tf_op args[3]
  1.9 0.7 maximum_select_fusion
  2.6 6.6 %collective-permute-start.3 = (f32[65,2,1,128]{3,0,2,1:T(8,128)S(1)}, f32[65,2,1,128]{3,0,2,1:T(8,128)S(1)}, u32[]{:S(2)}, u32[]{:S(2)}) collective-permute-start(f32[65,2,1,128]{3,0,2,1:T(8,128)S(1)} %get-tuple-element.22), channel_id=1, source_target_pairs={{2,0},{4,2},{6,4},{8,6},{10,8},{12,10},{14,12},{16,14},{18,16},{20... | collective-permute-start | bytes 199688 | tf_op jit(solution)/shard_map/ppermute | solution.py:26
  9.3 2.2 %collective-permute-start.2 = (f32[65,1,8,128]{3,0,2,1:T(8,128)S(1)}, f32[65,1,8,128]{3,0,2,1:T(8,128)S(1)}, u32[]{:S(2)}, u32[]{:S(2)}) collective-permute-start(f32[65,1,8,128]{3,0,2,1:T(8,128)S(1)} %get-tuple-element.24), channel_id=1, source_target_pairs={{32,0},{64,32},{96,64},{128,96},{160,128},{192,160},{224,192},{0,2... | collective-permute-start | bytes 798728 | tf_op jit(solution)/shard_map/ppermute | solution.py:26
  11.6 0.6 gather_fusion
  12.9 5.0 %collective-permute-done = f32[65,2,1,128]{3,0,2,1:T(8,128)S(1)} collective-permute-done((f32[65,2,1,128]{3,0,2,1:T(8,128)S(1)}, f32[65,2,1,128]{3,0,2,1:T(8,128)S(1)}, u32[]{:S(2)}, u32[]{:S(2)}) %collective-permute-start) | collective-permute-done | bytes 66592 | tf_op jit(solution)/shard_map/ppermute | solution.py:25
  17.9 0.9 collective-permute-done.1
  19.3 0.9 copy-done
  21.2 1.0 collective-permute-start.4
  22.2 0.6 collective-permute-start.6
  22.9 1.5 %collective-permute-start.7 = (f32[64,2,1,128]{3,0,2,1:T(8,128)S(1)}, f32[64,2,1,128]{3,0,2,1:T(8,128)S(1)}, u32[]{:S(2)}, u32[]{:S(2)}) collective-permute-start(f32[64,2,1,128]{3,0,2,1:T(8,128)S(1)} %get-tuple-element.33), channel_id=1, source_target_pairs={{0,2},{2,4},{4,6},{6,8},{8,10},{10,12},{12,14},{14,16},{16,18},{18... | collective-permute-start | bytes 196616 | tf_op jit(solution)/shard_map/ppermute | solution.py:25
  24.9 1.7 %collective-permute-done.6 = f32[64,2,1,128]{3,0,2,1:T(8,128)S(1)} collective-permute-done((f32[64,2,1,128]{3,0,2,1:T(8,128)S(1)}, f32[64,2,1,128]{3,0,2,1:T(8,128)S(1)}, u32[]{:S(2)}, u32[]{:S(2)}) %collective-permute-start.6) | collective-permute-done | bytes 65568 | tf_op jit(solution)/shard_map/ppermute | solution.py:26
  26.6 2.7 %collective-permute-done.7 = f32[64,2,1,128]{3,0,2,1:T(8,128)S(1)} collective-permute-done((f32[64,2,1,128]{3,0,2,1:T(8,128)S(1)}, f32[64,2,1,128]{3,0,2,1:T(8,128)S(1)}, u32[]{:S(2)}, u32[]{:S(2)}) %collective-permute-start.7) | collective-permute-done | bytes 65568 | tf_op jit(solution)/shard_map/ppermute | solution.py:25
  30.5 1.3 %collective-permute-start.8 = (f32[64,1,8,128]{3,0,2,1:T(8,128)S(1)}, f32[64,1,8,128]{3,0,2,1:T(8,128)S(1)}, u32[]{:S(2)}, u32[]{:S(2)}) collective-permute-start(f32[64,1,8,128]{3,0,2,1:T(8,128)S(1)} %get-tuple-element.32), channel_id=1, source_target_pairs={{32,0},{64,32},{96,64},{128,96},{160,128},{192,160},{224,192},{0,2... | collective-permute-start | bytes 786440 | tf_op jit(solution)/shard_map/ppermute | solution.py:26
  31.9 1.7 %collective-permute-start.11 = (f32[64,2,1,128]{3,0,2,1:T(8,128)S(1)}, f32[64,2,1,128]{3,0,2,1:T(8,128)S(1)}, u32[]{:S(2)}, u32[]{:S(2)}) collective-permute-start(f32[64,2,1,128]{3,0,2,1:T(8,128)S(1)} %get-tuple-element.29), channel_id=1, source_target_pairs={{0,2},{2,4},{4,6},{6,8},{8,10},{10,12},{12,14},{14,16},{16,18},{18... | collective-permute-start | bytes 196616 | tf_op jit(solution)/shard_map/ppermute | solution.py:25
  34.8 3.4 %collective-permute-done.11 = f32[64,2,1,128]{3,0,2,1:T(8,128)S(1)} collective-permute-done((f32[64,2,1,128]{3,0,2,1:T(8,128)S(1)}, f32[64,2,1,128]{3,0,2,1:T(8,128)S(1)}, u32[]{:S(2)}, u32[]{:S(2)}) %collective-permute-start.11) | collective-permute-done | bytes 65568 | tf_op jit(solution)/shard_map/ppermute | solution.py:25
  41.2 0.8 collective-permute-done.12
  42.1 1.5 %collective-permute-start.15 = (f32[4,64,64]{2,1,0:T(8,128)S(1)}, f32[4,64,64]{2,1,0:T(8,128)S(1)}, u32[]{:S(2)}, u32[]{:S(2)}) collective-permute-start(f32[4,64,64]{2,1,0:T(8,128)S(1)} %fusion.60), channel_id=1, source_target_pairs={{0,192},{32,224},{64,128},{96,160},{128,64},{160,96},{192,0},{224,... | collective-permute-start | bytes 196616 | tf_op jit(solution)/shard_map/ppermute | solution.py:50
  43.6 1.9 %collective-permute-start.13 = (f32[4,64,64]{2,1,0:T(8,128)S(1)}, f32[4,64,64]{2,1,0:T(8,128)S(1)}, u32[]{:S(2)}, u32[]{:S(2)}) collective-permute-start(f32[4,64,64]{2,1,0:T(8,128)S(1)} %fusion.60), channel_id=1, source_target_pairs={{0,64},{32,96},{64,0},{96,32},{128,192},{160,224},{192,128},{224,1... | collective-permute-start | bytes 196616 | tf_op jit(solution)/shard_map/ppermute | solution.py:50
  45.6 0.6 slice_select_fusion.6
  46.5 1.8 %collective-permute-start.25 = (f32[64,2,1,128]{3,0,2,1:T(8,128)}, f32[64,2,1,128]{3,0,2,1:T(8,128)}, u32[]{:S(2)}, u32[]{:S(2)}) collective-permute-start(f32[64,2,1,128]{3,0,2,1:T(8,128)} %get-tuple-element.25), channel_id=1, source_target_pairs={{0,2},{2,4},{4,6},{6,8},{8,10},{10,12},{12,14},{14,16},{16,18},{18... | collective-permute-start | bytes 196616 | tf_op jit(solution)/shard_map/ppermute | solution.py:25
  48.3 1.8 %collective-permute-done.14 = f32[4,64,64]{2,1,0:T(8,128)S(1)} collective-permute-done((f32[4,64,64]{2,1,0:T(8,128)S(1)}, f32[4,64,64]{2,1,0:T(8,128)S(1)}, u32[]{:S(2)}, u32[]{:S(2)}) %collective-permute-start.14) | collective-permute-done | bytes 65568 | tf_op jit(solution)/shard_map/ppermute | solution.py:50
  50.0 1.9 %collective-permute-done.15 = f32[4,64,64]{2,1,0:T(8,128)S(1)} collective-permute-done((f32[4,64,64]{2,1,0:T(8,128)S(1)}, f32[4,64,64]{2,1,0:T(8,128)S(1)}, u32[]{:S(2)}, u32[]{:S(2)}) %collective-permute-start.15) | collective-permute-done | bytes 65568 | tf_op jit(solution)/shard_map/ppermute | solution.py:50
  52.0 0.8 collective-permute-start.17
  52.8 3.4 %collective-permute-start.18 = (f32[4,64,64]{2,1,0:T(8,128)S(1)}, f32[4,64,64]{2,1,0:T(8,128)S(1)}, u32[]{:S(2)}, u32[]{:S(2)}) collective-permute-start(f32[4,64,64]{2,1,0:T(8,128)S(1)} %add_add_fusion.2), channel_id=1, source_target_pairs={{0,6},{2,4},{4,2},{6,0},{8,14},{10,12},{12,10},{14,8},{16,22},{18,... | collective-permute-start | bytes 196616 | tf_op jit(solution)/shard_map/ppermute | solution.py:50
  56.2 0.8 slice_select_fusion.1
  56.9 0.9 pad.56
  57.8 3.0 %collective-permute-start.22 = (f32[64,1,8,128]{3,0,2,1:T(8,128)}, f32[64,1,8,128]{3,0,2,1:T(8,128)S(1)}, u32[]{:S(2)}, u32[]{:S(2)}) collective-permute-start(f32[64,1,8,128]{3,0,2,1:T(8,128)} %get-tuple-element.27), channel_id=1, source_target_pairs={{32,0},{64,32},{96,64},{128,96},{160,128},{192,160},{224,192},{0,2... | collective-permute-start | bytes 786440 | tf_op jit(solution)/shard_map/ppermute | solution.py:26
  60.8 0.8 pad.57
  61.6 3.4 %collective-permute-done.17 = f32[4,64,64]{2,1,0:T(8,128)S(1)} collective-permute-done((f32[4,64,64]{2,1,0:T(8,128)S(1)}, f32[4,64,64]{2,1,0:T(8,128)S(1)}, u32[]{:S(2)}, u32[]{:S(2)}) %collective-permute-start.17) | collective-permute-done | bytes 65568 | tf_op jit(solution)/shard_map/ppermute | solution.py:50
  65.4 0.9 collective-permute-start.20
  66.3 6.6 %collective-permute-start.19 = (f32[4,64,64]{2,1,0:T(8,128)S(1)}, f32[4,64,64]{2,1,0:T(8,128)S(1)}, u32[]{:S(2)}, u32[]{:S(2)}) collective-permute-start(f32[4,64,64]{2,1,0:T(8,128)S(1)} %add_add_fusion.1), channel_id=1, source_target_pairs={{0,8},{2,10},{4,12},{6,14},{8,0},{10,2},{12,4},{14,6},{16,24},{18,... | collective-permute-start | bytes 196616 | tf_op jit(solution)/shard_map/ppermute | solution.py:50
  72.9 1.0 constant_dynamic-update-slice_fusion.2
  73.9 1.2 %constant_dynamic-update-slice_fusion.1 = f32[64,4,8,128]{3,0,2,1:T(8,128)S(1)} fusion(f32[64,4,8,128]{3,0,2,1:T(8,128)S(1)} %constant_dynamic-update-slice_fusion.2, f32[64,2,8,128]{3,2,1,0:T(8,128)} %param.9), kind=kLoop, calls=%fused_computation.186 | loop fusion | bytes 1048576
  75.1 0.7 copy-done.18
  75.8 2.2 %select_maximum_fusion = f32[64,4,10,130]{3,0,2,1:T(8,128)} fusion(f32[64,4,1,128]{3,0,2,1:T(8,128)S(1)} %pad.56, f32[64,4,8,128]{3,0,2,1:T(8,128)S(1)} %constant_dynamic-update-slice_fusion, f32[64,4,1,128]{3,0,2,1:T(8,128)S(1)} %pad.57), kind=kLoop, calls=%fused_computation.11 | loop fusion | flops 2662400 | bytes 2641920 | tf_op jit(solution)/shard_map/concatenate | solution.py:35
  78.2 4.8 %collective-permute-done.19 = f32[4,64,64]{2,1,0:T(8,128)S(1)} collective-permute-done((f32[4,64,64]{2,1,0:T(8,128)S(1)}, f32[4,64,64]{2,1,0:T(8,128)S(1)}, u32[]{:S(2)}, u32[]{:S(2)}) %collective-permute-start.19) | collective-permute-done | bytes 65568 | tf_op jit(solution)/shard_map/ppermute | solution.py:50
  83.0 0.7 add_add_fusion.grams_ref
  83.7 8.6 %shard_map.68 = f32[2,64,64]{2,1,0:T(8,128)} custom-call(f32[4,64,64]{2,1,0:T(8,128)} %add_add_fusion.grams_ref), custom_call_target="tpu_custom_call" | custom-call | flops 20000000000 | bytes 98304 | tf_op jit(solution)/shard_map/pallas_call | solution.py:219
  92.3 1.6 %fusion.48 = f32[64,4,10,128]{3,0,2,1:T(8,128)S(1)} fusion(f32[2,64,64]{2,1,0:T(8,128)} %shard_map.68, f32[64,4,1,128]{3,0,2,1:T(8,128)S(1)} %copy-done.11, f32[64,1,8,128]{3,0,2,1:T(8,128)S(1)} %collective-permute-done.8, f32[64,2,8,128]{3,0,2,1:T(8,128)S(1)} %fusion.28, f32[64,1,8,128]{3,0,2,1:T(8,128)S(1)} %copy-done.6, f32[64,4,1,128]{3,0,2,1:T(8,128)S(1)} %copy-done.13), kind=kOutput, calls=%fused_computation.157 | convolution fusion | flops 127139840 | bytes 2654208 | tf_op jit(solution)/shard_map/axyz,ab->bxyz/dot_general | solution.py:273
  94.0 1.0 fusion.1
  95.4 0.8 copy-done.2
  96.1 0.6 fusion.10
  97.1 1.2 %fusion.12 = f32[3,8,128]{2,1,0:T(8,128)S(1)} fusion(f32[64,4,10,128]{3,0,2,1:T(8,128)S(1)} %fusion.1, f32[64,1,8,128]{3,0,2,1:T(8,128)S(1)} %copy-done.19, f32[64,2,8,128]{3,0,2,1:T(8,128)S(1)} %copy.44, f32[64,1,8,128]{3,0,2,1:T(8,128)} %collective-permute-done.23), kind=kLoop, calls=%fused_computation.37 | loop fusion | flops 1176576 | bytes 2633728 | tf_op jit(solution)/shard_map/reduce_sum | solution.py:102
  98.4 0.8 collective-permute-start.26
  99.3 1.1 %copy.50 = f32[64,2,8,128]{3,2,1,0:T(8,128)} copy(f32[64,2,8,128]{3,0,2,1:T(8,128)S(1)} %slice.407) | data formatting | bytes 1048576
  100.4 3.2 %collective-permute-done.26 = f32[2,8,64]{2,1,0:T(8,128)S(1)} collective-permute-done((f32[2,8,64]{2,1,0:T(8,128)S(1)}, f32[2,8,64]{2,1,0:T(8,128)S(1)}, u32[]{:S(2)}, u32[]{:S(2)}) %collective-permute-start.26) | collective-permute-done | bytes 4128 | tf_op jit(solution)/shard_map/ppermute | solution.py:296
  103.6 0.7 dynamic-slice_add_fusion
  (134 shorter events, 10.0 us)
Async XLA Ops:
  0.6 8.6 %copy-start.20 = (f32[2,8,128]{2,1,0:T(8,128)S(1)}, f32[2,8,128]{2,1,0:T(8,128)}, u32[]{:S(2)}) copy-start(f32[2,8,128]{2,1,0:T(8,128)} %param.5) | copy-start | bytes 24580
  0.6 10.8 %copy-start.23 = (s32[64]{0:T(128)S(1)}, s32[64]{0:T(128)}, u32[]{:S(2)}) copy-start(s32[64]{0:T(128)} %param.7) | copy-start | bytes 772
  0.7 10.8 %copy-start.22 = (s32[128,2]{0,1:T(2,128)S(1)}, s32[128,2]{0,1:T(2,128)}, u32[]{:S(2)}) copy-start(s32[128,2]{0,1:T(2,128)} %param.6) | copy-start | bytes 3076
  2.6 10.3 %collective-permute-start.3 = (f32[65,2,1,128]{3,0,2,1:T(8,128)S(1)}, f32[65,2,1,128]{3,0,2,1:T(8,128)S(1)}, u32[]{:S(2)}, u32[]{:S(2)}) collective-permute-start(f32[65,2,1,128]{3,0,2,1:T(8,128)S(1)} %get-tuple-element.22), channel_id=1, source_target_pairs={{2,0},{4,2},{6,4},{8,6},{10,8},{12,10},{14,12},{16,14},{18,16},{20... | collective-permute-start | bytes 199688 | tf_op jit(solution)/shard_map/ppermute | solution.py:26
  9.3 8.7 %collective-permute-start.2 = (f32[65,1,8,128]{3,0,2,1:T(8,128)S(1)}, f32[65,1,8,128]{3,0,2,1:T(8,128)S(1)}, u32[]{:S(2)}, u32[]{:S(2)}) collective-permute-start(f32[65,1,8,128]{3,0,2,1:T(8,128)S(1)} %get-tuple-element.24), channel_id=1, source_target_pairs={{32,0},{64,32},{96,64},{128,96},{160,128},{192,160},{224,192},{0,2... | collective-permute-start | bytes 798728 | tf_op jit(solution)/shard_map/ppermute | solution.py:26
  11.5 7.4 %collective-permute-start.1 = (f32[65,1,8,128]{3,0,2,1:T(8,128)S(1)}, f32[65,1,8,128]{3,0,2,1:T(8,128)S(1)}, u32[]{:S(2)}, u32[]{:S(2)}) collective-permute-start(f32[65,1,8,128]{3,0,2,1:T(8,128)S(1)} %get-tuple-element.23), channel_id=1, source_target_pairs={{0,32},{32,64},{64,96},{96,128},{128,160},{160,192},{192,224},{224... | collective-permute-start | bytes 798728 | tf_op jit(solution)/shard_map/ppermute | solution.py:25
  11.5 6.5 %collective-permute-start = (f32[65,2,1,128]{3,0,2,1:T(8,128)S(1)}, f32[65,2,1,128]{3,0,2,1:T(8,128)S(1)}, u32[]{:S(2)}, u32[]{:S(2)}) collective-permute-start(f32[65,2,1,128]{3,0,2,1:T(8,128)S(1)} %get-tuple-element.21), channel_id=1, source_target_pairs={{0,2},{2,4},{4,6},{6,8},{8,10},{10,12},{12,14},{14,16},{16,18},{18... | collective-permute-start | bytes 199688 | tf_op jit(solution)/shard_map/ppermute | solution.py:25
  19.0 1.1 %copy-start = (f32[65,4,10,128]{3,0,2,1:T(8,128)}, f32[65,4,10,128]{3,0,2,1:T(8,128)S(1)}, u32[]{:S(2)}) copy-start(f32[65,4,10,128]{3,0,2,1:T(8,128)S(1)} %pad_maximum_fusion) | copy-start | bytes 3993604
  21.2 8.0 %collective-permute-start.4 = (f32[64,1,8,128]{3,0,2,1:T(8,128)S(1)}, f32[64,1,8,128]{3,0,2,1:T(8,128)S(1)}, u32[]{:S(2)}, u32[]{:S(2)}) collective-permute-start(f32[64,1,8,128]{3,0,2,1:T(8,128)S(1)} %get-tuple-element.36), channel_id=1, source_target_pairs={{32,0},{64,32},{96,64},{128,96},{160,128},{192,160},{224,192},{0,2... | collective-permute-start | bytes 786440 | tf_op jit(solution)/shard_map/ppermute | solution.py:26
  22.2 7.1 %collective-permute-start.5 = (f32[64,1,8,128]{3,0,2,1:T(8,128)S(1)}, f32[64,1,8,128]{3,0,2,1:T(8,128)S(1)}, u32[]{:S(2)}, u32[]{:S(2)}) collective-permute-start(f32[64,1,8,128]{3,0,2,1:T(8,128)S(1)} %get-tuple-element.35), channel_id=1, source_target_pairs={{0,32},{32,64},{64,96},{96,128},{128,160},{160,192},{192,224},{224... | collective-permute-start | bytes 786440 | tf_op jit(solution)/shard_map/ppermute | solution.py:25
  22.2 4.3 %collective-permute-start.6 = (f32[64,2,1,128]{3,0,2,1:T(8,128)S(1)}, f32[64,2,1,128]{3,0,2,1:T(8,128)S(1)}, u32[]{:S(2)}, u32[]{:S(2)}) collective-permute-start(f32[64,2,1,128]{3,0,2,1:T(8,128)S(1)} %get-tuple-element.34), channel_id=1, source_target_pairs={{2,0},{4,2},{6,4},{8,6},{10,8},{12,10},{14,12},{16,14},{18,16},{20... | collective-permute-start | bytes 196616 | tf_op jit(solution)/shard_map/ppermute | solution.py:26
  22.9 6.4 %collective-permute-start.7 = (f32[64,2,1,128]{3,0,2,1:T(8,128)S(1)}, f32[64,2,1,128]{3,0,2,1:T(8,128)S(1)}, u32[]{:S(2)}, u32[]{:S(2)}) collective-permute-start(f32[64,2,1,128]{3,0,2,1:T(8,128)S(1)} %get-tuple-element.33), channel_id=1, source_target_pairs={{0,2},{2,4},{4,6},{6,8},{8,10},{10,12},{12,14},{14,16},{16,18},{18... | collective-permute-start | bytes 196616 | tf_op jit(solution)/shard_map/ppermute | solution.py:25
  30.4 4.3 %collective-permute-start.10 = (f32[64,2,1,128]{3,0,2,1:T(8,128)S(1)}, f32[64,2,1,128]{3,0,2,1:T(8,128)S(1)}, u32[]{:S(2)}, u32[]{:S(2)}) collective-permute-start(f32[64,2,1,128]{3,0,2,1:T(8,128)S(1)} %get-tuple-element.30), channel_id=1, source_target_pairs={{2,0},{4,2},{6,4},{8,6},{10,8},{12,10},{14,12},{16,14},{18,16},{20... | collective-permute-start | bytes 196616 | tf_op jit(solution)/shard_map/ppermute | solution.py:26
  30.5 7.7 %collective-permute-start.8 = (f32[64,1,8,128]{3,0,2,1:T(8,128)S(1)}, f32[64,1,8,128]{3,0,2,1:T(8,128)S(1)}, u32[]{:S(2)}, u32[]{:S(2)}) collective-permute-start(f32[64,1,8,128]{3,0,2,1:T(8,128)S(1)} %get-tuple-element.32), channel_id=1, source_target_pairs={{32,0},{64,32},{96,64},{128,96},{160,128},{192,160},{224,192},{0,2... | collective-permute-start | bytes 786440 | tf_op jit(solution)/shard_map/ppermute | solution.py:26
  31.9 7.0 %collective-permute-start.9 = (f32[64,1,8,128]{3,0,2,1:T(8,128)S(1)}, f32[64,1,8,128]{3,0,2,1:T(8,128)S(1)}, u32[]{:S(2)}, u32[]{:S(2)}) collective-permute-start(f32[64,1,8,128]{3,0,2,1:T(8,128)S(1)} %get-tuple-element.31), channel_id=1, source_target_pairs={{0,32},{32,64},{64,96},{96,128},{128,160},{160,192},{192,224},{224... | collective-permute-start | bytes 786440 | tf_op jit(solution)/shard_map/ppermute | solution.py:25
  31.9 6.4 %collective-permute-start.11 = (f32[64,2,1,128]{3,0,2,1:T(8,128)S(1)}, f32[64,2,1,128]{3,0,2,1:T(8,128)S(1)}, u32[]{:S(2)}, u32[]{:S(2)}) collective-permute-start(f32[64,2,1,128]{3,0,2,1:T(8,128)S(1)} %get-tuple-element.29), channel_id=1, source_target_pairs={{0,2},{2,4},{4,6},{6,8},{8,10},{10,12},{12,14},{14,16},{16,18},{18... | collective-permute-start | bytes 196616 | tf_op jit(solution)/shard_map/ppermute | solution.py:25
  34.8 4.6 %copy-start.10 = (f32[64,4,1,128]{3,0,2,1:T(8,128)}, f32[64,4,1,128]{3,0,2,1:T(8,128)S(1)}, u32[]{:S(2)}) copy-start(f32[64,4,1,128]{3,0,2,1:T(8,128)S(1)} %pad.53) | copy-start | bytes 393220
  38.3 1.1 %copy-start.12 = (f32[64,4,1,128]{3,0,2,1:T(8,128)}, f32[64,4,1,128]{3,0,2,1:T(8,128)S(1)}, u32[]{:S(2)}) copy-start(f32[64,4,1,128]{3,0,2,1:T(8,128)S(1)} %pad.54) | copy-start | bytes 393220
  39.9 1.0 %copy-start.7 = (f32[64,2,8,128]{3,2,1,0:T(8,128)S(1)}, f32[64,2,8,128]{3,2,1,0:T(8,128)}, u32[]{:S(2)}) copy-start(f32[64,2,8,128]{3,2,1,0:T(8,128)} %param.9) | copy-start | bytes 1572868
  40.6 1.4 %collective-permute-start.12 = (f32[4,64,64]{2,1,0:T(8,128)S(1)}, f32[4,64,64]{2,1,0:T(8,128)S(1)}, u32[]{:S(2)}, u32[]{:S(2)}) collective-permute-start(f32[4,64,64]{2,1,0:T(8,128)S(1)} %pad_maximum_fusion.29), channel_id=1, source_target_pairs={{0,32},{32,0},{64,96},{96,64},{128,160},{160,128},{192,224},{224,1... | collective-permute-start | bytes 196616 | tf_op jit(solution)/shard_map/ppermute | solution.py:46
  42.0 8.0 %collective-permute-start.14 = (f32[4,64,64]{2,1,0:T(8,128)S(1)}, f32[4,64,64]{2,1,0:T(8,128)S(1)}, u32[]{:S(2)}, u32[]{:S(2)}) collective-permute-start(f32[4,64,64]{2,1,0:T(8,128)S(1)} %fusion.60), channel_id=1, source_target_pairs={{0,128},{32,160},{64,192},{96,224},{128,0},{160,32},{192,64},{224,... | collective-permute-start | bytes 196616 | tf_op jit(solution)/shard_map/ppermute | solution.py:50
  42.1 9.8 %collective-permute-start.15 = (f32[4,64,64]{2,1,0:T(8,128)S(1)}, f32[4,64,64]{2,1,0:T(8,128)S(1)}, u32[]{:S(2)}, u32[]{:S(2)}) collective-permute-start(f32[4,64,64]{2,1,0:T(8,128)S(1)} %fusion.60), channel_id=1, source_target_pairs={{0,192},{32,224},{64,128},{96,160},{128,64},{160,96},{192,0},{224,... | collective-permute-start | bytes 196616 | tf_op jit(solution)/shard_map/ppermute | solution.py:50
  43.6 8.3 %collective-permute-start.13 = (f32[4,64,64]{2,1,0:T(8,128)S(1)}, f32[4,64,64]{2,1,0:T(8,128)S(1)}, u32[]{:S(2)}, u32[]{:S(2)}) collective-permute-start(f32[4,64,64]{2,1,0:T(8,128)S(1)} %fusion.60), channel_id=1, source_target_pairs={{0,64},{32,96},{64,0},{96,32},{128,192},{160,224},{192,128},{224,1... | collective-permute-start | bytes 196616 | tf_op jit(solution)/shard_map/ppermute | solution.py:50
  46.2 10.7 %collective-permute-start.24 = (f32[64,2,1,128]{3,0,2,1:T(8,128)S(1)}, f32[64,2,1,128]{3,0,2,1:T(8,128)}, u32[]{:S(2)}, u32[]{:S(2)}) collective-permute-start(f32[64,2,1,128]{3,0,2,1:T(8,128)S(1)} %get-tuple-element.26), channel_id=1, source_target_pairs={{2,0},{4,2},{6,4},{8,6},{10,8},{12,10},{14,12},{16,14},{18,16},{20... | collective-permute-start | bytes 196616 | tf_op jit(solution)/shard_map/ppermute | solution.py:26
  46.5 11.3 %collective-permute-start.25 = (f32[64,2,1,128]{3,0,2,1:T(8,128)}, f32[64,2,1,128]{3,0,2,1:T(8,128)}, u32[]{:S(2)}, u32[]{:S(2)}) collective-permute-start(f32[64,2,1,128]{3,0,2,1:T(8,128)} %get-tuple-element.25), channel_id=1, source_target_pairs={{0,2},{2,4},{4,6},{6,8},{8,10},{10,12},{12,14},{14,16},{16,18},{18... | collective-permute-start | bytes 196616 | tf_op jit(solution)/shard_map/ppermute | solution.py:25
  52.0 13.0 %collective-permute-start.17 = (f32[4,64,64]{2,1,0:T(8,128)S(1)}, f32[4,64,64]{2,1,0:T(8,128)S(1)}, u32[]{:S(2)}, u32[]{:S(2)}) collective-permute-start(f32[4,64,64]{2,1,0:T(8,128)S(1)} %add_add_fusion.2), channel_id=1, source_target_pairs={{0,4},{2,6},{4,0},{6,2},{8,12},{10,14},{12,8},{14,10},{16,20},{18,... | collective-permute-start | bytes 196616 | tf_op jit(solution)/shard_map/ppermute | solution.py:50
  52.8 12.2 %collective-permute-start.18 = (f32[4,64,64]{2,1,0:T(8,128)S(1)}, f32[4,64,64]{2,1,0:T(8,128)S(1)}, u32[]{:S(2)}, u32[]{:S(2)}) collective-permute-start(f32[4,64,64]{2,1,0:T(8,128)S(1)} %add_add_fusion.2), channel_id=1, source_target_pairs={{0,6},{2,4},{4,2},{6,0},{8,14},{10,12},{12,10},{14,8},{16,22},{18,... | collective-permute-start | bytes 196616 | tf_op jit(solution)/shard_map/ppermute | solution.py:50
  56.2 9.2 %collective-permute-start.16 = (f32[4,64,64]{2,1,0:T(8,128)S(1)}, f32[4,64,64]{2,1,0:T(8,128)S(1)}, u32[]{:S(2)}, u32[]{:S(2)}) collective-permute-start(f32[4,64,64]{2,1,0:T(8,128)S(1)} %add_add_fusion.2), channel_id=1, source_target_pairs={{0,2},{2,0},{4,6},{6,4},{8,10},{10,8},{12,14},{14,12},{16,18},{18,... | collective-permute-start | bytes 196616 | tf_op jit(solution)/shard_map/ppermute | solution.py:50
  56.9 16.0 %collective-permute-start.23 = (f32[64,1,8,128]{3,0,2,1:T(8,128)S(1)}, f32[64,1,8,128]{3,0,2,1:T(8,128)}, u32[]{:S(2)}, u32[]{:S(2)}) collective-permute-start(f32[64,1,8,128]{3,0,2,1:T(8,128)S(1)} %get-tuple-element.28), channel_id=1, source_target_pairs={{0,32},{32,64},{64,96},{96,128},{128,160},{160,192},{192,224},{224... | collective-permute-start | bytes 786440 | tf_op jit(solution)/shard_map/ppermute | solution.py:25
  57.8 18.0 %copy-start.14 = (f32[64,4,1,128]{3,0,2,1:T(8,128)}, f32[64,4,1,128]{3,0,2,1:T(8,128)S(1)}, u32[]{:S(2)}) copy-start(f32[64,4,1,128]{3,0,2,1:T(8,128)S(1)} %pad.56) | copy-start | bytes 393220
  57.8 17.3 %collective-permute-start.22 = (f32[64,1,8,128]{3,0,2,1:T(8,128)}, f32[64,1,8,128]{3,0,2,1:T(8,128)S(1)}, u32[]{:S(2)}, u32[]{:S(2)}) collective-permute-start(f32[64,1,8,128]{3,0,2,1:T(8,128)} %get-tuple-element.27), channel_id=1, source_target_pairs={{32,0},{64,32},{96,64},{128,96},{160,128},{192,160},{224,192},{0,2... | collective-permute-start | bytes 786440 | tf_op jit(solution)/shard_map/ppermute | solution.py:26
  61.6 14.2 %copy-start.16 = (f32[64,4,1,128]{3,0,2,1:T(8,128)}, f32[64,4,1,128]{3,0,2,1:T(8,128)S(1)}, u32[]{:S(2)}) copy-start(f32[64,4,1,128]{3,0,2,1:T(8,128)S(1)} %pad.57) | copy-start | bytes 393220
  65.4 12.7 %collective-permute-start.20 = (f32[4,64,64]{2,1,0:T(8,128)S(1)}, f32[4,64,64]{2,1,0:T(8,128)S(1)}, u32[]{:S(2)}, u32[]{:S(2)}) collective-permute-start(f32[4,64,64]{2,1,0:T(8,128)S(1)} %add_add_fusion.1), channel_id=1, source_target_pairs={{0,16},{2,18},{4,20},{6,22},{8,24},{10,26},{12,28},{14,30},{16,0},... | collective-permute-start | bytes 196616 | tf_op jit(solution)/shard_map/ppermute | solution.py:50
  66.3 11.9 %collective-permute-start.21 = (f32[4,64,64]{2,1,0:T(8,128)S(1)}, f32[4,64,64]{2,1,0:T(8,128)S(1)}, u32[]{:S(2)}, u32[]{:S(2)}) collective-permute-start(f32[4,64,64]{2,1,0:T(8,128)S(1)} %add_add_fusion.1), channel_id=1, source_target_pairs={{0,24},{2,26},{4,28},{6,30},{8,16},{10,18},{12,20},{14,22},{16,8},... | collective-permute-start | bytes 196616 | tf_op jit(solution)/shard_map/ppermute | solution.py:50
  66.3 16.7 %collective-permute-start.19 = (f32[4,64,64]{2,1,0:T(8,128)S(1)}, f32[4,64,64]{2,1,0:T(8,128)S(1)}, u32[]{:S(2)}, u32[]{:S(2)}) collective-permute-start(f32[4,64,64]{2,1,0:T(8,128)S(1)} %add_add_fusion.1), channel_id=1, source_target_pairs={{0,8},{2,10},{4,12},{6,14},{8,0},{10,2},{12,4},{14,6},{16,24},{18,... | collective-permute-start | bytes 196616 | tf_op jit(solution)/shard_map/ppermute | solution.py:50
  75.8 2.3 %copy-start.3 = (f32[64,4,8,128]{3,0,2,1:T(8,128)}, f32[64,4,8,128]{3,0,2,1:T(8,128)S(1)}, u32[]{:S(2)}) copy-start(f32[64,4,8,128]{3,0,2,1:T(8,128)S(1)} %constant_dynamic-update-slice_fusion) | copy-start | bytes 3145732
  83.7 8.6 %copy-start.6 = (f32[64,1,8,128]{3,0,2,1:T(8,128)S(1)}, f32[64,1,8,128]{3,0,2,1:T(8,128)}, u32[]{:S(2)}) copy-start(f32[64,1,8,128]{3,0,2,1:T(8,128)} %copy-done.5) | copy-start | bytes 786436
  83.7 8.6 %copy-start.11 = (f32[64,4,1,128]{3,0,2,1:T(8,128)S(1)}, f32[64,4,1,128]{3,0,2,1:T(8,128)}, u32[]{:S(2)}) copy-start(f32[64,4,1,128]{3,0,2,1:T(8,128)} %copy-done.10) | copy-start | bytes 393220
  83.7 8.6 %copy-start.13 = (f32[64,4,1,128]{3,0,2,1:T(8,128)S(1)}, f32[64,4,1,128]{3,0,2,1:T(8,128)}, u32[]{:S(2)}) copy-start(f32[64,4,1,128]{3,0,2,1:T(8,128)} %copy-done.12) | copy-start | bytes 393220
  92.3 1.6 %copy-start.1 = (f32[65,4,10,128]{3,0,2,1:T(8,128)S(1)}, f32[65,4,10,128]{3,0,2,1:T(8,128)}, u32[]{:S(2)}) copy-start(f32[65,4,10,128]{3,0,2,1:T(8,128)} %copy-done) | copy-start | bytes 3993604
  92.3 1.6 %copy-start.9 = (f32[64,4,1,128]{3,0,2,1:T(8,128)S(1)}, f32[64,4,1,128]{3,0,2,1:T(8,128)}, u32[]{:S(2)}) copy-start(f32[64,4,1,128]{3,0,2,1:T(8,128)} %copy-done.8) | copy-start | bytes 393220
  92.3 1.6 %copy-start.21 = (f32[2,64,64]{2,1,0:T(8,128)S(1)}, f32[2,64,64]{2,1,0:T(8,128)}, u32[]{:S(2)}) copy-start(f32[2,64,64]{2,1,0:T(8,128)} %shard_map.68) | copy-start | bytes 98308
  94.0 1.2 %copy-start.4 = (f32[64,4,8,128]{3,0,2,1:T(8,128)S(1)}, f32[64,4,8,128]{3,0,2,1:T(8,128)}, u32[]{:S(2)}) copy-start(f32[64,4,8,128]{3,0,2,1:T(8,128)} %copy-done.3) | copy-start | bytes 3145732
  94.0 1.2 %copy-start.15 = (f32[64,4,1,128]{3,0,2,1:T(8,128)S(1)}, f32[64,4,1,128]{3,0,2,1:T(8,128)}, u32[]{:S(2)}) copy-start(f32[64,4,1,128]{3,0,2,1:T(8,128)} %copy-done.14) | copy-start | bytes 393220
  94.0 1.2 %copy-start.17 = (f32[64,4,1,128]{3,0,2,1:T(8,128)S(1)}, f32[64,4,1,128]{3,0,2,1:T(8,128)}, u32[]{:S(2)}) copy-start(f32[64,4,1,128]{3,0,2,1:T(8,128)} %copy-done.16) | copy-start | bytes 393220
  94.0 2.1 %copy-start.2 = (f32[64,4,10,130]{3,0,2,1:T(8,128)S(1)}, f32[64,4,10,130]{3,0,2,1:T(8,128)}, u32[]{:S(2)}) copy-start(f32[64,4,10,130]{3,0,2,1:T(8,128)} %select_maximum_fusion) | copy-start | bytes 3993604
  96.1 0.9 copy-start.19
  98.4 5.2 %collective-permute-start.26 = (f32[2,8,64]{2,1,0:T(8,128)S(1)}, f32[2,8,64]{2,1,0:T(8,128)S(1)}, u32[]{:S(2)}, u32[]{:S(2)}) collective-permute-start(f32[2,8,64]{2,1,0:T(8,128)S(1)} %constant_dynamic-slice_fusion), channel_id=1, source_target_pairs={{0,1},{1,0},{2,3},{3,2},{4,5},{5,4},{6,7},{7,6},{8,9},{9,8},{10,11... | collective-permute-start | bytes 12296 | tf_op jit(solution)/shard_map/ppermute | solution.py:296
  (3 other events, 2.1 us)

commit v15 on v13

--- a/solution.py
+++ b/solution.py
@@ -244,7 +244,7 @@
 
     right = INJECT * (point_source(picked[:, 0]) - point_source(picked[:, 1]))
     sides = (("gx", 1), ("gy", 2))
-    grid_axes = ("gx", "gy")
+    grid_axes = ("gy", "gx")
     stacked = jnp.concatenate([conductivity[None], initial_fields], axis=0)
     padded = padded_2(stacked, sides, 1)
     conds = conductances(padded[0])

time: 106 us -> 108 us (1.019)
  starting transfers between devices: 36.1 us -> 41.4 us
  local copies, waits for them, and re-layouts: 10.4 us -> 8.38 us
    ppermute x8, starting transfers between devices: 15 us -> 18.7 us  [padded_2(): high = lax.ppermute(bottom, axis, backward)]
    ppermute x8, waiting for transfers between devices: 1.74 us -> 4.3 us  [padded_2(): high = lax.ppermute(bottom, axis, backward)]
    ppermute x9, waiting for transfers between devices: 12.3 us -> 9.94 us  [allsum(): lax.ppermute(value, axis, [(i, i ^ d << shift) for i in range(count)])]
    ppermute x8, starting transfers between devices: 5 us -> 6.49 us  [padded_2(): low = lax.ppermute(top, axis, forward)]
  transfers between devices with their start and end apart: 27 -> 27, of which waited for: 14 -> 11; matrix products, arithmetic and copies ran while one was open for 12% -> 10% of each run, Pallas kernels for 0% -> 0%
where the time goes in v15:
time: 108 us; the launch traced here: 107 us
  starting transfers between devices  41.4 us (38%)
  waiting for transfers between devices  30 us (28%)
  other arithmetic  11.8 us (11%)
  Pallas kernels  8.6 us (8%)
  local copies, waits for them, and re-layouts  8.38 us (8%)
  matrix products  5.88 us (5%)
  between operations  1.36 us (1%)
    ppermute x8, starting transfers between devices, padded_2(): high = lax.ppermute(bottom, axis, backward)  18.7 us
    ppermute x9, starting transfers between devices, allsum(): lax.ppermute(value, axis, [(i, i ^ d << shift) for i in range(count)])  15.2 us
    ppermute x8, waiting for transfers between devices, padded_2(): low = lax.ppermute(top, axis, forward)  12.6 us
    ppermute x9, waiting for transfers between devices, allsum(): lax.ppermute(value, axis, [(i, i ^ d << shift) for i in range(count)])  9.94 us
    pallas_call x1, Pallas kernels, steps(): pl.pallas_call(steps_kernel, out_shape=jax.ShapeDtypeStruct((2, n, n), jn...  8.6 us
    unnamed x53, local copies, waits for them, and re-layouts  7.23 us
    ppermute x8, starting transfers between devices, padded_2(): low = lax.ppermute(top, axis, forward)  6.49 us
    ppermute x8, waiting for transfers between devices, padded_2(): high = lax.ppermute(bottom, axis, backward)  4.3 us
  transfers between devices with their start and end apart: 27, of which 11 were waited for; matrix products, arithmetic and copies ran while one was open for 10% of the time, Pallas kernels for 0%

profile of v15, /device:TPU:4, one launch (start us, length us, event | category | flops | bytes accessed | tf_op | source)
XLA Modules:
  0.0 107.4 jit_solution(11605715184012099625)
XLA Ops:
  0.7 1.2 %copy.35 = f32[64,2,8,128]{3,0,2,1:T(8,128)S(1)} copy(f32[64,2,8,128]{3,2,1,0:T(8,128)} %param.8) | data formatting | bytes 1048576 | tf_op args[3]
  1.9 0.7 maximum_select_fusion
  2.6 6.6 %collective-permute-start.3 = (f32[65,2,1,128]{3,0,2,1:T(8,128)S(1)}, f32[65,2,1,128]{3,0,2,1:T(8,128)S(1)}, u32[]{:S(2)}, u32[]{:S(2)}) collective-permute-start(f32[65,2,1,128]{3,0,2,1:T(8,128)S(1)} %get-tuple-element.22), channel_id=1, source_target_pairs={{2,0},{4,2},{6,4},{8,6},{10,8},{12,10},{14,12},{16,14},{18,16},{20... | collective-permute-start | bytes 199688 | tf_op jit(solution)/shard_map/ppermute | solution.py:26
  9.3 2.2 %collective-permute-start.2 = (f32[65,1,8,128]{3,0,2,1:T(8,128)S(1)}, f32[65,1,8,128]{3,0,2,1:T(8,128)S(1)}, u32[]{:S(2)}, u32[]{:S(2)}) collective-permute-start(f32[65,1,8,128]{3,0,2,1:T(8,128)S(1)} %get-tuple-element.24), channel_id=1, source_target_pairs={{32,0},{64,32},{96,64},{128,96},{160,128},{192,160},{224,192},{0,2... | collective-permute-start | bytes 798728 | tf_op jit(solution)/shard_map/ppermute | solution.py:26
  11.6 0.6 gather_fusion
  12.9 5.0 %collective-permute-done = f32[65,2,1,128]{3,0,2,1:T(8,128)S(1)} collective-permute-done((f32[65,2,1,128]{3,0,2,1:T(8,128)S(1)}, f32[65,2,1,128]{3,0,2,1:T(8,128)S(1)}, u32[]{:S(2)}, u32[]{:S(2)}) %collective-permute-start) | collective-permute-done | bytes 66592 | tf_op jit(solution)/shard_map/ppermute | solution.py:25
  17.9 0.9 collective-permute-done.1
  19.3 0.9 copy-done
  21.2 1.0 collective-permute-start.4
  22.2 0.6 collective-permute-start.6
  22.9 1.5 %collective-permute-start.7 = (f32[64,2,1,128]{3,0,2,1:T(8,128)S(1)}, f32[64,2,1,128]{3,0,2,1:T(8,128)S(1)}, u32[]{:S(2)}, u32[]{:S(2)}) collective-permute-start(f32[64,2,1,128]{3,0,2,1:T(8,128)S(1)} %get-tuple-element.33), channel_id=1, source_target_pairs={{0,2},{2,4},{4,6},{6,8},{8,10},{10,12},{12,14},{14,16},{16,18},{18... | collective-permute-start | bytes 196616 | tf_op jit(solution)/shard_map/ppermute | solution.py:25
  24.3 0.6 convolution_bitcast_fusion.3
  24.9 1.7 %collective-permute-done.6 = f32[64,2,1,128]{3,0,2,1:T(8,128)S(1)} collective-permute-done((f32[64,2,1,128]{3,0,2,1:T(8,128)S(1)}, f32[64,2,1,128]{3,0,2,1:T(8,128)S(1)}, u32[]{:S(2)}, u32[]{:S(2)}) %collective-permute-start.6) | collective-permute-done | bytes 65568 | tf_op jit(solution)/shard_map/ppermute | solution.py:26
  26.6 2.7 %collective-permute-done.7 = f32[64,2,1,128]{3,0,2,1:T(8,128)S(1)} collective-permute-done((f32[64,2,1,128]{3,0,2,1:T(8,128)S(1)}, f32[64,2,1,128]{3,0,2,1:T(8,128)S(1)}, u32[]{:S(2)}, u32[]{:S(2)}) %collective-permute-start.7) | collective-permute-done | bytes 65568 | tf_op jit(solution)/shard_map/ppermute | solution.py:25
  30.5 1.3 %collective-permute-start.8 = (f32[64,1,8,128]{3,0,2,1:T(8,128)S(1)}, f32[64,1,8,128]{3,0,2,1:T(8,128)S(1)}, u32[]{:S(2)}, u32[]{:S(2)}) collective-permute-start(f32[64,1,8,128]{3,0,2,1:T(8,128)S(1)} %get-tuple-element.32), channel_id=1, source_target_pairs={{32,0},{64,32},{96,64},{128,96},{160,128},{192,160},{224,192},{0,2... | collective-permute-start | bytes 786440 | tf_op jit(solution)/shard_map/ppermute | solution.py:26
  31.9 1.7 %collective-permute-start.11 = (f32[64,2,1,128]{3,0,2,1:T(8,128)S(1)}, f32[64,2,1,128]{3,0,2,1:T(8,128)S(1)}, u32[]{:S(2)}, u32[]{:S(2)}) collective-permute-start(f32[64,2,1,128]{3,0,2,1:T(8,128)S(1)} %get-tuple-element.29), channel_id=1, source_target_pairs={{0,2},{2,4},{4,6},{6,8},{8,10},{10,12},{12,14},{14,16},{16,18},{18... | collective-permute-start | bytes 196616 | tf_op jit(solution)/shard_map/ppermute | solution.py:25
  34.2 0.6 convolution_bitcast_fusion.2
  34.8 3.4 %collective-permute-done.11 = f32[64,2,1,128]{3,0,2,1:T(8,128)S(1)} collective-permute-done((f32[64,2,1,128]{3,0,2,1:T(8,128)S(1)}, f32[64,2,1,128]{3,0,2,1:T(8,128)S(1)}, u32[]{:S(2)}, u32[]{:S(2)}) %collective-permute-start.11) | collective-permute-done | bytes 65568 | tf_op jit(solution)/shard_map/ppermute | solution.py:25
  38.3 0.6 collective-permute-done.9
  40.0 0.6 convolution_bitcast_fusion
  40.6 0.8 collective-permute-start.13
  41.3 3.4 %collective-permute-start.14 = (f32[4,64,64]{2,1,0:T(8,128)S(1)}, f32[4,64,64]{2,1,0:T(8,128)S(1)}, u32[]{:S(2)}, u32[]{:S(2)}) collective-permute-start(f32[4,64,64]{2,1,0:T(8,128)S(1)} %pad_maximum_fusion.29), channel_id=1, source_target_pairs={{0,6},{2,4},{4,2},{6,0},{8,14},{10,12},{12,10},{14,8},{16,22},{18,... | collective-permute-start | bytes 196616 | tf_op jit(solution)/shard_map/ppermute | solution.py:50
  44.9 0.8 slice_select_fusion.1
  45.7 5.1 %collective-permute-done.13 = f32[4,64,64]{2,1,0:T(8,128)S(1)} collective-permute-done((f32[4,64,64]{2,1,0:T(8,128)S(1)}, f32[4,64,64]{2,1,0:T(8,128)S(1)}, u32[]{:S(2)}, u32[]{:S(2)}) %collective-permute-start.13) | collective-permute-done | bytes 65568 | tf_op jit(solution)/shard_map/ppermute | solution.py:50
  50.7 0.6 collective-permute-done.12
  51.4 0.9 collective-permute-start.16
  52.6 6.3 %collective-permute-start.15 = (f32[4,64,64]{2,1,0:T(8,128)S(1)}, f32[4,64,64]{2,1,0:T(8,128)S(1)}, u32[]{:S(2)}, u32[]{:S(2)}) collective-permute-start(f32[4,64,64]{2,1,0:T(8,128)S(1)} %add_add_fusion.2), channel_id=1, source_target_pairs={{0,8},{2,10},{4,12},{6,14},{8,0},{10,2},{12,4},{14,6},{16,24},{18,... | collective-permute-start | bytes 196616 | tf_op jit(solution)/shard_map/ppermute | solution.py:50
  58.9 0.7 slice_select_fusion.6
  59.5 3.3 %collective-permute-start.25 = (f32[64,2,1,128]{3,0,2,1:T(8,128)}, f32[64,2,1,128]{3,0,2,1:T(8,128)S(1)}, u32[]{:S(2)}, u32[]{:S(2)}) collective-permute-start(f32[64,2,1,128]{3,0,2,1:T(8,128)} %get-tuple-element.25), channel_id=1, source_target_pairs={{0,2},{2,4},{4,6},{6,8},{8,10},{10,12},{12,14},{14,16},{16,18},{18... | collective-permute-start | bytes 196616 | tf_op jit(solution)/shard_map/ppermute | solution.py:25
  62.8 4.2 %collective-permute-done.15 = f32[4,64,64]{2,1,0:T(8,128)S(1)} collective-permute-done((f32[4,64,64]{2,1,0:T(8,128)S(1)}, f32[4,64,64]{2,1,0:T(8,128)S(1)}, u32[]{:S(2)}, u32[]{:S(2)}) %collective-permute-start.15) | collective-permute-done | bytes 65568 | tf_op jit(solution)/shard_map/ppermute | solution.py:50
  67.2 6.9 %collective-permute-start.22 = (f32[64,1,8,128]{3,0,2,1:T(8,128)}, f32[64,1,8,128]{3,0,2,1:T(8,128)S(1)}, u32[]{:S(2)}, u32[]{:S(2)}) collective-permute-start(f32[64,1,8,128]{3,0,2,1:T(8,128)} %get-tuple-element.27), channel_id=1, source_target_pairs={{32,0},{64,32},{96,64},{128,96},{160,128},{192,160},{224,192},{0,2... | collective-permute-start | bytes 786440 | tf_op jit(solution)/shard_map/ppermute | solution.py:26
  74.3 1.2 %collective-permute-start.21 = (f32[4,64,64]{2,1,0:T(8,128)S(1)}, f32[4,64,64]{2,1,0:T(8,128)S(1)}, u32[]{:S(2)}, u32[]{:S(2)}) collective-permute-start(f32[4,64,64]{2,1,0:T(8,128)S(1)} %add.204), channel_id=1, source_target_pairs={{0,192},{32,224},{64,128},{96,160},{128,64},{160,96},{192,0},{224,... | collective-permute-start | bytes 196616 | tf_op jit(solution)/shard_map/ppermute | solution.py:50
  75.5 2.2 %collective-permute-start.19 = (f32[4,64,64]{2,1,0:T(8,128)S(1)}, f32[4,64,64]{2,1,0:T(8,128)S(1)}, u32[]{:S(2)}, u32[]{:S(2)}) collective-permute-start(f32[4,64,64]{2,1,0:T(8,128)S(1)} %add.204), channel_id=1, source_target_pairs={{0,64},{32,96},{64,0},{96,32},{128,192},{160,224},{192,128},{224,1... | collective-permute-start | bytes 196616 | tf_op jit(solution)/shard_map/ppermute | solution.py:50
  77.8 1.0 constant_dynamic-update-slice_fusion.2
  78.8 1.2 %constant_dynamic-update-slice_fusion.1 = f32[64,4,8,128]{3,0,2,1:T(8,128)S(1)} fusion(f32[64,4,8,128]{3,0,2,1:T(8,128)S(1)} %constant_dynamic-update-slice_fusion.2, f32[64,2,8,128]{3,2,1,0:T(8,128)} %param.9), kind=kLoop, calls=%fused_computation.186 | loop fusion | bytes 1048576
  80.0 2.6 %collective-permute-done.22 = f32[64,1,8,128]{3,0,2,1:T(8,128)S(1)} collective-permute-done((f32[64,1,8,128]{3,0,2,1:T(8,128)}, f32[64,1,8,128]{3,0,2,1:T(8,128)S(1)}, u32[]{:S(2)}, u32[]{:S(2)}) %collective-permute-start.22) | collective-permute-done | bytes 262176 | tf_op jit(solution)/shard_map/ppermute | solution.py:26
  82.5 0.7 copy-done.18
  83.3 2.2 %select_maximum_fusion = f32[64,4,10,130]{3,0,2,1:T(8,128)} fusion(f32[64,4,1,128]{3,0,2,1:T(8,128)S(1)} %pad.56, f32[64,4,8,128]{3,0,2,1:T(8,128)S(1)} %constant_dynamic-update-slice_fusion, f32[64,4,1,128]{3,0,2,1:T(8,128)S(1)} %pad.57), kind=kLoop, calls=%fused_computation.11 | loop fusion | flops 2662400 | bytes 2641920 | tf_op jit(solution)/shard_map/concatenate | solution.py:35
  85.6 0.7 add_add_fusion.grams_ref
  86.3 8.6 %shard_map.68 = f32[2,64,64]{2,1,0:T(8,128)} custom-call(f32[4,64,64]{2,1,0:T(8,128)} %add_add_fusion.grams_ref), custom_call_target="tpu_custom_call" | custom-call | flops 20000000000 | bytes 98304 | tf_op jit(solution)/shard_map/pallas_call | solution.py:219
  94.9 2.1 %fusion.48 = f32[64,4,10,128]{3,0,2,1:T(8,128)S(1)} fusion(f32[2,64,64]{2,1,0:T(8,128)} %shard_map.68, f32[64,4,1,128]{3,0,2,1:T(8,128)S(1)} %copy-done.11, f32[64,1,8,128]{3,0,2,1:T(8,128)S(1)} %collective-permute-done.8, f32[64,2,8,128]{3,0,2,1:T(8,128)S(1)} %fusion.28, f32[64,1,8,128]{3,0,2,1:T(8,128)S(1)} %copy-done.6, f32[64,4,1,128]{3,0,2,1:T(8,128)S(1)} %copy-done.13), kind=kOutput, calls=%fused_computation.157 | convolution fusion | flops 252968960 | bytes 2654208 | tf_op jit(solution)/shard_map/axyz,ab->bxyz/dot_general | solution.py:84
  97.1 1.5 %fusion.1 = f32[64,4,10,128]{3,0,2,1:T(8,128)S(1)} fusion(f32[64,4,10,128]{3,0,2,1:T(8,128)S(1)} %fusion.48, f32[2,64,64]{2,1,0:T(8,128)S(1)} %copy-done.21, f32[65,4,10,128]{3,0,2,1:T(8,128)S(1)} %copy-done.1, f32[64,4,1,128]{3,0,2,1:T(8,128)S(1)} %pad.50, f32[64,1,8,128]{3,0,2,1:T(8,128)S(1)} %collective-permute-done.4, ...), kind=kOutput, calls=%fused_computation.16 | convolution fusion | flops 253624320 | bytes 5275648 | tf_op jit(solution)/shard_map/axyz,ab->bxyz/dot_general | solution.py:84
  99.2 0.6 fusion.10
  100.2 1.2 %fusion.12 = f32[3,8,128]{2,1,0:T(8,128)S(1)} fusion(f32[64,4,10,128]{3,0,2,1:T(8,128)S(1)} %fusion.1, f32[64,1,8,128]{3,0,2,1:T(8,128)S(1)} %copy-done.19, f32[64,2,8,128]{3,0,2,1:T(8,128)S(1)} %copy.44, f32[64,1,8,128]{3,0,2,1:T(8,128)} %collective-permute-done.23), kind=kLoop, calls=%fused_computation.37 | loop fusion | flops 1176576 | bytes 2633728 | tf_op jit(solution)/shard_map/reduce_sum | solution.py:102
  101.5 0.8 collective-permute-start.26
  102.4 1.1 %copy.50 = f32[64,2,8,128]{3,2,1,0:T(8,128)} copy(f32[64,2,8,128]{3,0,2,1:T(8,128)S(1)} %slice.407) | data formatting | bytes 1048576
  103.5 3.2 %collective-permute-done.26 = f32[2,8,64]{2,1,0:T(8,128)S(1)} collective-permute-done((f32[2,8,64]{2,1,0:T(8,128)S(1)}, f32[2,8,64]{2,1,0:T(8,128)S(1)}, u32[]{:S(2)}, u32[]{:S(2)}) %collective-permute-start.26) | collective-permute-done | bytes 4128 | tf_op jit(solution)/shard_map/ppermute | solution.py:293
  106.7 0.7 dynamic-slice_add_fusion
  (134 shorter events, 7.2 us)
Async XLA Ops:
  0.6 8.6 %copy-start.20 = (f32[2,8,128]{2,1,0:T(8,128)S(1)}, f32[2,8,128]{2,1,0:T(8,128)}, u32[]{:S(2)}) copy-start(f32[2,8,128]{2,1,0:T(8,128)} %param.5) | copy-start | bytes 24580
  0.6 10.8 %copy-start.23 = (s32[64]{0:T(128)S(1)}, s32[64]{0:T(128)}, u32[]{:S(2)}) copy-start(s32[64]{0:T(128)} %param.7) | copy-start | bytes 772
  0.7 10.8 %copy-start.22 = (s32[128,2]{0,1:T(2,128)S(1)}, s32[128,2]{0,1:T(2,128)}, u32[]{:S(2)}) copy-start(s32[128,2]{0,1:T(2,128)} %param.6) | copy-start | bytes 3076
  2.6 10.3 %collective-permute-start.3 = (f32[65,2,1,128]{3,0,2,1:T(8,128)S(1)}, f32[65,2,1,128]{3,0,2,1:T(8,128)S(1)}, u32[]{:S(2)}, u32[]{:S(2)}) collective-permute-start(f32[65,2,1,128]{3,0,2,1:T(8,128)S(1)} %get-tuple-element.22), channel_id=1, source_target_pairs={{2,0},{4,2},{6,4},{8,6},{10,8},{12,10},{14,12},{16,14},{18,16},{20... | collective-permute-start | bytes 199688 | tf_op jit(solution)/shard_map/ppermute | solution.py:26
  9.3 8.7 %collective-permute-start.2 = (f32[65,1,8,128]{3,0,2,1:T(8,128)S(1)}, f32[65,1,8,128]{3,0,2,1:T(8,128)S(1)}, u32[]{:S(2)}, u32[]{:S(2)}) collective-permute-start(f32[65,1,8,128]{3,0,2,1:T(8,128)S(1)} %get-tuple-element.24), channel_id=1, source_target_pairs={{32,0},{64,32},{96,64},{128,96},{160,128},{192,160},{224,192},{0,2... | collective-permute-start | bytes 798728 | tf_op jit(solution)/shard_map/ppermute | solution.py:26
  11.5 7.4 %collective-permute-start.1 = (f32[65,1,8,128]{3,0,2,1:T(8,128)S(1)}, f32[65,1,8,128]{3,0,2,1:T(8,128)S(1)}, u32[]{:S(2)}, u32[]{:S(2)}) collective-permute-start(f32[65,1,8,128]{3,0,2,1:T(8,128)S(1)} %get-tuple-element.23), channel_id=1, source_target_pairs={{0,32},{32,64},{64,96},{96,128},{128,160},{160,192},{192,224},{224... | collective-permute-start | bytes 798728 | tf_op jit(solution)/shard_map/ppermute | solution.py:25
  11.5 6.5 %collective-permute-start = (f32[65,2,1,128]{3,0,2,1:T(8,128)S(1)}, f32[65,2,1,128]{3,0,2,1:T(8,128)S(1)}, u32[]{:S(2)}, u32[]{:S(2)}) collective-permute-start(f32[65,2,1,128]{3,0,2,1:T(8,128)S(1)} %get-tuple-element.21), channel_id=1, source_target_pairs={{0,2},{2,4},{4,6},{6,8},{8,10},{10,12},{12,14},{14,16},{16,18},{18... | collective-permute-start | bytes 199688 | tf_op jit(solution)/shard_map/ppermute | solution.py:25
  19.0 1.1 %copy-start = (f32[65,4,10,128]{3,0,2,1:T(8,128)}, f32[65,4,10,128]{3,0,2,1:T(8,128)S(1)}, u32[]{:S(2)}) copy-start(f32[65,4,10,128]{3,0,2,1:T(8,128)S(1)} %pad_maximum_fusion) | copy-start | bytes 3993604
  21.2 8.0 %collective-permute-start.4 = (f32[64,1,8,128]{3,0,2,1:T(8,128)S(1)}, f32[64,1,8,128]{3,0,2,1:T(8,128)S(1)}, u32[]{:S(2)}, u32[]{:S(2)}) collective-permute-start(f32[64,1,8,128]{3,0,2,1:T(8,128)S(1)} %get-tuple-element.36), channel_id=1, source_target_pairs={{32,0},{64,32},{96,64},{128,96},{160,128},{192,160},{224,192},{0,2... | collective-permute-start | bytes 786440 | tf_op jit(solution)/shard_map/ppermute | solution.py:26
  22.2 7.1 %collective-permute-start.5 = (f32[64,1,8,128]{3,0,2,1:T(8,128)S(1)}, f32[64,1,8,128]{3,0,2,1:T(8,128)S(1)}, u32[]{:S(2)}, u32[]{:S(2)}) collective-permute-start(f32[64,1,8,128]{3,0,2,1:T(8,128)S(1)} %get-tuple-element.35), channel_id=1, source_target_pairs={{0,32},{32,64},{64,96},{96,128},{128,160},{160,192},{192,224},{224... | collective-permute-start | bytes 786440 | tf_op jit(solution)/shard_map/ppermute | solution.py:25
  22.2 4.3 %collective-permute-start.6 = (f32[64,2,1,128]{3,0,2,1:T(8,128)S(1)}, f32[64,2,1,128]{3,0,2,1:T(8,128)S(1)}, u32[]{:S(2)}, u32[]{:S(2)}) collective-permute-start(f32[64,2,1,128]{3,0,2,1:T(8,128)S(1)} %get-tuple-element.34), channel_id=1, source_target_pairs={{2,0},{4,2},{6,4},{8,6},{10,8},{12,10},{14,12},{16,14},{18,16},{20... | collective-permute-start | bytes 196616 | tf_op jit(solution)/shard_map/ppermute | solution.py:26
  22.9 6.4 %collective-permute-start.7 = (f32[64,2,1,128]{3,0,2,1:T(8,128)S(1)}, f32[64,2,1,128]{3,0,2,1:T(8,128)S(1)}, u32[]{:S(2)}, u32[]{:S(2)}) collective-permute-start(f32[64,2,1,128]{3,0,2,1:T(8,128)S(1)} %get-tuple-element.33), channel_id=1, source_target_pairs={{0,2},{2,4},{4,6},{6,8},{8,10},{10,12},{12,14},{14,16},{16,18},{18... | collective-permute-start | bytes 196616 | tf_op jit(solution)/shard_map/ppermute | solution.py:25
  30.4 4.3 %collective-permute-start.10 = (f32[64,2,1,128]{3,0,2,1:T(8,128)S(1)}, f32[64,2,1,128]{3,0,2,1:T(8,128)S(1)}, u32[]{:S(2)}, u32[]{:S(2)}) collective-permute-start(f32[64,2,1,128]{3,0,2,1:T(8,128)S(1)} %get-tuple-element.30), channel_id=1, source_target_pairs={{2,0},{4,2},{6,4},{8,6},{10,8},{12,10},{14,12},{16,14},{18,16},{20... | collective-permute-start | bytes 196616 | tf_op jit(solution)/shard_map/ppermute | solution.py:26
  30.5 7.7 %collective-permute-start.8 = (f32[64,1,8,128]{3,0,2,1:T(8,128)S(1)}, f32[64,1,8,128]{3,0,2,1:T(8,128)S(1)}, u32[]{:S(2)}, u32[]{:S(2)}) collective-permute-start(f32[64,1,8,128]{3,0,2,1:T(8,128)S(1)} %get-tuple-element.32), channel_id=1, source_target_pairs={{32,0},{64,32},{96,64},{128,96},{160,128},{192,160},{224,192},{0,2... | collective-permute-start | bytes 786440 | tf_op jit(solution)/shard_map/ppermute | solution.py:26
  31.9 7.0 %collective-permute-start.9 = (f32[64,1,8,128]{3,0,2,1:T(8,128)S(1)}, f32[64,1,8,128]{3,0,2,1:T(8,128)S(1)}, u32[]{:S(2)}, u32[]{:S(2)}) collective-permute-start(f32[64,1,8,128]{3,0,2,1:T(8,128)S(1)} %get-tuple-element.31), channel_id=1, source_target_pairs={{0,32},{32,64},{64,96},{96,128},{128,160},{160,192},{192,224},{224... | collective-permute-start | bytes 786440 | tf_op jit(solution)/shard_map/ppermute | solution.py:25
  31.9 6.4 %collective-permute-start.11 = (f32[64,2,1,128]{3,0,2,1:T(8,128)S(1)}, f32[64,2,1,128]{3,0,2,1:T(8,128)S(1)}, u32[]{:S(2)}, u32[]{:S(2)}) collective-permute-start(f32[64,2,1,128]{3,0,2,1:T(8,128)S(1)} %get-tuple-element.29), channel_id=1, source_target_pairs={{0,2},{2,4},{4,6},{6,8},{8,10},{10,12},{12,14},{14,16},{16,18},{18... | collective-permute-start | bytes 196616 | tf_op jit(solution)/shard_map/ppermute | solution.py:25
  34.8 4.6 %copy-start.10 = (f32[64,4,1,128]{3,0,2,1:T(8,128)}, f32[64,4,1,128]{3,0,2,1:T(8,128)S(1)}, u32[]{:S(2)}) copy-start(f32[64,4,1,128]{3,0,2,1:T(8,128)S(1)} %pad.53) | copy-start | bytes 393220
  38.3 1.1 %copy-start.12 = (f32[64,4,1,128]{3,0,2,1:T(8,128)}, f32[64,4,1,128]{3,0,2,1:T(8,128)S(1)}, u32[]{:S(2)}) copy-start(f32[64,4,1,128]{3,0,2,1:T(8,128)S(1)} %pad.54) | copy-start | bytes 393220
  39.9 4.8 %copy-start.7 = (f32[64,2,8,128]{3,2,1,0:T(8,128)S(1)}, f32[64,2,8,128]{3,2,1,0:T(8,128)}, u32[]{:S(2)}) copy-start(f32[64,2,8,128]{3,2,1,0:T(8,128)} %param.9) | copy-start | bytes 1572868
  40.6 10.2 %collective-permute-start.13 = (f32[4,64,64]{2,1,0:T(8,128)S(1)}, f32[4,64,64]{2,1,0:T(8,128)S(1)}, u32[]{:S(2)}, u32[]{:S(2)}) collective-permute-start(f32[4,64,64]{2,1,0:T(8,128)S(1)} %pad_maximum_fusion.29), channel_id=1, source_target_pairs={{0,4},{2,6},{4,0},{6,2},{8,12},{10,14},{12,8},{14,10},{16,20},{18,... | collective-permute-start | bytes 196616 | tf_op jit(solution)/shard_map/ppermute | solution.py:50
  41.3 9.4 %collective-permute-start.14 = (f32[4,64,64]{2,1,0:T(8,128)S(1)}, f32[4,64,64]{2,1,0:T(8,128)S(1)}, u32[]{:S(2)}, u32[]{:S(2)}) collective-permute-start(f32[4,64,64]{2,1,0:T(8,128)S(1)} %pad_maximum_fusion.29), channel_id=1, source_target_pairs={{0,6},{2,4},{4,2},{6,0},{8,14},{10,12},{12,10},{14,8},{16,22},{18,... | collective-permute-start | bytes 196616 | tf_op jit(solution)/shard_map/ppermute | solution.py:50
  44.7 6.6 %collective-permute-start.12 = (f32[4,64,64]{2,1,0:T(8,128)S(1)}, f32[4,64,64]{2,1,0:T(8,128)S(1)}, u32[]{:S(2)}, u32[]{:S(2)}) collective-permute-start(f32[4,64,64]{2,1,0:T(8,128)S(1)} %pad_maximum_fusion.29), channel_id=1, source_target_pairs={{0,2},{2,0},{4,6},{6,4},{8,10},{10,8},{12,14},{14,12},{16,18},{18,... | collective-permute-start | bytes 196616 | tf_op jit(solution)/shard_map/ppermute | solution.py:50
  51.4 8.2 %collective-permute-start.16 = (f32[4,64,64]{2,1,0:T(8,128)S(1)}, f32[4,64,64]{2,1,0:T(8,128)S(1)}, u32[]{:S(2)}, u32[]{:S(2)}) collective-permute-start(f32[4,64,64]{2,1,0:T(8,128)S(1)} %add_add_fusion.2), channel_id=1, source_target_pairs={{0,16},{2,18},{4,20},{6,22},{8,24},{10,26},{12,28},{14,30},{16,0},... | collective-permute-start | bytes 196616 | tf_op jit(solution)/shard_map/ppermute | solution.py:50
  52.3 10.5 %collective-permute-start.17 = (f32[4,64,64]{2,1,0:T(8,128)S(1)}, f32[4,64,64]{2,1,0:T(8,128)S(1)}, u32[]{:S(2)}, u32[]{:S(2)}) collective-permute-start(f32[4,64,64]{2,1,0:T(8,128)S(1)} %add_add_fusion.2), channel_id=1, source_target_pairs={{0,24},{2,26},{4,28},{6,30},{8,16},{10,18},{12,20},{14,22},{16,8},... | collective-permute-start | bytes 196616 | tf_op jit(solution)/shard_map/ppermute | solution.py:50
  52.6 14.5 %collective-permute-start.15 = (f32[4,64,64]{2,1,0:T(8,128)S(1)}, f32[4,64,64]{2,1,0:T(8,128)S(1)}, u32[]{:S(2)}, u32[]{:S(2)}) collective-permute-start(f32[4,64,64]{2,1,0:T(8,128)S(1)} %add_add_fusion.2), channel_id=1, source_target_pairs={{0,8},{2,10},{4,12},{6,14},{8,0},{10,2},{12,4},{14,6},{16,24},{18,... | collective-permute-start | bytes 196616 | tf_op jit(solution)/shard_map/ppermute | solution.py:50
  59.5 14.6 %collective-permute-start.24 = (f32[64,2,1,128]{3,0,2,1:T(8,128)}, f32[64,2,1,128]{3,0,2,1:T(8,128)S(1)}, u32[]{:S(2)}, u32[]{:S(2)}) collective-permute-start(f32[64,2,1,128]{3,0,2,1:T(8,128)} %get-tuple-element.26), channel_id=1, source_target_pairs={{2,0},{4,2},{6,4},{8,6},{10,8},{12,10},{14,12},{16,14},{18,16},{20... | collective-permute-start | bytes 196616 | tf_op jit(solution)/shard_map/ppermute | solution.py:26
  59.5 18.3 %collective-permute-start.23 = (f32[64,1,8,128]{3,0,2,1:T(8,128)S(1)}, f32[64,1,8,128]{3,0,2,1:T(8,128)}, u32[]{:S(2)}, u32[]{:S(2)}) collective-permute-start(f32[64,1,8,128]{3,0,2,1:T(8,128)S(1)} %get-tuple-element.28), channel_id=1, source_target_pairs={{0,32},{32,64},{64,96},{96,128},{128,160},{160,192},{192,224},{224... | collective-permute-start | bytes 786440 | tf_op jit(solution)/shard_map/ppermute | solution.py:25
  59.5 14.6 %collective-permute-start.25 = (f32[64,2,1,128]{3,0,2,1:T(8,128)}, f32[64,2,1,128]{3,0,2,1:T(8,128)S(1)}, u32[]{:S(2)}, u32[]{:S(2)}) collective-permute-start(f32[64,2,1,128]{3,0,2,1:T(8,128)} %get-tuple-element.25), channel_id=1, source_target_pairs={{0,2},{2,4},{4,6},{6,8},{8,10},{10,12},{12,14},{14,16},{16,18},{18... | collective-permute-start | bytes 196616 | tf_op jit(solution)/shard_map/ppermute | solution.py:25
  67.1 7.1 %collective-permute-start.18 = (f32[4,64,64]{2,1,0:T(8,128)S(1)}, f32[4,64,64]{2,1,0:T(8,128)S(1)}, u32[]{:S(2)}, u32[]{:S(2)}) collective-permute-start(f32[4,64,64]{2,1,0:T(8,128)S(1)} %add_add_fusion.1), channel_id=1, source_target_pairs={{0,32},{32,0},{64,96},{96,64},{128,160},{160,128},{192,224},{224,1... | collective-permute-start | bytes 196616 | tf_op jit(solution)/shard_map/ppermute | solution.py:46
  67.2 15.3 %collective-permute-start.22 = (f32[64,1,8,128]{3,0,2,1:T(8,128)}, f32[64,1,8,128]{3,0,2,1:T(8,128)S(1)}, u32[]{:S(2)}, u32[]{:S(2)}) collective-permute-start(f32[64,1,8,128]{3,0,2,1:T(8,128)} %get-tuple-element.27), channel_id=1, source_target_pairs={{32,0},{64,32},{96,64},{128,96},{160,128},{192,160},{224,192},{0,2... | collective-permute-start | bytes 786440 | tf_op jit(solution)/shard_map/ppermute | solution.py:26
  74.1 9.2 %copy-start.14 = (f32[64,4,1,128]{3,0,2,1:T(8,128)}, f32[64,4,1,128]{3,0,2,1:T(8,128)S(1)}, u32[]{:S(2)}) copy-start(f32[64,4,1,128]{3,0,2,1:T(8,128)S(1)} %pad.56) | copy-start | bytes 393220
  74.2 11.4 %copy-start.16 = (f32[64,4,1,128]{3,0,2,1:T(8,128)}, f32[64,4,1,128]{3,0,2,1:T(8,128)S(1)}, u32[]{:S(2)}) copy-start(f32[64,4,1,128]{3,0,2,1:T(8,128)S(1)} %pad.57) | copy-start | bytes 393220
  74.2 11.3 %collective-permute-start.20 = (f32[4,64,64]{2,1,0:T(8,128)S(1)}, f32[4,64,64]{2,1,0:T(8,128)S(1)}, u32[]{:S(2)}, u32[]{:S(2)}) collective-permute-start(f32[4,64,64]{2,1,0:T(8,128)S(1)} %add.204), channel_id=1, source_target_pairs={{0,128},{32,160},{64,192},{96,224},{128,0},{160,32},{192,64},{224,... | collective-permute-start | bytes 196616 | tf_op jit(solution)/shard_map/ppermute | solution.py:50
  74.3 11.2 %collective-permute-start.21 = (f32[4,64,64]{2,1,0:T(8,128)S(1)}, f32[4,64,64]{2,1,0:T(8,128)S(1)}, u32[]{:S(2)}, u32[]{:S(2)}) collective-permute-start(f32[4,64,64]{2,1,0:T(8,128)S(1)} %add.204), channel_id=1, source_target_pairs={{0,192},{32,224},{64,128},{96,160},{128,64},{160,96},{192,0},{224,... | collective-permute-start | bytes 196616 | tf_op jit(solution)/shard_map/ppermute | solution.py:50
  75.5 10.0 %collective-permute-start.19 = (f32[4,64,64]{2,1,0:T(8,128)S(1)}, f32[4,64,64]{2,1,0:T(8,128)S(1)}, u32[]{:S(2)}, u32[]{:S(2)}) collective-permute-start(f32[4,64,64]{2,1,0:T(8,128)S(1)} %add.204), channel_id=1, source_target_pairs={{0,64},{32,96},{64,0},{96,32},{128,192},{160,224},{192,128},{224,1... | collective-permute-start | bytes 196616 | tf_op jit(solution)/shard_map/ppermute | solution.py:50
  83.3 2.3 %copy-start.3 = (f32[64,4,8,128]{3,0,2,1:T(8,128)}, f32[64,4,8,128]{3,0,2,1:T(8,128)S(1)}, u32[]{:S(2)}) copy-start(f32[64,4,8,128]{3,0,2,1:T(8,128)S(1)} %constant_dynamic-update-slice_fusion) | copy-start | bytes 3145732
  86.3 8.6 %copy-start.6 = (f32[64,1,8,128]{3,0,2,1:T(8,128)S(1)}, f32[64,1,8,128]{3,0,2,1:T(8,128)}, u32[]{:S(2)}) copy-start(f32[64,1,8,128]{3,0,2,1:T(8,128)} %copy-done.5) | copy-start | bytes 786436
  86.3 8.6 %copy-start.11 = (f32[64,4,1,128]{3,0,2,1:T(8,128)S(1)}, f32[64,4,1,128]{3,0,2,1:T(8,128)}, u32[]{:S(2)}) copy-start(f32[64,4,1,128]{3,0,2,1:T(8,128)} %copy-done.10) | copy-start | bytes 393220
  86.3 8.6 %copy-start.13 = (f32[64,4,1,128]{3,0,2,1:T(8,128)S(1)}, f32[64,4,1,128]{3,0,2,1:T(8,128)}, u32[]{:S(2)}) copy-start(f32[64,4,1,128]{3,0,2,1:T(8,128)} %copy-done.12) | copy-start | bytes 393220
  94.9 2.2 %copy-start.1 = (f32[65,4,10,128]{3,0,2,1:T(8,128)S(1)}, f32[65,4,10,128]{3,0,2,1:T(8,128)}, u32[]{:S(2)}) copy-start(f32[65,4,10,128]{3,0,2,1:T(8,128)} %copy-done) | copy-start | bytes 3993604
  94.9 2.2 %copy-start.9 = (f32[64,4,1,128]{3,0,2,1:T(8,128)S(1)}, f32[64,4,1,128]{3,0,2,1:T(8,128)}, u32[]{:S(2)}) copy-start(f32[64,4,1,128]{3,0,2,1:T(8,128)} %copy-done.8) | copy-start | bytes 393220
  94.9 2.2 %copy-start.21 = (f32[2,64,64]{2,1,0:T(8,128)S(1)}, f32[2,64,64]{2,1,0:T(8,128)}, u32[]{:S(2)}) copy-start(f32[2,64,64]{2,1,0:T(8,128)} %shard_map.68) | copy-start | bytes 98308
  97.1 1.6 %copy-start.4 = (f32[64,4,8,128]{3,0,2,1:T(8,128)S(1)}, f32[64,4,8,128]{3,0,2,1:T(8,128)}, u32[]{:S(2)}) copy-start(f32[64,4,8,128]{3,0,2,1:T(8,128)} %copy-done.3) | copy-start | bytes 3145732
  97.1 1.6 %copy-start.15 = (f32[64,4,1,128]{3,0,2,1:T(8,128)S(1)}, f32[64,4,1,128]{3,0,2,1:T(8,128)}, u32[]{:S(2)}) copy-start(f32[64,4,1,128]{3,0,2,1:T(8,128)} %copy-done.14) | copy-start | bytes 393220
  97.1 1.6 %copy-start.17 = (f32[64,4,1,128]{3,0,2,1:T(8,128)S(1)}, f32[64,4,1,128]{3,0,2,1:T(8,128)}, u32[]{:S(2)}) copy-start(f32[64,4,1,128]{3,0,2,1:T(8,128)} %copy-done.16) | copy-start | bytes 393220
  97.1 2.1 %copy-start.2 = (f32[64,4,10,130]{3,0,2,1:T(8,128)S(1)}, f32[64,4,10,130]{3,0,2,1:T(8,128)}, u32[]{:S(2)}) copy-start(f32[64,4,10,130]{3,0,2,1:T(8,128)} %select_maximum_fusion) | copy-start | bytes 3993604
  99.2 0.9 copy-start.19
  101.5 5.2 %collective-permute-start.26 = (f32[2,8,64]{2,1,0:T(8,128)S(1)}, f32[2,8,64]{2,1,0:T(8,128)S(1)}, u32[]{:S(2)}, u32[]{:S(2)}) collective-permute-start(f32[2,8,64]{2,1,0:T(8,128)S(1)} %constant_dynamic-slice_fusion), channel_id=1, source_target_pairs={{0,1},{1,0},{2,3},{3,2},{4,5},{5,4},{6,7},{7,6},{8,9},{9,8},{10,11... | collective-permute-start | bytes 12296 | tf_op jit(solution)/shard_map/ppermute | solution.py:293
  (3 other events, 2.1 us)
